TPU v7x, 32 devices: a whole 2x2x4 slice. The times are simulated.
32 devices in a mesh: blk: 8 (over y, x, core), help: 4 (over z).
Axes of the slice: x: 2, y: 2, z: 4, core: 2. Of those that a mesh axis runs over, the one named last changes fastest.
Arguments:
- queries: bfloat16 [512, 8192], P('help', 'blk'), may hold values from -200 to 200
- query_key_value: bfloat16 [512, 2048], P('help'), may hold values from -8 to 8
- cached_key_value: bfloat16 [16384, 2048], P(('blk', 'help')), may hold values from -6 to 6
- selected: int32 [4, 64, 8], P('help'), may hold values from 0 to 15, as said below
Outputs:
- attended: float32 [512, 8192], P('help', 'blk')
Inputs may be any that keep to these rules, and one draw needn't show every extreme that they name: `selected`: each query block and head selects 8 distinct context blocks, at most one of each run of 2 blocks c * 2 to (c + 1) * 2 - 1.
All inputs are finite; a program needn't handle non-finite values.
Results may differ from a plain program's by a relative error of at most 0.0058.
Values may be sent and summed in bfloat16 or wider, within the bound.
No kernel may reach another device: no remote copies, remote signals or barrier semaphores. Data moves between devices by JAX's collectives and lax.ppermute only.
A program may use at most 128 MiB of HBM per device.

v0:
```python
import math

import jax
import jax.numpy as jnp
from jax import lax
from jax.sharding import PartitionSpec as P

HEAD_SIZE = 128
QUERY_HEADS = 64
KEY_VALUE_HEADS = 8
BLOCK_TOKENS = 1024
QUERY_GROUP_ROWS = 128


def from_behind(block, axis, distance):
    devices = range(lax.axis_size(axis))
    route = [((i - distance) % len(devices), i) for i in devices]
    return lax.ppermute(block, axis, route)


def local(queries, query_key_value, cached_key_value, selected):
    rows = queries.shape[0]
    heads_per_unit = queries.shape[1] // HEAD_SIZE
    blocks_per_unit = rows // QUERY_GROUP_ROWS
    head_group = QUERY_HEADS // KEY_VALUE_HEADS
    scale = 1.0 / math.sqrt(HEAD_SIZE)
    nshard = lax.axis_size("blk")
    worker_rank = lax.axis_index("blk")
    quer = queries.reshape(blocks_per_unit, QUERY_GROUP_ROWS, heads_per_unit, HEAD_SIZE)
    fresh_state = query_key_value.reshape(
        blocks_per_unit, QUERY_GROUP_ROWS, 2, KEY_VALUE_HEADS, HEAD_SIZE
    )
    causal = jnp.arange(QUERY_GROUP_ROWS)[:, None] >= jnp.arange(QUERY_GROUP_ROWS)[None, :]

    def attend_block(
        softmax_state, query_portion, leading_head, selection_table, lane_count, shard_piece
    ):
        best_now, total_now, accum_now = softmax_state
        count = query_portion.shape[2]
        key_block = selection_table.shape[0] // lane_count
        picks = lax.dynamic_slice_in_dim(selected, leading_head, count, 1)
        hit = picks // key_block == shard_piece
        local_part = jnp.sum(jnp.where(hit, picks % key_block, 0), axis=2)
        valid = jnp.any(hit, axis=2)
        worker_lanes = (leading_head + jnp.arange(count, dtype=jnp.int32)) // head_group
        block_index = (local_part * lane_count + worker_lanes[None, :]).reshape(-1)
        chosen = jnp.take(selection_table, block_index, axis=0).reshape(
            blocks_per_unit, count, 2, BLOCK_TOKENS, HEAD_SIZE
        )
        scores = (
            jnp.einsum(
                "bqhd,bhsd->bhqs",
                query_portion,
                chosen[:, :, 0],
                preferred_element_type=jnp.float32,
            )
            * scale
        )
        scores = jnp.where(valid[:, :, None, None], scores, -jnp.inf)
        best_new = jnp.maximum(best_now, jnp.max(scores, axis=-1))
        fade = jnp.exp(best_now - best_new)
        weights = jnp.exp(scores - best_new[..., None])
        total_new = total_now * fade + jnp.sum(weights, axis=-1)
        accum_new = accum_now * fade[..., None] + jnp.einsum(
            "bhqs,bhsd->bhqd",
            weights.astype(jnp.bfloat16),
            chosen[:, :, 1],
            preferred_element_type=jnp.float32,
        )
        return (best_new, total_new, accum_new)

    tile_rows = lax.all_gather(cached_key_value, "help", axis=0, tiled=True)
    key_block_list = tile_rows.shape[0] // BLOCK_TOKENS
    arranged_layout = jnp.transpose(
        tile_rows.reshape(key_block_list, BLOCK_TOKENS, 2, KEY_VALUE_HEADS, HEAD_SIZE),
        (0, 3, 2, 1, 4),
    )
    selection_table = arranged_layout.reshape(
        key_block_list * KEY_VALUE_HEADS, 2, BLOCK_TOKENS, HEAD_SIZE
    )
    count = quer.shape[2]
    worker_lanes = (worker_rank * heads_per_unit + jnp.arange(count, dtype=jnp.int32)) // head_group
    own = jnp.take(fresh_state, worker_lanes, axis=3)
    near = (
        jnp.einsum("bqhd,bshd->bhqs", quer, own[:, :, 0], preferred_element_type=jnp.float32)
        * scale
    )
    near = jnp.where(causal[None, None], near, -jnp.inf)
    best = jnp.max(near, axis=-1)
    weight = jnp.exp(near - best[..., None])
    total = jnp.sum(weight, axis=-1)
    accum = jnp.einsum(
        "bhqs,bshd->bhqd",
        weight.astype(jnp.bfloat16),
        own[:, :, 1],
        preferred_element_type=jnp.float32,
    )
    softmax_state = (best, total, accum)

    def forward_step(step, carry):
        inner_loop, moving_part = carry
        owner_rank = (worker_rank - step) % nshard
        inner_loop = attend_block(
            inner_loop,
            moving_part,
            owner_rank * heads_per_unit,
            selection_table,
            KEY_VALUE_HEADS,
            worker_rank,
        )
        moving_part = from_behind(moving_part, "blk", 1)
        inner_loop = from_behind((inner_loop[0], inner_loop[1], inner_loop[2]), "blk", 1)
        return (inner_loop, moving_part)

    softmax_state, moving_part = lax.fori_loop(0, nshard, forward_step, (softmax_state, quer))
    best, total, accum = softmax_state
    result = accum / total[..., None]
    result = jnp.transpose(result, (0, 2, 1, 3)).reshape(rows, heads_per_unit * HEAD_SIZE)
    return result


def solution(mesh):
    in_specs = (P("help", "blk"), P("help", None), P(("blk", "help"), None), P("help", None, None))
    out_specs = P("help", "blk")
    return jax.shard_map(local, mesh=mesh, in_specs=in_specs, out_specs=out_specs, check_vma=False)
```

profile of v0, /device:TPU:2, one launch (start us, length us, event | category | flops | bytes accessed | tf_op | source)
XLA Modules:
  0.0 365.8 jit_solution(17734389482068010232)
XLA Ops:
  7.3 1.1 copy.26
  8.6 1.3 copy.21
  11.8 148.1 %all-gather.2.cloned.1.call-done = bf16[2048,2048]{1,0:T(8,128)(2,1)} async-done(((bf16[512,2048]{1,0:T(8,128)(2,1)}), bf16[2048,2048]{1,0:T(8,128)(2,1)}) %all-gather.2.cloned.1.call-update) | async-done | bytes 8388624 | tf_op jit(solution)/shard_map/all_gather | solution.py:72
  159.8 9.7 %copy.33 = bf16[256,8,16,128]{3,2,1,0:T(8,128)(2,1)} copy(bf16[256,8,16,128]{3,1,2,0:T(8,128)(2,1)} %bitcast.126) | data formatting | bytes 16777216
  169.6 8.8 %copy.27 = bf16[2,1024,2,8,128]{4,1,2,3,0:T(8,128)(2,1)} copy(bf16[2,1024,2,8,128]{4,3,2,1,0:T(8,128)(2,1)} %bitcast.125) | data formatting | bytes 16777216 | tf_op jit(solution)/shard_map/reshape | solution.py:75
  178.4 179.2 %while.22 = (s32[]{:T(128)}, f32[1,8,128]{2,1,0:T(8,128)S(1)}, f32[1,8,128]{2,1,0:T(8,128)S(1)}, f32[1,8,128,128]{3,2,1,0:T(8,128)S(1)}, bf16[1,128,8,128]{3,1,2...) while((s32[]{:T(128)}, f32[1,8,128]{2,1,0:T(8,128)S(1)}, ...), condition=%wide.region_7.8_spmd, body=%wide.region_2.0_spmd.sunk | while | flops 550770816 | bytes 38640056 | solution.py:115
  178.7 6.4 %gather_fusion = bf16[8,2,1024,128]{3,2,1,0:T(8,128)(2,1)} fusion(bf16[16,2,1024,128]{3,2,1,0:T(8,128)(2,1)} %get-tuple-element.383, s32[1024]{0:T(1024)S(1)} %pad_clamp_fusion.3), kind=kCustom, calls=%fused_computation.clone.1 | custom fusion | bytes 8388640 | tf_op jit(solution)/shard_map/while/body/eval_jaxpr/jit(_take)/gather | solution.py:47
  185.2 2.7 bitcast_select_fusion.3
  187.8 0.7 bitcast_reduce_fusion.2
  188.6 1.6 collective-permute-start
  190.2 1.7 fusion.53
  191.9 0.9 fusion.52
  192.8 1.6 collective-permute-start.1
  194.4 6.1 %collective-permute-done.1 = f32[1,8,128]{2,1,0:T(8,128)S(1)} collective-permute-done((f32[1,8,128]{2,1,0:T(8,128)S(1)}, f32[1,8,128]{2,1,0:T(8,128)S(1)}, u32[]{:S(2)}, u32[]{:S(2)}) %collective-permute-start.1) | collective-permute-done | bytes 4128 | tf_op jit(solution)/shard_map/while/body/eval_jaxpr/ppermute | solution.py:18
  200.9 6.4 %gather_fusion = bf16[8,2,1024,128]{3,2,1,0:T(8,128)(2,1)} fusion(bf16[16,2,1024,128]{3,2,1,0:T(8,128)(2,1)} %get-tuple-element.383, s32[1024]{0:T(1024)S(1)} %pad_clamp_fusion.3), kind=kCustom, calls=%fused_computation.clone.1 | custom fusion | bytes 8388640 | tf_op jit(solution)/shard_map/while/body/eval_jaxpr/jit(_take)/gather | solution.py:47
  207.3 2.7 bitcast_select_fusion.3
  210.7 2.5 collective-permute-start
  213.2 1.7 fusion.53
  215.0 0.9 fusion.52
  216.0 7.6 %collective-permute-done.1 = f32[1,8,128]{2,1,0:T(8,128)S(1)} collective-permute-done((f32[1,8,128]{2,1,0:T(8,128)S(1)}, f32[1,8,128]{2,1,0:T(8,128)S(1)}, u32[]{:S(2)}, u32[]{:S(2)}) %collective-permute-start.1) | collective-permute-done | bytes 4128 | tf_op jit(solution)/shard_map/while/body/eval_jaxpr/ppermute | solution.py:18
  224.0 6.4 %gather_fusion = bf16[8,2,1024,128]{3,2,1,0:T(8,128)(2,1)} fusion(bf16[16,2,1024,128]{3,2,1,0:T(8,128)(2,1)} %get-tuple-element.383, s32[1024]{0:T(1024)S(1)} %pad_clamp_fusion.3), kind=kCustom, calls=%fused_computation.clone.1 | custom fusion | bytes 8388640 | tf_op jit(solution)/shard_map/while/body/eval_jaxpr/jit(_take)/gather | solution.py:47
  230.4 2.7 bitcast_select_fusion.3
  233.8 1.0 collective-permute-start
  234.8 1.7 fusion.53
  236.6 0.9 fusion.52
  237.5 1.3 collective-permute-start.1
  238.8 6.4 %collective-permute-done.1 = f32[1,8,128]{2,1,0:T(8,128)S(1)} collective-permute-done((f32[1,8,128]{2,1,0:T(8,128)S(1)}, f32[1,8,128]{2,1,0:T(8,128)S(1)}, u32[]{:S(2)}, u32[]{:S(2)}) %collective-permute-start.1) | collective-permute-done | bytes 4128 | tf_op jit(solution)/shard_map/while/body/eval_jaxpr/ppermute | solution.py:18
  245.6 6.4 %gather_fusion = bf16[8,2,1024,128]{3,2,1,0:T(8,128)(2,1)} fusion(bf16[16,2,1024,128]{3,2,1,0:T(8,128)(2,1)} %get-tuple-element.383, s32[1024]{0:T(1024)S(1)} %pad_clamp_fusion.3), kind=kCustom, calls=%fused_computation.clone.1 | custom fusion | bytes 8388640 | tf_op jit(solution)/shard_map/while/body/eval_jaxpr/jit(_take)/gather | solution.py:47
  252.0 2.7 bitcast_select_fusion.3
  254.7 0.7 bitcast_reduce_fusion.2
  255.4 2.2 collective-permute-start
  257.6 1.7 fusion.53
  259.3 0.9 fusion.52
  261.0 7.0 %collective-permute-done.1 = f32[1,8,128]{2,1,0:T(8,128)S(1)} collective-permute-done((f32[1,8,128]{2,1,0:T(8,128)S(1)}, f32[1,8,128]{2,1,0:T(8,128)S(1)}, u32[]{:S(2)}, u32[]{:S(2)}) %collective-permute-start.1) | collective-permute-done | bytes 4128 | tf_op jit(solution)/shard_map/while/body/eval_jaxpr/ppermute | solution.py:18
  268.3 6.4 %gather_fusion = bf16[8,2,1024,128]{3,2,1,0:T(8,128)(2,1)} fusion(bf16[16,2,1024,128]{3,2,1,0:T(8,128)(2,1)} %get-tuple-element.383, s32[1024]{0:T(1024)S(1)} %pad_clamp_fusion.3), kind=kCustom, calls=%fused_computation.clone.1 | custom fusion | bytes 8388640 | tf_op jit(solution)/shard_map/while/body/eval_jaxpr/jit(_take)/gather | solution.py:47
  274.8 2.7 bitcast_select_fusion.3
  277.4 0.7 bitcast_reduce_fusion.2
  278.2 1.6 collective-permute-start
  279.8 1.7 fusion.53
  281.5 0.9 fusion.52
  282.4 1.6 collective-permute-start.1
  284.0 6.1 %collective-permute-done.1 = f32[1,8,128]{2,1,0:T(8,128)S(1)} collective-permute-done((f32[1,8,128]{2,1,0:T(8,128)S(1)}, f32[1,8,128]{2,1,0:T(8,128)S(1)}, u32[]{:S(2)}, u32[]{:S(2)}) %collective-permute-start.1) | collective-permute-done | bytes 4128 | tf_op jit(solution)/shard_map/while/body/eval_jaxpr/ppermute | solution.py:18
  290.5 6.4 %gather_fusion = bf16[8,2,1024,128]{3,2,1,0:T(8,128)(2,1)} fusion(bf16[16,2,1024,128]{3,2,1,0:T(8,128)(2,1)} %get-tuple-element.383, s32[1024]{0:T(1024)S(1)} %pad_clamp_fusion.3), kind=kCustom, calls=%fused_computation.clone.1 | custom fusion | bytes 8388640 | tf_op jit(solution)/shard_map/while/body/eval_jaxpr/jit(_take)/gather | solution.py:47
  297.0 2.7 bitcast_select_fusion.3
  300.4 2.5 collective-permute-start
  302.9 1.7 fusion.53
  304.6 0.9 fusion.52
  305.6 7.6 %collective-permute-done.1 = f32[1,8,128]{2,1,0:T(8,128)S(1)} collective-permute-done((f32[1,8,128]{2,1,0:T(8,128)S(1)}, f32[1,8,128]{2,1,0:T(8,128)S(1)}, u32[]{:S(2)}, u32[]{:S(2)}) %collective-permute-start.1) | collective-permute-done | bytes 4128 | tf_op jit(solution)/shard_map/while/body/eval_jaxpr/ppermute | solution.py:18
  313.6 6.4 %gather_fusion = bf16[8,2,1024,128]{3,2,1,0:T(8,128)(2,1)} fusion(bf16[16,2,1024,128]{3,2,1,0:T(8,128)(2,1)} %get-tuple-element.383, s32[1024]{0:T(1024)S(1)} %pad_clamp_fusion.3), kind=kCustom, calls=%fused_computation.clone.1 | custom fusion | bytes 8388640 | tf_op jit(solution)/shard_map/while/body/eval_jaxpr/jit(_take)/gather | solution.py:47
  320.0 2.7 bitcast_select_fusion.3
  322.7 0.7 bitcast_reduce_fusion.2
  323.4 1.0 collective-permute-start
  324.4 1.7 fusion.53
  326.2 0.9 fusion.52
  327.1 1.3 collective-permute-start.1
  328.4 6.4 %collective-permute-done.1 = f32[1,8,128]{2,1,0:T(8,128)S(1)} collective-permute-done((f32[1,8,128]{2,1,0:T(8,128)S(1)}, f32[1,8,128]{2,1,0:T(8,128)S(1)}, u32[]{:S(2)}, u32[]{:S(2)}) %collective-permute-start.1) | collective-permute-done | bytes 4128 | tf_op jit(solution)/shard_map/while/body/eval_jaxpr/ppermute | solution.py:18
  335.2 6.4 %gather_fusion = bf16[8,2,1024,128]{3,2,1,0:T(8,128)(2,1)} fusion(bf16[16,2,1024,128]{3,2,1,0:T(8,128)(2,1)} %get-tuple-element.383, s32[1024]{0:T(1024)S(1)} %pad_clamp_fusion.3), kind=kCustom, calls=%fused_computation.clone.1 | custom fusion | bytes 8388640 | tf_op jit(solution)/shard_map/while/body/eval_jaxpr/jit(_take)/gather | solution.py:47
  341.6 2.7 bitcast_select_fusion.3
  344.3 0.7 bitcast_reduce_fusion.2
  345.0 2.2 collective-permute-start
  347.2 1.7 fusion.53
  349.0 0.9 fusion.52
  350.6 7.0 %collective-permute-done.1 = f32[1,8,128]{2,1,0:T(8,128)S(1)} collective-permute-done((f32[1,8,128]{2,1,0:T(8,128)S(1)}, f32[1,8,128]{2,1,0:T(8,128)S(1)}, u32[]{:S(2)}, u32[]{:S(2)}) %collective-permute-start.1) | collective-permute-done | bytes 4128 | tf_op jit(solution)/shard_map/while/body/eval_jaxpr/ppermute | solution.py:18
  358.1 0.9 copy.44
  (138 shorter events, 10.4 us)
Async XLA Ops:
  6.5 4.5 %copy-start.1 = (bf16[128,1024]{1,0:T(8,128)(2,1)S(1)}, bf16[128,1024]{1,0:T(8,128)(2,1)}, u32[]{:S(2)}) copy-start(bf16[128,1024]{1,0:T(8,128)(2,1)} %param.6) | copy-start | bytes 786436
  6.5 153.3 %all-gather.2.cloned.1.call-start = ((), (), s32[]{:S(2)}) async-start(), calls=%async_computation | async-start | bytes 10485760 | tf_op jit(solution)/shard_map/all_gather | solution.py:72
  169.6 8.8 %copy-start = (s32[1,64,8]{1,2,0:T(8,128)S(1)}, s32[1,64,8]{1,2,0:T(8,128)}, u32[]{:S(2)}) copy-start(s32[1,64,8]{1,2,0:T(8,128)} %param.9) | copy-start | bytes 6148
  178.4 22.2 %collective-permute-start.3 = (bf16[1,128,8,128]{3,1,2,0:T(8,128)(2,1)S(1)}, bf16[1,128,8,128]{3,1,2,0:T(8,128)(2,1)S(1)}, u32[]{:S(2)}, u32[]{:S(2)}) collective-permute-start(bf16[1,128,8,128]{3,1,2,0:T(8,128)(2,1)S(1)} %copy.56), channel_id=1, source_target_pairs={{28,0},{0,4},{4,8},{8,12},{12,16},{16,20},{20,24},{24,28},{29,1},{... | collective-permute-start | bytes 786440 | tf_op jit(solution)/shard_map/while/body/eval_jaxpr/ppermute | solution.py:18
  188.6 5.9 %collective-permute-start = (f32[1,8,128]{2,1,0:T(8,128)S(1)}, f32[1,8,128]{2,1,0:T(8,128)S(1)}, u32[]{:S(2)}, u32[]{:S(2)}) collective-permute-start(f32[1,8,128]{2,1,0:T(8,128)S(1)} %get-tuple-element.347), channel_id=1, source_target_pairs={{28,0},{0,4},{4,8},{8,12},{12,16},{16,20},{20,24},{24,28},{29,1},{... | collective-permute-start | bytes 12296 | tf_op jit(solution)/shard_map/while/body/eval_jaxpr/ppermute | solution.py:18
  191.8 8.7 %collective-permute-start.2 = (f32[1,8,128,128]{3,2,1,0:T(8,128)S(1)}, f32[1,8,128,128]{3,2,1,0:T(8,128)S(1)}, u32[]{:S(2)}, u32[]{:S(2)}) collective-permute-start(f32[1,8,128,128]{3,2,1,0:T(8,128)S(1)} %fusion.53), channel_id=1, source_target_pairs={{28,0},{0,4},{4,8},{8,12},{12,16},{16,20},{20,24},{24,28},{29,1},{... | collective-permute-start | bytes 1572872 | tf_op jit(solution)/shard_map/while/body/eval_jaxpr/ppermute | solution.py:18
  192.8 7.7 %collective-permute-start.1 = (f32[1,8,128]{2,1,0:T(8,128)S(1)}, f32[1,8,128]{2,1,0:T(8,128)S(1)}, u32[]{:S(2)}, u32[]{:S(2)}) collective-permute-start(f32[1,8,128]{2,1,0:T(8,128)S(1)} %bitcast_add_fusion.3), channel_id=1, source_target_pairs={{28,0},{0,4},{4,8},{8,12},{12,16},{16,20},{20,24},{24,28},{29,1},{... | collective-permute-start | bytes 12296 | tf_op jit(solution)/shard_map/while/body/eval_jaxpr/ppermute | solution.py:18
  200.6 23.1 %collective-permute-start.3 = (bf16[1,128,8,128]{3,1,2,0:T(8,128)(2,1)S(1)}, bf16[1,128,8,128]{3,1,2,0:T(8,128)(2,1)S(1)}, u32[]{:S(2)}, u32[]{:S(2)}) collective-permute-start(bf16[1,128,8,128]{3,1,2,0:T(8,128)(2,1)S(1)} %copy.56), channel_id=1, source_target_pairs={{28,0},{0,4},{4,8},{8,12},{12,16},{16,20},{20,24},{24,28},{29,1},{... | collective-permute-start | bytes 786440 | tf_op jit(solution)/shard_map/while/body/eval_jaxpr/ppermute | solution.py:18
  210.7 5.3 %collective-permute-start = (f32[1,8,128]{2,1,0:T(8,128)S(1)}, f32[1,8,128]{2,1,0:T(8,128)S(1)}, u32[]{:S(2)}, u32[]{:S(2)}) collective-permute-start(f32[1,8,128]{2,1,0:T(8,128)S(1)} %get-tuple-element.347), channel_id=1, source_target_pairs={{28,0},{0,4},{4,8},{8,12},{12,16},{16,20},{20,24},{24,28},{29,1},{... | collective-permute-start | bytes 12296 | tf_op jit(solution)/shard_map/while/body/eval_jaxpr/ppermute | solution.py:18
  214.9 8.7 %collective-permute-start.2 = (f32[1,8,128,128]{3,2,1,0:T(8,128)S(1)}, f32[1,8,128,128]{3,2,1,0:T(8,128)S(1)}, u32[]{:S(2)}, u32[]{:S(2)}) collective-permute-start(f32[1,8,128,128]{3,2,1,0:T(8,128)S(1)} %fusion.53), channel_id=1, source_target_pairs={{28,0},{0,4},{4,8},{8,12},{12,16},{16,20},{20,24},{24,28},{29,1},{... | collective-permute-start | bytes 1572872 | tf_op jit(solution)/shard_map/while/body/eval_jaxpr/ppermute | solution.py:18
  215.9 7.7 %collective-permute-start.1 = (f32[1,8,128]{2,1,0:T(8,128)S(1)}, f32[1,8,128]{2,1,0:T(8,128)S(1)}, u32[]{:S(2)}, u32[]{:S(2)}) collective-permute-start(f32[1,8,128]{2,1,0:T(8,128)S(1)} %bitcast_add_fusion.3), channel_id=1, source_target_pairs={{28,0},{0,4},{4,8},{8,12},{12,16},{16,20},{20,24},{24,28},{29,1},{... | collective-permute-start | bytes 12296 | tf_op jit(solution)/shard_map/while/body/eval_jaxpr/ppermute | solution.py:18
  223.6 21.5 %collective-permute-start.3 = (bf16[1,128,8,128]{3,1,2,0:T(8,128)(2,1)S(1)}, bf16[1,128,8,128]{3,1,2,0:T(8,128)(2,1)S(1)}, u32[]{:S(2)}, u32[]{:S(2)}) collective-permute-start(bf16[1,128,8,128]{3,1,2,0:T(8,128)(2,1)S(1)} %copy.56), channel_id=1, source_target_pairs={{28,0},{0,4},{4,8},{8,12},{12,16},{16,20},{20,24},{24,28},{29,1},{... | collective-permute-start | bytes 786440 | tf_op jit(solution)/shard_map/while/body/eval_jaxpr/ppermute | solution.py:18
  233.8 4.9 %collective-permute-start = (f32[1,8,128]{2,1,0:T(8,128)S(1)}, f32[1,8,128]{2,1,0:T(8,128)S(1)}, u32[]{:S(2)}, u32[]{:S(2)}) collective-permute-start(f32[1,8,128]{2,1,0:T(8,128)S(1)} %get-tuple-element.347), channel_id=1, source_target_pairs={{28,0},{0,4},{4,8},{8,12},{12,16},{16,20},{20,24},{24,28},{29,1},{... | collective-permute-start | bytes 12296 | tf_op jit(solution)/shard_map/while/body/eval_jaxpr/ppermute | solution.py:18
  236.5 8.7 %collective-permute-start.2 = (f32[1,8,128,128]{3,2,1,0:T(8,128)S(1)}, f32[1,8,128,128]{3,2,1,0:T(8,128)S(1)}, u32[]{:S(2)}, u32[]{:S(2)}) collective-permute-start(f32[1,8,128,128]{3,2,1,0:T(8,128)S(1)} %fusion.53), channel_id=1, source_target_pairs={{28,0},{0,4},{4,8},{8,12},{12,16},{16,20},{20,24},{24,28},{29,1},{... | collective-permute-start | bytes 1572872 | tf_op jit(solution)/shard_map/while/body/eval_jaxpr/ppermute | solution.py:18
  237.5 7.7 %collective-permute-start.1 = (f32[1,8,128]{2,1,0:T(8,128)S(1)}, f32[1,8,128]{2,1,0:T(8,128)S(1)}, u32[]{:S(2)}, u32[]{:S(2)}) collective-permute-start(f32[1,8,128]{2,1,0:T(8,128)S(1)} %bitcast_add_fusion.3), channel_id=1, source_target_pairs={{28,0},{0,4},{4,8},{8,12},{12,16},{16,20},{20,24},{24,28},{29,1},{... | collective-permute-start | bytes 12296 | tf_op jit(solution)/shard_map/while/body/eval_jaxpr/ppermute | solution.py:18
  245.2 22.7 %collective-permute-start.3 = (bf16[1,128,8,128]{3,1,2,0:T(8,128)(2,1)S(1)}, bf16[1,128,8,128]{3,1,2,0:T(8,128)(2,1)S(1)}, u32[]{:S(2)}, u32[]{:S(2)}) collective-permute-start(bf16[1,128,8,128]{3,1,2,0:T(8,128)(2,1)S(1)} %copy.56), channel_id=1, source_target_pairs={{28,0},{0,4},{4,8},{8,12},{12,16},{16,20},{20,24},{24,28},{29,1},{... | collective-permute-start | bytes 786440 | tf_op jit(solution)/shard_map/while/body/eval_jaxpr/ppermute | solution.py:18
  255.4 5.6 %collective-permute-start = (f32[1,8,128]{2,1,0:T(8,128)S(1)}, f32[1,8,128]{2,1,0:T(8,128)S(1)}, u32[]{:S(2)}, u32[]{:S(2)}) collective-permute-start(f32[1,8,128]{2,1,0:T(8,128)S(1)} %get-tuple-element.347), channel_id=1, source_target_pairs={{28,0},{0,4},{4,8},{8,12},{12,16},{16,20},{20,24},{24,28},{29,1},{... | collective-permute-start | bytes 12296 | tf_op jit(solution)/shard_map/while/body/eval_jaxpr/ppermute | solution.py:18
  259.3 8.7 %collective-permute-start.2 = (f32[1,8,128,128]{3,2,1,0:T(8,128)S(1)}, f32[1,8,128,128]{3,2,1,0:T(8,128)S(1)}, u32[]{:S(2)}, u32[]{:S(2)}) collective-permute-start(f32[1,8,128,128]{3,2,1,0:T(8,128)S(1)} %fusion.53), channel_id=1, source_target_pairs={{28,0},{0,4},{4,8},{8,12},{12,16},{16,20},{20,24},{24,28},{29,1},{... | collective-permute-start | bytes 1572872 | tf_op jit(solution)/shard_map/while/body/eval_jaxpr/ppermute | solution.py:18
  260.3 7.7 %collective-permute-start.1 = (f32[1,8,128]{2,1,0:T(8,128)S(1)}, f32[1,8,128]{2,1,0:T(8,128)S(1)}, u32[]{:S(2)}, u32[]{:S(2)}) collective-permute-start(f32[1,8,128]{2,1,0:T(8,128)S(1)} %bitcast_add_fusion.3), channel_id=1, source_target_pairs={{28,0},{0,4},{4,8},{8,12},{12,16},{16,20},{20,24},{24,28},{29,1},{... | collective-permute-start | bytes 12296 | tf_op jit(solution)/shard_map/while/body/eval_jaxpr/ppermute | solution.py:18
  268.0 22.2 %collective-permute-start.3 = (bf16[1,128,8,128]{3,1,2,0:T(8,128)(2,1)S(1)}, bf16[1,128,8,128]{3,1,2,0:T(8,128)(2,1)S(1)}, u32[]{:S(2)}, u32[]{:S(2)}) collective-permute-start(bf16[1,128,8,128]{3,1,2,0:T(8,128)(2,1)S(1)} %copy.56), channel_id=1, source_target_pairs={{28,0},{0,4},{4,8},{8,12},{12,16},{16,20},{20,24},{24,28},{29,1},{... | collective-permute-start | bytes 786440 | tf_op jit(solution)/shard_map/while/body/eval_jaxpr/ppermute | solution.py:18
  278.2 5.9 %collective-permute-start = (f32[1,8,128]{2,1,0:T(8,128)S(1)}, f32[1,8,128]{2,1,0:T(8,128)S(1)}, u32[]{:S(2)}, u32[]{:S(2)}) collective-permute-start(f32[1,8,128]{2,1,0:T(8,128)S(1)} %get-tuple-element.347), channel_id=1, source_target_pairs={{28,0},{0,4},{4,8},{8,12},{12,16},{16,20},{20,24},{24,28},{29,1},{... | collective-permute-start | bytes 12296 | tf_op jit(solution)/shard_map/while/body/eval_jaxpr/ppermute | solution.py:18
  281.4 8.7 %collective-permute-start.2 = (f32[1,8,128,128]{3,2,1,0:T(8,128)S(1)}, f32[1,8,128,128]{3,2,1,0:T(8,128)S(1)}, u32[]{:S(2)}, u32[]{:S(2)}) collective-permute-start(f32[1,8,128,128]{3,2,1,0:T(8,128)S(1)} %fusion.53), channel_id=1, source_target_pairs={{28,0},{0,4},{4,8},{8,12},{12,16},{16,20},{20,24},{24,28},{29,1},{... | collective-permute-start | bytes 1572872 | tf_op jit(solution)/shard_map/while/body/eval_jaxpr/ppermute | solution.py:18
  282.4 7.7 %collective-permute-start.1 = (f32[1,8,128]{2,1,0:T(8,128)S(1)}, f32[1,8,128]{2,1,0:T(8,128)S(1)}, u32[]{:S(2)}, u32[]{:S(2)}) collective-permute-start(f32[1,8,128]{2,1,0:T(8,128)S(1)} %bitcast_add_fusion.3), channel_id=1, source_target_pairs={{28,0},{0,4},{4,8},{8,12},{12,16},{16,20},{20,24},{24,28},{29,1},{... | collective-permute-start | bytes 12296 | tf_op jit(solution)/shard_map/while/body/eval_jaxpr/ppermute | solution.py:18
  290.2 23.1 %collective-permute-start.3 = (bf16[1,128,8,128]{3,1,2,0:T(8,128)(2,1)S(1)}, bf16[1,128,8,128]{3,1,2,0:T(8,128)(2,1)S(1)}, u32[]{:S(2)}, u32[]{:S(2)}) collective-permute-start(bf16[1,128,8,128]{3,1,2,0:T(8,128)(2,1)S(1)} %copy.56), channel_id=1, source_target_pairs={{28,0},{0,4},{4,8},{8,12},{12,16},{16,20},{20,24},{24,28},{29,1},{... | collective-permute-start | bytes 786440 | tf_op jit(solution)/shard_map/while/body/eval_jaxpr/ppermute | solution.py:18
  300.4 5.3 %collective-permute-start = (f32[1,8,128]{2,1,0:T(8,128)S(1)}, f32[1,8,128]{2,1,0:T(8,128)S(1)}, u32[]{:S(2)}, u32[]{:S(2)}) collective-permute-start(f32[1,8,128]{2,1,0:T(8,128)S(1)} %get-tuple-element.347), channel_id=1, source_target_pairs={{28,0},{0,4},{4,8},{8,12},{12,16},{16,20},{20,24},{24,28},{29,1},{... | collective-permute-start | bytes 12296 | tf_op jit(solution)/shard_map/while/body/eval_jaxpr/ppermute | solution.py:18
  304.5 8.7 %collective-permute-start.2 = (f32[1,8,128,128]{3,2,1,0:T(8,128)S(1)}, f32[1,8,128,128]{3,2,1,0:T(8,128)S(1)}, u32[]{:S(2)}, u32[]{:S(2)}) collective-permute-start(f32[1,8,128,128]{3,2,1,0:T(8,128)S(1)} %fusion.53), channel_id=1, source_target_pairs={{28,0},{0,4},{4,8},{8,12},{12,16},{16,20},{20,24},{24,28},{29,1},{... | collective-permute-start | bytes 1572872 | tf_op jit(solution)/shard_map/while/body/eval_jaxpr/ppermute | solution.py:18
  305.5 7.7 %collective-permute-start.1 = (f32[1,8,128]{2,1,0:T(8,128)S(1)}, f32[1,8,128]{2,1,0:T(8,128)S(1)}, u32[]{:S(2)}, u32[]{:S(2)}) collective-permute-start(f32[1,8,128]{2,1,0:T(8,128)S(1)} %bitcast_add_fusion.3), channel_id=1, source_target_pairs={{28,0},{0,4},{4,8},{8,12},{12,16},{16,20},{20,24},{24,28},{29,1},{... | collective-permute-start | bytes 12296 | tf_op jit(solution)/shard_map/while/body/eval_jaxpr/ppermute | solution.py:18
  313.3 21.5 %collective-permute-start.3 = (bf16[1,128,8,128]{3,1,2,0:T(8,128)(2,1)S(1)}, bf16[1,128,8,128]{3,1,2,0:T(8,128)(2,1)S(1)}, u32[]{:S(2)}, u32[]{:S(2)}) collective-permute-start(bf16[1,128,8,128]{3,1,2,0:T(8,128)(2,1)S(1)} %copy.56), channel_id=1, source_target_pairs={{28,0},{0,4},{4,8},{8,12},{12,16},{16,20},{20,24},{24,28},{29,1},{... | collective-permute-start | bytes 786440 | tf_op jit(solution)/shard_map/while/body/eval_jaxpr/ppermute | solution.py:18
  323.4 4.9 %collective-permute-start = (f32[1,8,128]{2,1,0:T(8,128)S(1)}, f32[1,8,128]{2,1,0:T(8,128)S(1)}, u32[]{:S(2)}, u32[]{:S(2)}) collective-permute-start(f32[1,8,128]{2,1,0:T(8,128)S(1)} %get-tuple-element.347), channel_id=1, source_target_pairs={{28,0},{0,4},{4,8},{8,12},{12,16},{16,20},{20,24},{24,28},{29,1},{... | collective-permute-start | bytes 12296 | tf_op jit(solution)/shard_map/while/body/eval_jaxpr/ppermute | solution.py:18
  326.1 8.7 %collective-permute-start.2 = (f32[1,8,128,128]{3,2,1,0:T(8,128)S(1)}, f32[1,8,128,128]{3,2,1,0:T(8,128)S(1)}, u32[]{:S(2)}, u32[]{:S(2)}) collective-permute-start(f32[1,8,128,128]{3,2,1,0:T(8,128)S(1)} %fusion.53), channel_id=1, source_target_pairs={{28,0},{0,4},{4,8},{8,12},{12,16},{16,20},{20,24},{24,28},{29,1},{... | collective-permute-start | bytes 1572872 | tf_op jit(solution)/shard_map/while/body/eval_jaxpr/ppermute | solution.py:18
  327.1 7.7 %collective-permute-start.1 = (f32[1,8,128]{2,1,0:T(8,128)S(1)}, f32[1,8,128]{2,1,0:T(8,128)S(1)}, u32[]{:S(2)}, u32[]{:S(2)}) collective-permute-start(f32[1,8,128]{2,1,0:T(8,128)S(1)} %bitcast_add_fusion.3), channel_id=1, source_target_pairs={{28,0},{0,4},{4,8},{8,12},{12,16},{16,20},{20,24},{24,28},{29,1},{... | collective-permute-start | bytes 12296 | tf_op jit(solution)/shard_map/while/body/eval_jaxpr/ppermute | solution.py:18
  334.8 22.7 %collective-permute-start.3 = (bf16[1,128,8,128]{3,1,2,0:T(8,128)(2,1)S(1)}, bf16[1,128,8,128]{3,1,2,0:T(8,128)(2,1)S(1)}, u32[]{:S(2)}, u32[]{:S(2)}) collective-permute-start(bf16[1,128,8,128]{3,1,2,0:T(8,128)(2,1)S(1)} %copy.56), channel_id=1, source_target_pairs={{28,0},{0,4},{4,8},{8,12},{12,16},{16,20},{20,24},{24,28},{29,1},{... | collective-permute-start | bytes 786440 | tf_op jit(solution)/shard_map/while/body/eval_jaxpr/ppermute | solution.py:18
  345.0 5.5 %collective-permute-start = (f32[1,8,128]{2,1,0:T(8,128)S(1)}, f32[1,8,128]{2,1,0:T(8,128)S(1)}, u32[]{:S(2)}, u32[]{:S(2)}) collective-permute-start(f32[1,8,128]{2,1,0:T(8,128)S(1)} %get-tuple-element.347), channel_id=1, source_target_pairs={{28,0},{0,4},{4,8},{8,12},{12,16},{16,20},{20,24},{24,28},{29,1},{... | collective-permute-start | bytes 12296 | tf_op jit(solution)/shard_map/while/body/eval_jaxpr/ppermute | solution.py:18
  348.9 8.7 %collective-permute-start.2 = (f32[1,8,128,128]{3,2,1,0:T(8,128)S(1)}, f32[1,8,128,128]{3,2,1,0:T(8,128)S(1)}, u32[]{:S(2)}, u32[]{:S(2)}) collective-permute-start(f32[1,8,128,128]{3,2,1,0:T(8,128)S(1)} %fusion.53), channel_id=1, source_target_pairs={{28,0},{0,4},{4,8},{8,12},{12,16},{16,20},{20,24},{24,28},{29,1},{... | collective-permute-start | bytes 1572872 | tf_op jit(solution)/shard_map/while/body/eval_jaxpr/ppermute | solution.py:18
  349.9 7.7 %collective-permute-start.1 = (f32[1,8,128]{2,1,0:T(8,128)S(1)}, f32[1,8,128]{2,1,0:T(8,128)S(1)}, u32[]{:S(2)}, u32[]{:S(2)}) collective-permute-start(f32[1,8,128]{2,1,0:T(8,128)S(1)} %bitcast_add_fusion.3), channel_id=1, source_target_pairs={{28,0},{0,4},{4,8},{8,12},{12,16},{16,20},{20,24},{24,28},{29,1},{... | collective-permute-start | bytes 12296 | tf_op jit(solution)/shard_map/while/body/eval_jaxpr/ppermute | solution.py:18
Sparse Core Ops, SparseCore 0:
  8.9 150.8 all-gather.1
where the time goes:
time: 368 us; the launch traced here: 366 us
  waiting for transfers between devices  203 us (55%)
  local copies, waits for them, and re-layouts  75 us (20%)
  other arithmetic  30.8 us (8%)
  starting transfers between devices  23.1 us (6%)
  matrix products  19.7 us (5%)
  between operations  13.5 us (4%)
    all_gather x1, waiting for transfers between devices, local(): tile_rows = lax.all_gather(cached_key_value, 'help', axis=0, tiled=True)  148 us
    ppermute x32, waiting for transfers between devices, from_behind(): return lax.ppermute(block, axis, route)  54.3 us
    gather x8, local copies, waits for them, and re-layouts, attend_block(): jnp.take(selection_table, block_index, axis=0)  51.5 us
    ppermute x32, starting transfers between devices, from_behind(): return lax.ppermute(block, axis, route)  23.1 us
    select_n x16, other arithmetic, attend_block(): jnp.take(selection_table, block_index, axis=0)  21.3 us
    dot_general x8, matrix products, attend_block(): jnp.einsum('bhqs,bhsd->bhqd', weights.astype(jnp.bfloat16), chosen[:, :,...  13.3 us
    unnamed x8, local copies, waits for them, and re-layouts  13.1 us
    reshape x1, local copies, waits for them, and re-layouts, local(): tile_rows.reshape(key_block_list, BLOCK_TOKENS, 2, KEY_VALUE_HEADS, HEAD_...  8.77 us
  transfers between devices with their start and end apart: 33, of which 9 were waited for; matrix products, arithmetic and copies ran while one was open for 29% of the time, Pallas kernels for 0%

commit v1 on v0

v1 whole, which is shorter than its diff:
```python
import functools
import math

import jax
import jax.numpy as jnp
import numpy as np
from jax import lax
from jax.experimental import pallas as pl
from jax.experimental.pallas import tpu as pltpu
from jax.sharding import PartitionSpec as P

HEAD_SIZE = 128
QUERY_HEADS = 64
KEY_VALUE_HEADS = 8
BLOCK_TOKENS = 1024
QUERY_GROUP_ROWS = 128


def attend_kernel(sel_ref, home_ref, q_ref, kv_ref, own_ref, acc_ref, m_ref, l_ref,
                  s_buf, own_buf, m_scr, l_scr, acc_scr, *, groups, heads, scale):
    b = pl.program_id(0)
    rows = QUERY_GROUP_ROWS
    is_home = b == home_ref[0]
    causal = lax.broadcasted_iota(jnp.int32, (rows, rows), 0) >= lax.broadcasted_iota(
        jnp.int32, (rows, rows), 1)
    contract_last = (((1,), (1,)), ((), ()))

    for h in range(heads):
        q = q_ref[0, :, h * HEAD_SIZE:(h + 1) * HEAD_SIZE]
        base = (b * heads + h) * groups
        m_scr[...] = jnp.full(m_scr.shape, -jnp.inf, jnp.float32)
        l_scr[...] = jnp.zeros(l_scr.shape, jnp.float32)
        acc_scr[...] = jnp.zeros(acc_scr.shape, jnp.float32)

        def scores(g, carry):
            @pl.when(sel_ref[base + g] != 0)
            def _():
                s = lax.dot_general(q, kv_ref[g, 0], contract_last,
                                    preferred_element_type=jnp.float32)
                s_buf[g] = s
                m_scr[...] = jnp.maximum(m_scr[...], jnp.max(s, axis=1, keepdims=True))
            return carry

        lax.fori_loop(0, groups, scores, 0)

        @pl.when(is_home)
        def _():
            s = lax.dot_general(q, own_ref[0], contract_last, preferred_element_type=jnp.float32)
            s = jnp.where(causal, s, -jnp.inf)
            own_buf[...] = s
            m_scr[...] = jnp.maximum(m_scr[...], jnp.max(s, axis=1, keepdims=True))

        def mix(g, carry):
            @pl.when(sel_ref[base + g] != 0)
            def _():
                p = jnp.exp((s_buf[g] - m_scr[...]) * scale)
                l_scr[...] += jnp.sum(p, axis=1, keepdims=True)
                acc_scr[...] += jnp.dot(p.astype(jnp.bfloat16), kv_ref[g, 1],
                                        preferred_element_type=jnp.float32)
            return carry

        lax.fori_loop(0, groups, mix, 0)

        @pl.when(is_home)
        def _():
            p = jnp.exp((own_buf[...] - m_scr[...]) * scale)
            l_scr[...] += jnp.sum(p, axis=1, keepdims=True)
            acc_scr[...] += jnp.dot(p.astype(jnp.bfloat16), own_ref[1],
                                    preferred_element_type=jnp.float32)

        acc_ref[0, :, h * HEAD_SIZE:(h + 1) * HEAD_SIZE] = acc_scr[...]
        m_ref[0, :, h:h + 1] = m_scr[...] * scale
        l_ref[0, :, h:h + 1] = l_scr[...]


def local(queries, query_key_value, cached_key_value, selected):
    rows = queries.shape[0]
    heads = queries.shape[1] // HEAD_SIZE
    head_group = QUERY_HEADS // KEY_VALUE_HEADS
    scale = 1.0 / math.sqrt(HEAD_SIZE)
    groups = lax.axis_size("blk")
    helpers = lax.axis_size("help")
    worker = lax.axis_index("blk")
    helper = lax.axis_index("help")
    piece = cached_key_value.shape[0]
    assert rows == QUERY_GROUP_ROWS and head_group % heads == 0
    assert BLOCK_TOKENS % piece == 0
    per_group = piece * helpers // BLOCK_TOKENS
    query_blocks = helpers

    kv = cached_key_value.reshape(piece, 2, KEY_VALUE_HEADS, HEAD_SIZE)
    kv = jnp.transpose(kv, (2, 1, 0, 3))
    wanted = np.array([(t * heads) // head_group for t in range(groups)], np.int32)
    if not np.array_equal(wanted, np.arange(KEY_VALUE_HEADS)):
        kv = jnp.take(kv, wanted, axis=0)
    held = lax.all_to_all(kv, "blk", 0, 0, tiled=True)

    q_all = lax.all_gather(queries.reshape(1, rows, heads * HEAD_SIZE), "help", axis=0, tiled=True)
    sel_all = lax.all_gather(selected, "help", axis=0, tiled=True)

    kv_head = (worker * heads) // head_group
    own = query_key_value.reshape(rows, 2, KEY_VALUE_HEADS, HEAD_SIZE)
    own = lax.dynamic_index_in_dim(own, kv_head, axis=2, keepdims=False)
    own = jnp.transpose(own, (1, 0, 2))

    my_heads = lax.dynamic_slice_in_dim(sel_all, worker * heads, heads, axis=1)
    piece_block = per_group * jnp.arange(groups, dtype=jnp.int32) + (helper * piece) // BLOCK_TOKENS
    hit = jnp.any(my_heads[:, :, None, :] == piece_block[None, None, :, None], axis=3)
    sel_flat = hit.astype(jnp.int32).reshape(-1)
    home = helper.reshape(1).astype(jnp.int32)

    kernel = functools.partial(attend_kernel, groups=groups, heads=heads, scale=scale)
    width = heads * HEAD_SIZE
    acc, m, l = pl.pallas_call(
        kernel,
        grid_spec=pltpu.PrefetchScalarGridSpec(
            num_scalar_prefetch=2,
            grid=(query_blocks,),
            in_specs=[
                pl.BlockSpec((1, rows, width), lambda b, s, h: (b, 0, 0)),
                pl.BlockSpec((groups, 2, piece, HEAD_SIZE), lambda b, s, h: (0, 0, 0, 0)),
                pl.BlockSpec((2, rows, HEAD_SIZE), lambda b, s, h: (0, 0, 0)),
            ],
            out_specs=[
                pl.BlockSpec((1, rows, width), lambda b, s, h: (b, 0, 0)),
                pl.BlockSpec((1, rows, heads), lambda b, s, h: (b, 0, 0)),
                pl.BlockSpec((1, rows, heads), lambda b, s, h: (b, 0, 0)),
            ],
            scratch_shapes=[
                pltpu.VMEM((groups, rows, piece), jnp.float32),
                pltpu.VMEM((rows, rows), jnp.float32),
                pltpu.VMEM((rows, 1), jnp.float32),
                pltpu.VMEM((rows, 1), jnp.float32),
                pltpu.VMEM((rows, HEAD_SIZE), jnp.float32),
            ],
        ),
        out_shape=[
            jax.ShapeDtypeStruct((query_blocks, rows, width), jnp.float32),
            jax.ShapeDtypeStruct((query_blocks, rows, heads), jnp.float32),
            jax.ShapeDtypeStruct((query_blocks, rows, heads), jnp.float32),
        ],
    )(sel_flat, home, q_all, held, own)

    top = lax.pmax(m, "help")
    fade = jnp.exp(m - top)
    acc = acc.reshape(query_blocks, rows, heads, HEAD_SIZE) * fade[..., None]
    acc = lax.psum_scatter(acc, "help", scatter_dimension=0, tiled=True)
    total = lax.psum_scatter(l * fade, "help", scatter_dimension=0, tiled=True)
    result = acc / total[..., None]
    return result.reshape(rows, width)


def solution(mesh):
    in_specs = (P("help", "blk"), P("help", None), P(("blk", "help"), None), P("help", None, None))
    out_specs = P("help", "blk")
    return jax.shard_map(local, mesh=mesh, in_specs=in_specs, out_specs=out_specs, check_vma=False)
```

time: 368 us -> 234 us (0.64)
  waiting for transfers between devices: 203 us -> 75.5 us
  Pallas kernels: 0 us -> 89.1 us
  local copies, waits for them, and re-layouts: 75 us -> 11.4 us
  blocking collectives: 0 us -> 35.2 us
  other arithmetic: 30.8 us -> 4.67 us
  matrix products: 19.7 us -> 0 us
  starting transfers between devices: 23.1 us -> 4.47 us
    all_gather x1, waiting for transfers between devices: 148 us -> 14.9 us  [local(): lax.all_gather(queries.reshape(1, rows, heads * HEAD_SIZE), 'help', axis=...]
    pallas_call x0 -> x1, Pallas kernels: none -> 89.1 us  [local(): pl.pallas_call(kernel, grid_spec=pltpu.PrefetchScalarGridSpec(num_scalar_...]
    reduce_scatter x0 -> x2, waiting for transfers between devices: none -> 59.9 us  [the longest x1 44.5 us: local(): acc = lax.psum_scatter(acc, 'help', scatter_dimension=0, tiled=True)]
    ppermute x32 -> x0, waiting for transfers between devices: 54.3 us -> none  [from_behind(): return lax.ppermute(block, axis, route)]
    gather x9 -> x0, local copies, waits for them, and re-layouts: 52.2 us -> none  [the longest x8 51.5 us: attend_block(): jnp.take(selection_table, block_index, axis=0)]
    ppermute x32 -> x0, starting transfers between devices: 23.1 us -> none  [from_behind(): return lax.ppermute(block, axis, route)]
    pmax x0 -> x1, blocking collectives: none -> 21.8 us  [local(): top = lax.pmax(m, 'help')]
    select_n x18 -> x0, other arithmetic: 21.5 us -> none  [the longest x16 21.3 us: attend_block(): jnp.take(selection_table, block_index, axis=0)]
  transfers between devices with their start and end apart: 33 -> 4, of which waited for: 9 -> 3; matrix products, arithmetic and copies ran while one was open for 29% -> 2% of each run, Pallas kernels for 0% -> 0%
where the time goes in v1:
time: 234 us
  Pallas kernels  89.1 us (38%)
  waiting for transfers between devices  75.5 us (32%)
  blocking collectives  35.2 us (15%)
  between operations  13.2 us (6%)
  local copies, waits for them, and re-layouts  11.4 us (5%)
  other arithmetic  4.67 us (2%)
  starting transfers between devices  4.47 us (2%)
    pallas_call x1, Pallas kernels, local(): pl.pallas_call(kernel, grid_spec=pltpu.PrefetchScalarGridSpec(num_scalar_...  89.1 us
    reduce_scatter x1, waiting for transfers between devices, local(): acc = lax.psum_scatter(acc, 'help', scatter_dimension=0, tiled=True)  44.5 us
    pmax x1, blocking collectives, local(): top = lax.pmax(m, 'help')  21.8 us
    reduce_scatter x1, waiting for transfers between devices, local(): total = lax.psum_scatter(l * fade, 'help', scatter_dimension=0, tiled=True)  15.4 us
    all_gather x1, waiting for transfers between devices, local(): lax.all_gather(queries.reshape(1, rows, heads * HEAD_SIZE), 'help', axis=...  14.9 us
    all_gather x1, blocking collectives, local(): sel_all = lax.all_gather(selected, 'help', axis=0, tiled=True)  13.4 us
    unnamed x15, local copies, waits for them, and re-layouts  7.98 us
  transfers between devices with their start and end apart: 4, of which 3 were waited for; matrix products, arithmetic and copies ran while one was open for 2% of the time, Pallas kernels for 0%

profile of v1, /device:TPU:2, one launch (start us, length us, event | category | flops | bytes accessed | tf_op | source)
XLA Modules:
  0.0 233.5 jit_solution(3139582252427413935)
XLA Ops:
  6.5 2.9 %copy.16 = bf16[512,2048]{0,1:T(8,128)(2,1)S(1)} copy(bf16[512,2048]{1,0:T(8,128)(2,1)} %param.6) | data formatting | bytes 4194304 | tf_op args[2]
  9.4 2.4 %copy.17 = bf16[512,2,8,128]{3,0,1,2:T(8,128)(2,1)} copy(bf16[512,2,8,128]{0,3,2,1:T(8,128)(2,1)S(1)} %bitcast.26) | data formatting | bytes 4194304 | tf_op jit(solution)/shard_map/reshape | solution.py:91
  11.8 0.0 copy-start.4
  11.8 0.0 copy-start.2
  11.8 4.4 %all-to-all-start = ((bf16[8,2,512,128]{3,2,1,0:T(8,128)(2,1)}), bf16[8,2,512,128]{3,2,1,0:T(8,128)(2,1)S(1)}, u32[]{:S(2)}, u32[]{:S(2)}) async-start(bf16[8,2,512,128]{3,2,1,0:T(8,128)(2,1)} %bitcast.24), calls=%async_computation | async-start | bytes 4194304 | tf_op jit(solution)/shard_map/all_to_all | solution.py:96
  16.2 0.0 all-gather.3.cloned.1.call-start
  16.2 0.7 all-gather.3.cloned.1.call-update
  16.9 0.0 reduce-scatter.5.cloned.1.call-start
  17.0 0.0 copy-done.4
  17.0 13.4 %all_gather.6 = s32[4,64,8]{1,2,0:T(8,128)S(1)} all-gather(s32[1,64,8]{1,2,0:T(8,128)S(1)} %copy-done.4), channel_id=1, replica_groups=mesh['blk'=8,'help'=4] {'help'}, dimensions={0}, use_global_device_ids=true | all-gather | bytes 10240 | tf_op jit(solution)/shard_map/all_gather | solution.py:99
  30.4 0.1 constant_dynamic-slice_fusion.1
  30.4 0.1 copy.15
  30.5 0.7 compare_reduce_fusion
  31.2 0.7 reshape.38.sel_ref
  31.9 0.0 copy-done.2
  31.9 0.1 copy.20
  32.0 0.1 constant_dynamic-slice_fusion
  32.2 0.6 copy.26
  32.8 14.9 %all-gather.3.cloned.1.call-done = bf16[512,1024]{1,0:T(8,128)(2,1)} async-done(((bf16[128,1024]{1,0:T(8,128)(2,1)}), bf16[512,1024]{1,0:T(8,128)(2,1)}) %all-gather.3.cloned.1.call-update) | async-done | bytes 1048592 | tf_op jit(solution)/shard_map/all_gather | solution.py:98
  47.7 0.0 all-to-all-done.kv_ref
  47.7 0.0 copy-start
  47.7 1.4 copy-done
  49.1 89.1 %shard_map.46 = (f32[4,128,1024]{2,1,0:T(8,128)}, f32[4,128,8]{2,1,0:T(8,128)}, f32[4,128,8]{2,1,0:T(8,128)}) custom-call(s32[256]{0:T(256)} %reshape.38.sel_ref, s32[1]{0:T(128)} %bitcast.home_ref, bf16[4,128,1024]{2,1,0:T(8,128)(2,1)} %bitcast.29, bf16[8,2,512,128]{3,2,1,0:T(8,128)(2,1)} %copy-done, bf16[2,128,128]{2,1,0:T(8,128)(2,1)} %bitcast.32), custom_call_target="tpu_custom_call" | custom-call | tf_op jit(solution)/shard_map/pallas_call | solution.py:114
  138.2 0.0 copy-start.1
  138.2 0.0 copy-start.3
  138.2 2.1 copy.21
  140.3 0.0 copy-done.1
  140.3 21.8 %pmax.7 = f32[4,128,8]{2,1,0:T(8,128)S(1)} all-reduce(f32[4,128,8]{2,1,0:T(8,128)S(1)} %copy-done.1), channel_id=1, replica_groups=mesh['blk'=8,'help'=4] {'help'}, use_global_device_ids=true, to_apply=%region_1.2 | all-reduce | flops 4096 | bytes 32768 | tf_op jit(solution)/shard_map/pmax | solution.py:144
  162.1 0.0 copy-done.3
  162.1 0.8 fusion
  162.9 0.0 reduce-scatter.5.cloned.1.call-update
  162.9 0.0 reduce-scatter.3.cloned.1.call-start
  163.0 2.0 bitcast_multiply_fusion
  164.9 0.0 reduce-scatter.3.cloned.1.call-update
  165.0 15.4 %reduce-scatter.5.cloned.1.call-done = f32[1,128,8]{2,1,0:T(8,128)} async-done(((f32[4,128,8]{2,1,0:T(8,128)}), f32[1,128,8]{2,1,0:T(8,128)}) %reduce-scatter.5.cloned.1.call-update) | async-done | bytes 4112 | tf_op jit(solution)/shard_map/reduce_scatter | solution.py:148
  180.3 44.5 %reduce-scatter.3.cloned.1.call-done = f32[1,128,8,128]{3,2,1,0:T(8,128)} async-done(((f32[4,128,8,128]{3,2,1,0:T(8,128)}), f32[1,128,8,128]{3,2,1,0:T(8,128)}) %reduce-scatter.3.cloned.1.call-update) | async-done | bytes 524304 | tf_op jit(solution)/shard_map/reduce_scatter | solution.py:147
  224.8 1.2 broadcast_divide_fusion
  226.1 0.9 copy.25
  (2 shorter events, 0.0 us)
Async XLA Ops:
  11.8 5.2 %copy-start.4 = (s32[1,64,8]{1,2,0:T(8,128)S(1)}, s32[1,64,8]{1,2,0:T(8,128)}, u32[]{:S(2)}) copy-start(s32[1,64,8]{1,2,0:T(8,128)} %param.7) | copy-start | bytes 6148
  11.8 20.1 %copy-start.2 = (bf16[128,2048]{1,0:T(8,128)(2,1)S(1)}, bf16[128,2048]{1,0:T(8,128)(2,1)}, u32[]{:S(2)}) copy-start(bf16[128,2048]{1,0:T(8,128)(2,1)} %param.5) | copy-start | bytes 1572868
  11.8 35.9 %all-to-all-start = ((bf16[8,2,512,128]{3,2,1,0:T(8,128)(2,1)}), bf16[8,2,512,128]{3,2,1,0:T(8,128)(2,1)S(1)}, u32[]{:S(2)}, u32[]{:S(2)}) async-start(bf16[8,2,512,128]{3,2,1,0:T(8,128)(2,1)} %bitcast.24), calls=%async_computation | async-start | bytes 4194304 | tf_op jit(solution)/shard_map/all_to_all | solution.py:96
  16.2 31.5 %all-gather.3.cloned.1.call-start = ((), (), s32[]{:S(2)}) async-start(), calls=%async_computation.5 | async-start | bytes 1310720 | tf_op jit(solution)/shard_map/all_gather | solution.py:98
  16.9 163.4 %reduce-scatter.5.cloned.1.call-start = ((), (), s32[]{:S(2)}) async-start(), calls=%async_computation.4 | async-start | bytes 327680 | tf_op jit(solution)/shard_map/reduce_scatter | solution.py:148
  47.7 1.4 copy-start
  138.2 2.1 copy-start.1
  138.2 23.9 %copy-start.3 = (f32[4,128,8]{2,1,0:T(8,128)S(1)}, f32[4,128,8]{2,1,0:T(8,128)}, u32[]{:S(2)}) copy-start(f32[4,128,8]{2,1,0:T(8,128)} %get-tuple-element.10) | copy-start | bytes 49156
  162.9 61.9 %reduce-scatter.3.cloned.1.call-start = ((), (), s32[]{:S(2)}) async-start(), calls=%async_computation.3 | async-start | bytes 2621440 | tf_op jit(solution)/shard_map/reduce_scatter | solution.py:147
Sparse Core Ops, SparseCore 0:
  18.6 29.0 all-gather.2
  163.0 17.2 reduce-scatter.4
  182.7 42.0 reduce-scatter.2

commit v2 on v1

v2 whole, which is shorter than its diff:
```python
import functools
import math

import jax
import jax.numpy as jnp
import numpy as np
from jax import lax
from jax.experimental import pallas as pl
from jax.experimental.pallas import tpu as pltpu
from jax.sharding import PartitionSpec as P

HEAD_SIZE = 128
QUERY_HEADS = 64
KEY_VALUE_HEADS = 8
BLOCK_TOKENS = 1024
QUERY_GROUP_ROWS = 128


def attend_kernel(sel_ref, home_ref, q_ref, kt_ref, v_ref, own_ref, acc_ref, m_ref, l_ref,
                  p_buf, m_scr, l_scr, acc_scr, *, groups, heads, scale):
    b = pl.program_id(0)
    rows = QUERY_GROUP_ROWS
    q = q_ref[0].reshape(heads * rows, HEAD_SIZE)
    m_scr[...] = jnp.full(m_scr.shape, -jnp.inf, jnp.float32)
    l_scr[...] = jnp.zeros(l_scr.shape, jnp.float32)
    acc_scr[...] = jnp.zeros(acc_scr.shape, jnp.float32)

    def update(s, value, bias_of):
        for h in range(heads):
            s_h = s[h * rows:(h + 1) * rows] * scale + bias_of(h)
            m_old = m_scr[h]
            m_new = jnp.maximum(m_old, jnp.max(s_h, axis=1, keepdims=True))
            m_safe = jnp.where(m_new == -jnp.inf, 0.0, m_new)
            alpha = jnp.exp(m_old - m_safe)
            p = jnp.exp(s_h - m_safe)
            l_scr[h] = alpha * l_scr[h] + jnp.sum(p, axis=1, keepdims=True)
            m_scr[h] = m_new
            acc_scr[h] = alpha * acc_scr[h]
            p_buf[h * rows:(h + 1) * rows, :s.shape[1]] = p.astype(jnp.bfloat16)
        width = s.shape[1]
        pv = jnp.dot(p_buf[:, :width], value, preferred_element_type=jnp.float32)
        for h in range(heads):
            acc_scr[h] += pv[h * rows:(h + 1) * rows]

    def piece(g, carry):
        base = b * heads * groups + g

        def bias_of(h):
            return jnp.where(sel_ref[base + h * groups] != 0, 0.0, -jnp.inf)

        s = jnp.dot(q, kt_ref[g], preferred_element_type=jnp.float32)
        update(s, v_ref[g], bias_of)
        return carry

    lax.fori_loop(0, groups, piece, 0)

    @pl.when(b == home_ref[0])
    def _():
        causal = lax.broadcasted_iota(jnp.int32, (rows, rows), 0) >= lax.broadcasted_iota(
            jnp.int32, (rows, rows), 1)
        mask = jnp.where(causal, 0.0, -jnp.inf)
        s = jnp.dot(q, own_ref[0], preferred_element_type=jnp.float32)
        update(s, own_ref[1], lambda h: mask)

    for h in range(heads):
        acc_ref[0, :, h * HEAD_SIZE:(h + 1) * HEAD_SIZE] = acc_scr[h]
        m_ref[0, :, h:h + 1] = m_scr[h]
        l_ref[0, :, h:h + 1] = l_scr[h]


def join(a, b):
    acc_a, m_a, l_a = a
    acc_b, m_b, l_b = b
    m = jnp.maximum(m_a, m_b)
    m_safe = jnp.where(m == -jnp.inf, 0.0, m)
    f_a = jnp.exp(m_a - m_safe)
    f_b = jnp.exp(m_b - m_safe)
    acc = acc_a * f_a[..., None] + acc_b * f_b[..., None]
    return acc, m, l_a * f_a + l_b * f_b


def local(queries, query_key_value, cached_key_value, selected):
    rows = queries.shape[0]
    heads = queries.shape[1] // HEAD_SIZE
    head_group = QUERY_HEADS // KEY_VALUE_HEADS
    scale = 1.0 / math.sqrt(HEAD_SIZE)
    groups = lax.axis_size("blk")
    helpers = lax.axis_size("help")
    worker = lax.axis_index("blk")
    helper = lax.axis_index("help")
    piece = cached_key_value.shape[0]
    picks = selected.shape[1] * selected.shape[2]
    assert rows == QUERY_GROUP_ROWS and head_group % heads == 0 and selected.shape[0] == 1
    assert BLOCK_TOKENS % piece == 0 and picks % HEAD_SIZE == 0 and picks // HEAD_SIZE <= rows
    per_group = piece * helpers // BLOCK_TOKENS
    query_blocks = helpers

    kv = cached_key_value.reshape(piece, 2, KEY_VALUE_HEADS, HEAD_SIZE)
    wanted = np.array([(t * heads) // head_group for t in range(groups)], np.int32)
    keys = jnp.transpose(kv[:, 0], (1, 2, 0))
    values = jnp.transpose(kv[:, 1], (1, 0, 2))
    if not np.array_equal(wanted, np.arange(KEY_VALUE_HEADS)):
        keys = jnp.take(keys, wanted, axis=0)
        values = jnp.take(values, wanted, axis=0)
    keys = lax.all_to_all(keys, "blk", 0, 0, tiled=True)
    values = lax.all_to_all(values, "blk", 0, 0, tiled=True)

    q = jnp.transpose(queries.reshape(rows, heads, HEAD_SIZE), (1, 0, 2))
    sel_rows = selected.reshape(picks // HEAD_SIZE, HEAD_SIZE).astype(jnp.bfloat16)
    sel_rows = jnp.pad(sel_rows, ((0, rows - picks // HEAD_SIZE), (0, 0)))
    q = jnp.concatenate([q, sel_rows[None]], axis=0)
    q_all = lax.all_gather(q[None], "help", axis=0, tiled=True)
    sel_all = q_all[:, heads, :picks // HEAD_SIZE].astype(jnp.int32).reshape(
        query_blocks, selected.shape[1], selected.shape[2])

    kv_head = (worker * heads) // head_group
    own = query_key_value.reshape(rows, 2, KEY_VALUE_HEADS, HEAD_SIZE)
    own = lax.dynamic_index_in_dim(own, kv_head, axis=2, keepdims=False)
    own = jnp.stack([own[:, 0].T, own[:, 1]])

    my_heads = lax.dynamic_slice_in_dim(sel_all, worker * heads, heads, axis=1)
    piece_block = per_group * jnp.arange(groups, dtype=jnp.int32) + (helper * piece) // BLOCK_TOKENS
    hit = jnp.any(my_heads[:, :, None, :] == piece_block[None, None, :, None], axis=3)
    sel_flat = hit.astype(jnp.int32).reshape(-1)
    home = helper.reshape(1).astype(jnp.int32)

    kernel = functools.partial(attend_kernel, groups=groups, heads=heads, scale=scale)
    width = heads * HEAD_SIZE
    acc, m, l = pl.pallas_call(
        kernel,
        grid_spec=pltpu.PrefetchScalarGridSpec(
            num_scalar_prefetch=2,
            grid=(query_blocks,),
            in_specs=[
                pl.BlockSpec((1, heads, rows, HEAD_SIZE), lambda b, s, h: (b, 0, 0, 0)),
                pl.BlockSpec((groups, HEAD_SIZE, piece), lambda b, s, h: (0, 0, 0)),
                pl.BlockSpec((groups, piece, HEAD_SIZE), lambda b, s, h: (0, 0, 0)),
                pl.BlockSpec((2, rows, HEAD_SIZE), lambda b, s, h: (0, 0, 0)),
            ],
            out_specs=[
                pl.BlockSpec((1, rows, width), lambda b, s, h: (b, 0, 0)),
                pl.BlockSpec((1, rows, heads), lambda b, s, h: (b, 0, 0)),
                pl.BlockSpec((1, rows, heads), lambda b, s, h: (b, 0, 0)),
            ],
            scratch_shapes=[
                pltpu.VMEM((heads * rows, max(piece, rows)), jnp.bfloat16),
                pltpu.VMEM((heads, rows, 1), jnp.float32),
                pltpu.VMEM((heads, rows, 1), jnp.float32),
                pltpu.VMEM((heads, rows, HEAD_SIZE), jnp.float32),
            ],
        ),
        out_shape=[
            jax.ShapeDtypeStruct((query_blocks, rows, width), jnp.float32),
            jax.ShapeDtypeStruct((query_blocks, rows, heads), jnp.float32),
            jax.ShapeDtypeStruct((query_blocks, rows, heads), jnp.float32),
        ],
    )(sel_flat, home, q_all, keys, values, own)

    acc = acc.reshape(query_blocks, rows, heads, HEAD_SIZE)
    state = (acc, m, l)

    def pick(t):
        t = jnp.clip(t, 0, query_blocks - 1)
        return tuple(lax.dynamic_index_in_dim(x, t, axis=0, keepdims=False) for x in state)

    def put(t, part, valid):
        t = jnp.clip(t, 0, query_blocks - 1)
        old = pick(t)
        part = (part[0], jnp.where(valid, part[1], -jnp.inf), part[2])
        new = join(old, part)
        return tuple(lax.dynamic_update_index_in_dim(x, y, t, axis=0) for x, y in zip(state, new))

    for r in range(1, helpers):
        right = lax.ppermute(pick(helper + helpers - r), "help",
                             [(z, z + 1) for z in range(0, r)])
        left = lax.ppermute(pick(helper - helpers + r), "help",
                            [(z, z - 1) for z in range(helpers - r, helpers)])
        from_left = (helper >= 1) & (helper <= r)
        state = put(helper - 1 + helpers - r, right, from_left)
        from_right = (helper >= helpers - r - 1) & (helper <= helpers - 2)
        state = put(helper + 1 - helpers + r, left, from_right)

    acc, m, l = pick(helper)
    result = acc / l[..., None]
    return result.reshape(rows, width)


def solution(mesh):
    in_specs = (P("help", "blk"), P("help", None), P(("blk", "help"), None), P("help", None, None))
    out_specs = P("help", "blk")
    return jax.shard_map(local, mesh=mesh, in_specs=in_specs, out_specs=out_specs, check_vma=False)
```

time: 234 us -> 223 us (0.953)
  starting transfers between devices: 4.47 us -> 52.6 us
  blocking collectives: 35.2 us -> 0 us
  Pallas kernels: 89.1 us -> 70.2 us
  waiting for transfers between devices: 75.5 us -> 64.4 us
  other arithmetic: 4.67 us -> 7.13 us
    reduce_scatter x2 -> x0, waiting for transfers between devices: 59.9 us -> none  [the longest x1 44.5 us: local(): acc = lax.psum_scatter(acc, 'help', scatter_dimension=0, tiled=True)]
    ppermute x0 -> x18, starting transfers between devices: none -> 43.4 us  [the longest x9 35.5 us: local(): lax.ppermute(pick(helper + helpers - r), 'help', [(z, z + 1) for z in ran...]
    ppermute x0 -> x18, waiting for transfers between devices: none -> 39.9 us  [the longest x9 26.4 us: local(): lax.ppermute(pick(helper + helpers - r), 'help', [(z, z + 1) for z in ran...]
    all_to_all x1 -> x2, waiting for transfers between devices: 0.01 us -> 22.2 us  [the longest x1 13.8 us: local(): values = lax.all_to_all(values, 'blk', 0, 0, tiled=True)]
    pmax x1 -> x0, blocking collectives: 21.8 us -> none  [local(): top = lax.pmax(m, 'help')]
    pallas_call x1, Pallas kernels: 89.1 us -> 70.2 us  [local(): pl.pallas_call(kernel, grid_spec=pltpu.PrefetchScalarGridSpec(num_scalar_...]
    all_gather x1 -> x0, blocking collectives: 13.4 us -> none  [local(): sel_all = lax.all_gather(selected, 'help', axis=0, tiled=True)]
    all_gather x1, waiting for transfers between devices: 14.9 us -> 2.28 us  [local(): q_all = lax.all_gather(q[None], 'help', axis=0, tiled=True)]
  transfers between devices with their start and end apart: 4 -> 21, of which waited for: 3 -> 10; matrix products, arithmetic and copies ran while one was open for 2% -> 6% of each run, Pallas kernels for 0% -> 0%
where the time goes in v2:
time: 223 us; the launch traced here: 222 us
  Pallas kernels  70.2 us (31%)
  waiting for transfers between devices  64.4 us (29%)
  starting transfers between devices  52.6 us (24%)
  between operations  14 us (6%)
  local copies, waits for them, and re-layouts  13.7 us (6%)
  other arithmetic  7.13 us (3%)
    pallas_call x1, Pallas kernels, local(): pl.pallas_call(kernel, grid_spec=pltpu.PrefetchScalarGridSpec(num_scalar_...  70.2 us
    ppermute x9, starting transfers between devices, local(): lax.ppermute(pick(helper + helpers - r), 'help', [(z, z + 1) for z in ran...  35.5 us
    ppermute x9, waiting for transfers between devices, local(): lax.ppermute(pick(helper + helpers - r), 'help', [(z, z + 1) for z in ran...  26.4 us
    all_to_all x1, waiting for transfers between devices, local(): values = lax.all_to_all(values, 'blk', 0, 0, tiled=True)  13.8 us
    ppermute x9, waiting for transfers between devices, local(): lax.ppermute(pick(helper - helpers + r), 'help', [(z, z - 1) for z in ran...  13.5 us
    unnamed x16, local copies, waits for them, and re-layouts  8.56 us
    all_to_all x1, waiting for transfers between devices, local(): keys = lax.all_to_all(keys, 'blk', 0, 0, tiled=True)  8.42 us
    ppermute x9, starting transfers between devices, local(): lax.ppermute(pick(helper - helpers + r), 'help', [(z, z - 1) for z in ran...  7.92 us
  transfers between devices with their start and end apart: 21, of which 10 were waited for; matrix products, arithmetic and copies ran while one was open for 6% of the time, Pallas kernels for 0%

profile of v2, /device:TPU:2, one launch (start us, length us, event | category | flops | bytes accessed | tf_op | source)
XLA Modules:
  0.0 222.1 jit_solution(3352944980446820965)
XLA Ops:
  6.5 1.1 copy.28
  7.7 0.7 convert_element_type.22
  8.4 0.1 copy.29
  8.5 0.1 convert_element_type.23
  8.6 0.1 copy.30
  8.8 0.9 copy.31
  9.7 0.0 all-gather.3.cloned.1.call-update
  9.7 2.9 %copy.32 = bf16[512,2048]{0,1:T(8,128)(2,1)S(1)} copy(bf16[512,2048]{1,0:T(8,128)(2,1)} %param.6) | data formatting | bytes 4194304 | tf_op args[2]
  12.6 1.2 fusion.27
  13.8 1.3 copy.36
  15.1 4.3 %all-to-all-start.1 = ((bf16[8,512,128]{2,1,0:T(8,128)(2,1)}), bf16[8,512,128]{2,1,0:T(8,128)(2,1)S(1)}, u32[]{:S(2)}, u32[]{:S(2)}) async-start(bf16[8,512,128]{2,1,0:T(8,128)(2,1)} %bitcast.9), calls=%async_computation.1 | async-start | bytes 2097152 | tf_op jit(solution)/shard_map/all_to_all | solution.py:106
  19.3 0.1 copy.38
  19.5 13.8 %all-to-all-done.1.v_ref = bf16[8,512,128]{2,1,0:T(8,128)(2,1)S(1)} async-done(((bf16[8,512,128]{2,1,0:T(8,128)(2,1)}), bf16[8,512,128]{2,1,0:T(8,128)(2,1)S(1)}, u32[]{:S(2)}, u32[]{:S(2)}) %all-to-all-start.1) | async-done | bytes 1048608 | tf_op jit(solution)/shard_map/all_to_all | solution.py:106
  33.2 5.0 %all-to-all-start = ((bf16[8,128,512]{2,1,0:T(8,128)(2,1)}), bf16[8,128,512]{2,1,0:T(8,128)(2,1)S(1)}, u32[]{:S(2)}, u32[]{:S(2)}) async-start(bf16[8,128,512]{2,1,0:T(8,128)(2,1)} %get-tuple-element.47), calls=%async_computation | async-start | bytes 2097152 | tf_op jit(solution)/shard_map/all_to_all | solution.py:105
  38.2 0.1 constant_dynamic-slice_fusion.13
  38.4 0.1 copy.35
  38.6 0.6 pad_maximum_fusion.1.own_ref
  39.2 2.3 %all-gather.3.cloned.1.call-done = bf16[36,128,128]{2,1,0:T(8,128)(2,1)} async-done(((bf16[9,128,128]{2,1,0:T(8,128)(2,1)}), bf16[36,128,128]{2,1,0:T(8,128)(2,1)}) %all-gather.3.cloned.1.call-update) | async-done | bytes 1179664 | tf_op jit(solution)/shard_map/all_gather | solution.py:112
  41.5 0.7 slice_convert_fusion
  42.2 0.1 reshape.53
  42.3 0.7 compare_reduce_fusion
  43.0 0.7 reshape.54.sel_ref
  43.7 8.4 %all-to-all-done.kt_ref = bf16[8,128,512]{2,1,0:T(8,128)(2,1)S(1)} async-done(((bf16[8,128,512]{2,1,0:T(8,128)(2,1)}), bf16[8,128,512]{2,1,0:T(8,128)(2,1)S(1)}, u32[]{:S(2)}, u32[]{:S(2)}) %all-to-all-start) | async-done | bytes 1048608 | tf_op jit(solution)/shard_map/all_to_all | solution.py:105
  52.1 1.0 copy-done.1
  53.1 70.2 %shard_map.46 = (f32[4,128,1024]{2,1,0:T(8,128)}, f32[4,128,8]{2,1,0:T(8,128)}, f32[4,128,8]{2,1,0:T(8,128)}) custom-call(s32[256]{0:T(256)} %reshape.54.sel_ref, s32[1]{0:T(128)} %bitcast.4.home_ref, bf16[4,9,128,128]{3,2,1,0:T(8,128)(2,1)} %bitcast.241, bf16[8,128,512]{2,1,0:T(8,128)(2,1)} %copy-done.1, bf16[8,512,128]{2,1,0:T(8,128)(2,1)} %copy-done, ...), custom_call_target="tpu_custom_call" | custom-call | tf_op jit(solution)/shard_map/pallas_call | solution.py:129
  123.3 2.1 copy.39
  125.4 3.5 %collective-permute-start.12 = (f32[128,8]{1,0:T(8,128)S(1)}, f32[128,8]{1,0:T(8,128)S(1)}, u32[]{:S(2)}, u32[]{:S(2)}) collective-permute-start(f32[128,8]{1,0:T(8,128)S(1)} %get-tuple-element.61), channel_id=1, source_target_pairs={{0,1},{4,5},{8,9},{12,13},{16,17},{20,21},{24,25},{28,29}} | collective-permute-start | bytes 12296 | tf_op jit(solution)/shard_map/ppermute | solution.py:174
  128.9 1.3 collective-permute-start
  130.2 0.1 dynamic-slice_bitcast_fusion.5
  130.3 1.3 collective-permute-start.1
  131.7 0.0 collective-permute-done.12
  131.7 0.8 collective-permute-done
  132.5 0.7 collective-permute-start.2
  133.2 0.7 collective-permute-start.13
  133.9 9.4 %collective-permute-done.1 = f32[128,8,128]{2,1,0:T(8,128)S(1)} collective-permute-done((f32[128,8,128]{2,1,0:T(8,128)S(1)}, f32[128,8,128]{2,1,0:T(8,128)S(1)}, u32[]{:S(2)}, u32[]{:S(2)}) %collective-permute-start.1) | collective-permute-done | bytes 524320 | tf_op jit(solution)/shard_map/ppermute | solution.py:174
  143.3 0.3 dynamic-slice_bitcast_fusion.4
  143.7 0.7 collective-permute-start.3
  144.4 4.4 %collective-permute-start.4 = (f32[128,8]{1,0:T(8,128)S(1)}, f32[128,8]{1,0:T(8,128)S(1)}, u32[]{:S(2)}, u32[]{:S(2)}) collective-permute-start(f32[128,8]{1,0:T(8,128)S(1)} %dynamic-slice_bitcast_fusion.16), channel_id=1, source_target_pairs={{0,1},{1,2},{4,5},{5,6},{8,9},{9,10},{12,13},{13,14},{16,17},{17,1... | collective-permute-start | bytes 12296 | tf_op jit(solution)/shard_map/ppermute | solution.py:174
  148.8 1.9 collective-permute-start.14
  150.8 0.3 bitcast_dynamic-update-slice_fusion.4
  151.2 0.1 dynamic-slice_bitcast_fusion.3
  151.2 1.9 collective-permute-start.5
  153.2 0.0 collective-permute-done.4
  153.3 0.7 collective-permute-start.6
  154.0 0.7 collective-permute-start.15
  154.7 9.3 %collective-permute-done.5 = f32[128,8,128]{2,1,0:T(8,128)S(1)} collective-permute-done((f32[128,8,128]{2,1,0:T(8,128)S(1)}, f32[128,8,128]{2,1,0:T(8,128)S(1)}, u32[]{:S(2)}, u32[]{:S(2)}) %collective-permute-start.5) | collective-permute-done | bytes 524320 | tf_op jit(solution)/shard_map/ppermute | solution.py:174
  164.0 0.3 dynamic-slice_bitcast_fusion.2
  164.4 0.7 collective-permute-start.7
  165.2 5.0 %collective-permute-start.8 = (f32[128,8]{1,0:T(8,128)S(1)}, f32[128,8]{1,0:T(8,128)S(1)}, u32[]{:S(2)}, u32[]{:S(2)}) collective-permute-start(f32[128,8]{1,0:T(8,128)S(1)} %dynamic-slice_bitcast_fusion.14), channel_id=1, source_target_pairs={{0,1},{1,2},{2,3},{4,5},{5,6},{6,7},{8,9},{9,10},{10,11},{12,13},{... | collective-permute-start | bytes 12296 | tf_op jit(solution)/shard_map/ppermute | solution.py:174
  170.2 0.3 bitcast_dynamic-update-slice_fusion.2
  170.6 0.9 dynamic-slice_bitcast_fusion.1
  171.5 13.6 %collective-permute-start.9 = (f32[128,8,128]{2,1,0:T(8,128)}, f32[128,8,128]{2,1,0:T(8,128)}, u32[]{:S(2)}, u32[]{:S(2)}) collective-permute-start(f32[128,8,128]{2,1,0:T(8,128)} %get-tuple-element.36), channel_id=1, source_target_pairs={{0,1},{1,2},{2,3},{4,5},{5,6},{6,7},{8,9},{9,10},{10,11},{12,13},{... | collective-permute-start | bytes 1572872 | tf_op jit(solution)/shard_map/ppermute | solution.py:174
  185.1 2.5 %collective-permute-start.16 = (f32[128,8]{1,0:T(8,128)S(1)}, f32[128,8]{1,0:T(8,128)S(1)}, u32[]{:S(2)}, u32[]{:S(2)}) collective-permute-start(f32[128,8]{1,0:T(8,128)S(1)} %get-tuple-element.51), channel_id=1, source_target_pairs={{0,1},{1,2},{2,3},{4,5},{5,6},{6,7},{8,9},{9,10},{10,11},{12,13},{... | collective-permute-start | bytes 12296 | tf_op jit(solution)/shard_map/ppermute | solution.py:174
  187.7 6.9 %collective-permute-done.16 = f32[128,8]{1,0:T(8,128)S(1)} collective-permute-done((f32[128,8]{1,0:T(8,128)S(1)}, f32[128,8]{1,0:T(8,128)S(1)}, u32[]{:S(2)}, u32[]{:S(2)}) %collective-permute-start.16) | collective-permute-done | bytes 4128 | tf_op jit(solution)/shard_map/ppermute | solution.py:174
  194.7 1.3 collective-permute-start.10
  196.0 1.3 collective-permute-start.17
  197.3 1.4 dynamic-slice_bitcast_fusion
  198.7 1.3 collective-permute-start.11
  200.0 1.3 collective-permute-done.10
  201.3 2.6 %collective-permute-done.17 = f32[128,8]{1,0:T(8,128)S(1)} collective-permute-done((f32[128,8]{1,0:T(8,128)S(1)}, f32[128,8]{1,0:T(8,128)S(1)}, u32[]{:S(2)}, u32[]{:S(2)}) %collective-permute-start.17) | collective-permute-done | bytes 4128 | tf_op jit(solution)/shard_map/ppermute | solution.py:176
  204.0 9.6 %collective-permute-done.11 = f32[128,8,128]{2,1,0:T(8,128)S(1)} collective-permute-done((f32[128,8,128]{2,1,0:T(8,128)S(1)}, f32[128,8,128]{2,1,0:T(8,128)S(1)}, u32[]{:S(2)}, u32[]{:S(2)}) %collective-permute-start.11) | collective-permute-done | bytes 524320 | tf_op jit(solution)/shard_map/ppermute | solution.py:176
  213.6 0.3 bitcast_dynamic-update-slice_fusion
  214.0 0.2 div.35
  214.2 1.0 bitcast_divide_fusion
  (51 shorter events, 0.8 us)
Async XLA Ops:
  6.5 35.0 %all-gather.3.cloned.1.call-start = ((), (), s32[]{:S(2)}) async-start(), calls=%async_computation.2 | async-start | bytes 1474560 | tf_op jit(solution)/shard_map/all_gather | solution.py:112
  13.8 5.6 %copy-start.4 = (bf16[128,2048]{1,0:T(8,128)(2,1)S(1)}, bf16[128,2048]{1,0:T(8,128)(2,1)}, u32[]{:S(2)}) copy-start(bf16[128,2048]{1,0:T(8,128)(2,1)} %param.5) | copy-start | bytes 1572868
  15.1 18.2 %all-to-all-start.1 = ((bf16[8,512,128]{2,1,0:T(8,128)(2,1)}), bf16[8,512,128]{2,1,0:T(8,128)(2,1)S(1)}, u32[]{:S(2)}, u32[]{:S(2)}) async-start(bf16[8,512,128]{2,1,0:T(8,128)(2,1)} %bitcast.9), calls=%async_computation.1 | async-start | bytes 2097152 | tf_op jit(solution)/shard_map/all_to_all | solution.py:106
  33.2 18.9 %copy-start = (bf16[8,512,128]{2,1,0:T(8,128)(2,1)}, bf16[8,512,128]{2,1,0:T(8,128)(2,1)S(1)}, u32[]{:S(2)}) copy-start(bf16[8,512,128]{2,1,0:T(8,128)(2,1)S(1)} %all-to-all-done.1.v_ref) | copy-start | bytes 3145732
  33.2 18.9 %all-to-all-start = ((bf16[8,128,512]{2,1,0:T(8,128)(2,1)}), bf16[8,128,512]{2,1,0:T(8,128)(2,1)S(1)}, u32[]{:S(2)}, u32[]{:S(2)}) async-start(bf16[8,128,512]{2,1,0:T(8,128)(2,1)} %get-tuple-element.47), calls=%async_computation | async-start | bytes 2097152 | tf_op jit(solution)/shard_map/all_to_all | solution.py:105
  52.1 1.0 copy-start.1
  123.3 2.1 copy-start.2
  123.3 5.6 %copy-start.3 = (f32[4,128,8]{2,1,0:T(8,128)S(1)}, f32[4,128,8]{2,1,0:T(8,128)}, u32[]{:S(2)}) copy-start(f32[4,128,8]{2,1,0:T(8,128)} %get-tuple-element.9) | copy-start | bytes 49156
  125.4 6.2 %collective-permute-start.12 = (f32[128,8]{1,0:T(8,128)S(1)}, f32[128,8]{1,0:T(8,128)S(1)}, u32[]{:S(2)}, u32[]{:S(2)}) collective-permute-start(f32[128,8]{1,0:T(8,128)S(1)} %get-tuple-element.61), channel_id=1, source_target_pairs={{0,1},{4,5},{8,9},{12,13},{16,17},{20,21},{24,25},{28,29}} | collective-permute-start | bytes 12296 | tf_op jit(solution)/shard_map/ppermute | solution.py:174
  128.9 3.5 %collective-permute-start = (f32[128,8]{1,0:T(8,128)S(1)}, f32[128,8]{1,0:T(8,128)S(1)}, u32[]{:S(2)}, u32[]{:S(2)}) collective-permute-start(f32[128,8]{1,0:T(8,128)S(1)} %dynamic-slice_bitcast_fusion.18), channel_id=1, source_target_pairs={{0,1},{4,5},{8,9},{12,13},{16,17},{20,21},{24,25},{28,29}} | collective-permute-start | bytes 12296 | tf_op jit(solution)/shard_map/ppermute | solution.py:174
  130.3 13.0 %collective-permute-start.1 = (f32[128,8,128]{2,1,0:T(8,128)S(1)}, f32[128,8,128]{2,1,0:T(8,128)S(1)}, u32[]{:S(2)}, u32[]{:S(2)}) collective-permute-start(f32[128,8,128]{2,1,0:T(8,128)S(1)} %get-tuple-element.44), channel_id=1, source_target_pairs={{0,1},{4,5},{8,9},{12,13},{16,17},{20,21},{24,25},{28,29}} | collective-permute-start | bytes 1572872 | tf_op jit(solution)/shard_map/ppermute | solution.py:174
  132.5 1.4 collective-permute-start.2
  133.2 0.7 collective-permute-start.13
  143.7 7.1 %collective-permute-start.3 = (f32[128,8,128]{2,1,0:T(8,128)S(1)}, f32[128,8,128]{2,1,0:T(8,128)S(1)}, u32[]{:S(2)}, u32[]{:S(2)}) collective-permute-start(f32[128,8,128]{2,1,0:T(8,128)S(1)} %get-tuple-element.42), channel_id=1, source_target_pairs={{3,2},{7,6},{11,10},{15,14},{19,18},{23,22},{27,26},{31,30}} | collective-permute-start | bytes 1572872 | tf_op jit(solution)/shard_map/ppermute | solution.py:176
  144.4 8.8 %collective-permute-start.4 = (f32[128,8]{1,0:T(8,128)S(1)}, f32[128,8]{1,0:T(8,128)S(1)}, u32[]{:S(2)}, u32[]{:S(2)}) collective-permute-start(f32[128,8]{1,0:T(8,128)S(1)} %dynamic-slice_bitcast_fusion.16), channel_id=1, source_target_pairs={{0,1},{1,2},{4,5},{5,6},{8,9},{9,10},{12,13},{13,14},{16,17},{17,1... | collective-permute-start | bytes 12296 | tf_op jit(solution)/shard_map/ppermute | solution.py:174
  148.8 4.4 %collective-permute-start.14 = (f32[128,8]{1,0:T(8,128)S(1)}, f32[128,8]{1,0:T(8,128)S(1)}, u32[]{:S(2)}, u32[]{:S(2)}) collective-permute-start(f32[128,8]{1,0:T(8,128)S(1)} %get-tuple-element.56), channel_id=1, source_target_pairs={{0,1},{1,2},{4,5},{5,6},{8,9},{9,10},{12,13},{13,14},{16,17},{17,1... | collective-permute-start | bytes 12296 | tf_op jit(solution)/shard_map/ppermute | solution.py:174
  151.2 12.8 %collective-permute-start.5 = (f32[128,8,128]{2,1,0:T(8,128)S(1)}, f32[128,8,128]{2,1,0:T(8,128)S(1)}, u32[]{:S(2)}, u32[]{:S(2)}) collective-permute-start(f32[128,8,128]{2,1,0:T(8,128)S(1)} %get-tuple-element.40), channel_id=1, source_target_pairs={{0,1},{1,2},{4,5},{5,6},{8,9},{9,10},{12,13},{13,14},{16,17},{17,1... | collective-permute-start | bytes 1572872 | tf_op jit(solution)/shard_map/ppermute | solution.py:174
  153.3 11.8 %collective-permute-start.6 = (f32[128,8]{1,0:T(8,128)S(1)}, f32[128,8]{1,0:T(8,128)S(1)}, u32[]{:S(2)}, u32[]{:S(2)}) collective-permute-start(f32[128,8]{1,0:T(8,128)S(1)} %get-tuple-element.54), channel_id=1, source_target_pairs={{2,1},{3,2},{6,5},{7,6},{10,9},{11,10},{14,13},{15,14},{18,17},{19... | collective-permute-start | bytes 12296 | tf_op jit(solution)/shard_map/ppermute | solution.py:176
  154.0 11.1 %collective-permute-start.15 = (f32[128,8]{1,0:T(8,128)S(1)}, f32[128,8]{1,0:T(8,128)S(1)}, u32[]{:S(2)}, u32[]{:S(2)}) collective-permute-start(f32[128,8]{1,0:T(8,128)S(1)} %get-tuple-element.55), channel_id=1, source_target_pairs={{2,1},{3,2},{6,5},{7,6},{10,9},{11,10},{14,13},{15,14},{18,17},{19... | collective-permute-start | bytes 12296 | tf_op jit(solution)/shard_map/ppermute | solution.py:176
  164.4 5.9 %collective-permute-start.7 = (f32[128,8,128]{2,1,0:T(8,128)S(1)}, f32[128,8,128]{2,1,0:T(8,128)S(1)}, u32[]{:S(2)}, u32[]{:S(2)}) collective-permute-start(f32[128,8,128]{2,1,0:T(8,128)S(1)} %get-tuple-element.38), channel_id=1, source_target_pairs={{2,1},{3,2},{6,5},{7,6},{10,9},{11,10},{14,13},{15,14},{18,17},{19... | collective-permute-start | bytes 1572872 | tf_op jit(solution)/shard_map/ppermute | solution.py:176
  165.2 22.5 %collective-permute-start.8 = (f32[128,8]{1,0:T(8,128)S(1)}, f32[128,8]{1,0:T(8,128)S(1)}, u32[]{:S(2)}, u32[]{:S(2)}) collective-permute-start(f32[128,8]{1,0:T(8,128)S(1)} %dynamic-slice_bitcast_fusion.14), channel_id=1, source_target_pairs={{0,1},{1,2},{2,3},{4,5},{5,6},{6,7},{8,9},{9,10},{10,11},{12,13},{... | collective-permute-start | bytes 12296 | tf_op jit(solution)/shard_map/ppermute | solution.py:174
  171.5 25.8 %collective-permute-start.9 = (f32[128,8,128]{2,1,0:T(8,128)}, f32[128,8,128]{2,1,0:T(8,128)}, u32[]{:S(2)}, u32[]{:S(2)}) collective-permute-start(f32[128,8,128]{2,1,0:T(8,128)} %get-tuple-element.36), channel_id=1, source_target_pairs={{0,1},{1,2},{2,3},{4,5},{5,6},{6,7},{8,9},{9,10},{10,11},{12,13},{... | collective-permute-start | bytes 1572872 | tf_op jit(solution)/shard_map/ppermute | solution.py:174
  185.1 9.5 %collective-permute-start.16 = (f32[128,8]{1,0:T(8,128)S(1)}, f32[128,8]{1,0:T(8,128)S(1)}, u32[]{:S(2)}, u32[]{:S(2)}) collective-permute-start(f32[128,8]{1,0:T(8,128)S(1)} %get-tuple-element.51), channel_id=1, source_target_pairs={{0,1},{1,2},{2,3},{4,5},{5,6},{6,7},{8,9},{9,10},{10,11},{12,13},{... | collective-permute-start | bytes 12296 | tf_op jit(solution)/shard_map/ppermute | solution.py:174
  194.7 6.6 %collective-permute-start.10 = (f32[128,8]{1,0:T(8,128)S(1)}, f32[128,8]{1,0:T(8,128)S(1)}, u32[]{:S(2)}, u32[]{:S(2)}) collective-permute-start(f32[128,8]{1,0:T(8,128)S(1)} %get-tuple-element.48), channel_id=1, source_target_pairs={{1,0},{2,1},{3,2},{5,4},{6,5},{7,6},{9,8},{10,9},{11,10},{13,12},{... | collective-permute-start | bytes 12296 | tf_op jit(solution)/shard_map/ppermute | solution.py:176
  196.0 7.9 %collective-permute-start.17 = (f32[128,8]{1,0:T(8,128)S(1)}, f32[128,8]{1,0:T(8,128)S(1)}, u32[]{:S(2)}, u32[]{:S(2)}) collective-permute-start(f32[128,8]{1,0:T(8,128)S(1)} %get-tuple-element.50), channel_id=1, source_target_pairs={{1,0},{2,1},{3,2},{5,4},{6,5},{7,6},{9,8},{10,9},{11,10},{13,12},{... | collective-permute-start | bytes 12296 | tf_op jit(solution)/shard_map/ppermute | solution.py:176
  198.7 15.0 %collective-permute-start.11 = (f32[128,8,128]{2,1,0:T(8,128)S(1)}, f32[128,8,128]{2,1,0:T(8,128)S(1)}, u32[]{:S(2)}, u32[]{:S(2)}) collective-permute-start(f32[128,8,128]{2,1,0:T(8,128)S(1)} %get-tuple-element.34), channel_id=1, source_target_pairs={{1,0},{2,1},{3,2},{5,4},{6,5},{7,6},{9,8},{10,9},{11,10},{13,12},{... | collective-permute-start | bytes 1572872 | tf_op jit(solution)/shard_map/ppermute | solution.py:176
Sparse Core Ops, SparseCore 0:
  9.8 31.6 all-gather.2

commit v3 on v2

--- a/solution.py
+++ b/solution.py
@@ -16,8 +16,8 @@
 QUERY_GROUP_ROWS = 128
 
 
-def attend_kernel(sel_ref, home_ref, q_ref, kt_ref, v_ref, own_ref, acc_ref, m_ref, l_ref,
-                  p_buf, m_scr, l_scr, acc_scr, *, groups, heads, scale):
+def attend_kernel(sel_ref, home_ref, q_ref, kv_ref, own_ref, acc_ref, m_ref, l_ref,
+                  p_buf, m_scr, l_scr, acc_scr, *, groups, heads, chunks, factor):
     b = pl.program_id(0)
     rows = QUERY_GROUP_ROWS
     q = q_ref[0].reshape(heads * rows, HEAD_SIZE)
@@ -25,31 +25,46 @@
     l_scr[...] = jnp.zeros(l_scr.shape, jnp.float32)
     acc_scr[...] = jnp.zeros(acc_scr.shape, jnp.float32)
 
-    def update(s, value, bias_of):
+    def update(s, value, on_of, mask):
+        width = s.shape[1]
         for h in range(heads):
-            s_h = s[h * rows:(h + 1) * rows] * scale + bias_of(h)
-            m_old = m_scr[h]
-            m_new = jnp.maximum(m_old, jnp.max(s_h, axis=1, keepdims=True))
-            m_safe = jnp.where(m_new == -jnp.inf, 0.0, m_new)
-            alpha = jnp.exp(m_old - m_safe)
-            p = jnp.exp(s_h - m_safe)
-            l_scr[h] = alpha * l_scr[h] + jnp.sum(p, axis=1, keepdims=True)
-            m_scr[h] = m_new
-            acc_scr[h] = alpha * acc_scr[h]
-            p_buf[h * rows:(h + 1) * rows, :s.shape[1]] = p.astype(jnp.bfloat16)
-        width = s.shape[1]
+            on = on_of(h)
+
+            @pl.when(on)
+            def _():
+                s_h = s[h * rows:(h + 1) * rows] * factor
+                if mask is not None:
+                    s_h = jnp.where(mask, s_h, -jnp.inf)
+                m_old = m_scr[h]
+                m_new = jnp.maximum(m_old, jnp.max(s_h, axis=1, keepdims=True))
+                m_safe = jnp.where(m_new == -jnp.inf, 0.0, m_new)
+                alpha = jnp.exp2(m_old - m_safe)
+                p = jnp.exp2(s_h - m_safe)
+                l_scr[h] = alpha * l_scr[h] + jnp.sum(p, axis=1, keepdims=True)
+                m_scr[h] = m_new
+                acc_scr[h] = alpha * acc_scr[h]
+                p_buf[h * rows:(h + 1) * rows, :width] = p.astype(jnp.bfloat16)
+
+            @pl.when(jnp.logical_not(on))
+            def _():
+                p_buf[h * rows:(h + 1) * rows, :width] = jnp.zeros((rows, width), jnp.bfloat16)
+
         pv = jnp.dot(p_buf[:, :width], value, preferred_element_type=jnp.float32)
         for h in range(heads):
-            acc_scr[h] += pv[h * rows:(h + 1) * rows]
+            @pl.when(on_of(h))
+            def _():
+                acc_scr[h] += pv[h * rows:(h + 1) * rows]
 
     def piece(g, carry):
         base = b * heads * groups + g
-
-        def bias_of(h):
-            return jnp.where(sel_ref[base + h * groups] != 0, 0.0, -jnp.inf)
-
-        s = jnp.dot(q, kt_ref[g], preferred_element_type=jnp.float32)
-        update(s, v_ref[g], bias_of)
+        if chunks == 1:
+            s = jnp.dot(q, kv_ref[g, 0, 0], preferred_element_type=jnp.float32)
+        else:
+            s = jnp.concatenate(
+                [jnp.dot(q, kv_ref[g, 0, c], preferred_element_type=jnp.float32)
+                 for c in range(chunks)], axis=1)
+        value = kv_ref[g, 1].reshape(chunks * HEAD_SIZE, HEAD_SIZE)
+        update(s, value, lambda h: sel_ref[base + h * groups] != 0, None)
         return carry
 
     lax.fori_loop(0, groups, piece, 0)
@@ -58,9 +73,8 @@
     def _():
         causal = lax.broadcasted_iota(jnp.int32, (rows, rows), 0) >= lax.broadcasted_iota(
             jnp.int32, (rows, rows), 1)
-        mask = jnp.where(causal, 0.0, -jnp.inf)
         s = jnp.dot(q, own_ref[0], preferred_element_type=jnp.float32)
-        update(s, own_ref[1], lambda h: mask)
+        update(s, own_ref[1], lambda h: True, causal)
 
     for h in range(heads):
         acc_ref[0, :, h * HEAD_SIZE:(h + 1) * HEAD_SIZE] = acc_scr[h]
@@ -73,8 +87,8 @@
     acc_b, m_b, l_b = b
     m = jnp.maximum(m_a, m_b)
     m_safe = jnp.where(m == -jnp.inf, 0.0, m)
-    f_a = jnp.exp(m_a - m_safe)
-    f_b = jnp.exp(m_b - m_safe)
+    f_a = jnp.exp2(m_a - m_safe)
+    f_b = jnp.exp2(m_b - m_safe)
     acc = acc_a * f_a[..., None] + acc_b * f_b[..., None]
     return acc, m, l_a * f_a + l_b * f_b
 
@@ -91,19 +105,19 @@
     piece = cached_key_value.shape[0]
     picks = selected.shape[1] * selected.shape[2]
     assert rows == QUERY_GROUP_ROWS and head_group % heads == 0 and selected.shape[0] == 1
-    assert BLOCK_TOKENS % piece == 0 and picks % HEAD_SIZE == 0 and picks // HEAD_SIZE <= rows
+    assert BLOCK_TOKENS % piece == 0 and piece % HEAD_SIZE == 0 and picks % HEAD_SIZE == 0 and picks // HEAD_SIZE <= rows
     per_group = piece * helpers // BLOCK_TOKENS
     query_blocks = helpers
 
     kv = cached_key_value.reshape(piece, 2, KEY_VALUE_HEADS, HEAD_SIZE)
     wanted = np.array([(t * heads) // head_group for t in range(groups)], np.int32)
-    keys = jnp.transpose(kv[:, 0], (1, 2, 0))
-    values = jnp.transpose(kv[:, 1], (1, 0, 2))
     if not np.array_equal(wanted, np.arange(KEY_VALUE_HEADS)):
-        keys = jnp.take(keys, wanted, axis=0)
-        values = jnp.take(values, wanted, axis=0)
-    keys = lax.all_to_all(keys, "blk", 0, 0, tiled=True)
-    values = lax.all_to_all(values, "blk", 0, 0, tiled=True)
+        kv = jnp.take(kv, wanted, axis=2)
+    chunks = piece // HEAD_SIZE
+    kv = kv.reshape(chunks, HEAD_SIZE, 2, groups, HEAD_SIZE)
+    keys = jnp.transpose(kv[:, :, 0], (2, 0, 3, 1))
+    values = jnp.transpose(kv[:, :, 1], (2, 0, 1, 3))
+    held = lax.all_to_all(jnp.stack([keys, values], axis=1), "blk", 0, 0, tiled=True)
 
     q = jnp.transpose(queries.reshape(rows, heads, HEAD_SIZE), (1, 0, 2))
     sel_rows = selected.reshape(picks // HEAD_SIZE, HEAD_SIZE).astype(jnp.bfloat16)
@@ -124,7 +138,8 @@
     sel_flat = hit.astype(jnp.int32).reshape(-1)
     home = helper.reshape(1).astype(jnp.int32)
 
-    kernel = functools.partial(attend_kernel, groups=groups, heads=heads, scale=scale)
+    kernel = functools.partial(attend_kernel, groups=groups, heads=heads, chunks=chunks,
+                               factor=scale * math.log2(math.e))
     width = heads * HEAD_SIZE
     acc, m, l = pl.pallas_call(
         kernel,
@@ -133,8 +148,7 @@
             grid=(query_blocks,),
             in_specs=[
                 pl.BlockSpec((1, heads, rows, HEAD_SIZE), lambda b, s, h: (b, 0, 0, 0)),
-                pl.BlockSpec((groups, HEAD_SIZE, piece), lambda b, s, h: (0, 0, 0)),
-                pl.BlockSpec((groups, piece, HEAD_SIZE), lambda b, s, h: (0, 0, 0)),
+                pl.BlockSpec((groups, 2, chunks, HEAD_SIZE, HEAD_SIZE), lambda b, s, h: (0, 0, 0, 0, 0)),
                 pl.BlockSpec((2, rows, HEAD_SIZE), lambda b, s, h: (0, 0, 0)),
             ],
             out_specs=[
@@ -154,7 +168,7 @@
             jax.ShapeDtypeStruct((query_blocks, rows, heads), jnp.float32),
             jax.ShapeDtypeStruct((query_blocks, rows, heads), jnp.float32),
         ],
-    )(sel_flat, home, q_all, keys, values, own)
+    )(sel_flat, home, q_all, held, own)
 
     acc = acc.reshape(query_blocks, rows, heads, HEAD_SIZE)
     state = (acc, m, l)

time: 223 us -> 230 us (1.031)
  the two profiles are of different devices: /device:TPU:2 before, /device:TPU:0 now
where the time goes in v3:
time: 230 us; the launch traced here: 231 us
  Pallas kernels  76.3 us (33%)
  waiting for transfers between devices  63 us (27%)
  starting transfers between devices  58 us (25%)
  between operations  14 us (6%)
  local copies, waits for them, and re-layouts  10.7 us (5%)
  other arithmetic  8.7 us (4%)
    pallas_call x1, Pallas kernels, local(): pl.pallas_call(kernel, grid_spec=pltpu.PrefetchScalarGridSpec(num_scalar_...  76.3 us
    ppermute x9, starting transfers between devices, local(): lax.ppermute(pick(helper + helpers - r), 'help', [(z, z + 1) for z in ran...  44.8 us
    ppermute x9, waiting for transfers between devices, local(): lax.ppermute(pick(helper + helpers - r), 'help', [(z, z + 1) for z in ran...  24.5 us
    all_gather x1, waiting for transfers between devices, local(): q_all = lax.all_gather(q[None], 'help', axis=0, tiled=True)  23.3 us
    ppermute x9, waiting for transfers between devices, local(): lax.ppermute(pick(helper - helpers + r), 'help', [(z, z - 1) for z in ran...  15.1 us
    ppermute x9, starting transfers between devices, local(): lax.ppermute(pick(helper - helpers + r), 'help', [(z, z - 1) for z in ran...  7.92 us
    unnamed x17, local copies, waits for them, and re-layouts  6.51 us
    all_to_all x1, starting transfers between devices, local(): lax.all_to_all(jnp.stack([keys, values], axis=1), 'blk', 0, 0, tiled=True)  5.3 us
  transfers between devices with their start and end apart: 20, of which 9 were waited for; matrix products, arithmetic and copies ran while one was open for 5% of the time, Pallas kernels for 0%

profile of v3, /device:TPU:0, one launch (start us, length us, event | category | flops | bytes accessed | tf_op | source)
XLA Modules:
  0.0 230.8 jit_solution(12994644845754822030)
XLA Ops:
  6.5 1.3 copy.28
  7.8 0.7 convert_element_type.22
  8.5 0.1 copy.29
  8.6 0.1 convert_element_type.23
  8.7 0.1 copy.30
  8.9 0.9 copy.31
  9.8 0.6 copy.39
  10.5 0.4 fusion.34
  10.8 0.2 copy.48
  11.1 0.8 copy.36
  11.9 1.5 pad_maximum_fusion
  13.4 5.3 %all-to-all-start = ((bf16[8,2,4,128,128]{4,3,2,1,0:T(8,128)(2,1)}), bf16[8,2,4,128,128]{4,3,2,1,0:T(8,128)(2,1)S(1)}, u32[]{:S(2)}, u32[]{:S(2)}) async-start(bf16[8,2,4,128,128]{4,3,2,1,0:T(8,128)(2,1)} %pad_maximum_fusion), calls=%async_computation | async-start | bytes 4194304 | tf_op jit(solution)/shard_map/all_to_all | solution.py:120
  18.7 0.1 copy.40
  18.8 0.1 constant_dynamic-slice_fusion.13
  19.0 0.1 copy.35
  19.2 0.6 pad_maximum_fusion.2.own_ref
  19.8 23.3 %all-gather.3.cloned.1.call-done = bf16[36,128,128]{2,1,0:T(8,128)(2,1)} async-done(((bf16[9,128,128]{2,1,0:T(8,128)(2,1)}), bf16[36,128,128]{2,1,0:T(8,128)(2,1)}) %all-gather.3.cloned.1.call-update) | async-done | bytes 1179664 | tf_op jit(solution)/shard_map/all_gather | solution.py:126
  43.1 0.7 slice_convert_fusion
  43.8 0.1 reshape.49
  44.0 0.7 compare_reduce_fusion
  44.7 0.6 reshape.50.sel_ref
  45.3 0.1 all-to-all-done.kv_ref
  45.4 1.3 copy-done
  46.7 76.3 %shard_map.46 = (f32[4,128,1024]{2,1,0:T(8,128)}, f32[4,128,8]{2,1,0:T(8,128)}, f32[4,128,8]{2,1,0:T(8,128)}) custom-call(s32[256]{0:T(256)} %reshape.50.sel_ref, s32[1]{0:T(128)} %bitcast.4.home_ref, bf16[4,9,128,128]{3,2,1,0:T(8,128)(2,1)} %bitcast.265, bf16[8,2,4,128,128]{4,3,2,1,0:T(8,128)(2,1)} %copy-done, bf16[2,128,128]{2,1,0:T(8,128)(2,1)} %pad_maximum_fusion.2.own_ref), custom_call_target="tpu_custom_call" | custom-call | tf_op jit(solution)/shard_map/pallas_call | solution.py:144
  123.0 2.1 copy.41
  125.2 3.5 %collective-permute-start.12 = (f32[128,8]{1,0:T(8,128)S(1)}, f32[128,8]{1,0:T(8,128)S(1)}, u32[]{:S(2)}, u32[]{:S(2)}) collective-permute-start(f32[128,8]{1,0:T(8,128)S(1)} %get-tuple-element.61), channel_id=1, source_target_pairs={{0,1},{4,5},{8,9},{12,13},{16,17},{20,21},{24,25},{28,29}} | collective-permute-start | bytes 12296 | tf_op jit(solution)/shard_map/ppermute | solution.py:188
  128.7 1.3 collective-permute-start
  130.0 0.1 dynamic-slice_bitcast_fusion.5
  130.1 1.3 collective-permute-start.1
  131.4 1.2 collective-permute-done
  132.7 0.7 collective-permute-start.2
  133.4 0.7 collective-permute-start.13
  134.1 0.1 bitcast_dynamic-update-slice_fusion.10
  134.1 4.4 %collective-permute-done.1 = f32[128,8,128]{2,1,0:T(8,128)S(1)} collective-permute-done((f32[128,8,128]{2,1,0:T(8,128)S(1)}, f32[128,8,128]{2,1,0:T(8,128)S(1)}, u32[]{:S(2)}, u32[]{:S(2)}) %collective-permute-start.1) | collective-permute-done | bytes 524320 | tf_op jit(solution)/shard_map/ppermute | solution.py:188
  138.5 0.3 dynamic-slice_bitcast_fusion.4
  138.8 0.7 collective-permute-start.3
  139.6 4.4 %collective-permute-start.4 = (f32[128,8]{1,0:T(8,128)S(1)}, f32[128,8]{1,0:T(8,128)S(1)}, u32[]{:S(2)}, u32[]{:S(2)}) collective-permute-start(f32[128,8]{1,0:T(8,128)S(1)} %dynamic-slice_bitcast_fusion.16), channel_id=1, source_target_pairs={{0,1},{1,2},{4,5},{5,6},{8,9},{9,10},{12,13},{13,14},{16,17},{17,1... | collective-permute-start | bytes 12296 | tf_op jit(solution)/shard_map/ppermute | solution.py:188
  144.0 1.9 collective-permute-start.14
  146.0 0.3 bitcast_dynamic-update-slice_fusion.4
  146.3 0.1 dynamic-slice_bitcast_fusion.3
  146.4 1.9 collective-permute-start.5
  148.4 0.1 bitcast_dynamic-update-slice_fusion.9
  148.5 0.7 collective-permute-start.6
  149.2 0.7 collective-permute-start.15
  149.9 10.1 %collective-permute-done.5 = f32[128,8,128]{2,1,0:T(8,128)S(1)} collective-permute-done((f32[128,8,128]{2,1,0:T(8,128)S(1)}, f32[128,8,128]{2,1,0:T(8,128)S(1)}, u32[]{:S(2)}, u32[]{:S(2)}) %collective-permute-start.5) | collective-permute-done | bytes 524320 | tf_op jit(solution)/shard_map/ppermute | solution.py:188
  160.0 0.3 dynamic-slice_bitcast_fusion.2
  160.3 0.7 collective-permute-start.7
  161.0 0.1 bitcast_dynamic-update-slice_fusion.8
  161.1 11.7 %collective-permute-start.8 = (f32[128,8]{1,0:T(8,128)S(1)}, f32[128,8]{1,0:T(8,128)S(1)}, u32[]{:S(2)}, u32[]{:S(2)}) collective-permute-start(f32[128,8]{1,0:T(8,128)S(1)} %dynamic-slice_bitcast_fusion.14), channel_id=1, source_target_pairs={{0,1},{1,2},{2,3},{4,5},{5,6},{6,7},{8,9},{9,10},{10,11},{12,13},{... | collective-permute-start | bytes 12296 | tf_op jit(solution)/shard_map/ppermute | solution.py:188
  172.9 0.3 bitcast_dynamic-update-slice_fusion.2
  173.2 0.9 dynamic-slice_bitcast_fusion.1
  174.1 15.9 %collective-permute-start.9 = (f32[128,8,128]{2,1,0:T(8,128)}, f32[128,8,128]{2,1,0:T(8,128)}, u32[]{:S(2)}, u32[]{:S(2)}) collective-permute-start(f32[128,8,128]{2,1,0:T(8,128)} %get-tuple-element.36), channel_id=1, source_target_pairs={{0,1},{1,2},{2,3},{4,5},{5,6},{6,7},{8,9},{9,10},{10,11},{12,13},{... | collective-permute-start | bytes 1572872 | tf_op jit(solution)/shard_map/ppermute | solution.py:188
  190.0 2.9 %collective-permute-start.16 = (f32[128,8]{1,0:T(8,128)S(1)}, f32[128,8]{1,0:T(8,128)S(1)}, u32[]{:S(2)}, u32[]{:S(2)}) collective-permute-start(f32[128,8]{1,0:T(8,128)S(1)} %get-tuple-element.51), channel_id=1, source_target_pairs={{0,1},{1,2},{2,3},{4,5},{5,6},{6,7},{8,9},{9,10},{10,11},{12,13},{... | collective-permute-start | bytes 12296 | tf_op jit(solution)/shard_map/ppermute | solution.py:188
  192.9 8.8 %collective-permute-done.16 = f32[128,8]{1,0:T(8,128)S(1)} collective-permute-done((f32[128,8]{1,0:T(8,128)S(1)}, f32[128,8]{1,0:T(8,128)S(1)}, u32[]{:S(2)}, u32[]{:S(2)}) %collective-permute-start.16) | collective-permute-done | bytes 4128 | tf_op jit(solution)/shard_map/ppermute | solution.py:188
  201.8 1.3 collective-permute-start.10
  203.1 1.3 collective-permute-start.17
  204.4 1.4 dynamic-slice_bitcast_fusion
  205.8 1.3 collective-permute-start.11
  207.1 2.0 collective-permute-done.10
  209.1 1.3 collective-permute-done.17
  210.5 11.9 %collective-permute-done.11 = f32[128,8,128]{2,1,0:T(8,128)S(1)} collective-permute-done((f32[128,8,128]{2,1,0:T(8,128)S(1)}, f32[128,8,128]{2,1,0:T(8,128)S(1)}, u32[]{:S(2)}, u32[]{:S(2)}) %collective-permute-start.11) | collective-permute-done | bytes 524320 | tf_op jit(solution)/shard_map/ppermute | solution.py:190
  222.3 0.3 bitcast_dynamic-update-slice_fusion
  222.7 0.2 div.35
  222.9 1.0 bitcast_divide_fusion
  (51 shorter events, 0.7 us)
Async XLA Ops:
  6.5 3.3 %copy-start.3 = (bf16[512,2048]{1,0:T(8,128)(2,1)S(1)}, bf16[512,2048]{1,0:T(8,128)(2,1)}, u32[]{:S(2)}) copy-start(bf16[512,2048]{1,0:T(8,128)(2,1)} %param.6) | copy-start | bytes 6291460
  6.5 36.6 %all-gather.3.cloned.1.call-start = ((), (), s32[]{:S(2)}) async-start(), calls=%async_computation.1 | async-start | bytes 1474560 | tf_op jit(solution)/shard_map/all_gather | solution.py:126
  13.4 5.3 %copy-start.4 = (bf16[128,2048]{1,0:T(8,128)(2,1)S(1)}, bf16[128,2048]{1,0:T(8,128)(2,1)}, u32[]{:S(2)}) copy-start(bf16[128,2048]{1,0:T(8,128)(2,1)} %param.5) | copy-start | bytes 1572868
  13.4 31.9 %all-to-all-start = ((bf16[8,2,4,128,128]{4,3,2,1,0:T(8,128)(2,1)}), bf16[8,2,4,128,128]{4,3,2,1,0:T(8,128)(2,1)S(1)}, u32[]{:S(2)}, u32[]{:S(2)}) async-start(bf16[8,2,4,128,128]{4,3,2,1,0:T(8,128)(2,1)} %pad_maximum_fusion), calls=%async_computation | async-start | bytes 4194304 | tf_op jit(solution)/shard_map/all_to_all | solution.py:120
  45.4 1.3 copy-start
  123.0 2.1 copy-start.1
  123.0 5.7 %copy-start.2 = (f32[4,128,8]{2,1,0:T(8,128)S(1)}, f32[4,128,8]{2,1,0:T(8,128)}, u32[]{:S(2)}) copy-start(f32[4,128,8]{2,1,0:T(8,128)} %get-tuple-element.9) | copy-start | bytes 49156
  125.2 6.2 %collective-permute-start.12 = (f32[128,8]{1,0:T(8,128)S(1)}, f32[128,8]{1,0:T(8,128)S(1)}, u32[]{:S(2)}, u32[]{:S(2)}) collective-permute-start(f32[128,8]{1,0:T(8,128)S(1)} %get-tuple-element.61), channel_id=1, source_target_pairs={{0,1},{4,5},{8,9},{12,13},{16,17},{20,21},{24,25},{28,29}} | collective-permute-start | bytes 12296 | tf_op jit(solution)/shard_map/ppermute | solution.py:188
  128.7 3.9 %collective-permute-start = (f32[128,8]{1,0:T(8,128)S(1)}, f32[128,8]{1,0:T(8,128)S(1)}, u32[]{:S(2)}, u32[]{:S(2)}) collective-permute-start(f32[128,8]{1,0:T(8,128)S(1)} %dynamic-slice_bitcast_fusion.18), channel_id=1, source_target_pairs={{0,1},{4,5},{8,9},{12,13},{16,17},{20,21},{24,25},{28,29}} | collective-permute-start | bytes 12296 | tf_op jit(solution)/shard_map/ppermute | solution.py:188
  130.1 8.4 %collective-permute-start.1 = (f32[128,8,128]{2,1,0:T(8,128)S(1)}, f32[128,8,128]{2,1,0:T(8,128)S(1)}, u32[]{:S(2)}, u32[]{:S(2)}) collective-permute-start(f32[128,8,128]{2,1,0:T(8,128)S(1)} %get-tuple-element.44), channel_id=1, source_target_pairs={{0,1},{4,5},{8,9},{12,13},{16,17},{20,21},{24,25},{28,29}} | collective-permute-start | bytes 1572872 | tf_op jit(solution)/shard_map/ppermute | solution.py:188
  132.7 1.4 collective-permute-start.2
  133.4 0.7 collective-permute-start.13
  138.8 7.1 %collective-permute-start.3 = (f32[128,8,128]{2,1,0:T(8,128)S(1)}, f32[128,8,128]{2,1,0:T(8,128)S(1)}, u32[]{:S(2)}, u32[]{:S(2)}) collective-permute-start(f32[128,8,128]{2,1,0:T(8,128)S(1)} %get-tuple-element.42), channel_id=1, source_target_pairs={{3,2},{7,6},{11,10},{15,14},{19,18},{23,22},{27,26},{31,30}} | collective-permute-start | bytes 1572872 | tf_op jit(solution)/shard_map/ppermute | solution.py:190
  139.6 8.8 %collective-permute-start.4 = (f32[128,8]{1,0:T(8,128)S(1)}, f32[128,8]{1,0:T(8,128)S(1)}, u32[]{:S(2)}, u32[]{:S(2)}) collective-permute-start(f32[128,8]{1,0:T(8,128)S(1)} %dynamic-slice_bitcast_fusion.16), channel_id=1, source_target_pairs={{0,1},{1,2},{4,5},{5,6},{8,9},{9,10},{12,13},{13,14},{16,17},{17,1... | collective-permute-start | bytes 12296 | tf_op jit(solution)/shard_map/ppermute | solution.py:188
  144.0 4.4 %collective-permute-start.14 = (f32[128,8]{1,0:T(8,128)S(1)}, f32[128,8]{1,0:T(8,128)S(1)}, u32[]{:S(2)}, u32[]{:S(2)}) collective-permute-start(f32[128,8]{1,0:T(8,128)S(1)} %get-tuple-element.56), channel_id=1, source_target_pairs={{0,1},{1,2},{4,5},{5,6},{8,9},{9,10},{12,13},{13,14},{16,17},{17,1... | collective-permute-start | bytes 12296 | tf_op jit(solution)/shard_map/ppermute | solution.py:188
  146.4 13.5 %collective-permute-start.5 = (f32[128,8,128]{2,1,0:T(8,128)S(1)}, f32[128,8,128]{2,1,0:T(8,128)S(1)}, u32[]{:S(2)}, u32[]{:S(2)}) collective-permute-start(f32[128,8,128]{2,1,0:T(8,128)S(1)} %get-tuple-element.40), channel_id=1, source_target_pairs={{0,1},{1,2},{4,5},{5,6},{8,9},{9,10},{12,13},{13,14},{16,17},{17,1... | collective-permute-start | bytes 1572872 | tf_op jit(solution)/shard_map/ppermute | solution.py:188
  148.5 12.5 %collective-permute-start.6 = (f32[128,8]{1,0:T(8,128)S(1)}, f32[128,8]{1,0:T(8,128)S(1)}, u32[]{:S(2)}, u32[]{:S(2)}) collective-permute-start(f32[128,8]{1,0:T(8,128)S(1)} %get-tuple-element.54), channel_id=1, source_target_pairs={{2,1},{3,2},{6,5},{7,6},{10,9},{11,10},{14,13},{15,14},{18,17},{19... | collective-permute-start | bytes 12296 | tf_op jit(solution)/shard_map/ppermute | solution.py:190
  149.2 11.9 %collective-permute-start.15 = (f32[128,8]{1,0:T(8,128)S(1)}, f32[128,8]{1,0:T(8,128)S(1)}, u32[]{:S(2)}, u32[]{:S(2)}) collective-permute-start(f32[128,8]{1,0:T(8,128)S(1)} %get-tuple-element.55), channel_id=1, source_target_pairs={{2,1},{3,2},{6,5},{7,6},{10,9},{11,10},{14,13},{15,14},{18,17},{19... | collective-permute-start | bytes 12296 | tf_op jit(solution)/shard_map/ppermute | solution.py:190
  160.3 12.6 %collective-permute-start.7 = (f32[128,8,128]{2,1,0:T(8,128)S(1)}, f32[128,8,128]{2,1,0:T(8,128)S(1)}, u32[]{:S(2)}, u32[]{:S(2)}) collective-permute-start(f32[128,8,128]{2,1,0:T(8,128)S(1)} %get-tuple-element.38), channel_id=1, source_target_pairs={{2,1},{3,2},{6,5},{7,6},{10,9},{11,10},{14,13},{15,14},{18,17},{19... | collective-permute-start | bytes 1572872 | tf_op jit(solution)/shard_map/ppermute | solution.py:190
  161.1 31.7 %collective-permute-start.8 = (f32[128,8]{1,0:T(8,128)S(1)}, f32[128,8]{1,0:T(8,128)S(1)}, u32[]{:S(2)}, u32[]{:S(2)}) collective-permute-start(f32[128,8]{1,0:T(8,128)S(1)} %dynamic-slice_bitcast_fusion.14), channel_id=1, source_target_pairs={{0,1},{1,2},{2,3},{4,5},{5,6},{6,7},{8,9},{9,10},{10,11},{12,13},{... | collective-permute-start | bytes 12296 | tf_op jit(solution)/shard_map/ppermute | solution.py:188
  174.1 30.3 %collective-permute-start.9 = (f32[128,8,128]{2,1,0:T(8,128)}, f32[128,8,128]{2,1,0:T(8,128)}, u32[]{:S(2)}, u32[]{:S(2)}) collective-permute-start(f32[128,8,128]{2,1,0:T(8,128)} %get-tuple-element.36), channel_id=1, source_target_pairs={{0,1},{1,2},{2,3},{4,5},{5,6},{6,7},{8,9},{9,10},{10,11},{12,13},{... | collective-permute-start | bytes 1572872 | tf_op jit(solution)/shard_map/ppermute | solution.py:188
  190.0 11.7 %collective-permute-start.16 = (f32[128,8]{1,0:T(8,128)S(1)}, f32[128,8]{1,0:T(8,128)S(1)}, u32[]{:S(2)}, u32[]{:S(2)}) collective-permute-start(f32[128,8]{1,0:T(8,128)S(1)} %get-tuple-element.51), channel_id=1, source_target_pairs={{0,1},{1,2},{2,3},{4,5},{5,6},{6,7},{8,9},{9,10},{10,11},{12,13},{... | collective-permute-start | bytes 12296 | tf_op jit(solution)/shard_map/ppermute | solution.py:188
  201.8 7.3 %collective-permute-start.10 = (f32[128,8]{1,0:T(8,128)S(1)}, f32[128,8]{1,0:T(8,128)S(1)}, u32[]{:S(2)}, u32[]{:S(2)}) collective-permute-start(f32[128,8]{1,0:T(8,128)S(1)} %get-tuple-element.48), channel_id=1, source_target_pairs={{1,0},{2,1},{3,2},{5,4},{6,5},{7,6},{9,8},{10,9},{11,10},{13,12},{... | collective-permute-start | bytes 12296 | tf_op jit(solution)/shard_map/ppermute | solution.py:190
  203.1 7.3 %collective-permute-start.17 = (f32[128,8]{1,0:T(8,128)S(1)}, f32[128,8]{1,0:T(8,128)S(1)}, u32[]{:S(2)}, u32[]{:S(2)}) collective-permute-start(f32[128,8]{1,0:T(8,128)S(1)} %get-tuple-element.50), channel_id=1, source_target_pairs={{1,0},{2,1},{3,2},{5,4},{6,5},{7,6},{9,8},{10,9},{11,10},{13,12},{... | collective-permute-start | bytes 12296 | tf_op jit(solution)/shard_map/ppermute | solution.py:190
  205.8 16.5 %collective-permute-start.11 = (f32[128,8,128]{2,1,0:T(8,128)S(1)}, f32[128,8,128]{2,1,0:T(8,128)S(1)}, u32[]{:S(2)}, u32[]{:S(2)}) collective-permute-start(f32[128,8,128]{2,1,0:T(8,128)S(1)} %get-tuple-element.34), channel_id=1, source_target_pairs={{1,0},{2,1},{3,2},{5,4},{6,5},{7,6},{9,8},{10,9},{11,10},{13,12},{... | collective-permute-start | bytes 1572872 | tf_op jit(solution)/shard_map/ppermute | solution.py:190
Sparse Core Ops, SparseCore 0:
  9.9 33.1 all-gather.2

commit v4 on v3

--- a/solution.py
+++ b/solution.py
@@ -16,8 +16,8 @@
 QUERY_GROUP_ROWS = 128
 
 
-def attend_kernel(sel_ref, home_ref, q_ref, kv_ref, own_ref, acc_ref, m_ref, l_ref,
-                  p_buf, m_scr, l_scr, acc_scr, *, groups, heads, chunks, factor):
+def attend_kernel(sel_ref, home_ref, q_ref, kv_ref, own_ref, out_ref,
+                  p_buf, m_scr, l_scr, acc_scr, *, groups, heads, first, all_heads, chunks, factor):
     b = pl.program_id(0)
     rows = QUERY_GROUP_ROWS
     q = q_ref[0].reshape(heads * rows, HEAD_SIZE)
@@ -56,7 +56,7 @@
                 acc_scr[h] += pv[h * rows:(h + 1) * rows]
 
     def piece(g, carry):
-        base = b * heads * groups + g
+        base = (b * all_heads + first) * groups + g
         if chunks == 1:
             s = jnp.dot(q, kv_ref[g, 0, 0], preferred_element_type=jnp.float32)
         else:
@@ -76,10 +76,12 @@
         s = jnp.dot(q, own_ref[0], preferred_element_type=jnp.float32)
         update(s, own_ref[1], lambda h: True, causal)
 
+    stats = heads * HEAD_SIZE
+    out_ref[0, :, stats:] = jnp.zeros((rows, HEAD_SIZE), jnp.float32)
     for h in range(heads):
-        acc_ref[0, :, h * HEAD_SIZE:(h + 1) * HEAD_SIZE] = acc_scr[h]
-        m_ref[0, :, h:h + 1] = m_scr[h]
-        l_ref[0, :, h:h + 1] = l_scr[h]
+        out_ref[0, :, h * HEAD_SIZE:(h + 1) * HEAD_SIZE] = acc_scr[h]
+        out_ref[0, :, stats + h:stats + h + 1] = m_scr[h]
+        out_ref[0, :, stats + heads + h:stats + heads + h + 1] = l_scr[h]
 
 
 def join(a, b):
@@ -138,65 +140,49 @@
     sel_flat = hit.astype(jnp.int32).reshape(-1)
     home = helper.reshape(1).astype(jnp.int32)
 
-    kernel = functools.partial(attend_kernel, groups=groups, heads=heads, chunks=chunks,
-                               factor=scale * math.log2(math.e))
-    width = heads * HEAD_SIZE
-    acc, m, l = pl.pallas_call(
-        kernel,
-        grid_spec=pltpu.PrefetchScalarGridSpec(
-            num_scalar_prefetch=2,
-            grid=(query_blocks,),
-            in_specs=[
-                pl.BlockSpec((1, heads, rows, HEAD_SIZE), lambda b, s, h: (b, 0, 0, 0)),
-                pl.BlockSpec((groups, 2, chunks, HEAD_SIZE, HEAD_SIZE), lambda b, s, h: (0, 0, 0, 0, 0)),
-                pl.BlockSpec((2, rows, HEAD_SIZE), lambda b, s, h: (0, 0, 0)),
-            ],
-            out_specs=[
-                pl.BlockSpec((1, rows, width), lambda b, s, h: (b, 0, 0)),
-                pl.BlockSpec((1, rows, heads), lambda b, s, h: (b, 0, 0)),
-                pl.BlockSpec((1, rows, heads), lambda b, s, h: (b, 0, 0)),
-            ],
-            scratch_shapes=[
-                pltpu.VMEM((heads * rows, max(piece, rows)), jnp.bfloat16),
-                pltpu.VMEM((heads, rows, 1), jnp.float32),
-                pltpu.VMEM((heads, rows, 1), jnp.float32),
-                pltpu.VMEM((heads, rows, HEAD_SIZE), jnp.float32),
-            ],
-        ),
-        out_shape=[
-            jax.ShapeDtypeStruct((query_blocks, rows, width), jnp.float32),
-            jax.ShapeDtypeStruct((query_blocks, rows, heads), jnp.float32),
-            jax.ShapeDtypeStruct((query_blocks, rows, heads), jnp.float32),
-        ],
-    )(sel_flat, home, q_all, held, own)
-
-    acc = acc.reshape(query_blocks, rows, heads, HEAD_SIZE)
-    state = (acc, m, l)
-
-    def pick(t):
-        t = jnp.clip(t, 0, query_blocks - 1)
-        return tuple(lax.dynamic_index_in_dim(x, t, axis=0, keepdims=False) for x in state)
-
-    def put(t, part, valid):
-        t = jnp.clip(t, 0, query_blocks - 1)
-        old = pick(t)
-        part = (part[0], jnp.where(valid, part[1], -jnp.inf), part[2])
-        new = join(old, part)
-        return tuple(lax.dynamic_update_index_in_dim(x, y, t, axis=0) for x, y in zip(state, new))
-
-    for r in range(1, helpers):
-        right = lax.ppermute(pick(helper + helpers - r), "help",
-                             [(z, z + 1) for z in range(0, r)])
-        left = lax.ppermute(pick(helper - helpers + r), "help",
-                            [(z, z - 1) for z in range(helpers - r, helpers)])
-        from_left = (helper >= 1) & (helper <= r)
-        state = put(helper - 1 + helpers - r, right, from_left)
-        from_right = (helper >= helpers - r - 1) & (helper <= helpers - 2)
-        state = put(helper + 1 - helpers + r, left, from_right)
-
-    acc, m, l = pick(helper)
-    result = acc / l[..., None]
-    return result.reshape(rows, width)
+    slices = min(4, heads)
+    part = heads // slices
+    assert part * slices == heads and 2 * part <= HEAD_SIZE
+    width = (part + 1) * HEAD_SIZE
+    outs = []
+    for c in range(slices):
+        kernel = functools.partial(attend_kernel, groups=groups, heads=part, first=c * part,
+                                   all_heads=heads, chunks=chunks, factor=scale * math.log2(math.e))
+        partial = pl.pallas_call(
+            kernel,
+            grid_spec=pltpu.PrefetchScalarGridSpec(
+                num_scalar_prefetch=2,
+                grid=(query_blocks,),
+                in_specs=[
+                    pl.BlockSpec((1, part, rows, HEAD_SIZE), lambda b, s, h, c=c: (b, c, 0, 0)),
+                    pl.BlockSpec((groups, 2, chunks, HEAD_SIZE, HEAD_SIZE),
+                                 lambda b, s, h: (0, 0, 0, 0, 0)),
+                    pl.BlockSpec((2, rows, HEAD_SIZE), lambda b, s, h: (0, 0, 0)),
+                ],
+                out_specs=pl.BlockSpec((1, rows, width), lambda b, s, h: (b, 0, 0)),
+                scratch_shapes=[
+                    pltpu.VMEM((part * rows, max(piece, rows)), jnp.bfloat16),
+                    pltpu.VMEM((part, rows, 1), jnp.float32),
+                    pltpu.VMEM((part, rows, 1), jnp.float32),
+                    pltpu.VMEM((part, rows, HEAD_SIZE), jnp.float32),
+                ],
+            ),
+            out_shape=jax.ShapeDtypeStruct((query_blocks, rows, width), jnp.float32),
+            cost_estimate=pl.CostEstimate(
+                flops=4 * query_blocks * part * rows * groups * piece * HEAD_SIZE,
+                transcendentals=query_blocks * part * rows * groups * piece,
+                bytes_accessed=2 * groups * 2 * piece * HEAD_SIZE + 4 * query_blocks * rows * width),
+        )(sel_flat, home, q_all, held, own)
+        got = lax.all_to_all(partial, "help", 0, 0, tiled=True)
+        acc = got[:, :, :part * HEAD_SIZE].reshape(helpers, rows, part, HEAD_SIZE)
+        m = got[:, :, part * HEAD_SIZE:part * HEAD_SIZE + part]
+        l = got[:, :, part * HEAD_SIZE + part:part * HEAD_SIZE + 2 * part]
+        top = jnp.max(m, axis=0)
+        fade = jnp.exp2(m - jnp.where(top == -jnp.inf, 0.0, top))
+        total = jnp.sum(l * fade, axis=0)
+        acc = jnp.sum(acc * fade[..., None], axis=0)
+        outs.append((acc / total[..., None]).reshape(rows, part * HEAD_SIZE))
+    return jnp.concatenate(outs, axis=1)
 
 
 def solution(mesh):

time: 230 us -> 219 us (0.952)
  the two profiles are of different devices: /device:TPU:0 before, /device:TPU:2 now
where the time goes in v4:
time: 219 us; the launch traced here: 217 us
  Pallas kernels  113 us (52%)
  waiting for transfers between devices  35.9 us (16%)
  starting transfers between devices  23.4 us (11%)
  local copies, waits for them, and re-layouts  22.6 us (10%)
  between operations  13.7 us (6%)
  other arithmetic  7.51 us (3%)
    pallas_call x4, Pallas kernels, local(): pl.pallas_call(kernel, grid_spec=pltpu.PrefetchScalarGridSpec(num_scalar_...  113 us
    all_gather x1, waiting for transfers between devices, local(): q_all = lax.all_gather(q[None], 'help', axis=0, tiled=True)  22.8 us
    all_to_all x4, starting transfers between devices, local(): got = lax.all_to_all(partial, 'help', 0, 0, tiled=True)  19.1 us
    mul x8, local copies, waits for them, and re-layouts, local(): acc = jnp.sum(acc * fade[..., None], axis=0)  14.7 us
    all_to_all x4, waiting for transfers between devices, local(): got = lax.all_to_all(partial, 'help', 0, 0, tiled=True)  13.1 us
    unnamed x18, local copies, waits for them, and re-layouts  4.44 us
    all_to_all x1, starting transfers between devices, local(): lax.all_to_all(jnp.stack([keys, values], axis=1), 'blk', 0, 0, tiled=True)  4.39 us
  transfers between devices with their start and end apart: 6, of which 2 were waited for; matrix products, arithmetic and copies ran while one was open for 7% of the time, Pallas kernels for 39%

profile of v4, /device:TPU:2, one launch (start us, length us, event | category | flops | bytes accessed | tf_op | source)
XLA Modules:
  0.0 216.5 jit_solution(12789517692543222422)
XLA Ops:
  6.5 0.0 all-gather.3.cloned.1.call-start
  6.5 0.8 convert_element_type.22
  7.4 0.1 copy.29
  7.5 0.1 convert_element_type.23
  7.6 0.1 copy.30
  7.7 1.1 copy.28
  8.9 0.9 copy.31
  9.8 0.0 all-gather.3.cloned.1.call-update
  9.8 0.0 copy-done
  9.8 0.6 copy.39
  10.5 0.4 fusion.8
  10.8 0.8 copy.36
  11.7 0.2 copy.51
  11.9 1.5 pad_maximum_fusion
  13.4 4.4 %all-to-all-start = ((bf16[8,2,4,128,128]{4,3,2,1,0:T(8,128)(2,1)}), bf16[8,2,4,128,128]{4,3,2,1,0:T(8,128)(2,1)S(1)}, u32[]{:S(2)}, u32[]{:S(2)}) async-start(bf16[8,2,4,128,128]{4,3,2,1,0:T(8,128)(2,1)} %pad_maximum_fusion), calls=%async_computation | async-start | bytes 4194304 | tf_op jit(solution)/shard_map/all_to_all | solution.py:122
  17.8 0.0 copy-done.5
  17.8 0.1 copy.40
  17.9 0.1 constant_dynamic-slice_fusion
  18.1 0.1 copy.35
  18.3 0.6 pad_maximum_fusion.3.own_ref
  18.9 22.8 %all-gather.3.cloned.1.call-done = bf16[36,128,128]{2,1,0:T(8,128)(2,1)} async-done(((bf16[9,128,128]{2,1,0:T(8,128)(2,1)}), bf16[36,128,128]{2,1,0:T(8,128)(2,1)}) %all-gather.3.cloned.1.call-update) | async-done | bytes 1179664 | tf_op jit(solution)/shard_map/all_gather | solution.py:128
  41.7 0.7 slice_convert_fusion
  42.4 0.1 reshape.80
  42.5 0.7 compare_reduce_fusion
  43.2 0.7 reshape.81.sel_ref
  43.9 0.0 all-to-all-done.kv_ref
  43.9 1.4 copy-done.1
  45.2 28.7 %shard_map.49 = f32[4,128,384]{2,1,0:T(8,128)} custom-call(s32[256]{0:T(256)} %reshape.81.sel_ref, s32[1]{0:T(128)} %bitcast.4.home_ref, bf16[4,9,128,128]{3,2,1,0:T(8,128)(2,1)} %bitcast.61, bf16[8,2,4,128,128]{4,3,2,1,0:T(8,128)(2,1)} %copy-done.1, bf16[2,128,128]{2,1,0:T(8,128)(2,1)} %pad_maximum_fusion.3.own_ref), custom_call_target="tpu_custom_call" | custom-call | flops 2147483648 | bytes 2883584 | tf_op jit(solution)/shard_map/pallas_call | solution.py:151
  74.0 3.5 %all-to-all-start.4 = ((f32[4,128,384]{2,1,0:T(8,128)}), f32[4,128,384]{2,1,0:T(8,128)S(1)}, u32[]{:S(2)}, u32[]{:S(2)}) async-start(f32[4,128,384]{2,1,0:T(8,128)} %shard_map.49), calls=%async_computation.4 | async-start | bytes 1572864 | tf_op jit(solution)/shard_map/all_to_all | solution.py:176
  77.5 27.3 %shard_map.48 = f32[4,128,384]{2,1,0:T(8,128)} custom-call(s32[256]{0:T(256)} %reshape.81.sel_ref, s32[1]{0:T(128)} %bitcast.4.home_ref, bf16[4,9,128,128]{3,2,1,0:T(8,128)(2,1)} %bitcast.62, bf16[8,2,4,128,128]{4,3,2,1,0:T(8,128)(2,1)} %copy-done.1, bf16[2,128,128]{2,1,0:T(8,128)(2,1)} %pad_maximum_fusion.3.own_ref), custom_call_target="tpu_custom_call" | custom-call | flops 2147483648 | bytes 2883584 | tf_op jit(solution)/shard_map/pallas_call | solution.py:151
  104.7 0.0 all-to-all-done.4
  104.7 6.8 %all-to-all-start.3 = ((f32[4,128,384]{2,1,0:T(8,128)}), f32[4,128,384]{2,1,0:T(8,128)S(1)}, u32[]{:S(2)}, u32[]{:S(2)}) async-start(f32[4,128,384]{2,1,0:T(8,128)} %shard_map.48), calls=%async_computation.3 | async-start | bytes 1572864 | tf_op jit(solution)/shard_map/all_to_all | solution.py:176
  111.5 28.2 %shard_map.47 = f32[4,128,384]{2,1,0:T(8,128)} custom-call(s32[256]{0:T(256)} %reshape.81.sel_ref, s32[1]{0:T(128)} %bitcast.4.home_ref, bf16[4,9,128,128]{3,2,1,0:T(8,128)(2,1)} %bitcast.63, bf16[8,2,4,128,128]{4,3,2,1,0:T(8,128)(2,1)} %copy-done.1, bf16[2,128,128]{2,1,0:T(8,128)(2,1)} %pad_maximum_fusion.3.own_ref), custom_call_target="tpu_custom_call" | custom-call | flops 2147483648 | bytes 2883584 | tf_op jit(solution)/shard_map/pallas_call | solution.py:151
  139.7 0.0 all-to-all-done.3
  139.7 5.1 %all-to-all-start.2 = ((f32[4,128,384]{2,1,0:T(8,128)}), f32[4,128,384]{2,1,0:T(8,128)S(1)}, u32[]{:S(2)}, u32[]{:S(2)}) async-start(f32[4,128,384]{2,1,0:T(8,128)} %shard_map.47), calls=%async_computation.2 | async-start | bytes 1572864 | tf_op jit(solution)/shard_map/all_to_all | solution.py:176
  144.8 29.3 %shard_map.46 = f32[4,128,384]{2,1,0:T(8,128)} custom-call(s32[256]{0:T(256)} %reshape.81.sel_ref, s32[1]{0:T(128)} %bitcast.4.home_ref, bf16[4,9,128,128]{3,2,1,0:T(8,128)(2,1)} %bitcast.64, bf16[8,2,4,128,128]{4,3,2,1,0:T(8,128)(2,1)} %copy-done.1, bf16[2,128,128]{2,1,0:T(8,128)(2,1)} %pad_maximum_fusion.3.own_ref), custom_call_target="tpu_custom_call" | custom-call | flops 2147483648 | bytes 2883584 | tf_op jit(solution)/shard_map/pallas_call | solution.py:151
  174.1 0.0 all-to-all-done.2
  174.1 3.7 %all-to-all-start.1 = ((f32[4,128,384]{2,1,0:T(8,128)}), f32[4,128,384]{2,1,0:T(8,128)S(1)}, u32[]{:S(2)}, u32[]{:S(2)}) async-start(f32[4,128,384]{2,1,0:T(8,128)} %shard_map.46), calls=%async_computation.1 | async-start | bytes 1572864 | tf_op jit(solution)/shard_map/all_to_all | solution.py:176
  177.8 0.1 fusion.4
  177.9 1.4 mul.85
  179.3 2.2 %mul.86 = f32[4,128,256]{2,1,0:T(8,128)} reshape(f32[4,128,2,128]{3,2,1,0:T(2,128)} %mul.85) | data formatting | bytes 1048576 | tf_op jit(solution)/shard_map/mul | solution.py:183
  181.6 0.1 fusion.5
  181.8 1.4 mul.81
  183.2 2.3 %mul.82 = f32[4,128,256]{2,1,0:T(8,128)} reshape(f32[4,128,2,128]{3,2,1,0:T(2,128)} %mul.81) | data formatting | bytes 1048576 | tf_op jit(solution)/shard_map/mul | solution.py:183
  185.5 13.1 %all-to-all-done.1 = f32[4,128,384]{2,1,0:T(8,128)S(1)} async-done(((f32[4,128,384]{2,1,0:T(8,128)}), f32[4,128,384]{2,1,0:T(8,128)S(1)}, u32[]{:S(2)}, u32[]{:S(2)}) %all-to-all-start.1) | async-done | bytes 786464 | tf_op jit(solution)/shard_map/all_to_all | solution.py:176
  198.6 0.1 fusion.6
  198.7 1.4 mul.77
  200.1 2.3 %mul.78 = f32[4,128,256]{2,1,0:T(8,128)} reshape(f32[4,128,2,128]{3,2,1,0:T(2,128)} %mul.77) | data formatting | bytes 1048576 | tf_op jit(solution)/shard_map/mul | solution.py:183
  202.4 0.1 fusion.7
  202.6 1.4 mul.73
  204.0 2.3 %mul.74 = f32[4,128,256]{2,1,0:T(8,128)} reshape(f32[4,128,2,128]{3,2,1,0:T(2,128)} %mul.73) | data formatting | bytes 1048576 | tf_op jit(solution)/shard_map/mul | solution.py:183
  206.2 1.2 fusion
  207.4 0.0 copy-start.3
  207.4 0.2 div.74
  207.7 0.0 copy-done.2
  207.7 0.1 fusion.1
  207.8 0.2 div.71
  208.0 0.0 copy-done.4
  208.0 0.1 fusion.2
  208.1 0.2 div.68
  208.3 0.2 copy-done.3
  208.5 0.1 fusion.3
  208.6 0.2 div.65
  208.8 0.9 pad_maximum_fusion.1
  (24 shorter events, 0.3 us)
Async XLA Ops:
  6.5 3.3 %copy-start = (bf16[512,2048]{1,0:T(8,128)(2,1)S(1)}, bf16[512,2048]{1,0:T(8,128)(2,1)}, u32[]{:S(2)}) copy-start(bf16[512,2048]{1,0:T(8,128)(2,1)} %param.6) | copy-start | bytes 6291460
  6.5 35.1 %all-gather.3.cloned.1.call-start = ((), (), s32[]{:S(2)}) async-start(), calls=%async_computation.5 | async-start | bytes 1474560 | tf_op jit(solution)/shard_map/all_gather | solution.py:128
  13.4 4.4 %copy-start.5 = (bf16[128,2048]{1,0:T(8,128)(2,1)S(1)}, bf16[128,2048]{1,0:T(8,128)(2,1)}, u32[]{:S(2)}) copy-start(bf16[128,2048]{1,0:T(8,128)(2,1)} %param.5) | copy-start | bytes 1572868
  13.4 30.4 %all-to-all-start = ((bf16[8,2,4,128,128]{4,3,2,1,0:T(8,128)(2,1)}), bf16[8,2,4,128,128]{4,3,2,1,0:T(8,128)(2,1)S(1)}, u32[]{:S(2)}, u32[]{:S(2)}) async-start(bf16[8,2,4,128,128]{4,3,2,1,0:T(8,128)(2,1)} %pad_maximum_fusion), calls=%async_computation | async-start | bytes 4194304 | tf_op jit(solution)/shard_map/all_to_all | solution.py:122
  43.9 1.4 copy-start.1
  74.0 30.8 %all-to-all-start.4 = ((f32[4,128,384]{2,1,0:T(8,128)}), f32[4,128,384]{2,1,0:T(8,128)S(1)}, u32[]{:S(2)}, u32[]{:S(2)}) async-start(f32[4,128,384]{2,1,0:T(8,128)} %shard_map.49), calls=%async_computation.4 | async-start | bytes 1572864 | tf_op jit(solution)/shard_map/all_to_all | solution.py:176
  104.7 34.9 %all-to-all-start.3 = ((f32[4,128,384]{2,1,0:T(8,128)}), f32[4,128,384]{2,1,0:T(8,128)S(1)}, u32[]{:S(2)}, u32[]{:S(2)}) async-start(f32[4,128,384]{2,1,0:T(8,128)} %shard_map.48), calls=%async_computation.3 | async-start | bytes 1572864 | tf_op jit(solution)/shard_map/all_to_all | solution.py:176
  139.7 34.4 %all-to-all-start.2 = ((f32[4,128,384]{2,1,0:T(8,128)}), f32[4,128,384]{2,1,0:T(8,128)S(1)}, u32[]{:S(2)}, u32[]{:S(2)}) async-start(f32[4,128,384]{2,1,0:T(8,128)} %shard_map.47), calls=%async_computation.2 | async-start | bytes 1572864 | tf_op jit(solution)/shard_map/all_to_all | solution.py:176
  174.1 24.5 %all-to-all-start.1 = ((f32[4,128,384]{2,1,0:T(8,128)}), f32[4,128,384]{2,1,0:T(8,128)S(1)}, u32[]{:S(2)}, u32[]{:S(2)}) async-start(f32[4,128,384]{2,1,0:T(8,128)} %shard_map.46), calls=%async_computation.1 | async-start | bytes 1572864 | tf_op jit(solution)/shard_map/all_to_all | solution.py:176
  206.2 1.4 copy-start.2
  206.2 1.8 copy-start.4
  207.4 1.1 copy-start.3
Sparse Core Ops, SparseCore 0:
  9.9 31.6 all-gather.2

commit v5 on v4

--- a/solution.py
+++ b/solution.py
@@ -17,71 +17,80 @@
 
 
 def attend_kernel(sel_ref, home_ref, q_ref, kv_ref, own_ref, out_ref,
-                  p_buf, m_scr, l_scr, acc_scr, *, groups, heads, first, all_heads, chunks, factor):
-    b = pl.program_id(0)
+                  p_buf, m_scr, l_scr, acc_scr, *, groups, heads, first, all_heads, blocks, chunks,
+                  factor):
     rows = QUERY_GROUP_ROWS
-    q = q_ref[0].reshape(heads * rows, HEAD_SIZE)
+    slots = blocks * heads
+    q = q_ref[...].reshape(slots * rows, HEAD_SIZE)
     m_scr[...] = jnp.full(m_scr.shape, -jnp.inf, jnp.float32)
     l_scr[...] = jnp.zeros(l_scr.shape, jnp.float32)
     acc_scr[...] = jnp.zeros(acc_scr.shape, jnp.float32)
 
-    def update(s, value, on_of, mask):
-        width = s.shape[1]
-        for h in range(heads):
-            on = on_of(h)
-
-            @pl.when(on)
-            def _():
-                s_h = s[h * rows:(h + 1) * rows] * factor
-                if mask is not None:
-                    s_h = jnp.where(mask, s_h, -jnp.inf)
-                m_old = m_scr[h]
-                m_new = jnp.maximum(m_old, jnp.max(s_h, axis=1, keepdims=True))
-                m_safe = jnp.where(m_new == -jnp.inf, 0.0, m_new)
-                alpha = jnp.exp2(m_old - m_safe)
-                p = jnp.exp2(s_h - m_safe)
-                l_scr[h] = alpha * l_scr[h] + jnp.sum(p, axis=1, keepdims=True)
-                m_scr[h] = m_new
-                acc_scr[h] = alpha * acc_scr[h]
-                p_buf[h * rows:(h + 1) * rows, :width] = p.astype(jnp.bfloat16)
-
-            @pl.when(jnp.logical_not(on))
-            def _():
-                p_buf[h * rows:(h + 1) * rows, :width] = jnp.zeros((rows, width), jnp.bfloat16)
-
-        pv = jnp.dot(p_buf[:, :width], value, preferred_element_type=jnp.float32)
-        for h in range(heads):
-            @pl.when(on_of(h))
-            def _():
-                acc_scr[h] += pv[h * rows:(h + 1) * rows]
+    def soften(s_h, slot, mask):
+        s_h = s_h * factor
+        if mask is not None:
+            s_h = jnp.where(mask, s_h, -jnp.inf)
+        m_old = m_scr[slot]
+        m_new = jnp.maximum(m_old, jnp.max(s_h, axis=1, keepdims=True))
+        m_safe = jnp.where(m_new == -jnp.inf, 0.0, m_new)
+        alpha = jnp.exp2(m_old - m_safe)
+        p = jnp.exp2(s_h - m_safe)
+        l_scr[slot] = alpha * l_scr[slot] + jnp.sum(p, axis=1, keepdims=True)
+        m_scr[slot] = m_new
+        acc_scr[slot] = alpha * acc_scr[slot]
+        return p.astype(jnp.bfloat16)
 
     def piece(g, carry):
-        base = (b * all_heads + first) * groups + g
         if chunks == 1:
             s = jnp.dot(q, kv_ref[g, 0, 0], preferred_element_type=jnp.float32)
         else:
             s = jnp.concatenate(
                 [jnp.dot(q, kv_ref[g, 0, c], preferred_element_type=jnp.float32)
                  for c in range(chunks)], axis=1)
+        width = s.shape[1]
+        ons = []
+        for slot in range(slots):
+            b, h = divmod(slot, heads)
+            on = sel_ref[(b * all_heads + first + h) * groups + g] != 0
+            ons.append(on)
+
+            @pl.when(on)
+            def _():
+                p_buf[slot * rows:(slot + 1) * rows, :width] = soften(
+                    s[slot * rows:(slot + 1) * rows], slot, None)
+
+            @pl.when(jnp.logical_not(on))
+            def _():
+                p_buf[slot * rows:(slot + 1) * rows, :width] = jnp.zeros((rows, width), jnp.bfloat16)
+
         value = kv_ref[g, 1].reshape(chunks * HEAD_SIZE, HEAD_SIZE)
-        update(s, value, lambda h: sel_ref[base + h * groups] != 0, None)
+        pv = jnp.dot(p_buf[:, :width], value, preferred_element_type=jnp.float32)
+        for slot in range(slots):
+            @pl.when(ons[slot])
+            def _():
+                acc_scr[slot] += pv[slot * rows:(slot + 1) * rows]
         return carry
 
     lax.fori_loop(0, groups, piece, 0)
 
-    @pl.when(b == home_ref[0])
-    def _():
-        causal = lax.broadcasted_iota(jnp.int32, (rows, rows), 0) >= lax.broadcasted_iota(
-            jnp.int32, (rows, rows), 1)
-        s = jnp.dot(q, own_ref[0], preferred_element_type=jnp.float32)
-        update(s, own_ref[1], lambda h: True, causal)
+    home = home_ref[0]
+    causal = lax.broadcasted_iota(jnp.int32, (rows, rows), 0) >= lax.broadcasted_iota(
+        jnp.int32, (rows, rows), 1)
+    q_home = q_ref[home].reshape(heads * rows, HEAD_SIZE)
+    s = jnp.dot(q_home, own_ref[0], preferred_element_type=jnp.float32)
+    for h in range(heads):
+        slot = home * heads + h
+        p = soften(s[h * rows:(h + 1) * rows], slot, causal)
+        acc_scr[slot] += jnp.dot(p, own_ref[1], preferred_element_type=jnp.float32)
 
     stats = heads * HEAD_SIZE
-    out_ref[0, :, stats:] = jnp.zeros((rows, HEAD_SIZE), jnp.float32)
-    for h in range(heads):
-        out_ref[0, :, h * HEAD_SIZE:(h + 1) * HEAD_SIZE] = acc_scr[h]
-        out_ref[0, :, stats + h:stats + h + 1] = m_scr[h]
-        out_ref[0, :, stats + heads + h:stats + heads + h + 1] = l_scr[h]
+    for b in range(blocks):
+        out_ref[b, :, stats:] = jnp.zeros((rows, HEAD_SIZE), jnp.float32)
+        for h in range(heads):
+            slot = b * heads + h
+            out_ref[b, :, h * HEAD_SIZE:(h + 1) * HEAD_SIZE] = acc_scr[slot]
+            out_ref[b, :, stats + h:stats + h + 1] = m_scr[slot]
+            out_ref[b, :, stats + heads + h:stats + heads + h + 1] = l_scr[slot]
 
 
 def join(a, b):
@@ -147,24 +156,27 @@
     outs = []
     for c in range(slices):
         kernel = functools.partial(attend_kernel, groups=groups, heads=part, first=c * part,
-                                   all_heads=heads, chunks=chunks, factor=scale * math.log2(math.e))
+                                   all_heads=heads, blocks=query_blocks, chunks=chunks,
+                                   factor=scale * math.log2(math.e))
+        slots = query_blocks * part
         partial = pl.pallas_call(
             kernel,
             grid_spec=pltpu.PrefetchScalarGridSpec(
                 num_scalar_prefetch=2,
-                grid=(query_blocks,),
+                grid=(1,),
                 in_specs=[
-                    pl.BlockSpec((1, part, rows, HEAD_SIZE), lambda b, s, h, c=c: (b, c, 0, 0)),
+                    pl.BlockSpec((query_blocks, part, rows, HEAD_SIZE),
+                                 lambda i, s, h, c=c: (0, c, 0, 0)),
                     pl.BlockSpec((groups, 2, chunks, HEAD_SIZE, HEAD_SIZE),
-                                 lambda b, s, h: (0, 0, 0, 0, 0)),
-                    pl.BlockSpec((2, rows, HEAD_SIZE), lambda b, s, h: (0, 0, 0)),
+                                 lambda i, s, h: (0, 0, 0, 0, 0)),
+                    pl.BlockSpec((2, rows, HEAD_SIZE), lambda i, s, h: (0, 0, 0)),
                 ],
-                out_specs=pl.BlockSpec((1, rows, width), lambda b, s, h: (b, 0, 0)),
+                out_specs=pl.BlockSpec((query_blocks, rows, width), lambda i, s, h: (0, 0, 0)),
                 scratch_shapes=[
-                    pltpu.VMEM((part * rows, max(piece, rows)), jnp.bfloat16),
-                    pltpu.VMEM((part, rows, 1), jnp.float32),
-                    pltpu.VMEM((part, rows, 1), jnp.float32),
-                    pltpu.VMEM((part, rows, HEAD_SIZE), jnp.float32),
+                    pltpu.VMEM((slots * rows, piece), jnp.bfloat16),
+                    pltpu.VMEM((slots, rows, 1), jnp.float32),
+                    pltpu.VMEM((slots, rows, 1), jnp.float32),
+                    pltpu.VMEM((slots, rows, HEAD_SIZE), jnp.float32),
                 ],
             ),
             out_shape=jax.ShapeDtypeStruct((query_blocks, rows, width), jnp.float32),

time: 219 us -> 191 us (0.87)
  Pallas kernels: 113 us -> 86.1 us
    pallas_call x4, Pallas kernels: 113 us -> 86.1 us  [local(): pl.pallas_call(kernel, grid_spec=pltpu.PrefetchScalarGridSpec(num_scalar_...]
  transfers between devices with their start and end apart: 6 -> 6, of which waited for: 2 -> 3; matrix products, arithmetic and copies ran while one was open for 7% -> 8% of each run, Pallas kernels for 39% -> 34%
where the time goes in v5:
time: 191 us; the launch traced here: 190 us
  Pallas kernels  86.1 us (45%)
  waiting for transfers between devices  36.2 us (19%)
  starting transfers between devices  23.6 us (12%)
  local copies, waits for them, and re-layouts  22.6 us (12%)
  between operations  13.7 us (7%)
  other arithmetic  7.51 us (4%)
    pallas_call x4, Pallas kernels, local(): pl.pallas_call(kernel, grid_spec=pltpu.PrefetchScalarGridSpec(num_scalar_...  86.1 us
    all_gather x1, waiting for transfers between devices, local(): q_all = lax.all_gather(q[None], 'help', axis=0, tiled=True)  22.8 us
    all_to_all x4, starting transfers between devices, local(): got = lax.all_to_all(partial, 'help', 0, 0, tiled=True)  19.2 us
    mul x8, local copies, waits for them, and re-layouts, local(): acc = jnp.sum(acc * fade[..., None], axis=0)  14.7 us
    all_to_all x4, waiting for transfers between devices, local(): got = lax.all_to_all(partial, 'help', 0, 0, tiled=True)  13.4 us
    unnamed x18, local copies, waits for them, and re-layouts  4.44 us
    all_to_all x1, starting transfers between devices, local(): lax.all_to_all(jnp.stack([keys, values], axis=1), 'blk', 0, 0, tiled=True)  4.39 us
  transfers between devices with their start and end apart: 6, of which 3 were waited for; matrix products, arithmetic and copies ran while one was open for 8% of the time, Pallas kernels for 34%

profile of v5, /device:TPU:2, one launch (start us, length us, event | category | flops | bytes accessed | tf_op | source)
XLA Modules:
  0.0 189.6 jit_solution(5345212411498453392)
XLA Ops:
  6.5 0.0 all-gather.3.cloned.1.call-start
  6.5 0.8 convert_element_type.22
  7.4 0.1 copy.29
  7.5 0.1 convert_element_type.23
  7.6 0.1 copy.30
  7.7 1.1 copy.28
  8.9 0.9 copy.31
  9.8 0.0 all-gather.3.cloned.1.call-update
  9.8 0.0 copy-done
  9.8 0.6 copy.39
  10.5 0.4 fusion.8
  10.8 0.8 copy.36
  11.7 0.2 copy.51
  11.9 1.5 pad_maximum_fusion
  13.4 4.4 %all-to-all-start = ((bf16[8,2,4,128,128]{4,3,2,1,0:T(8,128)(2,1)}), bf16[8,2,4,128,128]{4,3,2,1,0:T(8,128)(2,1)S(1)}, u32[]{:S(2)}, u32[]{:S(2)}) async-start(bf16[8,2,4,128,128]{4,3,2,1,0:T(8,128)(2,1)} %pad_maximum_fusion), calls=%async_computation | async-start | bytes 4194304 | tf_op jit(solution)/shard_map/all_to_all | solution.py:131
  17.8 0.0 copy-done.5
  17.8 0.1 copy.40
  17.9 0.1 constant_dynamic-slice_fusion
  18.1 0.1 copy.35
  18.3 0.6 pad_maximum_fusion.3.own_ref
  18.9 22.8 %all-gather.3.cloned.1.call-done = bf16[36,128,128]{2,1,0:T(8,128)(2,1)} async-done(((bf16[9,128,128]{2,1,0:T(8,128)(2,1)}), bf16[36,128,128]{2,1,0:T(8,128)(2,1)}) %all-gather.3.cloned.1.call-update) | async-done | bytes 1179664 | tf_op jit(solution)/shard_map/all_gather | solution.py:137
  41.7 0.7 slice_convert_fusion
  42.4 0.1 reshape.80
  42.5 0.7 compare_reduce_fusion
  43.2 0.7 reshape.81.sel_ref
  43.9 0.0 all-to-all-done.kv_ref
  43.9 1.4 copy-done.1
  45.2 22.0 %shard_map.49 = f32[4,128,384]{2,1,0:T(8,128)} custom-call(s32[256]{0:T(256)} %reshape.81.sel_ref, s32[1]{0:T(128)} %bitcast.4.home_ref, bf16[4,9,128,128]{3,2,1,0:T(8,128)(2,1)} %bitcast.61, bf16[8,2,4,128,128]{4,3,2,1,0:T(8,128)(2,1)} %copy-done.1, bf16[2,128,128]{2,1,0:T(8,128)(2,1)} %pad_maximum_fusion.3.own_ref), custom_call_target="tpu_custom_call" | custom-call | flops 2147483648 | bytes 2883584 | tf_op jit(solution)/shard_map/pallas_call | solution.py:162
  67.2 3.5 %all-to-all-start.4 = ((f32[4,128,384]{2,1,0:T(8,128)}), f32[4,128,384]{2,1,0:T(8,128)S(1)}, u32[]{:S(2)}, u32[]{:S(2)}) async-start(f32[4,128,384]{2,1,0:T(8,128)} %shard_map.49), calls=%async_computation.4 | async-start | bytes 1572864 | tf_op jit(solution)/shard_map/all_to_all | solution.py:188
  70.7 21.1 %shard_map.48 = f32[4,128,384]{2,1,0:T(8,128)} custom-call(s32[256]{0:T(256)} %reshape.81.sel_ref, s32[1]{0:T(128)} %bitcast.4.home_ref, bf16[4,9,128,128]{3,2,1,0:T(8,128)(2,1)} %bitcast.62, bf16[8,2,4,128,128]{4,3,2,1,0:T(8,128)(2,1)} %copy-done.1, bf16[2,128,128]{2,1,0:T(8,128)(2,1)} %pad_maximum_fusion.3.own_ref), custom_call_target="tpu_custom_call" | custom-call | flops 2147483648 | bytes 2883584 | tf_op jit(solution)/shard_map/pallas_call | solution.py:162
  91.9 0.3 all-to-all-done.4
  92.2 5.4 %all-to-all-start.3 = ((f32[4,128,384]{2,1,0:T(8,128)}), f32[4,128,384]{2,1,0:T(8,128)S(1)}, u32[]{:S(2)}, u32[]{:S(2)}) async-start(f32[4,128,384]{2,1,0:T(8,128)} %shard_map.48), calls=%async_computation.3 | async-start | bytes 1572864 | tf_op jit(solution)/shard_map/all_to_all | solution.py:188
  97.5 20.6 %shard_map.47 = f32[4,128,384]{2,1,0:T(8,128)} custom-call(s32[256]{0:T(256)} %reshape.81.sel_ref, s32[1]{0:T(128)} %bitcast.4.home_ref, bf16[4,9,128,128]{3,2,1,0:T(8,128)(2,1)} %bitcast.63, bf16[8,2,4,128,128]{4,3,2,1,0:T(8,128)(2,1)} %copy-done.1, bf16[2,128,128]{2,1,0:T(8,128)(2,1)} %pad_maximum_fusion.3.own_ref), custom_call_target="tpu_custom_call" | custom-call | flops 2147483648 | bytes 2883584 | tf_op jit(solution)/shard_map/pallas_call | solution.py:162
  118.2 0.0 all-to-all-done.3
  118.2 6.8 %all-to-all-start.2 = ((f32[4,128,384]{2,1,0:T(8,128)}), f32[4,128,384]{2,1,0:T(8,128)S(1)}, u32[]{:S(2)}, u32[]{:S(2)}) async-start(f32[4,128,384]{2,1,0:T(8,128)} %shard_map.47), calls=%async_computation.2 | async-start | bytes 1572864 | tf_op jit(solution)/shard_map/all_to_all | solution.py:188
  125.0 22.3 %shard_map.46 = f32[4,128,384]{2,1,0:T(8,128)} custom-call(s32[256]{0:T(256)} %reshape.81.sel_ref, s32[1]{0:T(128)} %bitcast.4.home_ref, bf16[4,9,128,128]{3,2,1,0:T(8,128)(2,1)} %bitcast.64, bf16[8,2,4,128,128]{4,3,2,1,0:T(8,128)(2,1)} %copy-done.1, bf16[2,128,128]{2,1,0:T(8,128)(2,1)} %pad_maximum_fusion.3.own_ref), custom_call_target="tpu_custom_call" | custom-call | flops 2147483648 | bytes 2883584 | tf_op jit(solution)/shard_map/pallas_call | solution.py:162
  147.3 0.0 all-to-all-done.2
  147.4 3.5 %all-to-all-start.1 = ((f32[4,128,384]{2,1,0:T(8,128)}), f32[4,128,384]{2,1,0:T(8,128)S(1)}, u32[]{:S(2)}, u32[]{:S(2)}) async-start(f32[4,128,384]{2,1,0:T(8,128)} %shard_map.46), calls=%async_computation.1 | async-start | bytes 1572864 | tf_op jit(solution)/shard_map/all_to_all | solution.py:188
  150.9 0.1 fusion.4
  151.0 1.4 mul.85
  152.4 2.2 %mul.86 = f32[4,128,256]{2,1,0:T(8,128)} reshape(f32[4,128,2,128]{3,2,1,0:T(2,128)} %mul.85) | data formatting | bytes 1048576 | tf_op jit(solution)/shard_map/mul | solution.py:195
  154.7 0.1 fusion.5
  154.9 1.4 mul.81
  156.3 2.3 %mul.82 = f32[4,128,256]{2,1,0:T(8,128)} reshape(f32[4,128,2,128]{3,2,1,0:T(2,128)} %mul.81) | data formatting | bytes 1048576 | tf_op jit(solution)/shard_map/mul | solution.py:195
  158.6 13.1 %all-to-all-done.1 = f32[4,128,384]{2,1,0:T(8,128)S(1)} async-done(((f32[4,128,384]{2,1,0:T(8,128)}), f32[4,128,384]{2,1,0:T(8,128)S(1)}, u32[]{:S(2)}, u32[]{:S(2)}) %all-to-all-start.1) | async-done | bytes 786464 | tf_op jit(solution)/shard_map/all_to_all | solution.py:188
  171.7 0.1 fusion.6
  171.8 1.4 mul.77
  173.2 2.3 %mul.78 = f32[4,128,256]{2,1,0:T(8,128)} reshape(f32[4,128,2,128]{3,2,1,0:T(2,128)} %mul.77) | data formatting | bytes 1048576 | tf_op jit(solution)/shard_map/mul | solution.py:195
  175.5 0.1 fusion.7
  175.7 1.4 mul.73
  177.1 2.3 %mul.74 = f32[4,128,256]{2,1,0:T(8,128)} reshape(f32[4,128,2,128]{3,2,1,0:T(2,128)} %mul.73) | data formatting | bytes 1048576 | tf_op jit(solution)/shard_map/mul | solution.py:195
  179.3 1.2 fusion
  180.5 0.0 copy-start.3
  180.5 0.2 div.74
  180.8 0.0 copy-done.2
  180.8 0.1 fusion.1
  180.9 0.2 div.71
  181.1 0.0 copy-done.4
  181.1 0.1 fusion.2
  181.2 0.2 div.68
  181.4 0.2 copy-done.3
  181.6 0.1 fusion.3
  181.7 0.2 div.65
  181.9 0.9 pad_maximum_fusion.1
  (24 shorter events, 0.3 us)
Async XLA Ops:
  6.5 3.3 %copy-start = (bf16[512,2048]{1,0:T(8,128)(2,1)S(1)}, bf16[512,2048]{1,0:T(8,128)(2,1)}, u32[]{:S(2)}) copy-start(bf16[512,2048]{1,0:T(8,128)(2,1)} %param.6) | copy-start | bytes 6291460
  6.5 35.1 %all-gather.3.cloned.1.call-start = ((), (), s32[]{:S(2)}) async-start(), calls=%async_computation.5 | async-start | bytes 1474560 | tf_op jit(solution)/shard_map/all_gather | solution.py:137
  13.4 4.4 %copy-start.5 = (bf16[128,2048]{1,0:T(8,128)(2,1)S(1)}, bf16[128,2048]{1,0:T(8,128)(2,1)}, u32[]{:S(2)}) copy-start(bf16[128,2048]{1,0:T(8,128)(2,1)} %param.5) | copy-start | bytes 1572868
  13.4 30.4 %all-to-all-start = ((bf16[8,2,4,128,128]{4,3,2,1,0:T(8,128)(2,1)}), bf16[8,2,4,128,128]{4,3,2,1,0:T(8,128)(2,1)S(1)}, u32[]{:S(2)}, u32[]{:S(2)}) async-start(bf16[8,2,4,128,128]{4,3,2,1,0:T(8,128)(2,1)} %pad_maximum_fusion), calls=%async_computation | async-start | bytes 4194304 | tf_op jit(solution)/shard_map/all_to_all | solution.py:131
  43.9 1.4 copy-start.1
  67.2 25.0 %all-to-all-start.4 = ((f32[4,128,384]{2,1,0:T(8,128)}), f32[4,128,384]{2,1,0:T(8,128)S(1)}, u32[]{:S(2)}, u32[]{:S(2)}) async-start(f32[4,128,384]{2,1,0:T(8,128)} %shard_map.49), calls=%async_computation.4 | async-start | bytes 1572864 | tf_op jit(solution)/shard_map/all_to_all | solution.py:188
  92.2 26.0 %all-to-all-start.3 = ((f32[4,128,384]{2,1,0:T(8,128)}), f32[4,128,384]{2,1,0:T(8,128)S(1)}, u32[]{:S(2)}, u32[]{:S(2)}) async-start(f32[4,128,384]{2,1,0:T(8,128)} %shard_map.48), calls=%async_computation.3 | async-start | bytes 1572864 | tf_op jit(solution)/shard_map/all_to_all | solution.py:188
  118.2 29.2 %all-to-all-start.2 = ((f32[4,128,384]{2,1,0:T(8,128)}), f32[4,128,384]{2,1,0:T(8,128)S(1)}, u32[]{:S(2)}, u32[]{:S(2)}) async-start(f32[4,128,384]{2,1,0:T(8,128)} %shard_map.47), calls=%async_computation.2 | async-start | bytes 1572864 | tf_op jit(solution)/shard_map/all_to_all | solution.py:188
  147.4 24.3 %all-to-all-start.1 = ((f32[4,128,384]{2,1,0:T(8,128)}), f32[4,128,384]{2,1,0:T(8,128)S(1)}, u32[]{:S(2)}, u32[]{:S(2)}) async-start(f32[4,128,384]{2,1,0:T(8,128)} %shard_map.46), calls=%async_computation.1 | async-start | bytes 1572864 | tf_op jit(solution)/shard_map/all_to_all | solution.py:188
  179.3 1.4 copy-start.2
  179.3 1.8 copy-start.4
  180.5 1.1 copy-start.3
Sparse Core Ops, SparseCore 0:
  9.9 31.6 all-gather.2

commit v6 on v5

--- a/solution.py
+++ b/solution.py
@@ -27,14 +27,13 @@
     acc_scr[...] = jnp.zeros(acc_scr.shape, jnp.float32)
 
     def soften(s_h, slot, mask):
-        s_h = s_h * factor
         if mask is not None:
             s_h = jnp.where(mask, s_h, -jnp.inf)
         m_old = m_scr[slot]
-        m_new = jnp.maximum(m_old, jnp.max(s_h, axis=1, keepdims=True))
+        m_new = jnp.maximum(m_old, jnp.max(s_h, axis=1, keepdims=True) * factor)
         m_safe = jnp.where(m_new == -jnp.inf, 0.0, m_new)
         alpha = jnp.exp2(m_old - m_safe)
-        p = jnp.exp2(s_h - m_safe)
+        p = jnp.exp2(s_h * factor - m_safe)
         l_scr[slot] = alpha * l_scr[slot] + jnp.sum(p, axis=1, keepdims=True)
         m_scr[slot] = m_new
         acc_scr[slot] = alpha * acc_scr[slot]
@@ -91,6 +90,25 @@
             out_ref[b, :, h * HEAD_SIZE:(h + 1) * HEAD_SIZE] = acc_scr[slot]
             out_ref[b, :, stats + h:stats + h + 1] = m_scr[slot]
             out_ref[b, :, stats + heads + h:stats + heads + h + 1] = l_scr[slot]
+
+
+def join_kernel(got_ref, out_ref, *, sources, heads):
+    stats = heads * HEAD_SIZE
+    for h in range(heads):
+        ms = [got_ref[s, :, stats + h:stats + h + 1] for s in range(sources)]
+        top = ms[0]
+        for m in ms[1:]:
+            top = jnp.maximum(top, m)
+        top = jnp.where(top == -jnp.inf, 0.0, top)
+        total = None
+        acc = None
+        for s in range(sources):
+            fade = jnp.exp2(ms[s] - top)
+            part_total = fade * got_ref[s, :, stats + heads + h:stats + heads + h + 1]
+            part_acc = fade * got_ref[s, :, h * HEAD_SIZE:(h + 1) * HEAD_SIZE]
+            total = part_total if total is None else total + part_total
+            acc = part_acc if acc is None else acc + part_acc
+        out_ref[:, h * HEAD_SIZE:(h + 1) * HEAD_SIZE] = acc / total
 
 
 def join(a, b):
@@ -186,14 +204,12 @@
                 bytes_accessed=2 * groups * 2 * piece * HEAD_SIZE + 4 * query_blocks * rows * width),
         )(sel_flat, home, q_all, held, own)
         got = lax.all_to_all(partial, "help", 0, 0, tiled=True)
-        acc = got[:, :, :part * HEAD_SIZE].reshape(helpers, rows, part, HEAD_SIZE)
-        m = got[:, :, part * HEAD_SIZE:part * HEAD_SIZE + part]
-        l = got[:, :, part * HEAD_SIZE + part:part * HEAD_SIZE + 2 * part]
-        top = jnp.max(m, axis=0)
-        fade = jnp.exp2(m - jnp.where(top == -jnp.inf, 0.0, top))
-        total = jnp.sum(l * fade, axis=0)
-        acc = jnp.sum(acc * fade[..., None], axis=0)
-        outs.append((acc / total[..., None]).reshape(rows, part * HEAD_SIZE))
+        outs.append(pl.pallas_call(
+            functools.partial(join_kernel, sources=helpers, heads=part),
+            in_specs=[pl.BlockSpec(memory_space=pltpu.VMEM)],
+            out_specs=pl.BlockSpec(memory_space=pltpu.VMEM),
+            out_shape=jax.ShapeDtypeStruct((rows, part * HEAD_SIZE), jnp.float32),
+        )(got))
     return jnp.concatenate(outs, axis=1)
 
 

time: 191 us -> 184 us (0.963); the launches traced: 190 us -> 181 us
  local copies, waits for them, and re-layouts: 22.6 us -> 7.77 us
  Pallas kernels: 86.1 us -> 98.3 us
  starting transfers between devices: 23.6 us -> 20.4 us
    mul x8 -> x0, local copies, waits for them, and re-layouts: 14.7 us -> none  [local(): acc = jnp.sum(acc * fade[..., None], axis=0)]
    pallas_call x0 -> x4, Pallas kernels: none -> 9 us  [local(): pl.pallas_call(functools.partial(join_kernel, sources=helpers, heads=part...]
    all_to_all x4, starting transfers between devices: 19.2 us -> 16 us  [local(): got = lax.all_to_all(partial, 'help', 0, 0, tiled=True)]
    pallas_call x4, Pallas kernels: 86.1 us -> 89.3 us  [local(): pl.pallas_call(kernel, grid_spec=pltpu.PrefetchScalarGridSpec(num_scalar_...]
    reduce_sum x8 -> x0, other arithmetic: 2 us -> none  [the longest x4 1.44 us: local(): acc = jnp.sum(acc * fade[..., None], axis=0)]
    unnamed x18 -> x22, local copies, waits for them, and re-layouts: 4.44 us -> 5.13 us
  transfers between devices with their start and end apart: 6 -> 6, of which waited for: 3 -> 2; matrix products, arithmetic and copies ran while one was open for 8% -> 4% of each run, Pallas kernels for 34% -> 41%
where the time goes in v6:
time: 184 us; the launch traced here: 181 us
  Pallas kernels  98.3 us (53%)
  waiting for transfers between devices  34.3 us (19%)
  starting transfers between devices  20.4 us (11%)
  between operations  13.6 us (7%)
  local copies, waits for them, and re-layouts  7.77 us (4%)
  other arithmetic  6.31 us (3%)
    pallas_call x4, Pallas kernels, local(): pl.pallas_call(kernel, grid_spec=pltpu.PrefetchScalarGridSpec(num_scalar_...  89.3 us
    all_gather x1, waiting for transfers between devices, local(): q_all = lax.all_gather(q[None], 'help', axis=0, tiled=True)  22.8 us
    all_to_all x4, starting transfers between devices, local(): got = lax.all_to_all(partial, 'help', 0, 0, tiled=True)  16 us
    all_to_all x4, waiting for transfers between devices, local(): got = lax.all_to_all(partial, 'help', 0, 0, tiled=True)  11.5 us
    pallas_call x4, Pallas kernels, local(): pl.pallas_call(functools.partial(join_kernel, sources=helpers, heads=part...  9 us
    unnamed x22, local copies, waits for them, and re-layouts  5.13 us
    all_to_all x1, starting transfers between devices, local(): lax.all_to_all(jnp.stack([keys, values], axis=1), 'blk', 0, 0, tiled=True)  4.39 us
  transfers between devices with their start and end apart: 6, of which 2 were waited for; matrix products, arithmetic and copies ran while one was open for 4% of the time, Pallas kernels for 41%

profile of v6, /device:TPU:2, one launch (start us, length us, event | category | flops | bytes accessed | tf_op | source)
XLA Modules:
  0.0 180.6 jit_solution(952443417247222332)
XLA Ops:
  6.5 0.0 copy-start.4
  6.5 0.0 all-gather.3.cloned.1.call-start
  6.5 0.8 convert_element_type.22
  7.4 0.1 copy.29
  7.5 0.1 convert_element_type.23
  7.6 0.1 copy.30
  7.7 1.1 copy.28
  8.9 0.9 copy.31
  9.8 0.0 all-gather.3.cloned.1.call-update
  9.8 0.0 copy-done.4
  9.8 0.6 copy.39
  10.5 0.4 fusion
  10.8 0.2 copy.43
  11.1 0.8 copy.36
  11.9 1.5 pad_maximum_fusion
  13.4 0.0 copy-start.6
  13.4 4.4 %all-to-all-start = ((bf16[8,2,4,128,128]{4,3,2,1,0:T(8,128)(2,1)}), bf16[8,2,4,128,128]{4,3,2,1,0:T(8,128)(2,1)S(1)}, u32[]{:S(2)}, u32[]{:S(2)}) async-start(bf16[8,2,4,128,128]{4,3,2,1,0:T(8,128)(2,1)} %pad_maximum_fusion), calls=%async_computation | async-start | bytes 4194304 | tf_op jit(solution)/shard_map/all_to_all | solution.py:149
  17.8 0.0 copy-done.6
  17.8 0.1 copy.40
  17.9 0.1 constant_dynamic-slice_fusion
  18.1 0.1 copy.35
  18.2 0.6 pad_maximum_fusion.3.own_ref
  18.9 22.8 %all-gather.3.cloned.1.call-done = bf16[36,128,128]{2,1,0:T(8,128)(2,1)} async-done(((bf16[9,128,128]{2,1,0:T(8,128)(2,1)}), bf16[36,128,128]{2,1,0:T(8,128)(2,1)}) %all-gather.3.cloned.1.call-update) | async-done | bytes 1179664 | tf_op jit(solution)/shard_map/all_gather | solution.py:155
  41.7 0.7 slice_convert_fusion
  42.4 0.1 reshape.28
  42.5 0.7 compare_reduce_fusion
  43.2 0.7 reshape.29.sel_ref
  43.9 0.0 all-to-all-done.kv_ref
  43.9 0.0 copy-start.5
  43.9 1.3 copy-done.5
  45.2 21.3 %shard_map.52 = f32[4,128,384]{2,1,0:T(8,128)} custom-call(s32[256]{0:T(256)} %reshape.29.sel_ref, s32[1]{0:T(128)} %bitcast.4.home_ref, bf16[4,9,128,128]{3,2,1,0:T(8,128)(2,1)} %bitcast.45, bf16[8,2,4,128,128]{4,3,2,1,0:T(8,128)(2,1)} %copy-done.5, bf16[2,128,128]{2,1,0:T(8,128)(2,1)} %pad_maximum_fusion.3.own_ref), custom_call_target="tpu_custom_call" | custom-call | flops 2147483648 | bytes 2883584 | tf_op jit(solution)/shard_map/pallas_call | solution.py:180
  66.5 4.5 %all-to-all-start.4 = ((f32[4,128,384]{2,1,0:T(8,128)}), f32[4,128,384]{2,1,0:T(8,128)S(1)}, u32[]{:S(2)}, u32[]{:S(2)}) async-start(f32[4,128,384]{2,1,0:T(8,128)} %shard_map.52), calls=%async_computation.4 | async-start | bytes 1572864 | tf_op jit(solution)/shard_map/all_to_all | solution.py:206
  71.0 23.6 %shard_map.50 = f32[4,128,384]{2,1,0:T(8,128)} custom-call(s32[256]{0:T(256)} %reshape.29.sel_ref, s32[1]{0:T(128)} %bitcast.4.home_ref, bf16[4,9,128,128]{3,2,1,0:T(8,128)(2,1)} %bitcast.46, bf16[8,2,4,128,128]{4,3,2,1,0:T(8,128)(2,1)} %copy-done.5, bf16[2,128,128]{2,1,0:T(8,128)(2,1)} %pad_maximum_fusion.3.own_ref), custom_call_target="tpu_custom_call" | custom-call | flops 2147483648 | bytes 2883584 | tf_op jit(solution)/shard_map/pallas_call | solution.py:180
  94.7 0.0 all-to-all-done.4.got_ref
  94.7 0.0 copy-start
  94.7 3.5 %all-to-all-start.3 = ((f32[4,128,384]{2,1,0:T(8,128)}), f32[4,128,384]{2,1,0:T(8,128)S(1)}, u32[]{:S(2)}, u32[]{:S(2)}) async-start(f32[4,128,384]{2,1,0:T(8,128)} %shard_map.50), calls=%async_computation.3 | async-start | bytes 1572864 | tf_op jit(solution)/shard_map/all_to_all | solution.py:206
  98.2 21.9 %shard_map.48 = f32[4,128,384]{2,1,0:T(8,128)} custom-call(s32[256]{0:T(256)} %reshape.29.sel_ref, s32[1]{0:T(128)} %bitcast.4.home_ref, bf16[4,9,128,128]{3,2,1,0:T(8,128)(2,1)} %bitcast.47, bf16[8,2,4,128,128]{4,3,2,1,0:T(8,128)(2,1)} %copy-done.5, bf16[2,128,128]{2,1,0:T(8,128)(2,1)} %pad_maximum_fusion.3.own_ref), custom_call_target="tpu_custom_call" | custom-call | flops 2147483648 | bytes 2883584 | tf_op jit(solution)/shard_map/pallas_call | solution.py:180
  120.0 0.0 copy-done
  120.1 0.0 all-to-all-done.3.got_ref
  120.1 0.0 copy-start.1
  120.1 4.5 %all-to-all-start.2 = ((f32[4,128,384]{2,1,0:T(8,128)}), f32[4,128,384]{2,1,0:T(8,128)S(1)}, u32[]{:S(2)}, u32[]{:S(2)}) async-start(f32[4,128,384]{2,1,0:T(8,128)} %shard_map.48), calls=%async_computation.2 | async-start | bytes 1572864 | tf_op jit(solution)/shard_map/all_to_all | solution.py:206
  124.5 22.5 %shard_map.46 = f32[4,128,384]{2,1,0:T(8,128)} custom-call(s32[256]{0:T(256)} %reshape.29.sel_ref, s32[1]{0:T(128)} %bitcast.4.home_ref, bf16[4,9,128,128]{3,2,1,0:T(8,128)(2,1)} %bitcast.48, bf16[8,2,4,128,128]{4,3,2,1,0:T(8,128)(2,1)} %copy-done.5, bf16[2,128,128]{2,1,0:T(8,128)(2,1)} %pad_maximum_fusion.3.own_ref), custom_call_target="tpu_custom_call" | custom-call | flops 2147483648 | bytes 2883584 | tf_op jit(solution)/shard_map/pallas_call | solution.py:180
  147.0 0.0 copy-done.1
  147.0 0.0 all-to-all-done.2.got_ref
  147.0 0.0 copy-start.2
  147.0 3.5 %all-to-all-start.1 = ((f32[4,128,384]{2,1,0:T(8,128)}), f32[4,128,384]{2,1,0:T(8,128)S(1)}, u32[]{:S(2)}, u32[]{:S(2)}) async-start(f32[4,128,384]{2,1,0:T(8,128)} %shard_map.46), calls=%async_computation.1 | async-start | bytes 1572864 | tf_op jit(solution)/shard_map/all_to_all | solution.py:206
  150.5 2.2 %shard_map.53 = f32[128,256]{1,0:T(8,128)} custom-call(f32[4,128,384]{2,1,0:T(8,128)} %copy-done), custom_call_target="tpu_custom_call" | custom-call | tf_op jit(solution)/shard_map/pallas_call | solution.py:207
  152.7 0.0 copy-start.7
  152.8 2.3 %shard_map.51 = f32[128,256]{1,0:T(8,128)} custom-call(f32[4,128,384]{2,1,0:T(8,128)} %copy-done.1), custom_call_target="tpu_custom_call" | custom-call | tf_op jit(solution)/shard_map/pallas_call | solution.py:207
  155.0 0.0 copy-done.2
  155.0 2.2 %shard_map.49 = f32[128,256]{1,0:T(8,128)} custom-call(f32[4,128,384]{2,1,0:T(8,128)} %copy-done.2), custom_call_target="tpu_custom_call" | custom-call | tf_op jit(solution)/shard_map/pallas_call | solution.py:207
  157.3 11.5 %all-to-all-done.1.got_ref = f32[4,128,384]{2,1,0:T(8,128)S(1)} async-done(((f32[4,128,384]{2,1,0:T(8,128)}), f32[4,128,384]{2,1,0:T(8,128)S(1)}, u32[]{:S(2)}, u32[]{:S(2)}) %all-to-all-start.1) | async-done | bytes 786464 | tf_op jit(solution)/shard_map/all_to_all | solution.py:206
  168.8 0.0 copy-start.3
  168.8 0.9 copy-done.3
  169.7 2.2 %shard_map.47 = f32[128,256]{1,0:T(8,128)} custom-call(f32[4,128,384]{2,1,0:T(8,128)} %copy-done.3), custom_call_target="tpu_custom_call" | custom-call | tf_op jit(solution)/shard_map/pallas_call | solution.py:207
  171.9 0.0 copy-done.7
  171.9 1.9 %pad_maximum_fusion.1 = f32[128,1024]{1,0:T(8,128)} fusion(f32[128,256]{1,0:T(8,128)S(1)} %copy-done.7, f32[128,256]{1,0:T(8,128)} %shard_map.51, f32[128,256]{1,0:T(8,128)} %shard_map.49, f32[128,256]{1,0:T(8,128)} %shard_map.47), kind=kLoop, calls=%fused_computation.2 | loop fusion | flops 393216 | bytes 1048576 | tf_op jit(solution)/shard_map/concatenate | solution.py:213
  (7 shorter events, 0.1 us)
Async XLA Ops:
  6.5 3.3 %copy-start.4 = (bf16[512,2048]{1,0:T(8,128)(2,1)S(1)}, bf16[512,2048]{1,0:T(8,128)(2,1)}, u32[]{:S(2)}) copy-start(bf16[512,2048]{1,0:T(8,128)(2,1)} %param.6) | copy-start | bytes 6291460
  6.5 35.1 %all-gather.3.cloned.1.call-start = ((), (), s32[]{:S(2)}) async-start(), calls=%async_computation.5 | async-start | bytes 1474560 | tf_op jit(solution)/shard_map/all_gather | solution.py:155
  13.4 4.4 %copy-start.6 = (bf16[128,2048]{1,0:T(8,128)(2,1)S(1)}, bf16[128,2048]{1,0:T(8,128)(2,1)}, u32[]{:S(2)}) copy-start(bf16[128,2048]{1,0:T(8,128)(2,1)} %param.5) | copy-start | bytes 1572868
  13.4 30.5 %all-to-all-start = ((bf16[8,2,4,128,128]{4,3,2,1,0:T(8,128)(2,1)}), bf16[8,2,4,128,128]{4,3,2,1,0:T(8,128)(2,1)S(1)}, u32[]{:S(2)}, u32[]{:S(2)}) async-start(bf16[8,2,4,128,128]{4,3,2,1,0:T(8,128)(2,1)} %pad_maximum_fusion), calls=%async_computation | async-start | bytes 4194304 | tf_op jit(solution)/shard_map/all_to_all | solution.py:149
  43.9 1.3 copy-start.5
  66.5 28.2 %all-to-all-start.4 = ((f32[4,128,384]{2,1,0:T(8,128)}), f32[4,128,384]{2,1,0:T(8,128)S(1)}, u32[]{:S(2)}, u32[]{:S(2)}) async-start(f32[4,128,384]{2,1,0:T(8,128)} %shard_map.52), calls=%async_computation.4 | async-start | bytes 1572864 | tf_op jit(solution)/shard_map/all_to_all | solution.py:206
  94.7 25.4 %copy-start = (f32[4,128,384]{2,1,0:T(8,128)}, f32[4,128,384]{2,1,0:T(8,128)S(1)}, u32[]{:S(2)}) copy-start(f32[4,128,384]{2,1,0:T(8,128)S(1)} %all-to-all-done.4.got_ref) | copy-start | bytes 2359300
  94.7 25.4 %all-to-all-start.3 = ((f32[4,128,384]{2,1,0:T(8,128)}), f32[4,128,384]{2,1,0:T(8,128)S(1)}, u32[]{:S(2)}, u32[]{:S(2)}) async-start(f32[4,128,384]{2,1,0:T(8,128)} %shard_map.50), calls=%async_computation.3 | async-start | bytes 1572864 | tf_op jit(solution)/shard_map/all_to_all | solution.py:206
  120.1 26.9 %copy-start.1 = (f32[4,128,384]{2,1,0:T(8,128)}, f32[4,128,384]{2,1,0:T(8,128)S(1)}, u32[]{:S(2)}) copy-start(f32[4,128,384]{2,1,0:T(8,128)S(1)} %all-to-all-done.3.got_ref) | copy-start | bytes 2359300
  120.1 26.9 %all-to-all-start.2 = ((f32[4,128,384]{2,1,0:T(8,128)}), f32[4,128,384]{2,1,0:T(8,128)S(1)}, u32[]{:S(2)}, u32[]{:S(2)}) async-start(f32[4,128,384]{2,1,0:T(8,128)} %shard_map.48), calls=%async_computation.2 | async-start | bytes 1572864 | tf_op jit(solution)/shard_map/all_to_all | solution.py:206
  147.0 8.0 %copy-start.2 = (f32[4,128,384]{2,1,0:T(8,128)}, f32[4,128,384]{2,1,0:T(8,128)S(1)}, u32[]{:S(2)}) copy-start(f32[4,128,384]{2,1,0:T(8,128)S(1)} %all-to-all-done.2.got_ref) | copy-start | bytes 2359300
  147.0 21.8 %all-to-all-start.1 = ((f32[4,128,384]{2,1,0:T(8,128)}), f32[4,128,384]{2,1,0:T(8,128)S(1)}, u32[]{:S(2)}, u32[]{:S(2)}) async-start(f32[4,128,384]{2,1,0:T(8,128)} %shard_map.46), calls=%async_computation.1 | async-start | bytes 1572864 | tf_op jit(solution)/shard_map/all_to_all | solution.py:206
  152.7 19.1 %copy-start.7 = (f32[128,256]{1,0:T(8,128)S(1)}, f32[128,256]{1,0:T(8,128)}, u32[]{:S(2)}) copy-start(f32[128,256]{1,0:T(8,128)} %shard_map.53) | copy-start | bytes 393220
  168.8 0.9 copy-start.3
Sparse Core Ops, SparseCore 0:
  9.9 31.6 all-gather.2

commit v7 on v6

--- a/solution.py
+++ b/solution.py
@@ -17,70 +17,89 @@
 
 
 def attend_kernel(sel_ref, home_ref, q_ref, kv_ref, own_ref, out_ref,
-                  p_buf, m_scr, l_scr, acc_scr, *, groups, heads, first, all_heads, blocks, chunks,
-                  factor):
+                  s_buf, own_buf, p_buf, mpart, lpart, m_scr, acc_scr,
+                  *, groups, heads, first, all_heads, blocks, chunks, factor):
     rows = QUERY_GROUP_ROWS
     slots = blocks * heads
+    lanes = HEAD_SIZE
     q = q_ref[...].reshape(slots * rows, HEAD_SIZE)
-    m_scr[...] = jnp.full(m_scr.shape, -jnp.inf, jnp.float32)
-    l_scr[...] = jnp.zeros(l_scr.shape, jnp.float32)
+    home = home_ref[0]
+    mpart[...] = jnp.full(mpart.shape, -jnp.inf, jnp.float32)
+    lpart[...] = jnp.zeros(lpart.shape, jnp.float32)
     acc_scr[...] = jnp.zeros(acc_scr.shape, jnp.float32)
 
-    def soften(s_h, slot, mask):
-        if mask is not None:
-            s_h = jnp.where(mask, s_h, -jnp.inf)
-        m_old = m_scr[slot]
-        m_new = jnp.maximum(m_old, jnp.max(s_h, axis=1, keepdims=True) * factor)
-        m_safe = jnp.where(m_new == -jnp.inf, 0.0, m_new)
-        alpha = jnp.exp2(m_old - m_safe)
-        p = jnp.exp2(s_h * factor - m_safe)
-        l_scr[slot] = alpha * l_scr[slot] + jnp.sum(p, axis=1, keepdims=True)
-        m_scr[slot] = m_new
-        acc_scr[slot] = alpha * acc_scr[slot]
-        return p.astype(jnp.bfloat16)
-
-    def piece(g, carry):
+    def on(slot, g):
+        b, h = divmod(slot, heads)
+        return sel_ref[(b * all_heads + first + h) * groups + g] != 0
+
+    def fold(x, op):
+        out = x[:, :lanes]
+        for c in range(1, x.shape[1] // lanes):
+            out = op(out, x[:, c * lanes:(c + 1) * lanes])
+        return out
+
+    def score(g, carry):
         if chunks == 1:
             s = jnp.dot(q, kv_ref[g, 0, 0], preferred_element_type=jnp.float32)
         else:
             s = jnp.concatenate(
                 [jnp.dot(q, kv_ref[g, 0, c], preferred_element_type=jnp.float32)
                  for c in range(chunks)], axis=1)
-        width = s.shape[1]
-        ons = []
+        s_buf[g] = s
         for slot in range(slots):
-            b, h = divmod(slot, heads)
-            on = sel_ref[(b * all_heads + first + h) * groups + g] != 0
-            ons.append(on)
-
-            @pl.when(on)
-            def _():
-                p_buf[slot * rows:(slot + 1) * rows, :width] = soften(
-                    s[slot * rows:(slot + 1) * rows], slot, None)
-
-            @pl.when(jnp.logical_not(on))
-            def _():
-                p_buf[slot * rows:(slot + 1) * rows, :width] = jnp.zeros((rows, width), jnp.bfloat16)
-
-        value = kv_ref[g, 1].reshape(chunks * HEAD_SIZE, HEAD_SIZE)
-        pv = jnp.dot(p_buf[:, :width], value, preferred_element_type=jnp.float32)
+            @pl.when(on(slot, g))
+            def _():
+                mpart[slot] = jnp.maximum(mpart[slot], fold(s[slot * rows:(slot + 1) * rows],
+                                                            jnp.maximum))
+        return carry
+
+    lax.fori_loop(0, groups, score, 0)
+
+    causal = lax.broadcasted_iota(jnp.int32, (rows, rows), 0) >= lax.broadcasted_iota(
+        jnp.int32, (rows, rows), 1)
+    s_own = jnp.dot(q_ref[home].reshape(heads * rows, HEAD_SIZE), own_ref[0],
+                    preferred_element_type=jnp.float32)
+    for h in range(heads):
+        s_h = jnp.where(causal, s_own[h * rows:(h + 1) * rows], -jnp.inf)
+        own_buf[h] = s_h
+        slot = home * heads + h
+        mpart[slot] = jnp.maximum(mpart[slot], fold(s_h, jnp.maximum))
+
+    for slot in range(slots):
+        m = jnp.max(mpart[slot], axis=1, keepdims=True) * factor
+        m_scr[slot] = m
+        mpart[slot] = jnp.broadcast_to(jnp.where(m == -jnp.inf, 0.0, m), (rows, lanes))
+
+    def mix(g, carry):
+        width = s_buf.shape[2]
+        ons = [on(slot, g) for slot in range(slots)]
         for slot in range(slots):
             @pl.when(ons[slot])
             def _():
+                p = jnp.exp2(s_buf[g, slot * rows:(slot + 1) * rows] * factor - mpart[slot][:, :1])
+                lpart[slot] += fold(p, jnp.add)
+                p_buf[slot * rows:(slot + 1) * rows] = p.astype(jnp.bfloat16)
+
+            @pl.when(jnp.logical_not(ons[slot]))
+            def _():
+                p_buf[slot * rows:(slot + 1) * rows] = jnp.zeros((rows, width), jnp.bfloat16)
+
+        value = kv_ref[g, 1].reshape(chunks * HEAD_SIZE, HEAD_SIZE)
+        pv = jnp.dot(p_buf[...], value, preferred_element_type=jnp.float32)
+        for slot in range(slots):
+            @pl.when(ons[slot])
+            def _():
                 acc_scr[slot] += pv[slot * rows:(slot + 1) * rows]
         return carry
 
-    lax.fori_loop(0, groups, piece, 0)
-
-    home = home_ref[0]
-    causal = lax.broadcasted_iota(jnp.int32, (rows, rows), 0) >= lax.broadcasted_iota(
-        jnp.int32, (rows, rows), 1)
-    q_home = q_ref[home].reshape(heads * rows, HEAD_SIZE)
-    s = jnp.dot(q_home, own_ref[0], preferred_element_type=jnp.float32)
+    lax.fori_loop(0, groups, mix, 0)
+
     for h in range(heads):
         slot = home * heads + h
-        p = soften(s[h * rows:(h + 1) * rows], slot, causal)
-        acc_scr[slot] += jnp.dot(p, own_ref[1], preferred_element_type=jnp.float32)
+        p = jnp.exp2(own_buf[h] * factor - mpart[slot][:, :1])
+        lpart[slot] += p
+        acc_scr[slot] += jnp.dot(p.astype(jnp.bfloat16), own_ref[1],
+                                 preferred_element_type=jnp.float32)
 
     stats = heads * HEAD_SIZE
     for b in range(blocks):
@@ -89,7 +108,8 @@
             slot = b * heads + h
             out_ref[b, :, h * HEAD_SIZE:(h + 1) * HEAD_SIZE] = acc_scr[slot]
             out_ref[b, :, stats + h:stats + h + 1] = m_scr[slot]
-            out_ref[b, :, stats + heads + h:stats + heads + h + 1] = l_scr[slot]
+            out_ref[b, :, stats + heads + h:stats + heads + h + 1] = jnp.sum(
+                lpart[slot], axis=1, keepdims=True)
 
 
 def join_kernel(got_ref, out_ref, *, sources, heads):
@@ -191,12 +211,16 @@
                 ],
                 out_specs=pl.BlockSpec((query_blocks, rows, width), lambda i, s, h: (0, 0, 0)),
                 scratch_shapes=[
+                    pltpu.VMEM((groups, slots * rows, piece), jnp.float32),
+                    pltpu.VMEM((part, rows, rows), jnp.float32),
                     pltpu.VMEM((slots * rows, piece), jnp.bfloat16),
-                    pltpu.VMEM((slots, rows, 1), jnp.float32),
+                    pltpu.VMEM((slots, rows, HEAD_SIZE), jnp.float32),
+                    pltpu.VMEM((slots, rows, HEAD_SIZE), jnp.float32),
                     pltpu.VMEM((slots, rows, 1), jnp.float32),
                     pltpu.VMEM((slots, rows, HEAD_SIZE), jnp.float32),
                 ],
             ),
+            compiler_params=pltpu.CompilerParams(vmem_limit_bytes=48 * 1024 * 1024),
             out_shape=jax.ShapeDtypeStruct((query_blocks, rows, width), jnp.float32),
             cost_estimate=pl.CostEstimate(
                 flops=4 * query_blocks * part * rows * groups * piece * HEAD_SIZE,

time: 184 us -> 168 us (0.913); the launches traced: 181 us -> 167 us
  Pallas kernels: 98.3 us -> 69.1 us
  waiting for transfers between devices: 34.3 us -> 51.2 us
    pallas_call x4, Pallas kernels: 89.3 us -> 60 us  [local(): pl.pallas_call(kernel, grid_spec=pltpu.PrefetchScalarGridSpec(num_scalar_...]
    all_to_all x4, waiting for transfers between devices: 11.5 us -> 27.7 us  [local(): got = lax.all_to_all(partial, 'help', 0, 0, tiled=True)]
    unnamed x22 -> x18, local copies, waits for them, and re-layouts: 5.13 us -> 5.05 us
  transfers between devices with their start and end apart: 6 -> 6, of which waited for: 2 -> 5; matrix products, arithmetic and copies ran while one was open for 4% -> 3% of each run, Pallas kernels for 41% -> 31%
where the time goes in v7:
time: 168 us; the launch traced here: 167 us
  Pallas kernels  69.1 us (41%)
  waiting for transfers between devices  51.2 us (30%)
  starting transfers between devices  20.5 us (12%)
  between operations  13.6 us (8%)
  local copies, waits for them, and re-layouts  7.13 us (4%)
  other arithmetic  5.68 us (3%)
    pallas_call x4, Pallas kernels, local(): pl.pallas_call(kernel, grid_spec=pltpu.PrefetchScalarGridSpec(num_scalar_...  60 us
    all_to_all x4, waiting for transfers between devices, local(): got = lax.all_to_all(partial, 'help', 0, 0, tiled=True)  27.7 us
    all_gather x1, waiting for transfers between devices, local(): q_all = lax.all_gather(q[None], 'help', axis=0, tiled=True)  23.4 us
    all_to_all x4, starting transfers between devices, local(): got = lax.all_to_all(partial, 'help', 0, 0, tiled=True)  16.1 us
    pallas_call x4, Pallas kernels, local(): pl.pallas_call(functools.partial(join_kernel, sources=helpers, heads=part...  9.02 us
    unnamed x18, local copies, waits for them, and re-layouts  5.05 us
    all_to_all x1, starting transfers between devices, local(): lax.all_to_all(jnp.stack([keys, values], axis=1), 'blk', 0, 0, tiled=True)  4.39 us
  transfers between devices with their start and end apart: 6, of which 5 were waited for; matrix products, arithmetic and copies ran while one was open for 3% of the time, Pallas kernels for 31%

profile of v7, /device:TPU:2, one launch (start us, length us, event | category | flops | bytes accessed | tf_op | source)
XLA Modules:
  0.0 167.1 jit_solution(6678102428348241858)
XLA Ops:
  6.5 0.0 copy-start.3
  6.5 0.0 all-gather.3.cloned.1.call-start
  6.5 0.8 convert_element_type.22
  7.4 0.1 copy.29
  7.5 0.1 convert_element_type.23
  7.6 0.1 copy.30
  7.7 1.1 copy.28
  8.9 0.9 copy.31
  9.8 0.0 all-gather.3.cloned.1.call-update
  9.8 0.0 copy-done.3
  9.8 0.6 copy.39
  10.5 0.4 fusion
  10.8 0.2 copy.43
  11.1 0.8 copy.36
  11.9 1.5 pad_maximum_fusion
  13.4 0.0 copy-start.4
  13.4 4.4 %all-to-all-start = ((bf16[8,2,4,128,128]{4,3,2,1,0:T(8,128)(2,1)}), bf16[8,2,4,128,128]{4,3,2,1,0:T(8,128)(2,1)S(1)}, u32[]{:S(2)}, u32[]{:S(2)}) async-start(bf16[8,2,4,128,128]{4,3,2,1,0:T(8,128)(2,1)} %pad_maximum_fusion), calls=%async_computation | async-start | bytes 4194304 | tf_op jit(solution)/shard_map/all_to_all | solution.py:169
  17.8 0.0 copy-done.4
  17.8 0.1 copy.40
  17.9 0.1 constant_dynamic-slice_fusion
  18.1 0.1 copy.35
  18.2 23.4 %all-gather.3.cloned.1.call-done = bf16[36,128,128]{2,1,0:T(8,128)(2,1)} async-done(((bf16[9,128,128]{2,1,0:T(8,128)(2,1)}), bf16[36,128,128]{2,1,0:T(8,128)(2,1)}) %all-gather.3.cloned.1.call-update) | async-done | bytes 1179664 | tf_op jit(solution)/shard_map/all_gather | solution.py:175
  41.7 0.7 slice_convert_fusion
  42.4 0.1 reshape.28
  42.5 0.7 compare_reduce_fusion
  43.2 0.1 reshape.29.sel_ref
  43.3 0.0 all-to-all-done.kv_ref
  43.3 0.0 copy-start
  43.3 1.3 copy-done
  44.6 0.0 copy-start.1
  44.6 15.1 %shard_map.52 = f32[4,128,384]{2,1,0:T(8,128)} custom-call(s32[256]{0:T(256)S(1)} %reshape.29.sel_ref, s32[1]{0:T(128)} %bitcast.4.home_ref, bf16[4,9,128,128]{3,2,1,0:T(8,128)(2,1)S(1)} %bitcast.37, bf16[8,2,4,128,128]{4,3,2,1,0:T(8,128)(2,1)S(1)} %all-to-all-done.kv_ref, bf16[2,128,128]{2,1,0:T(8,128)(2,1)S(1)} %pad_maximum_fusion.3.own_ref), custom_call_target="tpu_custom_call" | custom-call | flops 2147483648 | bytes 2883584 | tf_op jit(solution)/shard_map/pallas_call | solution.py:200
  59.7 4.2 %all-to-all-start.4 = ((f32[4,128,384]{2,1,0:T(8,128)}), f32[4,128,384]{2,1,0:T(8,128)}, u32[]{:S(2)}, u32[]{:S(2)}) async-start(f32[4,128,384]{2,1,0:T(8,128)} %shard_map.52), calls=%async_computation.4 | async-start | bytes 1572864 | tf_op jit(solution)/shard_map/all_to_all | solution.py:230
  63.9 0.0 copy-done.1
  63.9 14.9 %shard_map.50 = f32[4,128,384]{2,1,0:T(8,128)} custom-call(s32[256]{0:T(256)S(1)} %reshape.29.sel_ref, s32[1]{0:T(128)} %bitcast.4.home_ref, bf16[4,9,128,128]{3,2,1,0:T(8,128)(2,1)S(1)} %bitcast.38, bf16[8,2,4,128,128]{4,3,2,1,0:T(8,128)(2,1)S(1)} %all-to-all-done.kv_ref, bf16[2,128,128]{2,1,0:T(8,128)(2,1)S(1)} %pad_maximum_fusion.3.own_ref), custom_call_target="tpu_custom_call" | custom-call | flops 2147483648 | bytes 2883584 | tf_op jit(solution)/shard_map/pallas_call | solution.py:200
  78.8 5.6 %all-to-all-done.4.got_ref = f32[4,128,384]{2,1,0:T(8,128)} async-done(((f32[4,128,384]{2,1,0:T(8,128)}), f32[4,128,384]{2,1,0:T(8,128)}, u32[]{:S(2)}, u32[]{:S(2)}) %all-to-all-start.4) | async-done | bytes 786464 | tf_op jit(solution)/shard_map/all_to_all | solution.py:230
  84.4 4.2 %all-to-all-start.3 = ((f32[4,128,384]{2,1,0:T(8,128)}), f32[4,128,384]{2,1,0:T(8,128)}, u32[]{:S(2)}, u32[]{:S(2)}) async-start(f32[4,128,384]{2,1,0:T(8,128)} %shard_map.50), calls=%async_computation.3 | async-start | bytes 1572864 | tf_op jit(solution)/shard_map/all_to_all | solution.py:230
  88.6 14.7 %shard_map.48 = f32[4,128,384]{2,1,0:T(8,128)} custom-call(s32[256]{0:T(256)S(1)} %reshape.29.sel_ref, s32[1]{0:T(128)} %bitcast.4.home_ref, bf16[4,9,128,128]{3,2,1,0:T(8,128)(2,1)S(1)} %bitcast.39, bf16[8,2,4,128,128]{4,3,2,1,0:T(8,128)(2,1)S(1)} %all-to-all-done.kv_ref, bf16[2,128,128]{2,1,0:T(8,128)(2,1)S(1)} %pad_maximum_fusion.3.own_ref), custom_call_target="tpu_custom_call" | custom-call | flops 2147483648 | bytes 2883584 | tf_op jit(solution)/shard_map/pallas_call | solution.py:200
  103.3 5.0 %all-to-all-done.3.got_ref = f32[4,128,384]{2,1,0:T(8,128)} async-done(((f32[4,128,384]{2,1,0:T(8,128)}), f32[4,128,384]{2,1,0:T(8,128)}, u32[]{:S(2)}, u32[]{:S(2)}) %all-to-all-start.3) | async-done | bytes 786464 | tf_op jit(solution)/shard_map/all_to_all | solution.py:230
  108.3 4.2 %all-to-all-start.2 = ((f32[4,128,384]{2,1,0:T(8,128)}), f32[4,128,384]{2,1,0:T(8,128)}, u32[]{:S(2)}, u32[]{:S(2)}) async-start(f32[4,128,384]{2,1,0:T(8,128)} %shard_map.48), calls=%async_computation.2 | async-start | bytes 1572864 | tf_op jit(solution)/shard_map/all_to_all | solution.py:230
  112.5 15.3 %shard_map.46 = f32[4,128,384]{2,1,0:T(8,128)} custom-call(s32[256]{0:T(256)S(1)} %reshape.29.sel_ref, s32[1]{0:T(128)} %bitcast.4.home_ref, bf16[4,9,128,128]{3,2,1,0:T(8,128)(2,1)S(1)} %bitcast.40, bf16[8,2,4,128,128]{4,3,2,1,0:T(8,128)(2,1)S(1)} %all-to-all-done.kv_ref, bf16[2,128,128]{2,1,0:T(8,128)(2,1)S(1)} %pad_maximum_fusion.3.own_ref), custom_call_target="tpu_custom_call" | custom-call | flops 2147483648 | bytes 2883584 | tf_op jit(solution)/shard_map/pallas_call | solution.py:200
  127.9 4.3 %all-to-all-done.2.got_ref = f32[4,128,384]{2,1,0:T(8,128)} async-done(((f32[4,128,384]{2,1,0:T(8,128)}), f32[4,128,384]{2,1,0:T(8,128)}, u32[]{:S(2)}, u32[]{:S(2)}) %all-to-all-start.2) | async-done | bytes 786464 | tf_op jit(solution)/shard_map/all_to_all | solution.py:230
  132.2 3.5 %all-to-all-start.1 = ((f32[4,128,384]{2,1,0:T(8,128)}), f32[4,128,384]{2,1,0:T(8,128)S(1)}, u32[]{:S(2)}, u32[]{:S(2)}) async-start(f32[4,128,384]{2,1,0:T(8,128)} %shard_map.46), calls=%async_computation.1 | async-start | bytes 1572864 | tf_op jit(solution)/shard_map/all_to_all | solution.py:230
  135.7 2.2 %shard_map.53 = f32[128,256]{1,0:T(8,128)} custom-call(f32[4,128,384]{2,1,0:T(8,128)} %all-to-all-done.4.got_ref), custom_call_target="tpu_custom_call" | custom-call | tf_op jit(solution)/shard_map/pallas_call | solution.py:231
  138.0 0.0 copy-start.5
  138.0 2.3 %shard_map.51 = f32[128,256]{1,0:T(8,128)} custom-call(f32[4,128,384]{2,1,0:T(8,128)} %all-to-all-done.3.got_ref), custom_call_target="tpu_custom_call" | custom-call | tf_op jit(solution)/shard_map/pallas_call | solution.py:231
  140.2 2.2 %shard_map.49 = f32[128,256]{1,0:T(8,128)} custom-call(f32[4,128,384]{2,1,0:T(8,128)} %all-to-all-done.2.got_ref), custom_call_target="tpu_custom_call" | custom-call | tf_op jit(solution)/shard_map/pallas_call | solution.py:231
  142.5 12.8 %all-to-all-done.1.got_ref = f32[4,128,384]{2,1,0:T(8,128)S(1)} async-done(((f32[4,128,384]{2,1,0:T(8,128)}), f32[4,128,384]{2,1,0:T(8,128)S(1)}, u32[]{:S(2)}, u32[]{:S(2)}) %all-to-all-start.1) | async-done | bytes 786464 | tf_op jit(solution)/shard_map/all_to_all | solution.py:230
  155.3 0.0 copy-start.2
  155.3 0.9 copy-done.2
  156.2 2.2 %shard_map.47 = f32[128,256]{1,0:T(8,128)} custom-call(f32[4,128,384]{2,1,0:T(8,128)} %copy-done.2), custom_call_target="tpu_custom_call" | custom-call | tf_op jit(solution)/shard_map/pallas_call | solution.py:231
  158.4 0.0 copy-done.5
  158.4 1.9 %pad_maximum_fusion.1 = f32[128,1024]{1,0:T(8,128)} fusion(f32[128,256]{1,0:T(8,128)S(1)} %copy-done.5, f32[128,256]{1,0:T(8,128)} %shard_map.51, f32[128,256]{1,0:T(8,128)} %shard_map.49, f32[128,256]{1,0:T(8,128)} %shard_map.47), kind=kLoop, calls=%fused_computation.2 | loop fusion | flops 393216 | bytes 1048576 | tf_op jit(solution)/shard_map/concatenate | solution.py:237
  (8 shorter events, 0.1 us)
Async XLA Ops:
  6.5 3.3 %copy-start.3 = (bf16[512,2048]{1,0:T(8,128)(2,1)S(1)}, bf16[512,2048]{1,0:T(8,128)(2,1)}, u32[]{:S(2)}) copy-start(bf16[512,2048]{1,0:T(8,128)(2,1)} %param.6) | copy-start | bytes 6291460
  6.5 35.1 %all-gather.3.cloned.1.call-start = ((), (), s32[]{:S(2)}) async-start(), calls=%async_computation.5 | async-start | bytes 1474560 | tf_op jit(solution)/shard_map/all_gather | solution.py:175
  13.4 4.4 %copy-start.4 = (bf16[128,2048]{1,0:T(8,128)(2,1)S(1)}, bf16[128,2048]{1,0:T(8,128)(2,1)}, u32[]{:S(2)}) copy-start(bf16[128,2048]{1,0:T(8,128)(2,1)} %param.5) | copy-start | bytes 1572868
  13.4 29.9 %all-to-all-start = ((bf16[8,2,4,128,128]{4,3,2,1,0:T(8,128)(2,1)}), bf16[8,2,4,128,128]{4,3,2,1,0:T(8,128)(2,1)S(1)}, u32[]{:S(2)}, u32[]{:S(2)}) async-start(bf16[8,2,4,128,128]{4,3,2,1,0:T(8,128)(2,1)} %pad_maximum_fusion), calls=%async_computation | async-start | bytes 4194304 | tf_op jit(solution)/shard_map/all_to_all | solution.py:169
  43.3 1.3 copy-start
  44.6 19.4 %copy-start.1 = (bf16[36,128,128]{2,1,0:T(8,128)(2,1)S(1)}, bf16[36,128,128]{2,1,0:T(8,128)(2,1)}, u32[]{:S(2)}) copy-start(bf16[36,128,128]{2,1,0:T(8,128)(2,1)} %all-gather.3.cloned.1.call-done) | copy-start | bytes 3538948
  59.7 24.7 %all-to-all-start.4 = ((f32[4,128,384]{2,1,0:T(8,128)}), f32[4,128,384]{2,1,0:T(8,128)}, u32[]{:S(2)}, u32[]{:S(2)}) async-start(f32[4,128,384]{2,1,0:T(8,128)} %shard_map.52), calls=%async_computation.4 | async-start | bytes 1572864 | tf_op jit(solution)/shard_map/all_to_all | solution.py:230
  84.4 23.9 %all-to-all-start.3 = ((f32[4,128,384]{2,1,0:T(8,128)}), f32[4,128,384]{2,1,0:T(8,128)}, u32[]{:S(2)}, u32[]{:S(2)}) async-start(f32[4,128,384]{2,1,0:T(8,128)} %shard_map.50), calls=%async_computation.3 | async-start | bytes 1572864 | tf_op jit(solution)/shard_map/all_to_all | solution.py:230
  108.3 23.9 %all-to-all-start.2 = ((f32[4,128,384]{2,1,0:T(8,128)}), f32[4,128,384]{2,1,0:T(8,128)}, u32[]{:S(2)}, u32[]{:S(2)}) async-start(f32[4,128,384]{2,1,0:T(8,128)} %shard_map.48), calls=%async_computation.2 | async-start | bytes 1572864 | tf_op jit(solution)/shard_map/all_to_all | solution.py:230
  132.2 23.1 %all-to-all-start.1 = ((f32[4,128,384]{2,1,0:T(8,128)}), f32[4,128,384]{2,1,0:T(8,128)S(1)}, u32[]{:S(2)}, u32[]{:S(2)}) async-start(f32[4,128,384]{2,1,0:T(8,128)} %shard_map.46), calls=%async_computation.1 | async-start | bytes 1572864 | tf_op jit(solution)/shard_map/all_to_all | solution.py:230
  138.0 20.5 %copy-start.5 = (f32[128,256]{1,0:T(8,128)S(1)}, f32[128,256]{1,0:T(8,128)}, u32[]{:S(2)}) copy-start(f32[128,256]{1,0:T(8,128)} %shard_map.53) | copy-start | bytes 393220
  155.3 0.9 copy-start.2
Sparse Core Ops, SparseCore 0:
  9.9 31.6 all-gather.2

commit v8 on v7

--- a/solution.py
+++ b/solution.py
@@ -14,10 +14,11 @@
 KEY_VALUE_HEADS = 8
 BLOCK_TOKENS = 1024
 QUERY_GROUP_ROWS = 128
+STAT_ROWS = 8
 
 
 def attend_kernel(sel_ref, home_ref, q_ref, kv_ref, own_ref, out_ref,
-                  s_buf, own_buf, p_buf, mpart, lpart, m_scr, acc_scr,
+                  s_buf, own_buf, p_buf, mpart, lpart, m_scr, acc_scr, st_scr,
                   *, groups, heads, first, all_heads, blocks, chunks, factor):
     rows = QUERY_GROUP_ROWS
     slots = blocks * heads
@@ -101,21 +102,24 @@
         acc_scr[slot] += jnp.dot(p.astype(jnp.bfloat16), own_ref[1],
                                  preferred_element_type=jnp.float32)
 
-    stats = heads * HEAD_SIZE
     for b in range(blocks):
-        out_ref[b, :, stats:] = jnp.zeros((rows, HEAD_SIZE), jnp.float32)
+        st_scr[...] = jnp.zeros(st_scr.shape, jnp.float32)
         for h in range(heads):
             slot = b * heads + h
-            out_ref[b, :, h * HEAD_SIZE:(h + 1) * HEAD_SIZE] = acc_scr[slot]
-            out_ref[b, :, stats + h:stats + h + 1] = m_scr[slot]
-            out_ref[b, :, stats + heads + h:stats + heads + h + 1] = jnp.sum(
-                lpart[slot], axis=1, keepdims=True)
-
-
-def join_kernel(got_ref, out_ref, *, sources, heads):
-    stats = heads * HEAD_SIZE
+            out_ref[b, :rows, h * HEAD_SIZE:(h + 1) * HEAD_SIZE] = acc_scr[slot]
+            st_scr[:, h:h + 1] = m_scr[slot]
+            st_scr[:, heads + h:heads + h + 1] = jnp.sum(lpart[slot], axis=1, keepdims=True)
+        out_ref[b, rows:, :HEAD_SIZE] = st_scr[...].T[:STAT_ROWS]
+        if heads > 1:
+            out_ref[b, rows:, HEAD_SIZE:] = jnp.zeros((STAT_ROWS, (heads - 1) * HEAD_SIZE), jnp.float32)
+
+
+def join_kernel(got_ref, prev_ref, out_ref, *, sources, heads):
+    rows = QUERY_GROUP_ROWS
+    del prev_ref
+    cols = [got_ref[s, rows:, :HEAD_SIZE].T for s in range(sources)]
     for h in range(heads):
-        ms = [got_ref[s, :, stats + h:stats + h + 1] for s in range(sources)]
+        ms = [c[:, h:h + 1] for c in cols]
         top = ms[0]
         for m in ms[1:]:
             top = jnp.maximum(top, m)
@@ -124,8 +128,8 @@
         acc = None
         for s in range(sources):
             fade = jnp.exp2(ms[s] - top)
-            part_total = fade * got_ref[s, :, stats + heads + h:stats + heads + h + 1]
-            part_acc = fade * got_ref[s, :, h * HEAD_SIZE:(h + 1) * HEAD_SIZE]
+            part_total = fade * cols[s][:, heads + h:heads + h + 1]
+            part_acc = fade * got_ref[s, :rows, h * HEAD_SIZE:(h + 1) * HEAD_SIZE]
             total = part_total if total is None else total + part_total
             acc = part_acc if acc is None else acc + part_acc
         out_ref[:, h * HEAD_SIZE:(h + 1) * HEAD_SIZE] = acc / total
@@ -189,9 +193,9 @@
 
     slices = min(4, heads)
     part = heads // slices
-    assert part * slices == heads and 2 * part <= HEAD_SIZE
-    width = (part + 1) * HEAD_SIZE
-    outs = []
+    assert part * slices == heads and 2 * part <= STAT_ROWS
+    width = part * HEAD_SIZE
+    result = jnp.zeros((rows, heads * HEAD_SIZE), jnp.float32)
     for c in range(slices):
         kernel = functools.partial(attend_kernel, groups=groups, heads=part, first=c * part,
                                    all_heads=heads, blocks=query_blocks, chunks=chunks,
@@ -209,7 +213,8 @@
                                  lambda i, s, h: (0, 0, 0, 0, 0)),
                     pl.BlockSpec((2, rows, HEAD_SIZE), lambda i, s, h: (0, 0, 0)),
                 ],
-                out_specs=pl.BlockSpec((query_blocks, rows, width), lambda i, s, h: (0, 0, 0)),
+                out_specs=pl.BlockSpec((query_blocks, rows + STAT_ROWS, width),
+                                       lambda i, s, h: (0, 0, 0)),
                 scratch_shapes=[
                     pltpu.VMEM((groups, slots * rows, piece), jnp.float32),
                     pltpu.VMEM((part, rows, rows), jnp.float32),
@@ -218,23 +223,27 @@
                     pltpu.VMEM((slots, rows, HEAD_SIZE), jnp.float32),
                     pltpu.VMEM((slots, rows, 1), jnp.float32),
                     pltpu.VMEM((slots, rows, HEAD_SIZE), jnp.float32),
+                    pltpu.VMEM((rows, HEAD_SIZE), jnp.float32),
                 ],
             ),
             compiler_params=pltpu.CompilerParams(vmem_limit_bytes=48 * 1024 * 1024),
-            out_shape=jax.ShapeDtypeStruct((query_blocks, rows, width), jnp.float32),
+            out_shape=jax.ShapeDtypeStruct((query_blocks, rows + STAT_ROWS, width), jnp.float32),
             cost_estimate=pl.CostEstimate(
                 flops=4 * query_blocks * part * rows * groups * piece * HEAD_SIZE,
                 transcendentals=query_blocks * part * rows * groups * piece,
                 bytes_accessed=2 * groups * 2 * piece * HEAD_SIZE + 4 * query_blocks * rows * width),
         )(sel_flat, home, q_all, held, own)
         got = lax.all_to_all(partial, "help", 0, 0, tiled=True)
-        outs.append(pl.pallas_call(
+        result = pl.pallas_call(
             functools.partial(join_kernel, sources=helpers, heads=part),
-            in_specs=[pl.BlockSpec(memory_space=pltpu.VMEM)],
-            out_specs=pl.BlockSpec(memory_space=pltpu.VMEM),
-            out_shape=jax.ShapeDtypeStruct((rows, part * HEAD_SIZE), jnp.float32),
-        )(got))
-    return jnp.concatenate(outs, axis=1)
+            grid=(1,),
+            in_specs=[pl.BlockSpec((helpers, rows + STAT_ROWS, width), lambda i: (0, 0, 0)),
+                      pl.BlockSpec(memory_space=pl.ANY)],
+            out_specs=pl.BlockSpec((rows, width), lambda i, c=c: (0, c)),
+            out_shape=jax.ShapeDtypeStruct((rows, heads * HEAD_SIZE), jnp.float32),
+            input_output_aliases={1: 0},
+        )(got, result)
+    return result
 
 
 def solution(mesh):

time: 168 us -> 149 us (0.89)
  waiting for transfers between devices: 51.2 us -> 31.5 us
  starting transfers between devices: 20.5 us -> 23.7 us
  other arithmetic: 5.68 us -> 3.66 us
  Pallas kernels: 69.1 us -> 67.4 us
    all_to_all x4, waiting for transfers between devices: 27.7 us -> 8.04 us  [local(): got = lax.all_to_all(partial, 'help', 0, 0, tiled=True)]
    all_to_all x4, starting transfers between devices: 16.1 us -> 19.3 us  [local(): got = lax.all_to_all(partial, 'help', 0, 0, tiled=True)]
    concatenate x1 -> x0, other arithmetic: 1.87 us -> none  [local(): return jnp.concatenate(outs, axis=1)]
    unnamed x18 -> x16, local copies, waits for them, and re-layouts: 5.05 us -> 5.11 us
  transfers between devices with their start and end apart: 6 -> 6, of which waited for: 5 -> 4; matrix products, arithmetic and copies ran while one was open for 3% -> 4% of each run, Pallas kernels for 31% -> 34%
where the time goes in v8:
time: 149 us; the launch traced here: 148 us
  Pallas kernels  67.4 us (45%)
  waiting for transfers between devices  31.5 us (21%)
  starting transfers between devices  23.7 us (16%)
  between operations  13.6 us (9%)
  local copies, waits for them, and re-layouts  8.04 us (5%)
  other arithmetic  3.66 us (2%)
    pallas_call x4, Pallas kernels, local(): pl.pallas_call(kernel, grid_spec=pltpu.PrefetchScalarGridSpec(num_scalar_...  58.7 us
    all_gather x1, waiting for transfers between devices, local(): q_all = lax.all_gather(q[None], 'help', axis=0, tiled=True)  23.4 us
    all_to_all x4, starting transfers between devices, local(): got = lax.all_to_all(partial, 'help', 0, 0, tiled=True)  19.3 us
    pallas_call x4, Pallas kernels, local(): pl.pallas_call(functools.partial(join_kernel, sources=helpers, heads=part...  8.73 us
    all_to_all x4, waiting for transfers between devices, local(): got = lax.all_to_all(partial, 'help', 0, 0, tiled=True)  8.04 us
    unnamed x16, local copies, waits for them, and re-layouts  5.11 us
    all_to_all x1, starting transfers between devices, local(): lax.all_to_all(jnp.stack([keys, values], axis=1), 'blk', 0, 0, tiled=True)  4.39 us
  transfers between devices with their start and end apart: 6, of which 4 were waited for; matrix products, arithmetic and copies ran while one was open for 4% of the time, Pallas kernels for 34%

profile of v8, /device:TPU:2, one launch (start us, length us, event | category | flops | bytes accessed | tf_op | source)
XLA Modules:
  0.0 147.9 jit_solution(7776455668295312188)
XLA Ops:
  6.5 0.0 copy-start.3
  6.5 0.0 all-gather.3.cloned.1.call-start
  6.5 1.3 copy.32
  7.8 0.7 convert_element_type.22
  8.5 0.1 copy.33
  8.6 0.1 convert_element_type.23
  8.7 0.1 copy.34
  8.9 0.9 copy.35
  9.8 0.0 all-gather.3.cloned.1.call-update
  9.8 0.0 copy-done.3
  9.8 0.6 copy.43
  10.5 0.4 fusion
  10.8 0.2 copy.47
  11.1 0.8 copy.40
  11.9 1.5 %pad_maximum_fusion = bf16[8,2,4,128,128]{4,3,2,1,0:T(8,128)(2,1)} fusion(bf16[8,1,4,128,128]{4,3,2,1,0:T(8,128)(2,1)S(1)} %bitcast.42, bf16[8,1,4,128,128]{4,3,2,1,0:T(8,128)(2,1)S(1)} %bitcast.43), kind=kLoop, calls=%fused_computation | loop fusion | flops 1048576 | bytes 4194304 | tf_op jit(solution)/shard_map/stack | solution.py:173
  13.4 0.0 copy-start.4
  13.4 4.4 %all-to-all-start = ((bf16[8,2,4,128,128]{4,3,2,1,0:T(8,128)(2,1)}), bf16[8,2,4,128,128]{4,3,2,1,0:T(8,128)(2,1)S(1)}, u32[]{:S(2)}, u32[]{:S(2)}) async-start(bf16[8,2,4,128,128]{4,3,2,1,0:T(8,128)(2,1)} %pad_maximum_fusion), calls=%async_computation | async-start | bytes 4194304 | tf_op jit(solution)/shard_map/all_to_all | solution.py:173
  17.8 0.0 copy-done.4
  17.8 0.1 copy.44
  17.9 0.1 constant_dynamic-slice_fusion
  18.1 0.1 copy.39
  18.3 23.4 %all-gather.3.cloned.1.call-done = bf16[36,128,128]{2,1,0:T(8,128)(2,1)} async-done(((bf16[9,128,128]{2,1,0:T(8,128)(2,1)}), bf16[36,128,128]{2,1,0:T(8,128)(2,1)}) %all-gather.3.cloned.1.call-update) | async-done | bytes 1179664 | tf_op jit(solution)/shard_map/all_gather | solution.py:179
  41.7 0.7 slice_convert_fusion
  42.4 0.1 reshape.28
  42.5 0.7 compare_reduce_fusion
  43.2 0.1 reshape.29.sel_ref
  43.3 0.0 all-to-all-done.kv_ref
  43.3 0.0 copy-start
  43.3 1.3 copy-done
  44.6 0.0 copy-start.1
  44.6 14.6 %shard_map.49 = f32[4,136,256]{2,1,0:T(8,128)} custom-call(s32[256]{0:T(256)S(1)} %reshape.29.sel_ref, s32[1]{0:T(128)} %bitcast.4.home_ref, bf16[4,9,128,128]{3,2,1,0:T(8,128)(2,1)S(1)} %bitcast.37, bf16[8,2,4,128,128]{4,3,2,1,0:T(8,128)(2,1)S(1)} %all-to-all-done.kv_ref, bf16[2,128,128]{2,1,0:T(8,128)(2,1)S(1)} %pad_maximum_fusion.2.own_ref), custom_call_target="tpu_custom_call" | custom-call | flops 2147483648 | bytes 2621440 | tf_op jit(solution)/shard_map/pallas_call | solution.py:204
  59.2 4.7 %all-to-all-start.4 = ((f32[4,136,256]{2,1,0:T(8,128)}), f32[4,136,256]{2,1,0:T(8,128)}, u32[]{:S(2)}, u32[]{:S(2)}) async-start(f32[4,136,256]{2,1,0:T(8,128)} %shard_map.49), calls=%async_computation.4 | async-start | bytes 1114112 | tf_op jit(solution)/shard_map/all_to_all | solution.py:236
  63.9 0.0 copy-done.1
  64.0 14.8 %shard_map.48 = f32[4,136,256]{2,1,0:T(8,128)} custom-call(s32[256]{0:T(256)S(1)} %reshape.29.sel_ref, s32[1]{0:T(128)} %bitcast.4.home_ref, bf16[4,9,128,128]{3,2,1,0:T(8,128)(2,1)S(1)} %bitcast.38, bf16[8,2,4,128,128]{4,3,2,1,0:T(8,128)(2,1)S(1)} %all-to-all-done.kv_ref, bf16[2,128,128]{2,1,0:T(8,128)(2,1)S(1)} %pad_maximum_fusion.2.own_ref), custom_call_target="tpu_custom_call" | custom-call | flops 2147483648 | bytes 2621440 | tf_op jit(solution)/shard_map/pallas_call | solution.py:204
  78.8 0.6 all-to-all-done.4.got_ref
  79.4 4.5 %all-to-all-start.3 = ((f32[4,136,256]{2,1,0:T(8,128)}), f32[4,136,256]{2,1,0:T(8,128)}, u32[]{:S(2)}, u32[]{:S(2)}) async-start(f32[4,136,256]{2,1,0:T(8,128)} %shard_map.48), calls=%async_computation.3 | async-start | bytes 1114112 | tf_op jit(solution)/shard_map/all_to_all | solution.py:236
  83.8 14.4 %shard_map.47 = f32[4,136,256]{2,1,0:T(8,128)} custom-call(s32[256]{0:T(256)S(1)} %reshape.29.sel_ref, s32[1]{0:T(128)} %bitcast.4.home_ref, bf16[4,9,128,128]{3,2,1,0:T(8,128)(2,1)S(1)} %bitcast.39, bf16[8,2,4,128,128]{4,3,2,1,0:T(8,128)(2,1)S(1)} %all-to-all-done.kv_ref, bf16[2,128,128]{2,1,0:T(8,128)(2,1)S(1)} %pad_maximum_fusion.2.own_ref), custom_call_target="tpu_custom_call" | custom-call | flops 2147483648 | bytes 2621440 | tf_op jit(solution)/shard_map/pallas_call | solution.py:204
  98.3 0.7 all-to-all-done.3.got_ref
  99.0 5.0 %all-to-all-start.2 = ((f32[4,136,256]{2,1,0:T(8,128)}), f32[4,136,256]{2,1,0:T(8,128)}, u32[]{:S(2)}, u32[]{:S(2)}) async-start(f32[4,136,256]{2,1,0:T(8,128)} %shard_map.47), calls=%async_computation.2 | async-start | bytes 1114112 | tf_op jit(solution)/shard_map/all_to_all | solution.py:236
  104.1 14.8 %shard_map.46 = f32[4,136,256]{2,1,0:T(8,128)} custom-call(s32[256]{0:T(256)S(1)} %reshape.29.sel_ref, s32[1]{0:T(128)} %bitcast.4.home_ref, bf16[4,9,128,128]{3,2,1,0:T(8,128)(2,1)S(1)} %bitcast.40, bf16[8,2,4,128,128]{4,3,2,1,0:T(8,128)(2,1)S(1)} %all-to-all-done.kv_ref, bf16[2,128,128]{2,1,0:T(8,128)(2,1)S(1)} %pad_maximum_fusion.2.own_ref), custom_call_target="tpu_custom_call" | custom-call | flops 2147483648 | bytes 2621440 | tf_op jit(solution)/shard_map/pallas_call | solution.py:204
  118.8 0.0 all-to-all-done.2.got_ref
  118.8 5.1 %all-to-all-start.1 = ((f32[4,136,256]{2,1,0:T(8,128)}), f32[4,136,256]{2,1,0:T(8,128)S(1)}, u32[]{:S(2)}, u32[]{:S(2)}) async-start(f32[4,136,256]{2,1,0:T(8,128)} %shard_map.46), calls=%async_computation.1 | async-start | bytes 1114112 | tf_op jit(solution)/shard_map/all_to_all | solution.py:236
  123.9 0.8 broadcast_in_dim.13.prev_ref
  124.8 2.2 %shard_map.50.prev_ref = f32[128,1024]{1,0:T(8,128)} custom-call(f32[4,136,256]{2,1,0:T(8,128)} %all-to-all-done.4.got_ref, f32[128,1024]{1,0:T(8,128)} %broadcast_in_dim.13.prev_ref), custom_call_target="tpu_custom_call", output_to_operand_aliasing={{}: (1, {})} | custom-call | tf_op jit(solution)/shard_map/pallas_call | solution.py:237
  127.0 2.2 %shard_map.51.prev_ref = f32[128,1024]{1,0:T(8,128)} custom-call(f32[4,136,256]{2,1,0:T(8,128)} %all-to-all-done.3.got_ref, f32[128,1024]{1,0:T(8,128)} %shard_map.50.prev_ref), custom_call_target="tpu_custom_call", output_to_operand_aliasing={{}: (1, {})} | custom-call | tf_op jit(solution)/shard_map/pallas_call | solution.py:237
  129.1 2.2 %shard_map.52.prev_ref = f32[128,1024]{1,0:T(8,128)} custom-call(f32[4,136,256]{2,1,0:T(8,128)} %all-to-all-done.2.got_ref, f32[128,1024]{1,0:T(8,128)} %shard_map.51.prev_ref), custom_call_target="tpu_custom_call", output_to_operand_aliasing={{}: (1, {})} | custom-call | tf_op jit(solution)/shard_map/pallas_call | solution.py:237
  131.3 6.7 %all-to-all-done.1.got_ref = f32[4,136,256]{2,1,0:T(8,128)S(1)} async-done(((f32[4,136,256]{2,1,0:T(8,128)}), f32[4,136,256]{2,1,0:T(8,128)S(1)}, u32[]{:S(2)}, u32[]{:S(2)}) %all-to-all-start.1) | async-done | bytes 557088 | tf_op jit(solution)/shard_map/all_to_all | solution.py:236
  138.0 0.0 copy-start.2
  138.0 0.8 copy-done.2
  138.8 2.2 %shard_map.53 = f32[128,1024]{1,0:T(8,128)} custom-call(f32[4,136,256]{2,1,0:T(8,128)} %copy-done.2, f32[128,1024]{1,0:T(8,128)} %shard_map.52.prev_ref), custom_call_target="tpu_custom_call", output_to_operand_aliasing={{}: (1, {})} | custom-call | tf_op jit(solution)/shard_map/pallas_call | solution.py:237
  (8 shorter events, 0.1 us)
Async XLA Ops:
  6.5 3.3 %copy-start.3 = (bf16[512,2048]{1,0:T(8,128)(2,1)S(1)}, bf16[512,2048]{1,0:T(8,128)(2,1)}, u32[]{:S(2)}) copy-start(bf16[512,2048]{1,0:T(8,128)(2,1)} %param.6) | copy-start | bytes 6291460
  6.5 35.1 %all-gather.3.cloned.1.call-start = ((), (), s32[]{:S(2)}) async-start(), calls=%async_computation.5 | async-start | bytes 1474560 | tf_op jit(solution)/shard_map/all_gather | solution.py:179
  13.4 4.4 %copy-start.4 = (bf16[128,2048]{1,0:T(8,128)(2,1)S(1)}, bf16[128,2048]{1,0:T(8,128)(2,1)}, u32[]{:S(2)}) copy-start(bf16[128,2048]{1,0:T(8,128)(2,1)} %param.5) | copy-start | bytes 1572868
  13.4 29.9 %all-to-all-start = ((bf16[8,2,4,128,128]{4,3,2,1,0:T(8,128)(2,1)}), bf16[8,2,4,128,128]{4,3,2,1,0:T(8,128)(2,1)S(1)}, u32[]{:S(2)}, u32[]{:S(2)}) async-start(bf16[8,2,4,128,128]{4,3,2,1,0:T(8,128)(2,1)} %pad_maximum_fusion), calls=%async_computation | async-start | bytes 4194304 | tf_op jit(solution)/shard_map/all_to_all | solution.py:173
  43.3 1.3 copy-start
  44.6 19.4 %copy-start.1 = (bf16[36,128,128]{2,1,0:T(8,128)(2,1)S(1)}, bf16[36,128,128]{2,1,0:T(8,128)(2,1)}, u32[]{:S(2)}) copy-start(bf16[36,128,128]{2,1,0:T(8,128)(2,1)} %all-gather.3.cloned.1.call-done) | copy-start | bytes 3538948
  59.2 20.1 %all-to-all-start.4 = ((f32[4,136,256]{2,1,0:T(8,128)}), f32[4,136,256]{2,1,0:T(8,128)}, u32[]{:S(2)}, u32[]{:S(2)}) async-start(f32[4,136,256]{2,1,0:T(8,128)} %shard_map.49), calls=%async_computation.4 | async-start | bytes 1114112 | tf_op jit(solution)/shard_map/all_to_all | solution.py:236
  79.4 19.7 %all-to-all-start.3 = ((f32[4,136,256]{2,1,0:T(8,128)}), f32[4,136,256]{2,1,0:T(8,128)}, u32[]{:S(2)}, u32[]{:S(2)}) async-start(f32[4,136,256]{2,1,0:T(8,128)} %shard_map.48), calls=%async_computation.3 | async-start | bytes 1114112 | tf_op jit(solution)/shard_map/all_to_all | solution.py:236
  99.0 19.8 %all-to-all-start.2 = ((f32[4,136,256]{2,1,0:T(8,128)}), f32[4,136,256]{2,1,0:T(8,128)}, u32[]{:S(2)}, u32[]{:S(2)}) async-start(f32[4,136,256]{2,1,0:T(8,128)} %shard_map.47), calls=%async_computation.2 | async-start | bytes 1114112 | tf_op jit(solution)/shard_map/all_to_all | solution.py:236
  118.8 19.2 %all-to-all-start.1 = ((f32[4,136,256]{2,1,0:T(8,128)}), f32[4,136,256]{2,1,0:T(8,128)S(1)}, u32[]{:S(2)}, u32[]{:S(2)}) async-start(f32[4,136,256]{2,1,0:T(8,128)} %shard_map.46), calls=%async_computation.1 | async-start | bytes 1114112 | tf_op jit(solution)/shard_map/all_to_all | solution.py:236
  138.0 0.8 copy-start.2
Sparse Core Ops, SparseCore 0:
  9.9 31.6 all-gather.2

commit v9 on v8

--- a/solution.py
+++ b/solution.py
@@ -58,7 +58,7 @@
 
     causal = lax.broadcasted_iota(jnp.int32, (rows, rows), 0) >= lax.broadcasted_iota(
         jnp.int32, (rows, rows), 1)
-    s_own = jnp.dot(q_ref[home].reshape(heads * rows, HEAD_SIZE), own_ref[0],
+    s_own = jnp.dot(q_ref[home], own_ref[0],
                     preferred_element_type=jnp.float32)
     for h in range(heads):
         s_h = jnp.where(causal, s_own[h * rows:(h + 1) * rows], -jnp.inf)
@@ -114,9 +114,9 @@
             out_ref[b, rows:, HEAD_SIZE:] = jnp.zeros((STAT_ROWS, (heads - 1) * HEAD_SIZE), jnp.float32)
 
 
-def join_kernel(got_ref, prev_ref, out_ref, *, sources, heads):
+def join_kernel(got_ref, *refs, sources, heads):
     rows = QUERY_GROUP_ROWS
-    del prev_ref
+    out_ref = refs[-1]
     cols = [got_ref[s, rows:, :HEAD_SIZE].T for s in range(sources)]
     for h in range(heads):
         ms = [c[:, h:h + 1] for c in cols]
@@ -158,7 +158,7 @@
     piece = cached_key_value.shape[0]
     picks = selected.shape[1] * selected.shape[2]
     assert rows == QUERY_GROUP_ROWS and head_group % heads == 0 and selected.shape[0] == 1
-    assert BLOCK_TOKENS % piece == 0 and piece % HEAD_SIZE == 0 and picks % HEAD_SIZE == 0 and picks // HEAD_SIZE <= rows
+    assert BLOCK_TOKENS % piece == 0 and piece % HEAD_SIZE == 0 and picks % HEAD_SIZE == 0
     per_group = piece * helpers // BLOCK_TOKENS
     query_blocks = helpers
 
@@ -172,12 +172,13 @@
     values = jnp.transpose(kv[:, :, 1], (2, 0, 1, 3))
     held = lax.all_to_all(jnp.stack([keys, values], axis=1), "blk", 0, 0, tiled=True)
 
-    q = jnp.transpose(queries.reshape(rows, heads, HEAD_SIZE), (1, 0, 2))
+    q = jnp.transpose(queries.reshape(rows, heads, HEAD_SIZE), (1, 0, 2)).reshape(heads * rows, HEAD_SIZE)
     sel_rows = selected.reshape(picks // HEAD_SIZE, HEAD_SIZE).astype(jnp.bfloat16)
-    sel_rows = jnp.pad(sel_rows, ((0, rows - picks // HEAD_SIZE), (0, 0)))
-    q = jnp.concatenate([q, sel_rows[None]], axis=0)
+    sel_pad = -(-(picks // HEAD_SIZE) // 16) * 16
+    sel_rows = jnp.pad(sel_rows, ((0, sel_pad - picks // HEAD_SIZE), (0, 0)))
+    q = jnp.concatenate([q, sel_rows], axis=0)
     q_all = lax.all_gather(q[None], "help", axis=0, tiled=True)
-    sel_all = q_all[:, heads, :picks // HEAD_SIZE].astype(jnp.int32).reshape(
+    sel_all = q_all[:, heads * rows:heads * rows + picks // HEAD_SIZE].astype(jnp.int32).reshape(
         query_blocks, selected.shape[1], selected.shape[2])
 
     kv_head = (worker * heads) // head_group
@@ -195,7 +196,7 @@
     part = heads // slices
     assert part * slices == heads and 2 * part <= STAT_ROWS
     width = part * HEAD_SIZE
-    result = jnp.zeros((rows, heads * HEAD_SIZE), jnp.float32)
+    result = None
     for c in range(slices):
         kernel = functools.partial(attend_kernel, groups=groups, heads=part, first=c * part,
                                    all_heads=heads, blocks=query_blocks, chunks=chunks,
@@ -207,8 +208,8 @@
                 num_scalar_prefetch=2,
                 grid=(1,),
                 in_specs=[
-                    pl.BlockSpec((query_blocks, part, rows, HEAD_SIZE),
-                                 lambda i, s, h, c=c: (0, c, 0, 0)),
+                    pl.BlockSpec((query_blocks, part * rows, HEAD_SIZE),
+                                 lambda i, s, h, c=c: (0, c, 0)),
                     pl.BlockSpec((groups, 2, chunks, HEAD_SIZE, HEAD_SIZE),
                                  lambda i, s, h: (0, 0, 0, 0, 0)),
                     pl.BlockSpec((2, rows, HEAD_SIZE), lambda i, s, h: (0, 0, 0)),
@@ -234,15 +235,16 @@
                 bytes_accessed=2 * groups * 2 * piece * HEAD_SIZE + 4 * query_blocks * rows * width),
         )(sel_flat, home, q_all, held, own)
         got = lax.all_to_all(partial, "help", 0, 0, tiled=True)
+        first_join = c == 0
         result = pl.pallas_call(
             functools.partial(join_kernel, sources=helpers, heads=part),
             grid=(1,),
-            in_specs=[pl.BlockSpec((helpers, rows + STAT_ROWS, width), lambda i: (0, 0, 0)),
-                      pl.BlockSpec(memory_space=pl.ANY)],
+            in_specs=[pl.BlockSpec((helpers, rows + STAT_ROWS, width), lambda i: (0, 0, 0))]
+            + ([] if first_join else [pl.BlockSpec(memory_space=pl.ANY)]),
             out_specs=pl.BlockSpec((rows, width), lambda i, c=c: (0, c)),
             out_shape=jax.ShapeDtypeStruct((rows, heads * HEAD_SIZE), jnp.float32),
-            input_output_aliases={1: 0},
-        )(got, result)
+            input_output_aliases={} if first_join else {1: 0},
+        )(*((got,) if first_join else (got, result)))
     return result
 
 

time: 149 us -> 150 us (level)
  starting transfers between devices: 23.7 us -> 21.9 us
  Pallas kernels: 67.4 us -> 69.2 us
    all_gather x1, waiting for transfers between devices: 23.4 us -> 19.6 us  [local(): q_all = lax.all_gather(q[None], 'help', axis=0, tiled=True)]
    all_to_all x1, waiting for transfers between devices: 0.01 us -> 3.48 us  [local(): lax.all_to_all(jnp.stack([keys, values], axis=1), 'blk', 0, 0, tiled=True)]
    all_to_all x4, starting transfers between devices: 19.3 us -> 17.5 us  [local(): got = lax.all_to_all(partial, 'help', 0, 0, tiled=True)]
    pallas_call x4, Pallas kernels: 58.7 us -> 60.4 us  [local(): pl.pallas_call(kernel, grid_spec=pltpu.PrefetchScalarGridSpec(num_scalar_...]
    unnamed x16 -> x14, local copies, waits for them, and re-layouts: 5.11 us -> 6.4 us
  transfers between devices with their start and end apart: 6 -> 6, of which waited for: 4 -> 3; matrix products, arithmetic and copies ran while one was open for 4% -> 5% of each run, Pallas kernels for 34% -> 35%
where the time goes in v9:
time: 150 us; the launch traced here: 148 us
  Pallas kernels  69.2 us (46%)
  waiting for transfers between devices  31.6 us (21%)
  starting transfers between devices  21.9 us (15%)
  between operations  13.6 us (9%)
  local copies, waits for them, and re-layouts  7.49 us (5%)
  other arithmetic  4.35 us (3%)
    pallas_call x4, Pallas kernels, local(): pl.pallas_call(kernel, grid_spec=pltpu.PrefetchScalarGridSpec(num_scalar_...  60.4 us
    all_gather x1, waiting for transfers between devices, local(): q_all = lax.all_gather(q[None], 'help', axis=0, tiled=True)  19.6 us
    all_to_all x4, starting transfers between devices, local(): got = lax.all_to_all(partial, 'help', 0, 0, tiled=True)  17.5 us
    pallas_call x4, Pallas kernels, local(): pl.pallas_call(functools.partial(join_kernel, sources=helpers, heads=part...  8.73 us
    all_to_all x4, waiting for transfers between devices, local(): got = lax.all_to_all(partial, 'help', 0, 0, tiled=True)  8.5 us
    unnamed x14, local copies, waits for them, and re-layouts  6.4 us
    all_to_all x1, starting transfers between devices, local(): lax.all_to_all(jnp.stack([keys, values], axis=1), 'blk', 0, 0, tiled=True)  4.39 us
    all_to_all x1, waiting for transfers between devices, local(): lax.all_to_all(jnp.stack([keys, values], axis=1), 'blk', 0, 0, tiled=True)  3.48 us
  transfers between devices with their start and end apart: 6, of which 3 were waited for; matrix products, arithmetic and copies ran while one was open for 5% of the time, Pallas kernels for 35%

profile of v9, /device:TPU:2, one launch (start us, length us, event | category | flops | bytes accessed | tf_op | source)
XLA Modules:
  0.0 148.1 jit_solution(16963919804803055373)
XLA Ops:
  6.5 0.0 all-gather.3.cloned.1.call-start
  6.5 0.7 convert_element_type.16
  7.2 0.1 copy.19
  7.3 0.1 convert_element_type.17
  7.4 1.0 copy.27
  8.5 0.7 fusion.1
  9.2 0.0 all-gather.3.cloned.1.call-update
  9.2 2.2 %copy.28 = bf16[64,8,16,128]{3,2,1,0:T(8,128)(2,1)S(1)} copy(bf16[64,8,16,128]{3,1,2,0:T(8,128)(2,1)} %bitcast.44) | data formatting | bytes 4194304
  11.4 0.4 fusion.2
  11.8 0.8 copy.24
  12.6 0.2 copy.32
  12.9 1.5 %pad_maximum_fusion = bf16[8,2,4,128,128]{4,3,2,1,0:T(8,128)(2,1)} fusion(bf16[8,1,4,128,128]{4,3,2,1,0:T(8,128)(2,1)S(1)} %bitcast.43, bf16[8,1,4,128,128]{4,3,2,1,0:T(8,128)(2,1)S(1)} %bitcast.42), kind=kLoop, calls=%fused_computation | loop fusion | flops 1048576 | bytes 4194304 | tf_op jit(solution)/shard_map/stack | solution.py:173
  14.4 0.0 copy-start.3
  14.4 4.4 %all-to-all-start = ((bf16[8,2,4,128,128]{4,3,2,1,0:T(8,128)(2,1)}), bf16[8,2,4,128,128]{4,3,2,1,0:T(8,128)(2,1)S(1)}, u32[]{:S(2)}, u32[]{:S(2)}) async-start(bf16[8,2,4,128,128]{4,3,2,1,0:T(8,128)(2,1)} %pad_maximum_fusion), calls=%async_computation | async-start | bytes 4194304 | tf_op jit(solution)/shard_map/all_to_all | solution.py:173
  18.8 0.0 copy-done.3
  18.8 0.1 copy.29
  18.9 0.1 constant_dynamic-slice_fusion
  19.1 0.1 copy.23
  19.3 19.6 %all-gather.3.cloned.1.call-done = bf16[4160,128]{1,0:T(8,128)(2,1)} async-done(((bf16[1040,128]{1,0:T(8,128)(2,1)}), bf16[4160,128]{1,0:T(8,128)(2,1)}) %all-gather.3.cloned.1.call-update) | async-done | bytes 1064976 | tf_op jit(solution)/shard_map/all_gather | solution.py:180
  38.8 0.7 slice_convert_fusion
  39.5 0.1 reshape.37
  39.6 0.7 compare_reduce_fusion
  40.4 0.1 reshape.38.sel_ref
  40.4 3.5 %all-to-all-done.kv_ref = bf16[8,2,4,128,128]{4,3,2,1,0:T(8,128)(2,1)S(1)} async-done(((bf16[8,2,4,128,128]{4,3,2,1,0:T(8,128)(2,1)}), bf16[8,2,4,128,128]{4,3,2,1,0:T(8,128)(2,1)S(1)}, u32[]{:S(2)}, u32[]{:S(2)}) %all-to-all-start) | async-done | bytes 2097184 | tf_op jit(solution)/shard_map/all_to_all | solution.py:173
  43.9 0.0 copy-start
  43.9 1.2 copy-done
  45.2 0.0 copy-start.1
  45.2 14.6 %shard_map.49 = f32[4,136,256]{2,1,0:T(8,128)} custom-call(s32[256]{0:T(256)S(1)} %reshape.38.sel_ref, s32[1]{0:T(128)} %bitcast.3.home_ref, bf16[4,1040,128]{2,1,0:T(8,128)(2,1)S(1)} %bitcast.37, bf16[8,2,4,128,128]{4,3,2,1,0:T(8,128)(2,1)S(1)} %all-to-all-done.kv_ref, bf16[2,128,128]{2,1,0:T(8,128)(2,1)S(1)} %pad_maximum_fusion.1.own_ref), custom_call_target="tpu_custom_call" | custom-call | flops 2147483648 | bytes 2621440 | tf_op jit(solution)/shard_map/pallas_call | solution.py:205
  59.7 5.3 %all-to-all-start.4 = ((f32[4,136,256]{2,1,0:T(8,128)}), f32[4,136,256]{2,1,0:T(8,128)}, u32[]{:S(2)}, u32[]{:S(2)}) async-start(f32[4,136,256]{2,1,0:T(8,128)} %shard_map.49), calls=%async_computation.4 | async-start | bytes 1114112 | tf_op jit(solution)/shard_map/all_to_all | solution.py:237
  65.0 0.0 copy-done.1
  65.0 15.2 %shard_map.48 = f32[4,136,256]{2,1,0:T(8,128)} custom-call(s32[256]{0:T(256)S(1)} %reshape.38.sel_ref, s32[1]{0:T(128)} %bitcast.3.home_ref, bf16[4,1040,128]{2,1,0:T(8,128)(2,1)S(1)} %bitcast.38, bf16[8,2,4,128,128]{4,3,2,1,0:T(8,128)(2,1)S(1)} %all-to-all-done.kv_ref, bf16[2,128,128]{2,1,0:T(8,128)(2,1)S(1)} %pad_maximum_fusion.1.own_ref), custom_call_target="tpu_custom_call" | custom-call | flops 2147483648 | bytes 2621440 | tf_op jit(solution)/shard_map/pallas_call | solution.py:205
  80.3 0.0 all-to-all-done.4.got_ref
  80.3 4.2 %all-to-all-start.3 = ((f32[4,136,256]{2,1,0:T(8,128)}), f32[4,136,256]{2,1,0:T(8,128)}, u32[]{:S(2)}, u32[]{:S(2)}) async-start(f32[4,136,256]{2,1,0:T(8,128)} %shard_map.48), calls=%async_computation.3 | async-start | bytes 1114112 | tf_op jit(solution)/shard_map/all_to_all | solution.py:237
  84.5 15.2 %shard_map.47 = f32[4,136,256]{2,1,0:T(8,128)} custom-call(s32[256]{0:T(256)S(1)} %reshape.38.sel_ref, s32[1]{0:T(128)} %bitcast.3.home_ref, bf16[4,1040,128]{2,1,0:T(8,128)(2,1)S(1)} %bitcast.39, bf16[8,2,4,128,128]{4,3,2,1,0:T(8,128)(2,1)S(1)} %all-to-all-done.kv_ref, bf16[2,128,128]{2,1,0:T(8,128)(2,1)S(1)} %pad_maximum_fusion.1.own_ref), custom_call_target="tpu_custom_call" | custom-call | flops 2147483648 | bytes 2621440 | tf_op jit(solution)/shard_map/pallas_call | solution.py:205
  99.8 0.0 all-to-all-done.3.got_ref
  99.8 4.3 %all-to-all-start.2 = ((f32[4,136,256]{2,1,0:T(8,128)}), f32[4,136,256]{2,1,0:T(8,128)}, u32[]{:S(2)}, u32[]{:S(2)}) async-start(f32[4,136,256]{2,1,0:T(8,128)} %shard_map.47), calls=%async_computation.2 | async-start | bytes 1114112 | tf_op jit(solution)/shard_map/all_to_all | solution.py:237
  104.1 15.4 %shard_map.46 = f32[4,136,256]{2,1,0:T(8,128)} custom-call(s32[256]{0:T(256)S(1)} %reshape.38.sel_ref, s32[1]{0:T(128)} %bitcast.3.home_ref, bf16[4,1040,128]{2,1,0:T(8,128)(2,1)S(1)} %bitcast.40, bf16[8,2,4,128,128]{4,3,2,1,0:T(8,128)(2,1)S(1)} %all-to-all-done.kv_ref, bf16[2,128,128]{2,1,0:T(8,128)(2,1)S(1)} %pad_maximum_fusion.1.own_ref), custom_call_target="tpu_custom_call" | custom-call | flops 2147483648 | bytes 2621440 | tf_op jit(solution)/shard_map/pallas_call | solution.py:205
  119.5 0.0 all-to-all-done.2.got_ref
  119.5 3.7 %all-to-all-start.1 = ((f32[4,136,256]{2,1,0:T(8,128)}), f32[4,136,256]{2,1,0:T(8,128)S(1)}, u32[]{:S(2)}, u32[]{:S(2)}) async-start(f32[4,136,256]{2,1,0:T(8,128)} %shard_map.46), calls=%async_computation.1 | async-start | bytes 1114112 | tf_op jit(solution)/shard_map/all_to_all | solution.py:237
  123.2 2.2 %shard_map.50.refs_0_ = f32[128,1024]{1,0:T(8,128)} custom-call(f32[4,136,256]{2,1,0:T(8,128)} %all-to-all-done.4.got_ref), custom_call_target="tpu_custom_call" | custom-call | tf_op jit(solution)/shard_map/pallas_call | solution.py:239
  125.4 2.2 %shard_map.51.refs_0_ = f32[128,1024]{1,0:T(8,128)} custom-call(f32[4,136,256]{2,1,0:T(8,128)} %all-to-all-done.3.got_ref, f32[128,1024]{1,0:T(8,128)} %shard_map.50.refs_0_), custom_call_target="tpu_custom_call", output_to_operand_aliasing={{}: (1, {})} | custom-call | tf_op jit(solution)/shard_map/pallas_call | solution.py:239
  127.6 2.2 %shard_map.52.refs_0_ = f32[128,1024]{1,0:T(8,128)} custom-call(f32[4,136,256]{2,1,0:T(8,128)} %all-to-all-done.2.got_ref, f32[128,1024]{1,0:T(8,128)} %shard_map.51.refs_0_), custom_call_target="tpu_custom_call", output_to_operand_aliasing={{}: (1, {})} | custom-call | tf_op jit(solution)/shard_map/pallas_call | solution.py:239
  129.8 8.4 %all-to-all-done.1.got_ref = f32[4,136,256]{2,1,0:T(8,128)S(1)} async-done(((f32[4,136,256]{2,1,0:T(8,128)}), f32[4,136,256]{2,1,0:T(8,128)S(1)}, u32[]{:S(2)}, u32[]{:S(2)}) %all-to-all-start.1) | async-done | bytes 557088 | tf_op jit(solution)/shard_map/all_to_all | solution.py:237
  138.2 0.0 copy-start.2
  138.2 0.8 copy-done.2
  139.0 2.2 %shard_map.53 = f32[128,1024]{1,0:T(8,128)} custom-call(f32[4,136,256]{2,1,0:T(8,128)} %copy-done.2, f32[128,1024]{1,0:T(8,128)} %shard_map.52.refs_0_), custom_call_target="tpu_custom_call", output_to_operand_aliasing={{}: (1, {})} | custom-call | tf_op jit(solution)/shard_map/pallas_call | solution.py:239
  (7 shorter events, 0.1 us)
Async XLA Ops:
  6.5 32.3 %all-gather.3.cloned.1.call-start = ((), (), s32[]{:S(2)}) async-start(), calls=%async_computation.5 | async-start | bytes 1331200 | tf_op jit(solution)/shard_map/all_gather | solution.py:180
  14.4 4.4 %copy-start.3 = (bf16[128,2048]{1,0:T(8,128)(2,1)S(1)}, bf16[128,2048]{1,0:T(8,128)(2,1)}, u32[]{:S(2)}) copy-start(bf16[128,2048]{1,0:T(8,128)(2,1)} %param.5) | copy-start | bytes 1572868
  14.4 29.5 %all-to-all-start = ((bf16[8,2,4,128,128]{4,3,2,1,0:T(8,128)(2,1)}), bf16[8,2,4,128,128]{4,3,2,1,0:T(8,128)(2,1)S(1)}, u32[]{:S(2)}, u32[]{:S(2)}) async-start(bf16[8,2,4,128,128]{4,3,2,1,0:T(8,128)(2,1)} %pad_maximum_fusion), calls=%async_computation | async-start | bytes 4194304 | tf_op jit(solution)/shard_map/all_to_all | solution.py:173
  43.9 1.2 copy-start
  45.2 19.9 %copy-start.1 = (bf16[4160,128]{1,0:T(8,128)(2,1)S(1)}, bf16[4160,128]{1,0:T(8,128)(2,1)}, u32[]{:S(2)}) copy-start(bf16[4160,128]{1,0:T(8,128)(2,1)} %all-gather.3.cloned.1.call-done) | copy-start | bytes 3194884
  59.7 20.6 %all-to-all-start.4 = ((f32[4,136,256]{2,1,0:T(8,128)}), f32[4,136,256]{2,1,0:T(8,128)}, u32[]{:S(2)}, u32[]{:S(2)}) async-start(f32[4,136,256]{2,1,0:T(8,128)} %shard_map.49), calls=%async_computation.4 | async-start | bytes 1114112 | tf_op jit(solution)/shard_map/all_to_all | solution.py:237
  80.3 19.4 %all-to-all-start.3 = ((f32[4,136,256]{2,1,0:T(8,128)}), f32[4,136,256]{2,1,0:T(8,128)}, u32[]{:S(2)}, u32[]{:S(2)}) async-start(f32[4,136,256]{2,1,0:T(8,128)} %shard_map.48), calls=%async_computation.3 | async-start | bytes 1114112 | tf_op jit(solution)/shard_map/all_to_all | solution.py:237
  99.8 19.7 %all-to-all-start.2 = ((f32[4,136,256]{2,1,0:T(8,128)}), f32[4,136,256]{2,1,0:T(8,128)}, u32[]{:S(2)}, u32[]{:S(2)}) async-start(f32[4,136,256]{2,1,0:T(8,128)} %shard_map.47), calls=%async_computation.2 | async-start | bytes 1114112 | tf_op jit(solution)/shard_map/all_to_all | solution.py:237
  119.5 18.7 %all-to-all-start.1 = ((f32[4,136,256]{2,1,0:T(8,128)}), f32[4,136,256]{2,1,0:T(8,128)S(1)}, u32[]{:S(2)}, u32[]{:S(2)}) async-start(f32[4,136,256]{2,1,0:T(8,128)} %shard_map.46), calls=%async_computation.1 | async-start | bytes 1114112 | tf_op jit(solution)/shard_map/all_to_all | solution.py:237
  138.2 0.8 copy-start.2
Sparse Core Ops, SparseCore 0:
  9.3 29.4 all-gather.2

commit v10 on v9

--- a/solution.py
+++ b/solution.py
@@ -15,6 +15,16 @@
 BLOCK_TOKENS = 1024
 QUERY_GROUP_ROWS = 128
 STAT_ROWS = 8
+
+
+def relayout_kernel(x_ref, out_ref, *, wanted, chunks):
+    for t, kv_head in enumerate(wanted):
+        for c in range(chunks):
+            tokens = slice(c * HEAD_SIZE, (c + 1) * HEAD_SIZE)
+            keys = x_ref[tokens, kv_head * HEAD_SIZE:(kv_head + 1) * HEAD_SIZE]
+            out_ref[t, 0, c] = keys.astype(jnp.float32).T.astype(jnp.bfloat16)
+            column = (KEY_VALUE_HEADS + kv_head) * HEAD_SIZE
+            out_ref[t, 1, c] = x_ref[tokens, column:column + HEAD_SIZE]
 
 
 def attend_kernel(sel_ref, home_ref, q_ref, kv_ref, own_ref, out_ref,
@@ -162,15 +172,15 @@
     per_group = piece * helpers // BLOCK_TOKENS
     query_blocks = helpers
 
-    kv = cached_key_value.reshape(piece, 2, KEY_VALUE_HEADS, HEAD_SIZE)
-    wanted = np.array([(t * heads) // head_group for t in range(groups)], np.int32)
-    if not np.array_equal(wanted, np.arange(KEY_VALUE_HEADS)):
-        kv = jnp.take(kv, wanted, axis=2)
+    wanted = tuple((t * heads) // head_group for t in range(groups))
     chunks = piece // HEAD_SIZE
-    kv = kv.reshape(chunks, HEAD_SIZE, 2, groups, HEAD_SIZE)
-    keys = jnp.transpose(kv[:, :, 0], (2, 0, 3, 1))
-    values = jnp.transpose(kv[:, :, 1], (2, 0, 1, 3))
-    held = lax.all_to_all(jnp.stack([keys, values], axis=1), "blk", 0, 0, tiled=True)
+    send = pl.pallas_call(
+        functools.partial(relayout_kernel, wanted=wanted, chunks=chunks),
+        in_specs=[pl.BlockSpec(memory_space=pltpu.VMEM)],
+        out_specs=pl.BlockSpec(memory_space=pltpu.VMEM),
+        out_shape=jax.ShapeDtypeStruct((groups, 2, chunks, HEAD_SIZE, HEAD_SIZE), jnp.bfloat16),
+    )(cached_key_value)
+    held = lax.all_to_all(send, "blk", 0, 0, tiled=True)
 
     q = jnp.transpose(queries.reshape(rows, heads, HEAD_SIZE), (1, 0, 2)).reshape(heads * rows, HEAD_SIZE)
     sel_rows = selected.reshape(picks // HEAD_SIZE, HEAD_SIZE).astype(jnp.bfloat16)

time: 150 us -> 148 us (0.987)
  starting transfers between devices: 21.9 us -> 25.9 us
  local copies, waits for them, and re-layouts: 7.49 us -> 3.86 us
  waiting for transfers between devices: 31.6 us -> 29.9 us
  other arithmetic: 4.35 us -> 2.83 us
    all_to_all x4, starting transfers between devices: 17.5 us -> 21.6 us  [local(): got = lax.all_to_all(partial, 'help', 0, 0, tiled=True)]
    pallas_call x0 -> x1, Pallas kernels: none -> 3.41 us  [local(): pl.pallas_call(functools.partial(relayout_kernel, wanted=wanted, chunks=c...]
    unnamed x14 -> x11, local copies, waits for them, and re-layouts: 6.4 us -> 3.16 us
    pallas_call x4, Pallas kernels: 60.4 us -> 58 us  [local(): pl.pallas_call(kernel, grid_spec=pltpu.PrefetchScalarGridSpec(num_scalar_...]
    all_to_all x1, waiting for transfers between devices: 3.48 us -> 1.72 us  [local(): held = lax.all_to_all(send, 'blk', 0, 0, tiled=True)]
    all_gather x1, waiting for transfers between devices: 19.6 us -> 21.3 us  [local(): q_all = lax.all_gather(q[None], 'help', axis=0, tiled=True)]
    all_to_all x4, waiting for transfers between devices: 8.5 us -> 6.84 us  [local(): got = lax.all_to_all(partial, 'help', 0, 0, tiled=True)]
    another operation x1 -> x0, other arithmetic: 1.52 us -> none  [local(): jnp.stack([keys, values], axis=1)]
  transfers between devices with their start and end apart: 6 -> 6, of which waited for: 3 -> 4; matrix products, arithmetic and copies ran while one was open for 5% -> 1% of each run, Pallas kernels for 35% -> 36%
where the time goes in v10:
time: 148 us; the launch traced here: 146 us
  Pallas kernels  70.1 us (47%)
  waiting for transfers between devices  29.9 us (20%)
  starting transfers between devices  25.9 us (18%)
  between operations  13.5 us (9%)
  local copies, waits for them, and re-layouts  3.86 us (3%)
  other arithmetic  2.83 us (2%)
    pallas_call x4, Pallas kernels, local(): pl.pallas_call(kernel, grid_spec=pltpu.PrefetchScalarGridSpec(num_scalar_...  58 us
    all_to_all x4, starting transfers between devices, local(): got = lax.all_to_all(partial, 'help', 0, 0, tiled=True)  21.6 us
    all_gather x1, waiting for transfers between devices, local(): q_all = lax.all_gather(q[None], 'help', axis=0, tiled=True)  21.3 us
    pallas_call x4, Pallas kernels, local(): pl.pallas_call(functools.partial(join_kernel, sources=helpers, heads=part...  8.73 us
    all_to_all x4, waiting for transfers between devices, local(): got = lax.all_to_all(partial, 'help', 0, 0, tiled=True)  6.84 us
    all_to_all x1, starting transfers between devices, local(): held = lax.all_to_all(send, 'blk', 0, 0, tiled=True)  4.39 us
    pallas_call x1, Pallas kernels, local(): pl.pallas_call(functools.partial(relayout_kernel, wanted=wanted, chunks=c...  3.41 us
    unnamed x11, local copies, waits for them, and re-layouts  3.16 us
  transfers between devices with their start and end apart: 6, of which 4 were waited for; matrix products, arithmetic and copies ran while one was open for 1% of the time, Pallas kernels for 36%

profile of v10, /device:TPU:2, one launch (start us, length us, event | category | flops | bytes accessed | tf_op | source)
XLA Modules:
  0.0 146.2 jit_solution(7149196713212237550)
XLA Ops:
  6.5 0.0 all-gather.3.cloned.1.call-start
  6.5 0.7 convert_element_type.16
  7.2 0.1 copy.16
  7.3 0.1 convert_element_type.17
  7.4 1.0 copy.20
  8.5 0.7 fusion.1
  9.2 0.0 all-gather.3.cloned.1.call-update
  9.2 3.4 %shard_map.46 = bf16[8,2,4,128,128]{4,3,2,1,0:T(8,128)(2,1)} custom-call(bf16[512,2048]{1,0:T(8,128)(2,1)} %x_ref.1), custom_call_target="tpu_custom_call" | custom-call | tf_op jit(solution)/shard_map/pallas_call | solution.py:177
  12.6 0.0 copy-start.3
  12.6 4.4 %all-to-all-start = ((bf16[8,2,4,128,128]{4,3,2,1,0:T(8,128)(2,1)}), bf16[8,2,4,128,128]{4,3,2,1,0:T(8,128)(2,1)S(1)}, u32[]{:S(2)}, u32[]{:S(2)}) async-start(bf16[8,2,4,128,128]{4,3,2,1,0:T(8,128)(2,1)} %shard_map.46), calls=%async_computation | async-start | bytes 4194304 | tf_op jit(solution)/shard_map/all_to_all | solution.py:183
  17.0 0.0 copy-done.3
  17.0 0.1 copy.21
  17.2 0.1 constant_dynamic-slice_fusion
  17.3 0.1 copy.18
  17.5 21.3 %all-gather.3.cloned.1.call-done = bf16[4160,128]{1,0:T(8,128)(2,1)} async-done(((bf16[1040,128]{1,0:T(8,128)(2,1)}), bf16[4160,128]{1,0:T(8,128)(2,1)}) %all-gather.3.cloned.1.call-update) | async-done | bytes 1064976 | tf_op jit(solution)/shard_map/all_gather | solution.py:190
  38.8 0.7 slice_convert_fusion
  39.5 0.1 reshape.37
  39.6 0.7 compare_reduce_fusion
  40.4 0.1 reshape.38.sel_ref
  40.4 1.7 %all-to-all-done.kv_ref = bf16[8,2,4,128,128]{4,3,2,1,0:T(8,128)(2,1)S(1)} async-done(((bf16[8,2,4,128,128]{4,3,2,1,0:T(8,128)(2,1)}), bf16[8,2,4,128,128]{4,3,2,1,0:T(8,128)(2,1)S(1)}, u32[]{:S(2)}, u32[]{:S(2)}) %all-to-all-start) | async-done | bytes 2097184 | tf_op jit(solution)/shard_map/all_to_all | solution.py:183
  42.2 0.0 copy-start
  42.2 1.2 copy-done
  43.4 0.0 copy-start.1
  43.4 14.6 %shard_map.50 = f32[4,136,256]{2,1,0:T(8,128)} custom-call(s32[256]{0:T(256)S(1)} %reshape.38.sel_ref, s32[1]{0:T(128)} %bitcast.3.home_ref, bf16[4,1040,128]{2,1,0:T(8,128)(2,1)S(1)} %bitcast.22, bf16[8,2,4,128,128]{4,3,2,1,0:T(8,128)(2,1)S(1)} %all-to-all-done.kv_ref, bf16[2,128,128]{2,1,0:T(8,128)(2,1)S(1)} %pad_maximum_fusion.own_ref), custom_call_target="tpu_custom_call" | custom-call | flops 2147483648 | bytes 2621440 | tf_op jit(solution)/shard_map/pallas_call | solution.py:215
  58.0 5.1 %all-to-all-start.4 = ((f32[4,136,256]{2,1,0:T(8,128)}), f32[4,136,256]{2,1,0:T(8,128)}, u32[]{:S(2)}, u32[]{:S(2)}) async-start(f32[4,136,256]{2,1,0:T(8,128)} %shard_map.50), calls=%async_computation.4 | async-start | bytes 1114112 | tf_op jit(solution)/shard_map/all_to_all | solution.py:247
  63.2 0.0 copy-done.1
  63.2 14.3 %shard_map.49 = f32[4,136,256]{2,1,0:T(8,128)} custom-call(s32[256]{0:T(256)S(1)} %reshape.38.sel_ref, s32[1]{0:T(128)} %bitcast.3.home_ref, bf16[4,1040,128]{2,1,0:T(8,128)(2,1)S(1)} %bitcast.23, bf16[8,2,4,128,128]{4,3,2,1,0:T(8,128)(2,1)S(1)} %all-to-all-done.kv_ref, bf16[2,128,128]{2,1,0:T(8,128)(2,1)S(1)} %pad_maximum_fusion.own_ref), custom_call_target="tpu_custom_call" | custom-call | flops 2147483648 | bytes 2621440 | tf_op jit(solution)/shard_map/pallas_call | solution.py:215
  77.5 1.0 all-to-all-done.4.got_ref
  78.5 5.1 %all-to-all-start.3 = ((f32[4,136,256]{2,1,0:T(8,128)}), f32[4,136,256]{2,1,0:T(8,128)}, u32[]{:S(2)}, u32[]{:S(2)}) async-start(f32[4,136,256]{2,1,0:T(8,128)} %shard_map.49), calls=%async_computation.3 | async-start | bytes 1114112 | tf_op jit(solution)/shard_map/all_to_all | solution.py:247
  83.5 14.7 %shard_map.48 = f32[4,136,256]{2,1,0:T(8,128)} custom-call(s32[256]{0:T(256)S(1)} %reshape.38.sel_ref, s32[1]{0:T(128)} %bitcast.3.home_ref, bf16[4,1040,128]{2,1,0:T(8,128)(2,1)S(1)} %bitcast.24, bf16[8,2,4,128,128]{4,3,2,1,0:T(8,128)(2,1)S(1)} %all-to-all-done.kv_ref, bf16[2,128,128]{2,1,0:T(8,128)(2,1)S(1)} %pad_maximum_fusion.own_ref), custom_call_target="tpu_custom_call" | custom-call | flops 2147483648 | bytes 2621440 | tf_op jit(solution)/shard_map/pallas_call | solution.py:215
  98.2 0.0 all-to-all-done.3.got_ref
  98.2 5.3 %all-to-all-start.2 = ((f32[4,136,256]{2,1,0:T(8,128)}), f32[4,136,256]{2,1,0:T(8,128)}, u32[]{:S(2)}, u32[]{:S(2)}) async-start(f32[4,136,256]{2,1,0:T(8,128)} %shard_map.48), calls=%async_computation.2 | async-start | bytes 1114112 | tf_op jit(solution)/shard_map/all_to_all | solution.py:247
  103.5 14.3 %shard_map.47 = f32[4,136,256]{2,1,0:T(8,128)} custom-call(s32[256]{0:T(256)S(1)} %reshape.38.sel_ref, s32[1]{0:T(128)} %bitcast.3.home_ref, bf16[4,1040,128]{2,1,0:T(8,128)(2,1)S(1)} %bitcast.25, bf16[8,2,4,128,128]{4,3,2,1,0:T(8,128)(2,1)S(1)} %all-to-all-done.kv_ref, bf16[2,128,128]{2,1,0:T(8,128)(2,1)S(1)} %pad_maximum_fusion.own_ref), custom_call_target="tpu_custom_call" | custom-call | flops 2147483648 | bytes 2621440 | tf_op jit(solution)/shard_map/pallas_call | solution.py:215
  117.9 0.0 all-to-all-done.2.got_ref
  117.9 6.0 %all-to-all-start.1 = ((f32[4,136,256]{2,1,0:T(8,128)}), f32[4,136,256]{2,1,0:T(8,128)S(1)}, u32[]{:S(2)}, u32[]{:S(2)}) async-start(f32[4,136,256]{2,1,0:T(8,128)} %shard_map.47), calls=%async_computation.1 | async-start | bytes 1114112 | tf_op jit(solution)/shard_map/all_to_all | solution.py:247
  123.9 2.2 %shard_map.51.refs_0_ = f32[128,1024]{1,0:T(8,128)} custom-call(f32[4,136,256]{2,1,0:T(8,128)} %all-to-all-done.4.got_ref), custom_call_target="tpu_custom_call" | custom-call | tf_op jit(solution)/shard_map/pallas_call | solution.py:249
  126.1 2.2 %shard_map.52.refs_0_ = f32[128,1024]{1,0:T(8,128)} custom-call(f32[4,136,256]{2,1,0:T(8,128)} %all-to-all-done.3.got_ref, f32[128,1024]{1,0:T(8,128)} %shard_map.51.refs_0_), custom_call_target="tpu_custom_call", output_to_operand_aliasing={{}: (1, {})} | custom-call | tf_op jit(solution)/shard_map/pallas_call | solution.py:249
  128.3 2.2 %shard_map.53.refs_0_ = f32[128,1024]{1,0:T(8,128)} custom-call(f32[4,136,256]{2,1,0:T(8,128)} %all-to-all-done.2.got_ref, f32[128,1024]{1,0:T(8,128)} %shard_map.52.refs_0_), custom_call_target="tpu_custom_call", output_to_operand_aliasing={{}: (1, {})} | custom-call | tf_op jit(solution)/shard_map/pallas_call | solution.py:249
  130.5 5.9 %all-to-all-done.1.got_ref = f32[4,136,256]{2,1,0:T(8,128)S(1)} async-done(((f32[4,136,256]{2,1,0:T(8,128)}), f32[4,136,256]{2,1,0:T(8,128)S(1)}, u32[]{:S(2)}, u32[]{:S(2)}) %all-to-all-start.1) | async-done | bytes 557088 | tf_op jit(solution)/shard_map/all_to_all | solution.py:247
  136.3 0.0 copy-start.2
  136.3 0.8 copy-done.2
  137.1 2.2 %shard_map.54 = f32[128,1024]{1,0:T(8,128)} custom-call(f32[4,136,256]{2,1,0:T(8,128)} %copy-done.2, f32[128,1024]{1,0:T(8,128)} %shard_map.53.refs_0_), custom_call_target="tpu_custom_call", output_to_operand_aliasing={{}: (1, {})} | custom-call | tf_op jit(solution)/shard_map/pallas_call | solution.py:249
  (7 shorter events, 0.1 us)
Async XLA Ops:
  6.5 32.3 %all-gather.3.cloned.1.call-start = ((), (), s32[]{:S(2)}) async-start(), calls=%async_computation.5 | async-start | bytes 1331200 | tf_op jit(solution)/shard_map/all_gather | solution.py:190
  12.6 4.4 %copy-start.3 = (bf16[128,2048]{1,0:T(8,128)(2,1)S(1)}, bf16[128,2048]{1,0:T(8,128)(2,1)}, u32[]{:S(2)}) copy-start(bf16[128,2048]{1,0:T(8,128)(2,1)} %param.5) | copy-start | bytes 1572868
  12.6 29.5 %all-to-all-start = ((bf16[8,2,4,128,128]{4,3,2,1,0:T(8,128)(2,1)}), bf16[8,2,4,128,128]{4,3,2,1,0:T(8,128)(2,1)S(1)}, u32[]{:S(2)}, u32[]{:S(2)}) async-start(bf16[8,2,4,128,128]{4,3,2,1,0:T(8,128)(2,1)} %shard_map.46), calls=%async_computation | async-start | bytes 4194304 | tf_op jit(solution)/shard_map/all_to_all | solution.py:183
  42.2 1.2 copy-start
  43.4 19.8 %copy-start.1 = (bf16[4160,128]{1,0:T(8,128)(2,1)S(1)}, bf16[4160,128]{1,0:T(8,128)(2,1)}, u32[]{:S(2)}) copy-start(bf16[4160,128]{1,0:T(8,128)(2,1)} %all-gather.3.cloned.1.call-done) | copy-start | bytes 3194884
  58.0 20.4 %all-to-all-start.4 = ((f32[4,136,256]{2,1,0:T(8,128)}), f32[4,136,256]{2,1,0:T(8,128)}, u32[]{:S(2)}, u32[]{:S(2)}) async-start(f32[4,136,256]{2,1,0:T(8,128)} %shard_map.50), calls=%async_computation.4 | async-start | bytes 1114112 | tf_op jit(solution)/shard_map/all_to_all | solution.py:247
  78.5 19.7 %all-to-all-start.3 = ((f32[4,136,256]{2,1,0:T(8,128)}), f32[4,136,256]{2,1,0:T(8,128)}, u32[]{:S(2)}, u32[]{:S(2)}) async-start(f32[4,136,256]{2,1,0:T(8,128)} %shard_map.49), calls=%async_computation.3 | async-start | bytes 1114112 | tf_op jit(solution)/shard_map/all_to_all | solution.py:247
  98.2 19.7 %all-to-all-start.2 = ((f32[4,136,256]{2,1,0:T(8,128)}), f32[4,136,256]{2,1,0:T(8,128)}, u32[]{:S(2)}, u32[]{:S(2)}) async-start(f32[4,136,256]{2,1,0:T(8,128)} %shard_map.48), calls=%async_computation.2 | async-start | bytes 1114112 | tf_op jit(solution)/shard_map/all_to_all | solution.py:247
  117.9 18.4 %all-to-all-start.1 = ((f32[4,136,256]{2,1,0:T(8,128)}), f32[4,136,256]{2,1,0:T(8,128)S(1)}, u32[]{:S(2)}, u32[]{:S(2)}) async-start(f32[4,136,256]{2,1,0:T(8,128)} %shard_map.47), calls=%async_computation.1 | async-start | bytes 1114112 | tf_op jit(solution)/shard_map/all_to_all | solution.py:247
  136.3 0.8 copy-start.2
Sparse Core Ops, SparseCore 0:
  9.3 29.4 all-gather.2

commit v11 on v10

--- a/solution.py
+++ b/solution.py
@@ -56,12 +56,12 @@
             s = jnp.concatenate(
                 [jnp.dot(q, kv_ref[g, 0, c], preferred_element_type=jnp.float32)
                  for c in range(chunks)], axis=1)
-        s_buf[g] = s
         for slot in range(slots):
             @pl.when(on(slot, g))
             def _():
-                mpart[slot] = jnp.maximum(mpart[slot], fold(s[slot * rows:(slot + 1) * rows],
-                                                            jnp.maximum))
+                s_slot = s[slot * rows:(slot + 1) * rows]
+                s_buf[g, slot * rows:(slot + 1) * rows] = s_slot
+                mpart[slot] = jnp.maximum(mpart[slot], fold(s_slot, jnp.maximum))
         return carry
 
     lax.fori_loop(0, groups, score, 0)
@@ -82,7 +82,6 @@
         mpart[slot] = jnp.broadcast_to(jnp.where(m == -jnp.inf, 0.0, m), (rows, lanes))
 
     def mix(g, carry):
-        width = s_buf.shape[2]
         ons = [on(slot, g) for slot in range(slots)]
         for slot in range(slots):
             @pl.when(ons[slot])
@@ -90,10 +89,6 @@
                 p = jnp.exp2(s_buf[g, slot * rows:(slot + 1) * rows] * factor - mpart[slot][:, :1])
                 lpart[slot] += fold(p, jnp.add)
                 p_buf[slot * rows:(slot + 1) * rows] = p.astype(jnp.bfloat16)
-
-            @pl.when(jnp.logical_not(ons[slot]))
-            def _():
-                p_buf[slot * rows:(slot + 1) * rows] = jnp.zeros((rows, width), jnp.bfloat16)
 
         value = kv_ref[g, 1].reshape(chunks * HEAD_SIZE, HEAD_SIZE)
         pv = jnp.dot(p_buf[...], value, preferred_element_type=jnp.float32)

time: 148 us -> 148 us (level)
  waiting for transfers between devices: 29.9 us -> 32.5 us
    all_to_all x4, waiting for transfers between devices: 6.84 us -> 9.43 us  [local(): got = lax.all_to_all(partial, 'help', 0, 0, tiled=True)]
  transfers between devices with their start and end apart: 6 -> 6, of which waited for: 4 -> 6; matrix products, arithmetic and copies ran while one was open for 1% -> 1% of each run, Pallas kernels for 36% -> 37%
where the time goes in v11:
time: 148 us; the launch traced here: 147 us
  Pallas kernels  70 us (47%)
  waiting for transfers between devices  32.5 us (22%)
  starting transfers between devices  24.5 us (17%)
  between operations  13.5 us (9%)
  local copies, waits for them, and re-layouts  3.86 us (3%)
  other arithmetic  2.83 us (2%)
    pallas_call x4, Pallas kernels, local(): pl.pallas_call(kernel, grid_spec=pltpu.PrefetchScalarGridSpec(num_scalar_...  57.9 us
    all_gather x1, waiting for transfers between devices, local(): q_all = lax.all_gather(q[None], 'help', axis=0, tiled=True)  21.3 us
    all_to_all x4, starting transfers between devices, local(): got = lax.all_to_all(partial, 'help', 0, 0, tiled=True)  20.2 us
    all_to_all x4, waiting for transfers between devices, local(): got = lax.all_to_all(partial, 'help', 0, 0, tiled=True)  9.43 us
    pallas_call x4, Pallas kernels, local(): pl.pallas_call(functools.partial(join_kernel, sources=helpers, heads=part...  8.73 us
    all_to_all x1, starting transfers between devices, local(): held = lax.all_to_all(send, 'blk', 0, 0, tiled=True)  4.39 us
    pallas_call x1, Pallas kernels, local(): pl.pallas_call(functools.partial(relayout_kernel, wanted=wanted, chunks=c...  3.41 us
    unnamed x11, local copies, waits for them, and re-layouts  3.16 us
  transfers between devices with their start and end apart: 6, of which 6 were waited for; matrix products, arithmetic and copies ran while one was open for 1% of the time, Pallas kernels for 37%

profile of v11, /device:TPU:2, one launch (start us, length us, event | category | flops | bytes accessed | tf_op | source)
XLA Modules:
  0.0 147.3 jit_solution(4541397242927096847)
XLA Ops:
  6.5 0.0 all-gather.3.cloned.1.call-start
  6.5 0.7 convert_element_type.16
  7.2 0.1 copy.16
  7.3 0.1 convert_element_type.17
  7.4 1.0 copy.20
  8.5 0.7 fusion.1
  9.2 0.0 all-gather.3.cloned.1.call-update
  9.2 3.4 %shard_map.46 = bf16[8,2,4,128,128]{4,3,2,1,0:T(8,128)(2,1)} custom-call(bf16[512,2048]{1,0:T(8,128)(2,1)} %x_ref.1), custom_call_target="tpu_custom_call" | custom-call | tf_op jit(solution)/shard_map/pallas_call | solution.py:172
  12.6 0.0 copy-start.3
  12.6 4.4 %all-to-all-start = ((bf16[8,2,4,128,128]{4,3,2,1,0:T(8,128)(2,1)}), bf16[8,2,4,128,128]{4,3,2,1,0:T(8,128)(2,1)S(1)}, u32[]{:S(2)}, u32[]{:S(2)}) async-start(bf16[8,2,4,128,128]{4,3,2,1,0:T(8,128)(2,1)} %shard_map.46), calls=%async_computation | async-start | bytes 4194304 | tf_op jit(solution)/shard_map/all_to_all | solution.py:178
  17.0 0.0 copy-done.3
  17.0 0.1 copy.21
  17.2 0.1 constant_dynamic-slice_fusion
  17.3 0.1 copy.18
  17.5 21.3 %all-gather.3.cloned.1.call-done = bf16[4160,128]{1,0:T(8,128)(2,1)} async-done(((bf16[1040,128]{1,0:T(8,128)(2,1)}), bf16[4160,128]{1,0:T(8,128)(2,1)}) %all-gather.3.cloned.1.call-update) | async-done | bytes 1064976 | tf_op jit(solution)/shard_map/all_gather | solution.py:185
  38.8 0.7 slice_convert_fusion
  39.5 0.1 reshape.37
  39.6 0.7 compare_reduce_fusion
  40.4 0.1 reshape.38.sel_ref
  40.4 1.7 %all-to-all-done.kv_ref = bf16[8,2,4,128,128]{4,3,2,1,0:T(8,128)(2,1)S(1)} async-done(((bf16[8,2,4,128,128]{4,3,2,1,0:T(8,128)(2,1)}), bf16[8,2,4,128,128]{4,3,2,1,0:T(8,128)(2,1)S(1)}, u32[]{:S(2)}, u32[]{:S(2)}) %all-to-all-start) | async-done | bytes 2097184 | tf_op jit(solution)/shard_map/all_to_all | solution.py:178
  42.2 0.0 copy-start
  42.2 1.2 copy-done
  43.4 0.0 copy-start.1
  43.4 14.0 %shard_map.50 = f32[4,136,256]{2,1,0:T(8,128)} custom-call(s32[256]{0:T(256)S(1)} %reshape.38.sel_ref, s32[1]{0:T(128)} %bitcast.3.home_ref, bf16[4,1040,128]{2,1,0:T(8,128)(2,1)S(1)} %bitcast.22, bf16[8,2,4,128,128]{4,3,2,1,0:T(8,128)(2,1)S(1)} %all-to-all-done.kv_ref, bf16[2,128,128]{2,1,0:T(8,128)(2,1)S(1)} %pad_maximum_fusion.own_ref), custom_call_target="tpu_custom_call" | custom-call | flops 2147483648 | bytes 2621440 | tf_op jit(solution)/shard_map/pallas_call | solution.py:210
  57.4 6.2 %all-to-all-start.4 = ((f32[4,136,256]{2,1,0:T(8,128)}), f32[4,136,256]{2,1,0:T(8,128)}, u32[]{:S(2)}, u32[]{:S(2)}) async-start(f32[4,136,256]{2,1,0:T(8,128)} %shard_map.50), calls=%async_computation.4 | async-start | bytes 1114112 | tf_op jit(solution)/shard_map/all_to_all | solution.py:242
  63.6 0.0 copy-done.1
  63.6 15.2 %shard_map.49 = f32[4,136,256]{2,1,0:T(8,128)} custom-call(s32[256]{0:T(256)S(1)} %reshape.38.sel_ref, s32[1]{0:T(128)} %bitcast.3.home_ref, bf16[4,1040,128]{2,1,0:T(8,128)(2,1)S(1)} %bitcast.23, bf16[8,2,4,128,128]{4,3,2,1,0:T(8,128)(2,1)S(1)} %all-to-all-done.kv_ref, bf16[2,128,128]{2,1,0:T(8,128)(2,1)S(1)} %pad_maximum_fusion.own_ref), custom_call_target="tpu_custom_call" | custom-call | flops 2147483648 | bytes 2621440 | tf_op jit(solution)/shard_map/pallas_call | solution.py:210
  78.8 0.3 all-to-all-done.4.got_ref
  79.2 4.1 %all-to-all-start.3 = ((f32[4,136,256]{2,1,0:T(8,128)}), f32[4,136,256]{2,1,0:T(8,128)}, u32[]{:S(2)}, u32[]{:S(2)}) async-start(f32[4,136,256]{2,1,0:T(8,128)} %shard_map.49), calls=%async_computation.3 | async-start | bytes 1114112 | tf_op jit(solution)/shard_map/all_to_all | solution.py:242
  83.3 14.4 %shard_map.48 = f32[4,136,256]{2,1,0:T(8,128)} custom-call(s32[256]{0:T(256)S(1)} %reshape.38.sel_ref, s32[1]{0:T(128)} %bitcast.3.home_ref, bf16[4,1040,128]{2,1,0:T(8,128)(2,1)S(1)} %bitcast.24, bf16[8,2,4,128,128]{4,3,2,1,0:T(8,128)(2,1)S(1)} %all-to-all-done.kv_ref, bf16[2,128,128]{2,1,0:T(8,128)(2,1)S(1)} %pad_maximum_fusion.own_ref), custom_call_target="tpu_custom_call" | custom-call | flops 2147483648 | bytes 2621440 | tf_op jit(solution)/shard_map/pallas_call | solution.py:210
  97.7 1.0 all-to-all-done.3.got_ref
  98.7 4.6 %all-to-all-start.2 = ((f32[4,136,256]{2,1,0:T(8,128)}), f32[4,136,256]{2,1,0:T(8,128)}, u32[]{:S(2)}, u32[]{:S(2)}) async-start(f32[4,136,256]{2,1,0:T(8,128)} %shard_map.48), calls=%async_computation.2 | async-start | bytes 1114112 | tf_op jit(solution)/shard_map/all_to_all | solution.py:242
  103.3 14.2 %shard_map.47 = f32[4,136,256]{2,1,0:T(8,128)} custom-call(s32[256]{0:T(256)S(1)} %reshape.38.sel_ref, s32[1]{0:T(128)} %bitcast.3.home_ref, bf16[4,1040,128]{2,1,0:T(8,128)(2,1)S(1)} %bitcast.25, bf16[8,2,4,128,128]{4,3,2,1,0:T(8,128)(2,1)S(1)} %all-to-all-done.kv_ref, bf16[2,128,128]{2,1,0:T(8,128)(2,1)S(1)} %pad_maximum_fusion.own_ref), custom_call_target="tpu_custom_call" | custom-call | flops 2147483648 | bytes 2621440 | tf_op jit(solution)/shard_map/pallas_call | solution.py:210
  117.5 0.9 all-to-all-done.2.got_ref
  118.4 5.2 %all-to-all-start.1 = ((f32[4,136,256]{2,1,0:T(8,128)}), f32[4,136,256]{2,1,0:T(8,128)S(1)}, u32[]{:S(2)}, u32[]{:S(2)}) async-start(f32[4,136,256]{2,1,0:T(8,128)} %shard_map.47), calls=%async_computation.1 | async-start | bytes 1114112 | tf_op jit(solution)/shard_map/all_to_all | solution.py:242
  123.7 2.2 %shard_map.51.refs_0_ = f32[128,1024]{1,0:T(8,128)} custom-call(f32[4,136,256]{2,1,0:T(8,128)} %all-to-all-done.4.got_ref), custom_call_target="tpu_custom_call" | custom-call | tf_op jit(solution)/shard_map/pallas_call | solution.py:244
  125.8 2.2 %shard_map.52.refs_0_ = f32[128,1024]{1,0:T(8,128)} custom-call(f32[4,136,256]{2,1,0:T(8,128)} %all-to-all-done.3.got_ref, f32[128,1024]{1,0:T(8,128)} %shard_map.51.refs_0_), custom_call_target="tpu_custom_call", output_to_operand_aliasing={{}: (1, {})} | custom-call | tf_op jit(solution)/shard_map/pallas_call | solution.py:244
  128.0 2.2 %shard_map.53.refs_0_ = f32[128,1024]{1,0:T(8,128)} custom-call(f32[4,136,256]{2,1,0:T(8,128)} %all-to-all-done.2.got_ref, f32[128,1024]{1,0:T(8,128)} %shard_map.52.refs_0_), custom_call_target="tpu_custom_call", output_to_operand_aliasing={{}: (1, {})} | custom-call | tf_op jit(solution)/shard_map/pallas_call | solution.py:244
  130.2 7.2 %all-to-all-done.1.got_ref = f32[4,136,256]{2,1,0:T(8,128)S(1)} async-done(((f32[4,136,256]{2,1,0:T(8,128)}), f32[4,136,256]{2,1,0:T(8,128)S(1)}, u32[]{:S(2)}, u32[]{:S(2)}) %all-to-all-start.1) | async-done | bytes 557088 | tf_op jit(solution)/shard_map/all_to_all | solution.py:242
  137.4 0.0 copy-start.2
  137.4 0.8 copy-done.2
  138.2 2.2 %shard_map.54 = f32[128,1024]{1,0:T(8,128)} custom-call(f32[4,136,256]{2,1,0:T(8,128)} %copy-done.2, f32[128,1024]{1,0:T(8,128)} %shard_map.53.refs_0_), custom_call_target="tpu_custom_call", output_to_operand_aliasing={{}: (1, {})} | custom-call | tf_op jit(solution)/shard_map/pallas_call | solution.py:244
  (7 shorter events, 0.1 us)
Async XLA Ops:
  6.5 32.3 %all-gather.3.cloned.1.call-start = ((), (), s32[]{:S(2)}) async-start(), calls=%async_computation.5 | async-start | bytes 1331200 | tf_op jit(solution)/shard_map/all_gather | solution.py:185
  12.6 4.4 %copy-start.3 = (bf16[128,2048]{1,0:T(8,128)(2,1)S(1)}, bf16[128,2048]{1,0:T(8,128)(2,1)}, u32[]{:S(2)}) copy-start(bf16[128,2048]{1,0:T(8,128)(2,1)} %param.5) | copy-start | bytes 1572868
  12.6 29.5 %all-to-all-start = ((bf16[8,2,4,128,128]{4,3,2,1,0:T(8,128)(2,1)}), bf16[8,2,4,128,128]{4,3,2,1,0:T(8,128)(2,1)S(1)}, u32[]{:S(2)}, u32[]{:S(2)}) async-start(bf16[8,2,4,128,128]{4,3,2,1,0:T(8,128)(2,1)} %shard_map.46), calls=%async_computation | async-start | bytes 4194304 | tf_op jit(solution)/shard_map/all_to_all | solution.py:178
  42.2 1.2 copy-start
  43.4 20.2 %copy-start.1 = (bf16[4160,128]{1,0:T(8,128)(2,1)S(1)}, bf16[4160,128]{1,0:T(8,128)(2,1)}, u32[]{:S(2)}) copy-start(bf16[4160,128]{1,0:T(8,128)(2,1)} %all-gather.3.cloned.1.call-done) | copy-start | bytes 3194884
  57.4 21.7 %all-to-all-start.4 = ((f32[4,136,256]{2,1,0:T(8,128)}), f32[4,136,256]{2,1,0:T(8,128)}, u32[]{:S(2)}, u32[]{:S(2)}) async-start(f32[4,136,256]{2,1,0:T(8,128)} %shard_map.50), calls=%async_computation.4 | async-start | bytes 1114112 | tf_op jit(solution)/shard_map/all_to_all | solution.py:242
  79.2 19.5 %all-to-all-start.3 = ((f32[4,136,256]{2,1,0:T(8,128)}), f32[4,136,256]{2,1,0:T(8,128)}, u32[]{:S(2)}, u32[]{:S(2)}) async-start(f32[4,136,256]{2,1,0:T(8,128)} %shard_map.49), calls=%async_computation.3 | async-start | bytes 1114112 | tf_op jit(solution)/shard_map/all_to_all | solution.py:242
  98.7 19.8 %all-to-all-start.2 = ((f32[4,136,256]{2,1,0:T(8,128)}), f32[4,136,256]{2,1,0:T(8,128)}, u32[]{:S(2)}, u32[]{:S(2)}) async-start(f32[4,136,256]{2,1,0:T(8,128)} %shard_map.48), calls=%async_computation.2 | async-start | bytes 1114112 | tf_op jit(solution)/shard_map/all_to_all | solution.py:242
  118.4 19.0 %all-to-all-start.1 = ((f32[4,136,256]{2,1,0:T(8,128)}), f32[4,136,256]{2,1,0:T(8,128)S(1)}, u32[]{:S(2)}, u32[]{:S(2)}) async-start(f32[4,136,256]{2,1,0:T(8,128)} %shard_map.47), calls=%async_computation.1 | async-start | bytes 1114112 | tf_op jit(solution)/shard_map/all_to_all | solution.py:242
  137.4 0.8 copy-start.2
Sparse Core Ops, SparseCore 0:
  9.3 29.4 all-gather.2

commit v12 on v11

--- a/solution.py
+++ b/solution.py
@@ -50,18 +50,14 @@
         return out
 
     def score(g, carry):
-        if chunks == 1:
-            s = jnp.dot(q, kv_ref[g, 0, 0], preferred_element_type=jnp.float32)
-        else:
-            s = jnp.concatenate(
-                [jnp.dot(q, kv_ref[g, 0, c], preferred_element_type=jnp.float32)
-                 for c in range(chunks)], axis=1)
+        for c in range(chunks):
+            s_buf[g, :, c * HEAD_SIZE:(c + 1) * HEAD_SIZE] = jnp.dot(
+                q, kv_ref[g, 0, c], preferred_element_type=jnp.float32)
         for slot in range(slots):
             @pl.when(on(slot, g))
             def _():
-                s_slot = s[slot * rows:(slot + 1) * rows]
-                s_buf[g, slot * rows:(slot + 1) * rows] = s_slot
-                mpart[slot] = jnp.maximum(mpart[slot], fold(s_slot, jnp.maximum))
+                mpart[slot] = jnp.maximum(
+                    mpart[slot], fold(s_buf[g, slot * rows:(slot + 1) * rows], jnp.maximum))
         return carry
 
     lax.fori_loop(0, groups, score, 0)

time: 148 us -> 147 us (level)
  Pallas kernels: 70 us -> 68.5 us
    pallas_call x4, Pallas kernels: 57.9 us -> 56.4 us  [local(): pl.pallas_call(kernel, grid_spec=pltpu.PrefetchScalarGridSpec(num_scalar_...]
  transfers between devices with their start and end apart: 6 -> 6, of which waited for: 6 -> 5; matrix products, arithmetic and copies ran while one was open for 1% -> 1% of each run, Pallas kernels for 37% -> 36%
where the time goes in v12:
time: 147 us; the launch traced here: 146 us
  Pallas kernels  68.5 us (47%)
  waiting for transfers between devices  32.9 us (22%)
  starting transfers between devices  24.3 us (17%)
  between operations  13.5 us (9%)
  local copies, waits for them, and re-layouts  3.86 us (3%)
  other arithmetic  2.83 us (2%)
    pallas_call x4, Pallas kernels, local(): pl.pallas_call(kernel, grid_spec=pltpu.PrefetchScalarGridSpec(num_scalar_...  56.4 us
    all_gather x1, waiting for transfers between devices, local(): q_all = lax.all_gather(q[None], 'help', axis=0, tiled=True)  21.3 us
    all_to_all x4, starting transfers between devices, local(): got = lax.all_to_all(partial, 'help', 0, 0, tiled=True)  19.9 us
    all_to_all x4, waiting for transfers between devices, local(): got = lax.all_to_all(partial, 'help', 0, 0, tiled=True)  9.86 us
    pallas_call x4, Pallas kernels, local(): pl.pallas_call(functools.partial(join_kernel, sources=helpers, heads=part...  8.73 us
    all_to_all x1, starting transfers between devices, local(): held = lax.all_to_all(send, 'blk', 0, 0, tiled=True)  4.39 us
    pallas_call x1, Pallas kernels, local(): pl.pallas_call(functools.partial(relayout_kernel, wanted=wanted, chunks=c...  3.41 us
    unnamed x11, local copies, waits for them, and re-layouts  3.16 us
  transfers between devices with their start and end apart: 6, of which 5 were waited for; matrix products, arithmetic and copies ran while one was open for 1% of the time, Pallas kernels for 36%

profile of v12, /device:TPU:2, one launch (start us, length us, event | category | flops | bytes accessed | tf_op | source)
XLA Modules:
  0.0 146.0 jit_solution(2281712008255714635)
XLA Ops:
  6.5 0.0 all-gather.3.cloned.1.call-start
  6.5 0.7 convert_element_type.16
  7.2 0.1 copy.16
  7.3 0.1 convert_element_type.17
  7.4 1.0 copy.20
  8.5 0.7 fusion.1
  9.2 0.0 all-gather.3.cloned.1.call-update
  9.2 3.4 %shard_map.46 = bf16[8,2,4,128,128]{4,3,2,1,0:T(8,128)(2,1)} custom-call(bf16[512,2048]{1,0:T(8,128)(2,1)} %x_ref.1), custom_call_target="tpu_custom_call" | custom-call | tf_op jit(solution)/shard_map/pallas_call | solution.py:168
  12.6 0.0 copy-start.3
  12.6 4.4 %all-to-all-start = ((bf16[8,2,4,128,128]{4,3,2,1,0:T(8,128)(2,1)}), bf16[8,2,4,128,128]{4,3,2,1,0:T(8,128)(2,1)S(1)}, u32[]{:S(2)}, u32[]{:S(2)}) async-start(bf16[8,2,4,128,128]{4,3,2,1,0:T(8,128)(2,1)} %shard_map.46), calls=%async_computation | async-start | bytes 4194304 | tf_op jit(solution)/shard_map/all_to_all | solution.py:174
  17.0 0.0 copy-done.3
  17.0 0.1 copy.21
  17.2 0.1 constant_dynamic-slice_fusion
  17.3 0.1 copy.18
  17.5 21.3 %all-gather.3.cloned.1.call-done = bf16[4160,128]{1,0:T(8,128)(2,1)} async-done(((bf16[1040,128]{1,0:T(8,128)(2,1)}), bf16[4160,128]{1,0:T(8,128)(2,1)}) %all-gather.3.cloned.1.call-update) | async-done | bytes 1064976 | tf_op jit(solution)/shard_map/all_gather | solution.py:181
  38.8 0.7 slice_convert_fusion
  39.5 0.1 reshape.37
  39.6 0.7 compare_reduce_fusion
  40.4 0.1 reshape.38.sel_ref
  40.4 1.7 %all-to-all-done.kv_ref = bf16[8,2,4,128,128]{4,3,2,1,0:T(8,128)(2,1)S(1)} async-done(((bf16[8,2,4,128,128]{4,3,2,1,0:T(8,128)(2,1)}), bf16[8,2,4,128,128]{4,3,2,1,0:T(8,128)(2,1)S(1)}, u32[]{:S(2)}, u32[]{:S(2)}) %all-to-all-start) | async-done | bytes 2097184 | tf_op jit(solution)/shard_map/all_to_all | solution.py:174
  42.2 0.0 copy-start
  42.2 1.2 copy-done
  43.4 0.0 copy-start.1
  43.4 14.1 %shard_map.50 = f32[4,136,256]{2,1,0:T(8,128)} custom-call(s32[256]{0:T(256)S(1)} %reshape.38.sel_ref, s32[1]{0:T(128)} %bitcast.3.home_ref, bf16[4,1040,128]{2,1,0:T(8,128)(2,1)S(1)} %bitcast.22, bf16[8,2,4,128,128]{4,3,2,1,0:T(8,128)(2,1)S(1)} %all-to-all-done.kv_ref, bf16[2,128,128]{2,1,0:T(8,128)(2,1)S(1)} %pad_maximum_fusion.own_ref), custom_call_target="tpu_custom_call" | custom-call | flops 2147483648 | bytes 2621440 | tf_op jit(solution)/shard_map/pallas_call | solution.py:206
  57.5 5.3 %all-to-all-start.4 = ((f32[4,136,256]{2,1,0:T(8,128)}), f32[4,136,256]{2,1,0:T(8,128)}, u32[]{:S(2)}, u32[]{:S(2)}) async-start(f32[4,136,256]{2,1,0:T(8,128)} %shard_map.50), calls=%async_computation.4 | async-start | bytes 1114112 | tf_op jit(solution)/shard_map/all_to_all | solution.py:238
  62.9 0.0 copy-done.1
  62.9 13.7 %shard_map.49 = f32[4,136,256]{2,1,0:T(8,128)} custom-call(s32[256]{0:T(256)S(1)} %reshape.38.sel_ref, s32[1]{0:T(128)} %bitcast.3.home_ref, bf16[4,1040,128]{2,1,0:T(8,128)(2,1)S(1)} %bitcast.23, bf16[8,2,4,128,128]{4,3,2,1,0:T(8,128)(2,1)S(1)} %all-to-all-done.kv_ref, bf16[2,128,128]{2,1,0:T(8,128)(2,1)S(1)} %pad_maximum_fusion.own_ref), custom_call_target="tpu_custom_call" | custom-call | flops 2147483648 | bytes 2621440 | tf_op jit(solution)/shard_map/pallas_call | solution.py:206
  76.5 1.9 %all-to-all-done.4.got_ref = f32[4,136,256]{2,1,0:T(8,128)} async-done(((f32[4,136,256]{2,1,0:T(8,128)}), f32[4,136,256]{2,1,0:T(8,128)}, u32[]{:S(2)}, u32[]{:S(2)}) %all-to-all-start.4) | async-done | bytes 557088 | tf_op jit(solution)/shard_map/all_to_all | solution.py:238
  78.4 4.7 %all-to-all-start.3 = ((f32[4,136,256]{2,1,0:T(8,128)}), f32[4,136,256]{2,1,0:T(8,128)}, u32[]{:S(2)}, u32[]{:S(2)}) async-start(f32[4,136,256]{2,1,0:T(8,128)} %shard_map.49), calls=%async_computation.3 | async-start | bytes 1114112 | tf_op jit(solution)/shard_map/all_to_all | solution.py:238
  83.1 13.9 %shard_map.48 = f32[4,136,256]{2,1,0:T(8,128)} custom-call(s32[256]{0:T(256)S(1)} %reshape.38.sel_ref, s32[1]{0:T(128)} %bitcast.3.home_ref, bf16[4,1040,128]{2,1,0:T(8,128)(2,1)S(1)} %bitcast.24, bf16[8,2,4,128,128]{4,3,2,1,0:T(8,128)(2,1)S(1)} %all-to-all-done.kv_ref, bf16[2,128,128]{2,1,0:T(8,128)(2,1)S(1)} %pad_maximum_fusion.own_ref), custom_call_target="tpu_custom_call" | custom-call | flops 2147483648 | bytes 2621440 | tf_op jit(solution)/shard_map/pallas_call | solution.py:206
  97.0 0.6 all-to-all-done.3.got_ref
  97.6 5.5 %all-to-all-start.2 = ((f32[4,136,256]{2,1,0:T(8,128)}), f32[4,136,256]{2,1,0:T(8,128)}, u32[]{:S(2)}, u32[]{:S(2)}) async-start(f32[4,136,256]{2,1,0:T(8,128)} %shard_map.48), calls=%async_computation.2 | async-start | bytes 1114112 | tf_op jit(solution)/shard_map/all_to_all | solution.py:238
  103.1 14.7 %shard_map.47 = f32[4,136,256]{2,1,0:T(8,128)} custom-call(s32[256]{0:T(256)S(1)} %reshape.38.sel_ref, s32[1]{0:T(128)} %bitcast.3.home_ref, bf16[4,1040,128]{2,1,0:T(8,128)(2,1)S(1)} %bitcast.25, bf16[8,2,4,128,128]{4,3,2,1,0:T(8,128)(2,1)S(1)} %all-to-all-done.kv_ref, bf16[2,128,128]{2,1,0:T(8,128)(2,1)S(1)} %pad_maximum_fusion.own_ref), custom_call_target="tpu_custom_call" | custom-call | flops 2147483648 | bytes 2621440 | tf_op jit(solution)/shard_map/pallas_call | solution.py:206
  117.8 0.0 all-to-all-done.2.got_ref
  117.8 4.4 %all-to-all-start.1 = ((f32[4,136,256]{2,1,0:T(8,128)}), f32[4,136,256]{2,1,0:T(8,128)S(1)}, u32[]{:S(2)}, u32[]{:S(2)}) async-start(f32[4,136,256]{2,1,0:T(8,128)} %shard_map.47), calls=%async_computation.1 | async-start | bytes 1114112 | tf_op jit(solution)/shard_map/all_to_all | solution.py:238
  122.2 2.2 %shard_map.51.refs_0_ = f32[128,1024]{1,0:T(8,128)} custom-call(f32[4,136,256]{2,1,0:T(8,128)} %all-to-all-done.4.got_ref), custom_call_target="tpu_custom_call" | custom-call | tf_op jit(solution)/shard_map/pallas_call | solution.py:240
  124.4 2.2 %shard_map.52.refs_0_ = f32[128,1024]{1,0:T(8,128)} custom-call(f32[4,136,256]{2,1,0:T(8,128)} %all-to-all-done.3.got_ref, f32[128,1024]{1,0:T(8,128)} %shard_map.51.refs_0_), custom_call_target="tpu_custom_call", output_to_operand_aliasing={{}: (1, {})} | custom-call | tf_op jit(solution)/shard_map/pallas_call | solution.py:240
  126.6 2.2 %shard_map.53.refs_0_ = f32[128,1024]{1,0:T(8,128)} custom-call(f32[4,136,256]{2,1,0:T(8,128)} %all-to-all-done.2.got_ref, f32[128,1024]{1,0:T(8,128)} %shard_map.52.refs_0_), custom_call_target="tpu_custom_call", output_to_operand_aliasing={{}: (1, {})} | custom-call | tf_op jit(solution)/shard_map/pallas_call | solution.py:240
  128.8 7.4 %all-to-all-done.1.got_ref = f32[4,136,256]{2,1,0:T(8,128)S(1)} async-done(((f32[4,136,256]{2,1,0:T(8,128)}), f32[4,136,256]{2,1,0:T(8,128)S(1)}, u32[]{:S(2)}, u32[]{:S(2)}) %all-to-all-start.1) | async-done | bytes 557088 | tf_op jit(solution)/shard_map/all_to_all | solution.py:238
  136.1 0.0 copy-start.2
  136.1 0.8 copy-done.2
  136.9 2.2 %shard_map.54 = f32[128,1024]{1,0:T(8,128)} custom-call(f32[4,136,256]{2,1,0:T(8,128)} %copy-done.2, f32[128,1024]{1,0:T(8,128)} %shard_map.53.refs_0_), custom_call_target="tpu_custom_call", output_to_operand_aliasing={{}: (1, {})} | custom-call | tf_op jit(solution)/shard_map/pallas_call | solution.py:240
  (7 shorter events, 0.1 us)
Async XLA Ops:
  6.5 32.3 %all-gather.3.cloned.1.call-start = ((), (), s32[]{:S(2)}) async-start(), calls=%async_computation.5 | async-start | bytes 1331200 | tf_op jit(solution)/shard_map/all_gather | solution.py:181
  12.6 4.4 %copy-start.3 = (bf16[128,2048]{1,0:T(8,128)(2,1)S(1)}, bf16[128,2048]{1,0:T(8,128)(2,1)}, u32[]{:S(2)}) copy-start(bf16[128,2048]{1,0:T(8,128)(2,1)} %param.5) | copy-start | bytes 1572868
  12.6 29.5 %all-to-all-start = ((bf16[8,2,4,128,128]{4,3,2,1,0:T(8,128)(2,1)}), bf16[8,2,4,128,128]{4,3,2,1,0:T(8,128)(2,1)S(1)}, u32[]{:S(2)}, u32[]{:S(2)}) async-start(bf16[8,2,4,128,128]{4,3,2,1,0:T(8,128)(2,1)} %shard_map.46), calls=%async_computation | async-start | bytes 4194304 | tf_op jit(solution)/shard_map/all_to_all | solution.py:174
  42.2 1.2 copy-start
  43.4 19.5 %copy-start.1 = (bf16[4160,128]{1,0:T(8,128)(2,1)S(1)}, bf16[4160,128]{1,0:T(8,128)(2,1)}, u32[]{:S(2)}) copy-start(bf16[4160,128]{1,0:T(8,128)(2,1)} %all-gather.3.cloned.1.call-done) | copy-start | bytes 3194884
  57.5 20.9 %all-to-all-start.4 = ((f32[4,136,256]{2,1,0:T(8,128)}), f32[4,136,256]{2,1,0:T(8,128)}, u32[]{:S(2)}, u32[]{:S(2)}) async-start(f32[4,136,256]{2,1,0:T(8,128)} %shard_map.50), calls=%async_computation.4 | async-start | bytes 1114112 | tf_op jit(solution)/shard_map/all_to_all | solution.py:238
  78.4 19.1 %all-to-all-start.3 = ((f32[4,136,256]{2,1,0:T(8,128)}), f32[4,136,256]{2,1,0:T(8,128)}, u32[]{:S(2)}, u32[]{:S(2)}) async-start(f32[4,136,256]{2,1,0:T(8,128)} %shard_map.49), calls=%async_computation.3 | async-start | bytes 1114112 | tf_op jit(solution)/shard_map/all_to_all | solution.py:238
  97.6 20.3 %all-to-all-start.2 = ((f32[4,136,256]{2,1,0:T(8,128)}), f32[4,136,256]{2,1,0:T(8,128)}, u32[]{:S(2)}, u32[]{:S(2)}) async-start(f32[4,136,256]{2,1,0:T(8,128)} %shard_map.48), calls=%async_computation.2 | async-start | bytes 1114112 | tf_op jit(solution)/shard_map/all_to_all | solution.py:238
  117.8 18.3 %all-to-all-start.1 = ((f32[4,136,256]{2,1,0:T(8,128)}), f32[4,136,256]{2,1,0:T(8,128)S(1)}, u32[]{:S(2)}, u32[]{:S(2)}) async-start(f32[4,136,256]{2,1,0:T(8,128)} %shard_map.47), calls=%async_computation.1 | async-start | bytes 1114112 | tf_op jit(solution)/shard_map/all_to_all | solution.py:238
  136.1 0.8 copy-start.2
Sparse Core Ops, SparseCore 0:
  9.3 29.4 all-gather.2

commit v13 on v12

--- a/solution.py
+++ b/solution.py
@@ -60,7 +60,7 @@
                     mpart[slot], fold(s_buf[g, slot * rows:(slot + 1) * rows], jnp.maximum))
         return carry
 
-    lax.fori_loop(0, groups, score, 0)
+    lax.fori_loop(0, groups, score, 0, unroll=2)
 
     causal = lax.broadcasted_iota(jnp.int32, (rows, rows), 0) >= lax.broadcasted_iota(
         jnp.int32, (rows, rows), 1)
@@ -94,7 +94,7 @@
                 acc_scr[slot] += pv[slot * rows:(slot + 1) * rows]
         return carry
 
-    lax.fori_loop(0, groups, mix, 0)
+    lax.fori_loop(0, groups, mix, 0, unroll=2)
 
     for h in range(heads):
         slot = home * heads + h

time: 147 us -> 154 us (1.048)
  Pallas kernels: 68.5 us -> 76.8 us
  waiting for transfers between devices: 32.9 us -> 30.5 us
  starting transfers between devices: 24.3 us -> 26.2 us
    pallas_call x4, Pallas kernels: 56.4 us -> 64.7 us  [local(): pl.pallas_call(kernel, grid_spec=pltpu.PrefetchScalarGridSpec(num_scalar_...]
    all_to_all x4, waiting for transfers between devices: 9.86 us -> 7.4 us  [local(): got = lax.all_to_all(partial, 'help', 0, 0, tiled=True)]
    all_to_all x4, starting transfers between devices: 19.9 us -> 21.9 us  [local(): got = lax.all_to_all(partial, 'help', 0, 0, tiled=True)]
  transfers between devices with their start and end apart: 6 -> 6, of which waited for: 5 -> 3; matrix products, arithmetic and copies ran while one was open for 1% -> 1% of each run, Pallas kernels for 36% -> 38%
where the time goes in v13:
time: 154 us
  Pallas kernels  76.8 us (50%)
  waiting for transfers between devices  30.5 us (20%)
  starting transfers between devices  26.2 us (17%)
  between operations  13.5 us (9%)
  local copies, waits for them, and re-layouts  3.86 us (3%)
  other arithmetic  2.83 us (2%)
    pallas_call x4, Pallas kernels, local(): pl.pallas_call(kernel, grid_spec=pltpu.PrefetchScalarGridSpec(num_scalar_...  64.7 us
    all_to_all x4, starting transfers between devices, local(): got = lax.all_to_all(partial, 'help', 0, 0, tiled=True)  21.9 us
    all_gather x1, waiting for transfers between devices, local(): q_all = lax.all_gather(q[None], 'help', axis=0, tiled=True)  21.3 us
    pallas_call x4, Pallas kernels, local(): pl.pallas_call(functools.partial(join_kernel, sources=helpers, heads=part...  8.73 us
    all_to_all x4, waiting for transfers between devices, local(): got = lax.all_to_all(partial, 'help', 0, 0, tiled=True)  7.4 us
    all_to_all x1, starting transfers between devices, local(): held = lax.all_to_all(send, 'blk', 0, 0, tiled=True)  4.39 us
    pallas_call x1, Pallas kernels, local(): pl.pallas_call(functools.partial(relayout_kernel, wanted=wanted, chunks=c...  3.41 us
    unnamed x11, local copies, waits for them, and re-layouts  3.16 us
  transfers between devices with their start and end apart: 6, of which 3 were waited for; matrix products, arithmetic and copies ran while one was open for 1% of the time, Pallas kernels for 38%

profile of v13, /device:TPU:2, one launch (start us, length us, event | category | flops | bytes accessed | tf_op | source)
XLA Modules:
  0.0 153.7 jit_solution(9113104317066630157)
XLA Ops:
  6.5 0.0 all-gather.3.cloned.1.call-start
  6.5 0.7 convert_element_type.16
  7.2 0.1 copy.16
  7.3 0.1 convert_element_type.17
  7.4 1.0 copy.20
  8.5 0.7 fusion.1
  9.2 0.0 all-gather.3.cloned.1.call-update
  9.2 3.4 %shard_map.46 = bf16[8,2,4,128,128]{4,3,2,1,0:T(8,128)(2,1)} custom-call(bf16[512,2048]{1,0:T(8,128)(2,1)} %x_ref.1), custom_call_target="tpu_custom_call" | custom-call | tf_op jit(solution)/shard_map/pallas_call | solution.py:168
  12.6 0.0 copy-start.3
  12.6 4.4 %all-to-all-start = ((bf16[8,2,4,128,128]{4,3,2,1,0:T(8,128)(2,1)}), bf16[8,2,4,128,128]{4,3,2,1,0:T(8,128)(2,1)S(1)}, u32[]{:S(2)}, u32[]{:S(2)}) async-start(bf16[8,2,4,128,128]{4,3,2,1,0:T(8,128)(2,1)} %shard_map.46), calls=%async_computation | async-start | bytes 4194304 | tf_op jit(solution)/shard_map/all_to_all | solution.py:174
  17.0 0.0 copy-done.3
  17.0 0.1 copy.21
  17.2 0.1 constant_dynamic-slice_fusion
  17.3 0.1 copy.18
  17.5 21.3 %all-gather.3.cloned.1.call-done = bf16[4160,128]{1,0:T(8,128)(2,1)} async-done(((bf16[1040,128]{1,0:T(8,128)(2,1)}), bf16[4160,128]{1,0:T(8,128)(2,1)}) %all-gather.3.cloned.1.call-update) | async-done | bytes 1064976 | tf_op jit(solution)/shard_map/all_gather | solution.py:181
  38.8 0.7 slice_convert_fusion
  39.5 0.1 reshape.37
  39.6 0.7 compare_reduce_fusion
  40.4 0.1 reshape.38.sel_ref
  40.4 1.7 %all-to-all-done.kv_ref = bf16[8,2,4,128,128]{4,3,2,1,0:T(8,128)(2,1)S(1)} async-done(((bf16[8,2,4,128,128]{4,3,2,1,0:T(8,128)(2,1)}), bf16[8,2,4,128,128]{4,3,2,1,0:T(8,128)(2,1)S(1)}, u32[]{:S(2)}, u32[]{:S(2)}) %all-to-all-start) | async-done | bytes 2097184 | tf_op jit(solution)/shard_map/all_to_all | solution.py:174
  42.2 0.0 copy-start
  42.2 1.2 copy-done
  43.4 0.0 copy-start.1
  43.4 15.5 %shard_map.50 = f32[4,136,256]{2,1,0:T(8,128)} custom-call(s32[256]{0:T(256)S(1)} %reshape.38.sel_ref, s32[1]{0:T(128)} %bitcast.3.home_ref, bf16[4,1040,128]{2,1,0:T(8,128)(2,1)S(1)} %bitcast.22, bf16[8,2,4,128,128]{4,3,2,1,0:T(8,128)(2,1)S(1)} %all-to-all-done.kv_ref, bf16[2,128,128]{2,1,0:T(8,128)(2,1)S(1)} %pad_maximum_fusion.own_ref), custom_call_target="tpu_custom_call" | custom-call | flops 2147483648 | bytes 2621440 | tf_op jit(solution)/shard_map/pallas_call | solution.py:206
  58.9 6.6 %all-to-all-start.4 = ((f32[4,136,256]{2,1,0:T(8,128)}), f32[4,136,256]{2,1,0:T(8,128)}, u32[]{:S(2)}, u32[]{:S(2)}) async-start(f32[4,136,256]{2,1,0:T(8,128)} %shard_map.50), calls=%async_computation.4 | async-start | bytes 1114112 | tf_op jit(solution)/shard_map/all_to_all | solution.py:238
  65.5 0.0 copy-done.1
  65.5 16.5 %shard_map.49 = f32[4,136,256]{2,1,0:T(8,128)} custom-call(s32[256]{0:T(256)S(1)} %reshape.38.sel_ref, s32[1]{0:T(128)} %bitcast.3.home_ref, bf16[4,1040,128]{2,1,0:T(8,128)(2,1)S(1)} %bitcast.23, bf16[8,2,4,128,128]{4,3,2,1,0:T(8,128)(2,1)S(1)} %all-to-all-done.kv_ref, bf16[2,128,128]{2,1,0:T(8,128)(2,1)S(1)} %pad_maximum_fusion.own_ref), custom_call_target="tpu_custom_call" | custom-call | flops 2147483648 | bytes 2621440 | tf_op jit(solution)/shard_map/pallas_call | solution.py:206
  82.0 0.0 all-to-all-done.4.got_ref
  82.0 4.8 %all-to-all-start.3 = ((f32[4,136,256]{2,1,0:T(8,128)}), f32[4,136,256]{2,1,0:T(8,128)}, u32[]{:S(2)}, u32[]{:S(2)}) async-start(f32[4,136,256]{2,1,0:T(8,128)} %shard_map.49), calls=%async_computation.3 | async-start | bytes 1114112 | tf_op jit(solution)/shard_map/all_to_all | solution.py:238
  86.9 16.5 %shard_map.48 = f32[4,136,256]{2,1,0:T(8,128)} custom-call(s32[256]{0:T(256)S(1)} %reshape.38.sel_ref, s32[1]{0:T(128)} %bitcast.3.home_ref, bf16[4,1040,128]{2,1,0:T(8,128)(2,1)S(1)} %bitcast.24, bf16[8,2,4,128,128]{4,3,2,1,0:T(8,128)(2,1)S(1)} %all-to-all-done.kv_ref, bf16[2,128,128]{2,1,0:T(8,128)(2,1)S(1)} %pad_maximum_fusion.own_ref), custom_call_target="tpu_custom_call" | custom-call | flops 2147483648 | bytes 2621440 | tf_op jit(solution)/shard_map/pallas_call | solution.py:206
  103.4 0.0 all-to-all-done.3.got_ref
  103.4 4.8 %all-to-all-start.2 = ((f32[4,136,256]{2,1,0:T(8,128)}), f32[4,136,256]{2,1,0:T(8,128)}, u32[]{:S(2)}, u32[]{:S(2)}) async-start(f32[4,136,256]{2,1,0:T(8,128)} %shard_map.48), calls=%async_computation.2 | async-start | bytes 1114112 | tf_op jit(solution)/shard_map/all_to_all | solution.py:238
  108.2 16.2 %shard_map.47 = f32[4,136,256]{2,1,0:T(8,128)} custom-call(s32[256]{0:T(256)S(1)} %reshape.38.sel_ref, s32[1]{0:T(128)} %bitcast.3.home_ref, bf16[4,1040,128]{2,1,0:T(8,128)(2,1)S(1)} %bitcast.25, bf16[8,2,4,128,128]{4,3,2,1,0:T(8,128)(2,1)S(1)} %all-to-all-done.kv_ref, bf16[2,128,128]{2,1,0:T(8,128)(2,1)S(1)} %pad_maximum_fusion.own_ref), custom_call_target="tpu_custom_call" | custom-call | flops 2147483648 | bytes 2621440 | tf_op jit(solution)/shard_map/pallas_call | solution.py:206
  124.3 0.0 all-to-all-done.2.got_ref
  124.3 5.6 %all-to-all-start.1 = ((f32[4,136,256]{2,1,0:T(8,128)}), f32[4,136,256]{2,1,0:T(8,128)S(1)}, u32[]{:S(2)}, u32[]{:S(2)}) async-start(f32[4,136,256]{2,1,0:T(8,128)} %shard_map.47), calls=%async_computation.1 | async-start | bytes 1114112 | tf_op jit(solution)/shard_map/all_to_all | solution.py:238
  129.9 2.2 %shard_map.51.refs_0_ = f32[128,1024]{1,0:T(8,128)} custom-call(f32[4,136,256]{2,1,0:T(8,128)} %all-to-all-done.4.got_ref), custom_call_target="tpu_custom_call" | custom-call | tf_op jit(solution)/shard_map/pallas_call | solution.py:240
  132.1 2.2 %shard_map.52.refs_0_ = f32[128,1024]{1,0:T(8,128)} custom-call(f32[4,136,256]{2,1,0:T(8,128)} %all-to-all-done.3.got_ref, f32[128,1024]{1,0:T(8,128)} %shard_map.51.refs_0_), custom_call_target="tpu_custom_call", output_to_operand_aliasing={{}: (1, {})} | custom-call | tf_op jit(solution)/shard_map/pallas_call | solution.py:240
  134.3 2.2 %shard_map.53.refs_0_ = f32[128,1024]{1,0:T(8,128)} custom-call(f32[4,136,256]{2,1,0:T(8,128)} %all-to-all-done.2.got_ref, f32[128,1024]{1,0:T(8,128)} %shard_map.52.refs_0_), custom_call_target="tpu_custom_call", output_to_operand_aliasing={{}: (1, {})} | custom-call | tf_op jit(solution)/shard_map/pallas_call | solution.py:240
  136.5 7.4 %all-to-all-done.1.got_ref = f32[4,136,256]{2,1,0:T(8,128)S(1)} async-done(((f32[4,136,256]{2,1,0:T(8,128)}), f32[4,136,256]{2,1,0:T(8,128)S(1)}, u32[]{:S(2)}, u32[]{:S(2)}) %all-to-all-start.1) | async-done | bytes 557088 | tf_op jit(solution)/shard_map/all_to_all | solution.py:238
  143.9 0.0 copy-start.2
  143.9 0.8 copy-done.2
  144.7 2.2 %shard_map.54 = f32[128,1024]{1,0:T(8,128)} custom-call(f32[4,136,256]{2,1,0:T(8,128)} %copy-done.2, f32[128,1024]{1,0:T(8,128)} %shard_map.53.refs_0_), custom_call_target="tpu_custom_call", output_to_operand_aliasing={{}: (1, {})} | custom-call | tf_op jit(solution)/shard_map/pallas_call | solution.py:240
  (7 shorter events, 0.1 us)
Async XLA Ops:
  6.5 32.3 %all-gather.3.cloned.1.call-start = ((), (), s32[]{:S(2)}) async-start(), calls=%async_computation.5 | async-start | bytes 1331200 | tf_op jit(solution)/shard_map/all_gather | solution.py:181
  12.6 4.4 %copy-start.3 = (bf16[128,2048]{1,0:T(8,128)(2,1)S(1)}, bf16[128,2048]{1,0:T(8,128)(2,1)}, u32[]{:S(2)}) copy-start(bf16[128,2048]{1,0:T(8,128)(2,1)} %param.5) | copy-start | bytes 1572868
  12.6 29.5 %all-to-all-start = ((bf16[8,2,4,128,128]{4,3,2,1,0:T(8,128)(2,1)}), bf16[8,2,4,128,128]{4,3,2,1,0:T(8,128)(2,1)S(1)}, u32[]{:S(2)}, u32[]{:S(2)}) async-start(bf16[8,2,4,128,128]{4,3,2,1,0:T(8,128)(2,1)} %shard_map.46), calls=%async_computation | async-start | bytes 4194304 | tf_op jit(solution)/shard_map/all_to_all | solution.py:174
  42.2 1.2 copy-start
  43.4 22.1 %copy-start.1 = (bf16[4160,128]{1,0:T(8,128)(2,1)S(1)}, bf16[4160,128]{1,0:T(8,128)(2,1)}, u32[]{:S(2)}) copy-start(bf16[4160,128]{1,0:T(8,128)(2,1)} %all-gather.3.cloned.1.call-done) | copy-start | bytes 3194884
  58.9 23.2 %all-to-all-start.4 = ((f32[4,136,256]{2,1,0:T(8,128)}), f32[4,136,256]{2,1,0:T(8,128)}, u32[]{:S(2)}, u32[]{:S(2)}) async-start(f32[4,136,256]{2,1,0:T(8,128)} %shard_map.50), calls=%async_computation.4 | async-start | bytes 1114112 | tf_op jit(solution)/shard_map/all_to_all | solution.py:238
  82.0 21.4 %all-to-all-start.3 = ((f32[4,136,256]{2,1,0:T(8,128)}), f32[4,136,256]{2,1,0:T(8,128)}, u32[]{:S(2)}, u32[]{:S(2)}) async-start(f32[4,136,256]{2,1,0:T(8,128)} %shard_map.49), calls=%async_computation.3 | async-start | bytes 1114112 | tf_op jit(solution)/shard_map/all_to_all | solution.py:238
  103.4 20.9 %all-to-all-start.2 = ((f32[4,136,256]{2,1,0:T(8,128)}), f32[4,136,256]{2,1,0:T(8,128)}, u32[]{:S(2)}, u32[]{:S(2)}) async-start(f32[4,136,256]{2,1,0:T(8,128)} %shard_map.48), calls=%async_computation.2 | async-start | bytes 1114112 | tf_op jit(solution)/shard_map/all_to_all | solution.py:238
  124.3 19.5 %all-to-all-start.1 = ((f32[4,136,256]{2,1,0:T(8,128)}), f32[4,136,256]{2,1,0:T(8,128)S(1)}, u32[]{:S(2)}, u32[]{:S(2)}) async-start(f32[4,136,256]{2,1,0:T(8,128)} %shard_map.47), calls=%async_computation.1 | async-start | bytes 1114112 | tf_op jit(solution)/shard_map/all_to_all | solution.py:238
  143.9 0.8 copy-start.2
Sparse Core Ops, SparseCore 0:
  9.3 29.4 all-gather.2

commit v14 on v12

--- a/solution.py
+++ b/solution.py
@@ -193,7 +193,7 @@
     sel_flat = hit.astype(jnp.int32).reshape(-1)
     home = helper.reshape(1).astype(jnp.int32)
 
-    slices = min(4, heads)
+    slices = min(2, heads)
     part = heads // slices
     assert part * slices == heads and 2 * part <= STAT_ROWS
     width = part * HEAD_SIZE

time: 147 us -> 142 us (0.966)
  waiting for transfers between devices: 32.9 us -> 50.1 us
  Pallas kernels: 68.5 us -> 56.6 us
  starting transfers between devices: 24.3 us -> 14.5 us
    all_to_all x4 -> x2, waiting for transfers between devices: 9.86 us -> 27 us  [local(): got = lax.all_to_all(partial, 'help', 0, 0, tiled=True)]
    all_to_all x4 -> x2, starting transfers between devices: 19.9 us -> 10.2 us  [local(): got = lax.all_to_all(partial, 'help', 0, 0, tiled=True)]
    pallas_call x4 -> x2, Pallas kernels: 56.4 us -> 48 us  [local(): pl.pallas_call(kernel, grid_spec=pltpu.PrefetchScalarGridSpec(num_scalar_...]
    pallas_call x4 -> x2, Pallas kernels: 8.73 us -> 5.24 us  [local(): pl.pallas_call(functools.partial(join_kernel, sources=helpers, heads=part...]
  transfers between devices with their start and end apart: 6 -> 4, of which waited for: 5 -> 4; matrix products, arithmetic and copies ran while one was open for 1% -> 1% of each run, Pallas kernels for 36% -> 21%
where the time goes in v14:
time: 142 us
  Pallas kernels  56.6 us (40%)
  waiting for transfers between devices  50.1 us (35%)
  starting transfers between devices  14.5 us (10%)
  between operations  13.5 us (10%)
  local copies, waits for them, and re-layouts  4.06 us (3%)
  other arithmetic  2.83 us (2%)
    pallas_call x2, Pallas kernels, local(): pl.pallas_call(kernel, grid_spec=pltpu.PrefetchScalarGridSpec(num_scalar_...  48 us
    all_to_all x2, waiting for transfers between devices, local(): got = lax.all_to_all(partial, 'help', 0, 0, tiled=True)  27 us
    all_gather x1, waiting for transfers between devices, local(): q_all = lax.all_gather(q[None], 'help', axis=0, tiled=True)  21.3 us
    all_to_all x2, starting transfers between devices, local(): got = lax.all_to_all(partial, 'help', 0, 0, tiled=True)  10.2 us
    pallas_call x2, Pallas kernels, local(): pl.pallas_call(functools.partial(join_kernel, sources=helpers, heads=part...  5.24 us
    all_to_all x1, starting transfers between devices, local(): held = lax.all_to_all(send, 'blk', 0, 0, tiled=True)  4.39 us
    pallas_call x1, Pallas kernels, local(): pl.pallas_call(functools.partial(relayout_kernel, wanted=wanted, chunks=c...  3.41 us
    unnamed x11, local copies, waits for them, and re-layouts  3.36 us
  transfers between devices with their start and end apart: 4, of which 4 were waited for; matrix products, arithmetic and copies ran while one was open for 1% of the time, Pallas kernels for 21%

profile of v14, /device:TPU:2, one launch (start us, length us, event | category | flops | bytes accessed | tf_op | source)
XLA Modules:
  0.0 141.6 jit_solution(17032757199363990665)
XLA Ops:
  6.5 0.0 all-gather.3.cloned.1.call-start
  6.5 0.7 convert_element_type.16
  7.2 0.1 copy.14
  7.3 0.1 convert_element_type.17
  7.4 1.0 copy.18
  8.5 0.7 fusion.1
  9.2 0.0 all-gather.3.cloned.1.call-update
  9.2 3.4 %shard_map.46 = bf16[8,2,4,128,128]{4,3,2,1,0:T(8,128)(2,1)} custom-call(bf16[512,2048]{1,0:T(8,128)(2,1)} %x_ref.1), custom_call_target="tpu_custom_call" | custom-call | tf_op jit(solution)/shard_map/pallas_call | solution.py:168
  12.6 0.0 copy-start.3
  12.6 4.4 %all-to-all-start = ((bf16[8,2,4,128,128]{4,3,2,1,0:T(8,128)(2,1)}), bf16[8,2,4,128,128]{4,3,2,1,0:T(8,128)(2,1)S(1)}, u32[]{:S(2)}, u32[]{:S(2)}) async-start(bf16[8,2,4,128,128]{4,3,2,1,0:T(8,128)(2,1)} %shard_map.46), calls=%async_computation | async-start | bytes 4194304 | tf_op jit(solution)/shard_map/all_to_all | solution.py:174
  17.0 0.0 copy-done.3
  17.0 0.1 copy.19
  17.1 0.1 constant_dynamic-slice_fusion
  17.3 0.1 copy.16
  17.5 21.3 %all-gather.3.cloned.1.call-done = bf16[4160,128]{1,0:T(8,128)(2,1)} async-done(((bf16[1040,128]{1,0:T(8,128)(2,1)}), bf16[4160,128]{1,0:T(8,128)(2,1)}) %all-gather.3.cloned.1.call-update) | async-done | bytes 1064976 | tf_op jit(solution)/shard_map/all_gather | solution.py:181
  38.8 0.7 slice_convert_fusion
  39.5 0.1 reshape.37
  39.6 0.7 compare_reduce_fusion
  40.4 0.1 reshape.38.sel_ref
  40.4 1.7 %all-to-all-done.kv_ref = bf16[8,2,4,128,128]{4,3,2,1,0:T(8,128)(2,1)S(1)} async-done(((bf16[8,2,4,128,128]{4,3,2,1,0:T(8,128)(2,1)}), bf16[8,2,4,128,128]{4,3,2,1,0:T(8,128)(2,1)S(1)}, u32[]{:S(2)}, u32[]{:S(2)}) %all-to-all-start) | async-done | bytes 2097184 | tf_op jit(solution)/shard_map/all_to_all | solution.py:174
  42.2 0.0 copy-start
  42.2 1.2 copy-done
  43.4 24.0 %shard_map.48 = f32[4,136,512]{2,1,0:T(8,128)} custom-call(s32[256]{0:T(256)S(1)} %reshape.38.sel_ref, s32[1]{0:T(128)} %bitcast.3.home_ref, bf16[4,1040,128]{2,1,0:T(8,128)(2,1)S(1)} %bitcast.22, bf16[8,2,4,128,128]{4,3,2,1,0:T(8,128)(2,1)S(1)} %all-to-all-done.kv_ref, bf16[2,128,128]{2,1,0:T(8,128)(2,1)S(1)} %pad_maximum_fusion.own_ref), custom_call_target="tpu_custom_call" | custom-call | flops 4294967296 | bytes 3145728 | tf_op jit(solution)/shard_map/pallas_call | solution.py:206
  67.4 0.0 copy-start.1
  67.4 6.5 %all-to-all-start.2 = ((f32[4,136,512]{2,1,0:T(8,128)}), f32[4,136,512]{2,1,0:T(8,128)}, u32[]{:S(2)}, u32[]{:S(2)}) async-start(f32[4,136,512]{2,1,0:T(8,128)} %shard_map.48), calls=%async_computation.2 | async-start | bytes 2228224 | tf_op jit(solution)/shard_map/all_to_all | solution.py:238
  73.9 0.0 copy-done.1
  73.9 23.9 %shard_map.47 = f32[4,136,512]{2,1,0:T(8,128)} custom-call(s32[256]{0:T(256)S(1)} %reshape.38.sel_ref, s32[1]{0:T(128)} %bitcast.3.home_ref, bf16[4,1040,128]{2,1,0:T(8,128)(2,1)S(1)} %bitcast.23, bf16[8,2,4,128,128]{4,3,2,1,0:T(8,128)(2,1)S(1)} %all-to-all-done.kv_ref, bf16[2,128,128]{2,1,0:T(8,128)(2,1)S(1)} %pad_maximum_fusion.own_ref), custom_call_target="tpu_custom_call" | custom-call | flops 4294967296 | bytes 3145728 | tf_op jit(solution)/shard_map/pallas_call | solution.py:206
  97.9 3.2 %all-to-all-done.2.got_ref = f32[4,136,512]{2,1,0:T(8,128)} async-done(((f32[4,136,512]{2,1,0:T(8,128)}), f32[4,136,512]{2,1,0:T(8,128)}, u32[]{:S(2)}, u32[]{:S(2)}) %all-to-all-start.2) | async-done | bytes 1114144 | tf_op jit(solution)/shard_map/all_to_all | solution.py:238
  101.0 3.7 %all-to-all-start.1 = ((f32[4,136,512]{2,1,0:T(8,128)}), f32[4,136,512]{2,1,0:T(8,128)S(1)}, u32[]{:S(2)}, u32[]{:S(2)}) async-start(f32[4,136,512]{2,1,0:T(8,128)} %shard_map.47), calls=%async_computation.1 | async-start | bytes 2228224 | tf_op jit(solution)/shard_map/all_to_all | solution.py:238
  104.7 2.6 %shard_map.49.refs_0_ = f32[128,1024]{1,0:T(8,128)} custom-call(f32[4,136,512]{2,1,0:T(8,128)} %all-to-all-done.2.got_ref), custom_call_target="tpu_custom_call" | custom-call | tf_op jit(solution)/shard_map/pallas_call | solution.py:240
  107.3 23.8 %all-to-all-done.1.got_ref = f32[4,136,512]{2,1,0:T(8,128)S(1)} async-done(((f32[4,136,512]{2,1,0:T(8,128)}), f32[4,136,512]{2,1,0:T(8,128)S(1)}, u32[]{:S(2)}, u32[]{:S(2)}) %all-to-all-start.1) | async-done | bytes 1114144 | tf_op jit(solution)/shard_map/all_to_all | solution.py:238
  131.2 0.0 copy-start.2
  131.2 1.0 copy-done.2
  132.2 2.6 %shard_map.50 = f32[128,1024]{1,0:T(8,128)} custom-call(f32[4,136,512]{2,1,0:T(8,128)} %copy-done.2, f32[128,1024]{1,0:T(8,128)} %shard_map.49.refs_0_), custom_call_target="tpu_custom_call", output_to_operand_aliasing={{}: (1, {})} | custom-call | tf_op jit(solution)/shard_map/pallas_call | solution.py:240
  (7 shorter events, 0.1 us)
Async XLA Ops:
  6.5 32.3 %all-gather.3.cloned.1.call-start = ((), (), s32[]{:S(2)}) async-start(), calls=%async_computation.3 | async-start | bytes 1331200 | tf_op jit(solution)/shard_map/all_gather | solution.py:181
  12.6 4.4 %copy-start.3 = (bf16[128,2048]{1,0:T(8,128)(2,1)S(1)}, bf16[128,2048]{1,0:T(8,128)(2,1)}, u32[]{:S(2)}) copy-start(bf16[128,2048]{1,0:T(8,128)(2,1)} %param.5) | copy-start | bytes 1572868
  12.6 29.5 %all-to-all-start = ((bf16[8,2,4,128,128]{4,3,2,1,0:T(8,128)(2,1)}), bf16[8,2,4,128,128]{4,3,2,1,0:T(8,128)(2,1)S(1)}, u32[]{:S(2)}, u32[]{:S(2)}) async-start(bf16[8,2,4,128,128]{4,3,2,1,0:T(8,128)(2,1)} %shard_map.46), calls=%async_computation | async-start | bytes 4194304 | tf_op jit(solution)/shard_map/all_to_all | solution.py:174
  42.2 1.2 copy-start
  67.4 6.5 %copy-start.1 = (bf16[4160,128]{1,0:T(8,128)(2,1)S(1)}, bf16[4160,128]{1,0:T(8,128)(2,1)}, u32[]{:S(2)}) copy-start(bf16[4160,128]{1,0:T(8,128)(2,1)} %all-gather.3.cloned.1.call-done) | copy-start | bytes 3194884
  67.4 33.6 %all-to-all-start.2 = ((f32[4,136,512]{2,1,0:T(8,128)}), f32[4,136,512]{2,1,0:T(8,128)}, u32[]{:S(2)}, u32[]{:S(2)}) async-start(f32[4,136,512]{2,1,0:T(8,128)} %shard_map.48), calls=%async_computation.2 | async-start | bytes 2228224 | tf_op jit(solution)/shard_map/all_to_all | solution.py:238
  101.0 30.1 %all-to-all-start.1 = ((f32[4,136,512]{2,1,0:T(8,128)}), f32[4,136,512]{2,1,0:T(8,128)S(1)}, u32[]{:S(2)}, u32[]{:S(2)}) async-start(f32[4,136,512]{2,1,0:T(8,128)} %shard_map.47), calls=%async_computation.1 | async-start | bytes 2228224 | tf_op jit(solution)/shard_map/all_to_all | solution.py:238
  131.2 1.0 copy-start.2
Sparse Core Ops, SparseCore 0:
  9.3 29.4 all-gather.2

commit v15 on v14

--- a/solution.py
+++ b/solution.py
@@ -29,7 +29,7 @@
 
 def attend_kernel(sel_ref, home_ref, q_ref, kv_ref, own_ref, out_ref,
                   s_buf, own_buf, p_buf, mpart, lpart, m_scr, acc_scr, st_scr,
-                  *, groups, heads, first, all_heads, blocks, chunks, factor):
+                  *, groups, heads, first, all_heads, blocks, chunks, factor, mode):
     rows = QUERY_GROUP_ROWS
     slots = blocks * heads
     lanes = HEAD_SIZE
@@ -41,7 +41,12 @@
 
     def on(slot, g):
         b, h = divmod(slot, heads)
-        return sel_ref[(b * all_heads + first + h) * groups + g] != 0
+        if mode == "home":
+            b = home
+        hit = sel_ref[(b * all_heads + first + h) * groups + g] != 0
+        if mode == "remote":
+            hit = jnp.logical_and(hit, b != home)
+        return hit
 
     def fold(x, op):
         out = x[:, :lanes]
@@ -62,15 +67,16 @@
 
     lax.fori_loop(0, groups, score, 0)
 
+    home_block = 0 if mode == "home" else home
     causal = lax.broadcasted_iota(jnp.int32, (rows, rows), 0) >= lax.broadcasted_iota(
         jnp.int32, (rows, rows), 1)
-    s_own = jnp.dot(q_ref[home], own_ref[0],
-                    preferred_element_type=jnp.float32)
-    for h in range(heads):
-        s_h = jnp.where(causal, s_own[h * rows:(h + 1) * rows], -jnp.inf)
-        own_buf[h] = s_h
-        slot = home * heads + h
-        mpart[slot] = jnp.maximum(mpart[slot], fold(s_h, jnp.maximum))
+    if mode != "remote":
+        s_own = jnp.dot(q_ref[home_block], own_ref[0], preferred_element_type=jnp.float32)
+        for h in range(heads):
+            s_h = jnp.where(causal, s_own[h * rows:(h + 1) * rows], -jnp.inf)
+            own_buf[h] = s_h
+            slot = home_block * heads + h
+            mpart[slot] = jnp.maximum(mpart[slot], fold(s_h, jnp.maximum))
 
     for slot in range(slots):
         m = jnp.max(mpart[slot], axis=1, keepdims=True) * factor
@@ -96,8 +102,8 @@
 
     lax.fori_loop(0, groups, mix, 0)
 
-    for h in range(heads):
-        slot = home * heads + h
+    for h in range(heads if mode != "remote" else 0):
+        slot = home_block * heads + h
         p = jnp.exp2(own_buf[h] * factor - mpart[slot][:, :1])
         lpart[slot] += p
         acc_scr[slot] += jnp.dot(p.astype(jnp.bfloat16), own_ref[1],
@@ -115,10 +121,11 @@
             out_ref[b, rows:, HEAD_SIZE:] = jnp.zeros((STAT_ROWS, (heads - 1) * HEAD_SIZE), jnp.float32)
 
 
-def join_kernel(got_ref, *refs, sources, heads):
+def join_kernel(got_ref, *refs, sources, heads, extra):
     rows = QUERY_GROUP_ROWS
     out_ref = refs[-1]
-    cols = [got_ref[s, rows:, :HEAD_SIZE].T for s in range(sources)]
+    blocks = [(got_ref, s) for s in range(sources)] + ([(refs[0], 0)] if extra else [])
+    cols = [ref[s, rows:, :HEAD_SIZE].T for ref, s in blocks]
     for h in range(heads):
         ms = [c[:, h:h + 1] for c in cols]
         top = ms[0]
@@ -127,10 +134,10 @@
         top = jnp.where(top == -jnp.inf, 0.0, top)
         total = None
         acc = None
-        for s in range(sources):
-            fade = jnp.exp2(ms[s] - top)
-            part_total = fade * cols[s][:, heads + h:heads + h + 1]
-            part_acc = fade * got_ref[s, :rows, h * HEAD_SIZE:(h + 1) * HEAD_SIZE]
+        for (ref, s), col, m in zip(blocks, cols, ms):
+            fade = jnp.exp2(m - top)
+            part_total = fade * col[:, heads + h:heads + h + 1]
+            part_acc = fade * ref[s, :rows, h * HEAD_SIZE:(h + 1) * HEAD_SIZE]
             total = part_total if total is None else total + part_total
             acc = part_acc if acc is None else acc + part_acc
         out_ref[:, h * HEAD_SIZE:(h + 1) * HEAD_SIZE] = acc / total
@@ -198,25 +205,29 @@
     assert part * slices == heads and 2 * part <= STAT_ROWS
     width = part * HEAD_SIZE
     result = None
-    for c in range(slices):
+
+    def attend_call(c, mode):
+        blocks = 1 if mode == "home" else query_blocks
+        slots = blocks * part
         kernel = functools.partial(attend_kernel, groups=groups, heads=part, first=c * part,
-                                   all_heads=heads, blocks=query_blocks, chunks=chunks,
-                                   factor=scale * math.log2(math.e))
-        slots = query_blocks * part
-        partial = pl.pallas_call(
+                                   all_heads=heads, blocks=blocks, chunks=chunks,
+                                   factor=scale * math.log2(math.e), mode=mode)
+        if mode == "home":
+            q_spec = pl.BlockSpec((1, part * rows, HEAD_SIZE), lambda i, s, h, c=c: (h[0], c, 0))
+        else:
+            q_spec = pl.BlockSpec((query_blocks, part * rows, HEAD_SIZE), lambda i, s, h, c=c: (0, c, 0))
+        return pl.pallas_call(
             kernel,
             grid_spec=pltpu.PrefetchScalarGridSpec(
                 num_scalar_prefetch=2,
                 grid=(1,),
                 in_specs=[
-                    pl.BlockSpec((query_blocks, part * rows, HEAD_SIZE),
-                                 lambda i, s, h, c=c: (0, c, 0)),
+                    q_spec,
                     pl.BlockSpec((groups, 2, chunks, HEAD_SIZE, HEAD_SIZE),
                                  lambda i, s, h: (0, 0, 0, 0, 0)),
                     pl.BlockSpec((2, rows, HEAD_SIZE), lambda i, s, h: (0, 0, 0)),
                 ],
-                out_specs=pl.BlockSpec((query_blocks, rows + STAT_ROWS, width),
-                                       lambda i, s, h: (0, 0, 0)),
+                out_specs=pl.BlockSpec((blocks, rows + STAT_ROWS, width), lambda i, s, h: (0, 0, 0)),
                 scratch_shapes=[
                     pltpu.VMEM((groups, slots * rows, piece), jnp.float32),
                     pltpu.VMEM((part, rows, rows), jnp.float32),
@@ -229,23 +240,29 @@
                 ],
             ),
             compiler_params=pltpu.CompilerParams(vmem_limit_bytes=48 * 1024 * 1024),
-            out_shape=jax.ShapeDtypeStruct((query_blocks, rows + STAT_ROWS, width), jnp.float32),
+            out_shape=jax.ShapeDtypeStruct((blocks, rows + STAT_ROWS, width), jnp.float32),
             cost_estimate=pl.CostEstimate(
-                flops=4 * query_blocks * part * rows * groups * piece * HEAD_SIZE,
-                transcendentals=query_blocks * part * rows * groups * piece,
-                bytes_accessed=2 * groups * 2 * piece * HEAD_SIZE + 4 * query_blocks * rows * width),
+                flops=4 * blocks * part * rows * groups * piece * HEAD_SIZE,
+                transcendentals=blocks * part * rows * groups * piece,
+                bytes_accessed=2 * groups * 2 * piece * HEAD_SIZE + 4 * blocks * rows * width),
         )(sel_flat, home, q_all, held, own)
+
+    for c in range(slices):
+        last = c == slices - 1
+        partial = attend_call(c, "remote" if last else "all")
         got = lax.all_to_all(partial, "help", 0, 0, tiled=True)
+        extra = [attend_call(c, "home")] if last else []
         first_join = c == 0
         result = pl.pallas_call(
-            functools.partial(join_kernel, sources=helpers, heads=part),
+            functools.partial(join_kernel, sources=helpers, heads=part, extra=last),
             grid=(1,),
             in_specs=[pl.BlockSpec((helpers, rows + STAT_ROWS, width), lambda i: (0, 0, 0))]
+            + [pl.BlockSpec((1, rows + STAT_ROWS, width), lambda i: (0, 0, 0))] * len(extra)
             + ([] if first_join else [pl.BlockSpec(memory_space=pl.ANY)]),
             out_specs=pl.BlockSpec((rows, width), lambda i, c=c: (0, c)),
             out_shape=jax.ShapeDtypeStruct((rows, heads * HEAD_SIZE), jnp.float32),
-            input_output_aliases={} if first_join else {1: 0},
-        )(*((got,) if first_join else (got, result)))
+            input_output_aliases={} if first_join else {1 + len(extra): 0},
+        )(got, *extra, *(() if first_join else (result,)))
     return result
 
 

time: 142 us -> 142 us (level)
  Pallas kernels: 56.6 us -> 66.4 us
  waiting for transfers between devices: 50.1 us -> 41.9 us
  starting transfers between devices: 14.5 us -> 13 us
    pallas_call x2 -> x3, Pallas kernels: 48 us -> 57.6 us  [attend_call(): pl.pallas_call(kernel, grid_spec=pltpu.PrefetchScalarGridSpec(num_scalar_...]
    all_to_all x2, waiting for transfers between devices: 27 us -> 18.9 us  [local(): got = lax.all_to_all(partial, 'help', 0, 0, tiled=True)]
    all_to_all x2, starting transfers between devices: 10.2 us -> 8.64 us  [local(): got = lax.all_to_all(partial, 'help', 0, 0, tiled=True)]
  transfers between devices with their start and end apart: 4 -> 4, of which waited for: 4 -> 4; matrix products, arithmetic and copies ran while one was open for 1% -> 1% of each run, Pallas kernels for 21% -> 26%
where the time goes in v15:
time: 142 us
  Pallas kernels  66.4 us (47%)
  waiting for transfers between devices  41.9 us (30%)
  between operations  13.5 us (10%)
  starting transfers between devices  13 us (9%)
  local copies, waits for them, and re-layouts  3.79 us (3%)
  other arithmetic  2.84 us (2%)
    pallas_call x3, Pallas kernels, attend_call(): pl.pallas_call(kernel, grid_spec=pltpu.PrefetchScalarGridSpec(num_scalar_...  57.6 us
    all_gather x1, waiting for transfers between devices, local(): q_all = lax.all_gather(q[None], 'help', axis=0, tiled=True)  21.3 us
    all_to_all x2, waiting for transfers between devices, local(): got = lax.all_to_all(partial, 'help', 0, 0, tiled=True)  18.9 us
    all_to_all x2, starting transfers between devices, local(): got = lax.all_to_all(partial, 'help', 0, 0, tiled=True)  8.64 us
    pallas_call x2, Pallas kernels, local(): pl.pallas_call(functools.partial(join_kernel, sources=helpers, heads=part...  5.45 us
    all_to_all x1, starting transfers between devices, local(): held = lax.all_to_all(send, 'blk', 0, 0, tiled=True)  4.39 us
    pallas_call x1, Pallas kernels, local(): pl.pallas_call(functools.partial(relayout_kernel, wanted=wanted, chunks=c...  3.4 us
    unnamed x11, local copies, waits for them, and re-layouts  3.08 us
  transfers between devices with their start and end apart: 4, of which 4 were waited for; matrix products, arithmetic and copies ran while one was open for 1% of the time, Pallas kernels for 26%

profile of v15, /device:TPU:2, one launch (start us, length us, event | category | flops | bytes accessed | tf_op | source)
XLA Modules:
  0.0 141.5 jit_solution(1875767820991418105)
XLA Ops:
  6.5 0.0 all-gather.3.cloned.1.call-start
  6.5 1.0 copy.18
  7.6 0.7 convert_element_type.16
  8.3 0.1 copy.14
  8.4 0.1 convert_element_type.17
  8.5 0.7 fusion.1
  9.2 0.0 all-gather.3.cloned.1.call-update
  9.2 3.4 %shard_map.46 = bf16[8,2,4,128,128]{4,3,2,1,0:T(8,128)(2,1)} custom-call(bf16[512,2048]{1,0:T(8,128)(2,1)} %x_ref.1), custom_call_target="tpu_custom_call" | custom-call | tf_op jit(solution)/shard_map/pallas_call | solution.py:175
  12.6 0.0 copy-start.3
  12.6 4.4 %all-to-all-start = ((bf16[8,2,4,128,128]{4,3,2,1,0:T(8,128)(2,1)}), bf16[8,2,4,128,128]{4,3,2,1,0:T(8,128)(2,1)S(1)}, u32[]{:S(2)}, u32[]{:S(2)}) async-start(bf16[8,2,4,128,128]{4,3,2,1,0:T(8,128)(2,1)} %shard_map.46), calls=%async_computation | async-start | bytes 4194304 | tf_op jit(solution)/shard_map/all_to_all | solution.py:181
  17.0 0.0 copy-done.3
  17.0 0.1 copy.19
  17.1 0.1 constant_dynamic-slice_fusion
  17.3 0.1 copy.16
  17.5 21.3 %all-gather.3.cloned.1.call-done = bf16[4160,128]{1,0:T(8,128)(2,1)} async-done(((bf16[1040,128]{1,0:T(8,128)(2,1)}), bf16[4160,128]{1,0:T(8,128)(2,1)}) %all-gather.3.cloned.1.call-update) | async-done | bytes 1064976 | tf_op jit(solution)/shard_map/all_gather | solution.py:188
  38.8 0.7 slice_convert_fusion
  39.5 0.1 reshape.37
  39.7 0.7 compare_reduce_fusion
  40.4 0.1 reshape.38.sel_ref
  40.5 1.7 %all-to-all-done.kv_ref = bf16[8,2,4,128,128]{4,3,2,1,0:T(8,128)(2,1)S(1)} async-done(((bf16[8,2,4,128,128]{4,3,2,1,0:T(8,128)(2,1)}), bf16[8,2,4,128,128]{4,3,2,1,0:T(8,128)(2,1)S(1)}, u32[]{:S(2)}, u32[]{:S(2)}) %all-to-all-start) | async-done | bytes 2097184 | tf_op jit(solution)/shard_map/all_to_all | solution.py:181
  42.2 0.0 copy-start.1
  42.2 1.2 copy-done.1
  43.4 27.2 %shard_map.49 = f32[4,136,512]{2,1,0:T(8,128)} custom-call(s32[256]{0:T(256)S(1)} %reshape.38.sel_ref, s32[1]{0:T(128)} %bitcast.3.home_ref, bf16[4,1040,128]{2,1,0:T(8,128)(2,1)S(1)} %bitcast.22, bf16[8,2,4,128,128]{4,3,2,1,0:T(8,128)(2,1)S(1)} %all-to-all-done.kv_ref, bf16[2,128,128]{2,1,0:T(8,128)(2,1)S(1)} %pad_maximum_fusion.own_ref), custom_call_target="tpu_custom_call" | custom-call | flops 4294967296 | bytes 3145728 | tf_op jit(solution)/shard_map/pallas_call | solution.py:219
  70.6 0.0 copy-start.2
  70.6 4.4 %all-to-all-start.2 = ((f32[4,136,512]{2,1,0:T(8,128)}), f32[4,136,512]{2,1,0:T(8,128)}, u32[]{:S(2)}, u32[]{:S(2)}) async-start(f32[4,136,512]{2,1,0:T(8,128)} %shard_map.49), calls=%async_computation.2 | async-start | bytes 2228224 | tf_op jit(solution)/shard_map/all_to_all | solution.py:253
  74.9 0.0 copy-done.2
  75.0 22.4 %shard_map.47 = f32[4,136,512]{2,1,0:T(8,128)} custom-call(s32[256]{0:T(256)S(1)} %reshape.38.sel_ref, s32[1]{0:T(128)} %bitcast.3.home_ref, bf16[4,1040,128]{2,1,0:T(8,128)(2,1)S(1)} %bitcast.23, bf16[8,2,4,128,128]{4,3,2,1,0:T(8,128)(2,1)S(1)} %all-to-all-done.kv_ref, bf16[2,128,128]{2,1,0:T(8,128)(2,1)S(1)} %pad_maximum_fusion.own_ref), custom_call_target="tpu_custom_call" | custom-call | flops 4294967296 | bytes 3145728 | tf_op jit(solution)/shard_map/pallas_call | solution.py:219
  97.4 3.5 %all-to-all-done.2.got_ref = f32[4,136,512]{2,1,0:T(8,128)} async-done(((f32[4,136,512]{2,1,0:T(8,128)}), f32[4,136,512]{2,1,0:T(8,128)}, u32[]{:S(2)}, u32[]{:S(2)}) %all-to-all-start.2) | async-done | bytes 1114144 | tf_op jit(solution)/shard_map/all_to_all | solution.py:253
  100.9 4.3 %all-to-all-start.1 = ((f32[4,136,512]{2,1,0:T(8,128)}), f32[4,136,512]{2,1,0:T(8,128)}, u32[]{:S(2)}, u32[]{:S(2)}) async-start(f32[4,136,512]{2,1,0:T(8,128)} %shard_map.47), calls=%async_computation.1 | async-start | bytes 2228224 | tf_op jit(solution)/shard_map/all_to_all | solution.py:253
  105.2 8.0 %shard_map.48.refs_0_ = f32[1,136,512]{2,1,0:T(8,128)S(1)} custom-call(s32[256]{0:T(256)S(1)} %reshape.38.sel_ref, s32[1]{0:T(128)} %bitcast.3.home_ref, bf16[4,1040,128]{2,1,0:T(8,128)(2,1)S(1)} %bitcast.24, bf16[8,2,4,128,128]{4,3,2,1,0:T(8,128)(2,1)S(1)} %all-to-all-done.kv_ref, bf16[2,128,128]{2,1,0:T(8,128)(2,1)S(1)} %pad_maximum_fusion.own_ref), custom_call_target="tpu_custom_call" | custom-call | flops 1073741824 | bytes 2359296 | tf_op jit(solution)/shard_map/pallas_call | solution.py:219
  113.2 0.0 copy-start
  113.2 0.7 copy-done
  113.9 2.6 %shard_map.50.refs_1_ = f32[128,1024]{1,0:T(8,128)} custom-call(f32[4,136,512]{2,1,0:T(8,128)} %all-to-all-done.2.got_ref), custom_call_target="tpu_custom_call" | custom-call | tf_op jit(solution)/shard_map/pallas_call | solution.py:256
  116.5 15.3 %all-to-all-done.1.got_ref = f32[4,136,512]{2,1,0:T(8,128)} async-done(((f32[4,136,512]{2,1,0:T(8,128)}), f32[4,136,512]{2,1,0:T(8,128)}, u32[]{:S(2)}, u32[]{:S(2)}) %all-to-all-start.1) | async-done | bytes 1114144 | tf_op jit(solution)/shard_map/all_to_all | solution.py:253
  131.9 2.8 %shard_map.51 = f32[128,1024]{1,0:T(8,128)} custom-call(f32[4,136,512]{2,1,0:T(8,128)} %all-to-all-done.1.got_ref, f32[1,136,512]{2,1,0:T(8,128)} %copy-done, f32[128,1024]{1,0:T(8,128)} %shard_map.50.refs_1_), custom_call_target="tpu_custom_call", output_to_operand_aliasing={{}: (2, {})} | custom-call | tf_op jit(solution)/shard_map/pallas_call | solution.py:256
  (7 shorter events, 0.1 us)
Async XLA Ops:
  6.5 32.3 %all-gather.3.cloned.1.call-start = ((), (), s32[]{:S(2)}) async-start(), calls=%async_computation.3 | async-start | bytes 1331200 | tf_op jit(solution)/shard_map/all_gather | solution.py:188
  12.6 4.4 %copy-start.3 = (bf16[128,2048]{1,0:T(8,128)(2,1)S(1)}, bf16[128,2048]{1,0:T(8,128)(2,1)}, u32[]{:S(2)}) copy-start(bf16[128,2048]{1,0:T(8,128)(2,1)} %param.5) | copy-start | bytes 1572868
  12.6 29.5 %all-to-all-start = ((bf16[8,2,4,128,128]{4,3,2,1,0:T(8,128)(2,1)}), bf16[8,2,4,128,128]{4,3,2,1,0:T(8,128)(2,1)S(1)}, u32[]{:S(2)}, u32[]{:S(2)}) async-start(bf16[8,2,4,128,128]{4,3,2,1,0:T(8,128)(2,1)} %shard_map.46), calls=%async_computation | async-start | bytes 4194304 | tf_op jit(solution)/shard_map/all_to_all | solution.py:181
  42.2 1.2 copy-start.1
  70.6 4.4 %copy-start.2 = (bf16[4160,128]{1,0:T(8,128)(2,1)S(1)}, bf16[4160,128]{1,0:T(8,128)(2,1)}, u32[]{:S(2)}) copy-start(bf16[4160,128]{1,0:T(8,128)(2,1)} %all-gather.3.cloned.1.call-done) | copy-start | bytes 3194884
  70.6 30.4 %all-to-all-start.2 = ((f32[4,136,512]{2,1,0:T(8,128)}), f32[4,136,512]{2,1,0:T(8,128)}, u32[]{:S(2)}, u32[]{:S(2)}) async-start(f32[4,136,512]{2,1,0:T(8,128)} %shard_map.49), calls=%async_computation.2 | async-start | bytes 2228224 | tf_op jit(solution)/shard_map/all_to_all | solution.py:253
  100.9 30.9 %all-to-all-start.1 = ((f32[4,136,512]{2,1,0:T(8,128)}), f32[4,136,512]{2,1,0:T(8,128)}, u32[]{:S(2)}, u32[]{:S(2)}) async-start(f32[4,136,512]{2,1,0:T(8,128)} %shard_map.47), calls=%async_computation.1 | async-start | bytes 2228224 | tf_op jit(solution)/shard_map/all_to_all | solution.py:253
  113.2 0.7 copy-start
Sparse Core Ops, SparseCore 0:
  9.4 29.4 all-gather.2

commit v16 on v14

--- a/solution.py
+++ b/solution.py
@@ -33,7 +33,8 @@
     rows = QUERY_GROUP_ROWS
     slots = blocks * heads
     lanes = HEAD_SIZE
-    q = q_ref[...].reshape(slots * rows, HEAD_SIZE)
+    q = jnp.concatenate([q_ref[b, :, h * HEAD_SIZE:(h + 1) * HEAD_SIZE]
+                         for b in range(blocks) for h in range(heads)], axis=0)
     home = home_ref[0]
     mpart[...] = jnp.full(mpart.shape, -jnp.inf, jnp.float32)
     lpart[...] = jnp.zeros(lpart.shape, jnp.float32)
@@ -64,8 +65,10 @@
 
     causal = lax.broadcasted_iota(jnp.int32, (rows, rows), 0) >= lax.broadcasted_iota(
         jnp.int32, (rows, rows), 1)
-    s_own = jnp.dot(q_ref[home], own_ref[0],
-                    preferred_element_type=jnp.float32)
+    q_home = q_ref[home]
+    s_own = jnp.dot(jnp.concatenate([q_home[:, h * HEAD_SIZE:(h + 1) * HEAD_SIZE]
+                                     for h in range(heads)], axis=0),
+                    own_ref[0], preferred_element_type=jnp.float32)
     for h in range(heads):
         s_h = jnp.where(causal, s_own[h * rows:(h + 1) * rows], -jnp.inf)
         own_buf[h] = s_h
@@ -173,13 +176,13 @@
     )(cached_key_value)
     held = lax.all_to_all(send, "blk", 0, 0, tiled=True)
 
-    q = jnp.transpose(queries.reshape(rows, heads, HEAD_SIZE), (1, 0, 2)).reshape(heads * rows, HEAD_SIZE)
-    sel_rows = selected.reshape(picks // HEAD_SIZE, HEAD_SIZE).astype(jnp.bfloat16)
-    sel_pad = -(-(picks // HEAD_SIZE) // 16) * 16
-    sel_rows = jnp.pad(sel_rows, ((0, sel_pad - picks // HEAD_SIZE), (0, 0)))
-    q = jnp.concatenate([q, sel_rows], axis=0)
+    full_width = heads * HEAD_SIZE
+    assert picks <= full_width
+    sel_rows = jnp.pad(selected.reshape(1, picks).astype(jnp.bfloat16),
+                       ((0, 15), (0, full_width - picks)))
+    q = jnp.concatenate([queries, sel_rows], axis=0)
     q_all = lax.all_gather(q[None], "help", axis=0, tiled=True)
-    sel_all = q_all[:, heads * rows:heads * rows + picks // HEAD_SIZE].astype(jnp.int32).reshape(
+    sel_all = q_all[:, rows, :picks].astype(jnp.int32).reshape(
         query_blocks, selected.shape[1], selected.shape[2])
 
     kv_head = (worker * heads) // head_group
@@ -209,8 +212,8 @@
                 num_scalar_prefetch=2,
                 grid=(1,),
                 in_specs=[
-                    pl.BlockSpec((query_blocks, part * rows, HEAD_SIZE),
-                                 lambda i, s, h, c=c: (0, c, 0)),
+                    pl.BlockSpec((query_blocks, rows, part * HEAD_SIZE),
+                                 lambda i, s, h, c=c: (0, 0, c)),
                     pl.BlockSpec((groups, 2, chunks, HEAD_SIZE, HEAD_SIZE),
                                  lambda i, s, h: (0, 0, 0, 0, 0)),
                     pl.BlockSpec((2, rows, HEAD_SIZE), lambda i, s, h: (0, 0, 0)),

time: 142 us -> 143 us (level)
  Pallas kernels: 56.6 us -> 59.6 us
  starting transfers between devices: 14.5 us -> 12.3 us
    pallas_call x2, Pallas kernels: 48 us -> 51 us  [local(): pl.pallas_call(kernel, grid_spec=pltpu.PrefetchScalarGridSpec(num_scalar_...]
    all_gather x1, waiting for transfers between devices: 21.3 us -> 23.6 us  [local(): q_all = lax.all_gather(q[None], 'help', axis=0, tiled=True)]
    all_to_all x2, starting transfers between devices: 10.2 us -> 7.92 us  [local(): got = lax.all_to_all(partial, 'help', 0, 0, tiled=True)]
    all_to_all x1, waiting for transfers between devices: 1.72 us -> 0.01 us  [local(): held = lax.all_to_all(send, 'blk', 0, 0, tiled=True)]
    all_to_all x2, waiting for transfers between devices: 27 us -> 25.6 us  [local(): got = lax.all_to_all(partial, 'help', 0, 0, tiled=True)]
    unnamed x11 -> x10, local copies, waits for them, and re-layouts: 3.36 us -> 2.39 us
  transfers between devices with their start and end apart: 4 -> 4, of which waited for: 4 -> 3; matrix products, arithmetic and copies ran while one was open for 1% -> 1% of each run, Pallas kernels for 21% -> 22%
where the time goes in v16:
time: 143 us; the launch traced here: 142 us
  Pallas kernels  59.6 us (42%)
  waiting for transfers between devices  49.2 us (34%)
  between operations  13.5 us (9%)
  starting transfers between devices  12.3 us (9%)
  other arithmetic  3.88 us (3%)
  local copies, waits for them, and re-layouts  3.06 us (2%)
    pallas_call x2, Pallas kernels, local(): pl.pallas_call(kernel, grid_spec=pltpu.PrefetchScalarGridSpec(num_scalar_...  51 us
    all_to_all x2, waiting for transfers between devices, local(): got = lax.all_to_all(partial, 'help', 0, 0, tiled=True)  25.6 us
    all_gather x1, waiting for transfers between devices, local(): q_all = lax.all_gather(q[None], 'help', axis=0, tiled=True)  23.6 us
    all_to_all x2, starting transfers between devices, local(): got = lax.all_to_all(partial, 'help', 0, 0, tiled=True)  7.92 us
    pallas_call x2, Pallas kernels, local(): pl.pallas_call(functools.partial(join_kernel, sources=helpers, heads=part...  5.24 us
    all_to_all x1, starting transfers between devices, local(): held = lax.all_to_all(send, 'blk', 0, 0, tiled=True)  4.39 us
    pallas_call x1, Pallas kernels, local(): pl.pallas_call(functools.partial(relayout_kernel, wanted=wanted, chunks=c...  3.39 us
  transfers between devices with their start and end apart: 4, of which 3 were waited for; matrix products, arithmetic and copies ran while one was open for 1% of the time, Pallas kernels for 22%

profile of v16, /device:TPU:2, one launch (start us, length us, event | category | flops | bytes accessed | tf_op | source)
XLA Modules:
  0.0 141.6 jit_solution(7258420830058949492)
XLA Ops:
  6.5 0.0 all-gather.3.cloned.1.call-start
  6.5 0.7 convert_element_type.30
  7.2 0.1 copy.11
  7.3 0.1 convert_element_type.31
  7.4 1.7 %fusion.1 = bf16[144,1024]{1,0:T(8,128)(2,1)} fusion(bf16[1,512]{1,0:T(2,128)(2,1)S(1)} %convert_element_type.31, bf16[128,1024]{1,0:T(8,128)(2,1)} %param.4), kind=kLoop, calls=%fused_computation.2 | loop fusion | flops 884736 | bytes 558080 | tf_op jit(solution)/shard_map/concatenate | solution.py:183
  9.1 0.0 all-gather.3.cloned.1.call-update
  9.1 3.4 %shard_map.46 = bf16[8,2,4,128,128]{4,3,2,1,0:T(8,128)(2,1)} custom-call(bf16[512,2048]{1,0:T(8,128)(2,1)} %x_ref.1), custom_call_target="tpu_custom_call" | custom-call | tf_op jit(solution)/shard_map/pallas_call | solution.py:171
  12.5 0.0 copy-start.3
  12.5 4.4 %all-to-all-start = ((bf16[8,2,4,128,128]{4,3,2,1,0:T(8,128)(2,1)}), bf16[8,2,4,128,128]{4,3,2,1,0:T(8,128)(2,1)S(1)}, u32[]{:S(2)}, u32[]{:S(2)}) async-start(bf16[8,2,4,128,128]{4,3,2,1,0:T(8,128)(2,1)} %shard_map.46), calls=%async_computation | async-start | bytes 4194304 | tf_op jit(solution)/shard_map/all_to_all | solution.py:177
  16.9 0.0 copy-done.3
  16.9 0.1 copy.15
  17.0 0.1 constant_dynamic-slice_fusion
  17.2 0.1 copy.13
  17.4 23.6 %all-gather.3.cloned.1.call-done = bf16[576,1024]{1,0:T(8,128)(2,1)} async-done(((bf16[144,1024]{1,0:T(8,128)(2,1)}), bf16[576,1024]{1,0:T(8,128)(2,1)}) %all-gather.3.cloned.1.call-update) | async-done | bytes 1179664 | tf_op jit(solution)/shard_map/all_gather | solution.py:184
  41.0 0.8 fusion.2
  41.8 0.1 reshape.36
  41.9 0.7 compare_reduce_fusion
  42.6 0.1 reshape.37.sel_ref
  42.7 0.0 all-to-all-done.kv_ref
  42.7 0.0 copy-start
  42.7 1.3 copy-done
  44.0 25.6 %shard_map.48 = f32[4,136,512]{2,1,0:T(8,128)} custom-call(s32[256]{0:T(256)S(1)} %reshape.37.sel_ref, s32[1]{0:T(128)} %bitcast.1.home_ref, bf16[4,144,1024]{2,1,0:T(8,128)(2,1)S(1)} %bitcast.17, bf16[8,2,4,128,128]{4,3,2,1,0:T(8,128)(2,1)S(1)} %all-to-all-done.kv_ref, bf16[2,128,128]{2,1,0:T(8,128)(2,1)S(1)} %pad_maximum_fusion.own_ref), custom_call_target="tpu_custom_call" | custom-call | flops 4294967296 | bytes 3145728 | tf_op jit(solution)/shard_map/pallas_call | solution.py:209
  69.6 0.0 copy-start.1
  69.6 4.4 %all-to-all-start.2 = ((f32[4,136,512]{2,1,0:T(8,128)}), f32[4,136,512]{2,1,0:T(8,128)}, u32[]{:S(2)}, u32[]{:S(2)}) async-start(f32[4,136,512]{2,1,0:T(8,128)} %shard_map.48), calls=%async_computation.2 | async-start | bytes 2228224 | tf_op jit(solution)/shard_map/all_to_all | solution.py:241
  74.0 0.0 copy-done.1
  74.0 25.4 %shard_map.47 = f32[4,136,512]{2,1,0:T(8,128)} custom-call(s32[256]{0:T(256)S(1)} %reshape.37.sel_ref, s32[1]{0:T(128)} %bitcast.1.home_ref, bf16[4,144,1024]{2,1,0:T(8,128)(2,1)S(1)} %bitcast.18, bf16[8,2,4,128,128]{4,3,2,1,0:T(8,128)(2,1)S(1)} %all-to-all-done.kv_ref, bf16[2,128,128]{2,1,0:T(8,128)(2,1)S(1)} %pad_maximum_fusion.own_ref), custom_call_target="tpu_custom_call" | custom-call | flops 4294967296 | bytes 3145728 | tf_op jit(solution)/shard_map/pallas_call | solution.py:209
  99.4 1.6 %all-to-all-done.2.got_ref = f32[4,136,512]{2,1,0:T(8,128)} async-done(((f32[4,136,512]{2,1,0:T(8,128)}), f32[4,136,512]{2,1,0:T(8,128)}, u32[]{:S(2)}, u32[]{:S(2)}) %all-to-all-start.2) | async-done | bytes 1114144 | tf_op jit(solution)/shard_map/all_to_all | solution.py:241
  101.0 3.5 %all-to-all-start.1 = ((f32[4,136,512]{2,1,0:T(8,128)}), f32[4,136,512]{2,1,0:T(8,128)S(1)}, u32[]{:S(2)}, u32[]{:S(2)}) async-start(f32[4,136,512]{2,1,0:T(8,128)} %shard_map.47), calls=%async_computation.1 | async-start | bytes 2228224 | tf_op jit(solution)/shard_map/all_to_all | solution.py:241
  104.5 2.6 %shard_map.49.refs_0_ = f32[128,1024]{1,0:T(8,128)} custom-call(f32[4,136,512]{2,1,0:T(8,128)} %all-to-all-done.2.got_ref), custom_call_target="tpu_custom_call" | custom-call | tf_op jit(solution)/shard_map/pallas_call | solution.py:243
  107.1 24.0 %all-to-all-done.1.got_ref = f32[4,136,512]{2,1,0:T(8,128)S(1)} async-done(((f32[4,136,512]{2,1,0:T(8,128)}), f32[4,136,512]{2,1,0:T(8,128)S(1)}, u32[]{:S(2)}, u32[]{:S(2)}) %all-to-all-start.1) | async-done | bytes 1114144 | tf_op jit(solution)/shard_map/all_to_all | solution.py:241
  131.1 0.0 copy-start.2
  131.1 1.0 copy-done.2
  132.1 2.6 %shard_map.50 = f32[128,1024]{1,0:T(8,128)} custom-call(f32[4,136,512]{2,1,0:T(8,128)} %copy-done.2, f32[128,1024]{1,0:T(8,128)} %shard_map.49.refs_0_), custom_call_target="tpu_custom_call", output_to_operand_aliasing={{}: (1, {})} | custom-call | tf_op jit(solution)/shard_map/pallas_call | solution.py:243
  (6 shorter events, 0.1 us)
Async XLA Ops:
  6.5 34.4 %all-gather.3.cloned.1.call-start = ((), (), s32[]{:S(2)}) async-start(), calls=%async_computation.3 | async-start | bytes 1474560 | tf_op jit(solution)/shard_map/all_gather | solution.py:184
  12.5 4.4 %copy-start.3 = (bf16[128,2048]{1,0:T(8,128)(2,1)S(1)}, bf16[128,2048]{1,0:T(8,128)(2,1)}, u32[]{:S(2)}) copy-start(bf16[128,2048]{1,0:T(8,128)(2,1)} %param.5) | copy-start | bytes 1572868
  12.5 30.2 %all-to-all-start = ((bf16[8,2,4,128,128]{4,3,2,1,0:T(8,128)(2,1)}), bf16[8,2,4,128,128]{4,3,2,1,0:T(8,128)(2,1)S(1)}, u32[]{:S(2)}, u32[]{:S(2)}) async-start(bf16[8,2,4,128,128]{4,3,2,1,0:T(8,128)(2,1)} %shard_map.46), calls=%async_computation | async-start | bytes 4194304 | tf_op jit(solution)/shard_map/all_to_all | solution.py:177
  42.7 1.3 copy-start
  69.6 4.4 %copy-start.1 = (bf16[576,1024]{1,0:T(8,128)(2,1)S(1)}, bf16[576,1024]{1,0:T(8,128)(2,1)}, u32[]{:S(2)}) copy-start(bf16[576,1024]{1,0:T(8,128)(2,1)} %all-gather.3.cloned.1.call-done) | copy-start | bytes 3538948
  69.6 31.4 %all-to-all-start.2 = ((f32[4,136,512]{2,1,0:T(8,128)}), f32[4,136,512]{2,1,0:T(8,128)}, u32[]{:S(2)}, u32[]{:S(2)}) async-start(f32[4,136,512]{2,1,0:T(8,128)} %shard_map.48), calls=%async_computation.2 | async-start | bytes 2228224 | tf_op jit(solution)/shard_map/all_to_all | solution.py:241
  101.0 30.1 %all-to-all-start.1 = ((f32[4,136,512]{2,1,0:T(8,128)}), f32[4,136,512]{2,1,0:T(8,128)S(1)}, u32[]{:S(2)}, u32[]{:S(2)}) async-start(f32[4,136,512]{2,1,0:T(8,128)} %shard_map.47), calls=%async_computation.1 | async-start | bytes 2228224 | tf_op jit(solution)/shard_map/all_to_all | solution.py:241
  131.1 1.0 copy-start.2
Sparse Core Ops, SparseCore 0:
  9.3 31.6 all-gather.2

commit v17 on v14

--- a/solution.py
+++ b/solution.py
@@ -211,8 +211,7 @@
                 in_specs=[
                     pl.BlockSpec((query_blocks, part * rows, HEAD_SIZE),
                                  lambda i, s, h, c=c: (0, c, 0)),
-                    pl.BlockSpec((groups, 2, chunks, HEAD_SIZE, HEAD_SIZE),
-                                 lambda i, s, h: (0, 0, 0, 0, 0)),
+                    pl.BlockSpec(memory_space=pltpu.VMEM),
                     pl.BlockSpec((2, rows, HEAD_SIZE), lambda i, s, h: (0, 0, 0)),
                 ],
                 out_specs=pl.BlockSpec((query_blocks, rows + STAT_ROWS, width),

time: 142 us -> 142 us (level)
  transfers between devices with their start and end apart: 4 -> 4, of which waited for: 4 -> 4; matrix products, arithmetic and copies ran while one was open for 1% -> 1% of each run, Pallas kernels for 21% -> 22%
where the time goes in v17:
time: 142 us
  Pallas kernels  57.5 us (40%)
  waiting for transfers between devices  49 us (35%)
  starting transfers between devices  14.6 us (10%)
  between operations  13.5 us (10%)
  local copies, waits for them, and re-layouts  4.06 us (3%)
  other arithmetic  2.83 us (2%)
    pallas_call x2, Pallas kernels, local(): pl.pallas_call(kernel, grid_spec=pltpu.PrefetchScalarGridSpec(num_scalar_...  48.8 us
    all_to_all x2, waiting for transfers between devices, local(): got = lax.all_to_all(partial, 'help', 0, 0, tiled=True)  26 us
    all_gather x1, waiting for transfers between devices, local(): q_all = lax.all_gather(q[None], 'help', axis=0, tiled=True)  21.3 us
    all_to_all x2, starting transfers between devices, local(): got = lax.all_to_all(partial, 'help', 0, 0, tiled=True)  10.2 us
    pallas_call x2, Pallas kernels, local(): pl.pallas_call(functools.partial(join_kernel, sources=helpers, heads=part...  5.24 us
    all_to_all x1, starting transfers between devices, local(): held = lax.all_to_all(send, 'blk', 0, 0, tiled=True)  4.39 us
    pallas_call x1, Pallas kernels, local(): pl.pallas_call(functools.partial(relayout_kernel, wanted=wanted, chunks=c...  3.41 us
    unnamed x11, local copies, waits for them, and re-layouts  3.36 us
  transfers between devices with their start and end apart: 4, of which 4 were waited for; matrix products, arithmetic and copies ran while one was open for 1% of the time, Pallas kernels for 22%

profile of v17, /device:TPU:2, one launch (start us, length us, event | category | flops | bytes accessed | tf_op | source)
XLA Modules:
  0.0 141.5 jit_solution(17032757199363990665)
XLA Ops:
  6.5 0.0 all-gather.3.cloned.1.call-start
  6.5 0.7 convert_element_type.16
  7.2 0.1 copy.14
  7.3 0.1 convert_element_type.17
  7.4 1.0 copy.18
  8.5 0.7 fusion.1
  9.2 0.0 all-gather.3.cloned.1.call-update
  9.2 3.4 %shard_map.46 = bf16[8,2,4,128,128]{4,3,2,1,0:T(8,128)(2,1)} custom-call(bf16[512,2048]{1,0:T(8,128)(2,1)} %x_ref.1), custom_call_target="tpu_custom_call" | custom-call | tf_op jit(solution)/shard_map/pallas_call | solution.py:168
  12.6 0.0 copy-start.3
  12.6 4.4 %all-to-all-start = ((bf16[8,2,4,128,128]{4,3,2,1,0:T(8,128)(2,1)}), bf16[8,2,4,128,128]{4,3,2,1,0:T(8,128)(2,1)S(1)}, u32[]{:S(2)}, u32[]{:S(2)}) async-start(bf16[8,2,4,128,128]{4,3,2,1,0:T(8,128)(2,1)} %shard_map.46), calls=%async_computation | async-start | bytes 4194304 | tf_op jit(solution)/shard_map/all_to_all | solution.py:174
  17.0 0.0 copy-done.3
  17.0 0.1 copy.19
  17.1 0.1 constant_dynamic-slice_fusion
  17.3 0.1 copy.16
  17.5 21.3 %all-gather.3.cloned.1.call-done = bf16[4160,128]{1,0:T(8,128)(2,1)} async-done(((bf16[1040,128]{1,0:T(8,128)(2,1)}), bf16[4160,128]{1,0:T(8,128)(2,1)}) %all-gather.3.cloned.1.call-update) | async-done | bytes 1064976 | tf_op jit(solution)/shard_map/all_gather | solution.py:181
  38.8 0.7 slice_convert_fusion
  39.5 0.1 reshape.37
  39.6 0.7 compare_reduce_fusion
  40.4 0.1 reshape.38.sel_ref
  40.4 1.7 %all-to-all-done.kv_ref = bf16[8,2,4,128,128]{4,3,2,1,0:T(8,128)(2,1)S(1)} async-done(((bf16[8,2,4,128,128]{4,3,2,1,0:T(8,128)(2,1)}), bf16[8,2,4,128,128]{4,3,2,1,0:T(8,128)(2,1)S(1)}, u32[]{:S(2)}, u32[]{:S(2)}) %all-to-all-start) | async-done | bytes 2097184 | tf_op jit(solution)/shard_map/all_to_all | solution.py:174
  42.2 0.0 copy-start
  42.2 1.2 copy-done
  43.4 23.9 %shard_map.48 = f32[4,136,512]{2,1,0:T(8,128)} custom-call(s32[256]{0:T(256)S(1)} %reshape.38.sel_ref, s32[1]{0:T(128)} %bitcast.3.home_ref, bf16[4,1040,128]{2,1,0:T(8,128)(2,1)S(1)} %bitcast.22, bf16[8,2,4,128,128]{4,3,2,1,0:T(8,128)(2,1)S(1)} %all-to-all-done.kv_ref, bf16[2,128,128]{2,1,0:T(8,128)(2,1)S(1)} %pad_maximum_fusion.own_ref), custom_call_target="tpu_custom_call" | custom-call | flops 4294967296 | bytes 3145728 | tf_op jit(solution)/shard_map/pallas_call | solution.py:206
  67.3 0.0 copy-start.1
  67.3 6.7 %all-to-all-start.2 = ((f32[4,136,512]{2,1,0:T(8,128)}), f32[4,136,512]{2,1,0:T(8,128)}, u32[]{:S(2)}, u32[]{:S(2)}) async-start(f32[4,136,512]{2,1,0:T(8,128)} %shard_map.48), calls=%async_computation.2 | async-start | bytes 2228224 | tf_op jit(solution)/shard_map/all_to_all | solution.py:237
  74.0 0.0 copy-done.1
  74.0 24.9 %shard_map.47 = f32[4,136,512]{2,1,0:T(8,128)} custom-call(s32[256]{0:T(256)S(1)} %reshape.38.sel_ref, s32[1]{0:T(128)} %bitcast.3.home_ref, bf16[4,1040,128]{2,1,0:T(8,128)(2,1)S(1)} %bitcast.23, bf16[8,2,4,128,128]{4,3,2,1,0:T(8,128)(2,1)S(1)} %all-to-all-done.kv_ref, bf16[2,128,128]{2,1,0:T(8,128)(2,1)S(1)} %pad_maximum_fusion.own_ref), custom_call_target="tpu_custom_call" | custom-call | flops 4294967296 | bytes 3145728 | tf_op jit(solution)/shard_map/pallas_call | solution.py:206
  98.9 2.0 %all-to-all-done.2.got_ref = f32[4,136,512]{2,1,0:T(8,128)} async-done(((f32[4,136,512]{2,1,0:T(8,128)}), f32[4,136,512]{2,1,0:T(8,128)}, u32[]{:S(2)}, u32[]{:S(2)}) %all-to-all-start.2) | async-done | bytes 1114144 | tf_op jit(solution)/shard_map/all_to_all | solution.py:237
  100.9 3.5 %all-to-all-start.1 = ((f32[4,136,512]{2,1,0:T(8,128)}), f32[4,136,512]{2,1,0:T(8,128)S(1)}, u32[]{:S(2)}, u32[]{:S(2)}) async-start(f32[4,136,512]{2,1,0:T(8,128)} %shard_map.47), calls=%async_computation.1 | async-start | bytes 2228224 | tf_op jit(solution)/shard_map/all_to_all | solution.py:237
  104.5 2.6 %shard_map.49.refs_0_ = f32[128,1024]{1,0:T(8,128)} custom-call(f32[4,136,512]{2,1,0:T(8,128)} %all-to-all-done.2.got_ref), custom_call_target="tpu_custom_call" | custom-call | tf_op jit(solution)/shard_map/pallas_call | solution.py:239
  107.1 24.0 %all-to-all-done.1.got_ref = f32[4,136,512]{2,1,0:T(8,128)S(1)} async-done(((f32[4,136,512]{2,1,0:T(8,128)}), f32[4,136,512]{2,1,0:T(8,128)S(1)}, u32[]{:S(2)}, u32[]{:S(2)}) %all-to-all-start.1) | async-done | bytes 1114144 | tf_op jit(solution)/shard_map/all_to_all | solution.py:237
  131.0 0.0 copy-start.2
  131.1 1.0 copy-done.2
  132.0 2.6 %shard_map.50 = f32[128,1024]{1,0:T(8,128)} custom-call(f32[4,136,512]{2,1,0:T(8,128)} %copy-done.2, f32[128,1024]{1,0:T(8,128)} %shard_map.49.refs_0_), custom_call_target="tpu_custom_call", output_to_operand_aliasing={{}: (1, {})} | custom-call | tf_op jit(solution)/shard_map/pallas_call | solution.py:239
  (7 shorter events, 0.1 us)
Async XLA Ops:
  6.5 32.3 %all-gather.3.cloned.1.call-start = ((), (), s32[]{:S(2)}) async-start(), calls=%async_computation.3 | async-start | bytes 1331200 | tf_op jit(solution)/shard_map/all_gather | solution.py:181
  12.6 4.4 %copy-start.3 = (bf16[128,2048]{1,0:T(8,128)(2,1)S(1)}, bf16[128,2048]{1,0:T(8,128)(2,1)}, u32[]{:S(2)}) copy-start(bf16[128,2048]{1,0:T(8,128)(2,1)} %param.5) | copy-start | bytes 1572868
  12.6 29.5 %all-to-all-start = ((bf16[8,2,4,128,128]{4,3,2,1,0:T(8,128)(2,1)}), bf16[8,2,4,128,128]{4,3,2,1,0:T(8,128)(2,1)S(1)}, u32[]{:S(2)}, u32[]{:S(2)}) async-start(bf16[8,2,4,128,128]{4,3,2,1,0:T(8,128)(2,1)} %shard_map.46), calls=%async_computation | async-start | bytes 4194304 | tf_op jit(solution)/shard_map/all_to_all | solution.py:174
  42.2 1.2 copy-start
  67.3 6.7 %copy-start.1 = (bf16[4160,128]{1,0:T(8,128)(2,1)S(1)}, bf16[4160,128]{1,0:T(8,128)(2,1)}, u32[]{:S(2)}) copy-start(bf16[4160,128]{1,0:T(8,128)(2,1)} %all-gather.3.cloned.1.call-done) | copy-start | bytes 3194884
  67.3 33.6 %all-to-all-start.2 = ((f32[4,136,512]{2,1,0:T(8,128)}), f32[4,136,512]{2,1,0:T(8,128)}, u32[]{:S(2)}, u32[]{:S(2)}) async-start(f32[4,136,512]{2,1,0:T(8,128)} %shard_map.48), calls=%async_computation.2 | async-start | bytes 2228224 | tf_op jit(solution)/shard_map/all_to_all | solution.py:237
  100.9 30.1 %all-to-all-start.1 = ((f32[4,136,512]{2,1,0:T(8,128)}), f32[4,136,512]{2,1,0:T(8,128)S(1)}, u32[]{:S(2)}, u32[]{:S(2)}) async-start(f32[4,136,512]{2,1,0:T(8,128)} %shard_map.47), calls=%async_computation.1 | async-start | bytes 2228224 | tf_op jit(solution)/shard_map/all_to_all | solution.py:237
  131.0 1.0 copy-start.2
Sparse Core Ops, SparseCore 0:
  9.3 29.4 all-gather.2

commit v18 on v14

--- a/solution.py
+++ b/solution.py
@@ -62,16 +62,6 @@
 
     lax.fori_loop(0, groups, score, 0)
 
-    causal = lax.broadcasted_iota(jnp.int32, (rows, rows), 0) >= lax.broadcasted_iota(
-        jnp.int32, (rows, rows), 1)
-    s_own = jnp.dot(q_ref[home], own_ref[0],
-                    preferred_element_type=jnp.float32)
-    for h in range(heads):
-        s_h = jnp.where(causal, s_own[h * rows:(h + 1) * rows], -jnp.inf)
-        own_buf[h] = s_h
-        slot = home * heads + h
-        mpart[slot] = jnp.maximum(mpart[slot], fold(s_h, jnp.maximum))
-
     for slot in range(slots):
         m = jnp.max(mpart[slot], axis=1, keepdims=True) * factor
         m_scr[slot] = m
@@ -95,13 +85,6 @@
         return carry
 
     lax.fori_loop(0, groups, mix, 0)
-
-    for h in range(heads):
-        slot = home * heads + h
-        p = jnp.exp2(own_buf[h] * factor - mpart[slot][:, :1])
-        lpart[slot] += p
-        acc_scr[slot] += jnp.dot(p.astype(jnp.bfloat16), own_ref[1],
-                                 preferred_element_type=jnp.float32)
 
     for b in range(blocks):
         st_scr[...] = jnp.zeros(st_scr.shape, jnp.float32)
@@ -115,10 +98,33 @@
             out_ref[b, rows:, HEAD_SIZE:] = jnp.zeros((STAT_ROWS, (heads - 1) * HEAD_SIZE), jnp.float32)
 
 
-def join_kernel(got_ref, *refs, sources, heads):
+def own_kernel(q_ref, own_ref, out_ref, st_scr, *, heads, factor):
+    rows = QUERY_GROUP_ROWS
+    causal = lax.broadcasted_iota(jnp.int32, (rows, rows), 0) >= lax.broadcasted_iota(
+        jnp.int32, (rows, rows), 1)
+    for c in range(out_ref.shape[0]):
+        st_scr[...] = jnp.zeros(st_scr.shape, jnp.float32)
+        for h in range(heads):
+            column = (c * heads + h) * HEAD_SIZE
+            s = jnp.dot(q_ref[:, column:column + HEAD_SIZE], own_ref[0],
+                        preferred_element_type=jnp.float32)
+            s = jnp.where(causal, s, -jnp.inf)
+            m = jnp.max(s, axis=1, keepdims=True) * factor
+            p = jnp.exp2(s * factor - m)
+            out_ref[c, :rows, h * HEAD_SIZE:(h + 1) * HEAD_SIZE] = jnp.dot(
+                p.astype(jnp.bfloat16), own_ref[1], preferred_element_type=jnp.float32)
+            st_scr[:, h:h + 1] = m
+            st_scr[:, heads + h:heads + h + 1] = jnp.sum(p, axis=1, keepdims=True)
+        out_ref[c, rows:, :HEAD_SIZE] = st_scr[...].T[:STAT_ROWS]
+        if heads > 1:
+            out_ref[c, rows:, HEAD_SIZE:] = jnp.zeros((STAT_ROWS, (heads - 1) * HEAD_SIZE), jnp.float32)
+
+
+def join_kernel(got_ref, own_ref, *refs, sources, heads):
     rows = QUERY_GROUP_ROWS
     out_ref = refs[-1]
-    cols = [got_ref[s, rows:, :HEAD_SIZE].T for s in range(sources)]
+    blocks = [(got_ref, s) for s in range(sources)] + [(own_ref, 0)]
+    cols = [ref[s, rows:, :HEAD_SIZE].T for ref, s in blocks]
     for h in range(heads):
         ms = [c[:, h:h + 1] for c in cols]
         top = ms[0]
@@ -127,10 +133,10 @@
         top = jnp.where(top == -jnp.inf, 0.0, top)
         total = None
         acc = None
-        for s in range(sources):
-            fade = jnp.exp2(ms[s] - top)
-            part_total = fade * cols[s][:, heads + h:heads + h + 1]
-            part_acc = fade * got_ref[s, :rows, h * HEAD_SIZE:(h + 1) * HEAD_SIZE]
+        for (ref, s), col, m in zip(blocks, cols, ms):
+            fade = jnp.exp2(m - top)
+            part_total = fade * col[:, heads + h:heads + h + 1]
+            part_acc = fade * ref[s, :rows, h * HEAD_SIZE:(h + 1) * HEAD_SIZE]
             total = part_total if total is None else total + part_total
             acc = part_acc if acc is None else acc + part_acc
         out_ref[:, h * HEAD_SIZE:(h + 1) * HEAD_SIZE] = acc / total
@@ -197,6 +203,13 @@
     part = heads // slices
     assert part * slices == heads and 2 * part <= STAT_ROWS
     width = part * HEAD_SIZE
+    own_part = pl.pallas_call(
+        functools.partial(own_kernel, heads=part, factor=scale * math.log2(math.e)),
+        in_specs=[pl.BlockSpec(memory_space=pltpu.VMEM)] * 2,
+        out_specs=pl.BlockSpec(memory_space=pltpu.VMEM),
+        out_shape=jax.ShapeDtypeStruct((slices, rows + STAT_ROWS, width), jnp.float32),
+        scratch_shapes=[pltpu.VMEM((rows, HEAD_SIZE), jnp.float32)],
+    )(queries, own)
     result = None
     for c in range(slices):
         kernel = functools.partial(attend_kernel, groups=groups, heads=part, first=c * part,
@@ -240,12 +253,13 @@
         result = pl.pallas_call(
             functools.partial(join_kernel, sources=helpers, heads=part),
             grid=(1,),
-            in_specs=[pl.BlockSpec((helpers, rows + STAT_ROWS, width), lambda i: (0, 0, 0))]
+            in_specs=[pl.BlockSpec((helpers, rows + STAT_ROWS, width), lambda i: (0, 0, 0)),
+                      pl.BlockSpec((1, rows + STAT_ROWS, width), lambda i, c=c: (c, 0, 0))]
             + ([] if first_join else [pl.BlockSpec(memory_space=pl.ANY)]),
             out_specs=pl.BlockSpec((rows, width), lambda i, c=c: (0, c)),
             out_shape=jax.ShapeDtypeStruct((rows, heads * HEAD_SIZE), jnp.float32),
-            input_output_aliases={} if first_join else {1: 0},
-        )(*((got,) if first_join else (got, result)))
+            input_output_aliases={} if first_join else {2: 0},
+        )(*((got, own_part) if first_join else (got, own_part, result)))
     return result
 
 

time: 142 us -> 142 us (level)
  waiting for transfers between devices: 50.1 us -> 46.1 us
  Pallas kernels: 56.6 us -> 58.7 us
  starting transfers between devices: 14.5 us -> 16 us
    all_to_all x2, waiting for transfers between devices: 27 us -> 23.1 us  [local(): got = lax.all_to_all(partial, 'help', 0, 0, tiled=True)]
    pallas_call x0 -> x1, Pallas kernels: none -> 2.36 us  [local(): pl.pallas_call(functools.partial(own_kernel, heads=part, factor=scale * m...]
    all_to_all x2, starting transfers between devices: 10.2 us -> 11.6 us  [local(): got = lax.all_to_all(partial, 'help', 0, 0, tiled=True)]
    unnamed x11 -> x13, local copies, waits for them, and re-layouts: 3.36 us -> 3.35 us
  transfers between devices with their start and end apart: 4 -> 4, of which waited for: 4 -> 4; matrix products, arithmetic and copies ran while one was open for 1% -> 1% of each run, Pallas kernels for 21% -> 23%
where the time goes in v18:
time: 142 us; the launch traced here: 141 us
  Pallas kernels  58.7 us (41%)
  waiting for transfers between devices  46.1 us (32%)
  starting transfers between devices  16 us (11%)
  between operations  13.5 us (10%)
  local copies, waits for them, and re-layouts  4.06 us (3%)
  other arithmetic  2.84 us (2%)
    pallas_call x2, Pallas kernels, local(): pl.pallas_call(kernel, grid_spec=pltpu.PrefetchScalarGridSpec(num_scalar_...  47.2 us
    all_to_all x2, waiting for transfers between devices, local(): got = lax.all_to_all(partial, 'help', 0, 0, tiled=True)  23.1 us
    all_gather x1, waiting for transfers between devices, local(): q_all = lax.all_gather(q[None], 'help', axis=0, tiled=True)  21.3 us
    all_to_all x2, starting transfers between devices, local(): got = lax.all_to_all(partial, 'help', 0, 0, tiled=True)  11.6 us
    pallas_call x2, Pallas kernels, local(): pl.pallas_call(functools.partial(join_kernel, sources=helpers, heads=part...  5.67 us
    all_to_all x1, starting transfers between devices, local(): held = lax.all_to_all(send, 'blk', 0, 0, tiled=True)  4.39 us
    pallas_call x1, Pallas kernels, local(): pl.pallas_call(functools.partial(relayout_kernel, wanted=wanted, chunks=c...  3.41 us
    unnamed x13, local copies, waits for them, and re-layouts  3.35 us
  transfers between devices with their start and end apart: 4, of which 4 were waited for; matrix products, arithmetic and copies ran while one was open for 1% of the time, Pallas kernels for 23%

profile of v18, /device:TPU:2, one launch (start us, length us, event | category | flops | bytes accessed | tf_op | source)
XLA Modules:
  0.0 141.2 jit_solution(16728144080375073188)
XLA Ops:
  6.5 0.0 all-gather.3.cloned.1.call-start
  6.5 1.0 copy.18
  7.6 0.7 convert_element_type.16
  8.3 0.1 copy.14
  8.4 0.1 convert_element_type.17
  8.5 0.7 fusion.1
  9.2 0.0 all-gather.3.cloned.1.call-update
  9.2 3.4 %shard_map.46 = bf16[8,2,4,128,128]{4,3,2,1,0:T(8,128)(2,1)} custom-call(bf16[512,2048]{1,0:T(8,128)(2,1)} %x_ref.1), custom_call_target="tpu_custom_call" | custom-call | tf_op jit(solution)/shard_map/pallas_call | solution.py:174
  12.6 0.0 copy-start.4
  12.6 4.4 %all-to-all-start = ((bf16[8,2,4,128,128]{4,3,2,1,0:T(8,128)(2,1)}), bf16[8,2,4,128,128]{4,3,2,1,0:T(8,128)(2,1)S(1)}, u32[]{:S(2)}, u32[]{:S(2)}) async-start(bf16[8,2,4,128,128]{4,3,2,1,0:T(8,128)(2,1)} %shard_map.46), calls=%async_computation | async-start | bytes 4194304 | tf_op jit(solution)/shard_map/all_to_all | solution.py:180
  17.0 0.0 copy-done.4
  17.0 0.1 copy.19
  17.2 0.1 constant_dynamic-slice_fusion
  17.3 0.1 copy.16
  17.5 0.0 copy-start
  17.5 21.3 %all-gather.3.cloned.1.call-done = bf16[4160,128]{1,0:T(8,128)(2,1)} async-done(((bf16[1040,128]{1,0:T(8,128)(2,1)}), bf16[4160,128]{1,0:T(8,128)(2,1)}) %all-gather.3.cloned.1.call-update) | async-done | bytes 1064976 | tf_op jit(solution)/shard_map/all_gather | solution.py:187
  38.8 0.7 slice_convert_fusion
  39.5 0.1 reshape.37
  39.7 0.7 compare_reduce_fusion
  40.4 0.1 reshape.38.sel_ref
  40.5 1.7 %all-to-all-done.kv_ref = bf16[8,2,4,128,128]{4,3,2,1,0:T(8,128)(2,1)S(1)} async-done(((bf16[8,2,4,128,128]{4,3,2,1,0:T(8,128)(2,1)}), bf16[8,2,4,128,128]{4,3,2,1,0:T(8,128)(2,1)S(1)}, u32[]{:S(2)}, u32[]{:S(2)}) %all-to-all-start) | async-done | bytes 2097184 | tf_op jit(solution)/shard_map/all_to_all | solution.py:180
  42.2 0.0 copy-start.1
  42.2 1.2 copy-done.1
  43.4 22.9 %shard_map.49 = f32[4,136,512]{2,1,0:T(8,128)} custom-call(s32[256]{0:T(256)S(1)} %reshape.38.sel_ref, s32[1]{0:T(128)} %bitcast.3.home_ref, bf16[4,1040,128]{2,1,0:T(8,128)(2,1)S(1)} %bitcast.22, bf16[8,2,4,128,128]{4,3,2,1,0:T(8,128)(2,1)S(1)} %all-to-all-done.kv_ref, bf16[2,128,128]{2,1,0:T(8,128)(2,1)S(1)} %pad_maximum_fusion.own_ref), custom_call_target="tpu_custom_call" | custom-call | flops 4294967296 | bytes 3145728 | tf_op jit(solution)/shard_map/pallas_call | solution.py:219
  66.3 0.0 copy-start.2
  66.3 8.0 %all-to-all-start.2 = ((f32[4,136,512]{2,1,0:T(8,128)}), f32[4,136,512]{2,1,0:T(8,128)}, u32[]{:S(2)}, u32[]{:S(2)}) async-start(f32[4,136,512]{2,1,0:T(8,128)} %shard_map.49), calls=%async_computation.2 | async-start | bytes 2228224 | tf_op jit(solution)/shard_map/all_to_all | solution.py:251
  74.4 0.0 copy-done
  74.4 0.0 copy-done.2
  74.4 24.3 %shard_map.47 = f32[4,136,512]{2,1,0:T(8,128)} custom-call(s32[256]{0:T(256)S(1)} %reshape.38.sel_ref, s32[1]{0:T(128)} %bitcast.3.home_ref, bf16[4,1040,128]{2,1,0:T(8,128)(2,1)S(1)} %bitcast.23, bf16[8,2,4,128,128]{4,3,2,1,0:T(8,128)(2,1)S(1)} %all-to-all-done.kv_ref, bf16[2,128,128]{2,1,0:T(8,128)(2,1)S(1)} %pad_maximum_fusion.own_ref), custom_call_target="tpu_custom_call" | custom-call | flops 4294967296 | bytes 3145728 | tf_op jit(solution)/shard_map/pallas_call | solution.py:219
  98.7 1.8 %all-to-all-done.2.got_ref = f32[4,136,512]{2,1,0:T(8,128)} async-done(((f32[4,136,512]{2,1,0:T(8,128)}), f32[4,136,512]{2,1,0:T(8,128)}, u32[]{:S(2)}, u32[]{:S(2)}) %all-to-all-start.2) | async-done | bytes 1114144 | tf_op jit(solution)/shard_map/all_to_all | solution.py:251
  100.4 3.6 %all-to-all-start.1 = ((f32[4,136,512]{2,1,0:T(8,128)}), f32[4,136,512]{2,1,0:T(8,128)S(1)}, u32[]{:S(2)}, u32[]{:S(2)}) async-start(f32[4,136,512]{2,1,0:T(8,128)} %shard_map.47), calls=%async_computation.1 | async-start | bytes 2228224 | tf_op jit(solution)/shard_map/all_to_all | solution.py:251
  104.0 2.4 %shard_map.48.own_ref = f32[2,136,512]{2,1,0:T(8,128)} custom-call(bf16[128,1024]{1,0:T(8,128)(2,1)} %q_ref.1, bf16[2,128,128]{2,1,0:T(8,128)(2,1)} %copy-done), custom_call_target="tpu_custom_call" | custom-call | tf_op jit(solution)/shard_map/pallas_call | solution.py:206
  106.4 2.8 %shard_map.50.refs_0_ = f32[128,1024]{1,0:T(8,128)} custom-call(f32[4,136,512]{2,1,0:T(8,128)} %all-to-all-done.2.got_ref, f32[2,136,512]{2,1,0:T(8,128)} %shard_map.48.own_ref), custom_call_target="tpu_custom_call" | custom-call | tf_op jit(solution)/shard_map/pallas_call | solution.py:253
  109.2 21.3 %all-to-all-done.1.got_ref = f32[4,136,512]{2,1,0:T(8,128)S(1)} async-done(((f32[4,136,512]{2,1,0:T(8,128)}), f32[4,136,512]{2,1,0:T(8,128)S(1)}, u32[]{:S(2)}, u32[]{:S(2)}) %all-to-all-start.1) | async-done | bytes 1114144 | tf_op jit(solution)/shard_map/all_to_all | solution.py:251
  130.6 0.0 copy-start.3
  130.6 1.0 copy-done.3
  131.6 2.8 %shard_map.51 = f32[128,1024]{1,0:T(8,128)} custom-call(f32[4,136,512]{2,1,0:T(8,128)} %copy-done.3, f32[2,136,512]{2,1,0:T(8,128)} %shard_map.48.own_ref, f32[128,1024]{1,0:T(8,128)} %shard_map.50.refs_0_), custom_call_target="tpu_custom_call", output_to_operand_aliasing={{}: (2, {})} | custom-call | tf_op jit(solution)/shard_map/pallas_call | solution.py:253
  (7 shorter events, 0.1 us)
Async XLA Ops:
  6.5 32.3 %all-gather.3.cloned.1.call-start = ((), (), s32[]{:S(2)}) async-start(), calls=%async_computation.3 | async-start | bytes 1331200 | tf_op jit(solution)/shard_map/all_gather | solution.py:187
  12.6 4.4 %copy-start.4 = (bf16[128,2048]{1,0:T(8,128)(2,1)S(1)}, bf16[128,2048]{1,0:T(8,128)(2,1)}, u32[]{:S(2)}) copy-start(bf16[128,2048]{1,0:T(8,128)(2,1)} %param.5) | copy-start | bytes 1572868
  12.6 29.5 %all-to-all-start = ((bf16[8,2,4,128,128]{4,3,2,1,0:T(8,128)(2,1)}), bf16[8,2,4,128,128]{4,3,2,1,0:T(8,128)(2,1)S(1)}, u32[]{:S(2)}, u32[]{:S(2)}) async-start(bf16[8,2,4,128,128]{4,3,2,1,0:T(8,128)(2,1)} %shard_map.46), calls=%async_computation | async-start | bytes 4194304 | tf_op jit(solution)/shard_map/all_to_all | solution.py:180
  17.5 56.9 %copy-start = (bf16[2,128,128]{2,1,0:T(8,128)(2,1)}, bf16[2,128,128]{2,1,0:T(8,128)(2,1)S(1)}, u32[]{:S(2)}) copy-start(bf16[2,128,128]{2,1,0:T(8,128)(2,1)S(1)} %pad_maximum_fusion.own_ref) | copy-start | bytes 196612
  42.2 1.2 copy-start.1
  66.3 8.0 %copy-start.2 = (bf16[4160,128]{1,0:T(8,128)(2,1)S(1)}, bf16[4160,128]{1,0:T(8,128)(2,1)}, u32[]{:S(2)}) copy-start(bf16[4160,128]{1,0:T(8,128)(2,1)} %all-gather.3.cloned.1.call-done) | copy-start | bytes 3194884
  66.3 34.1 %all-to-all-start.2 = ((f32[4,136,512]{2,1,0:T(8,128)}), f32[4,136,512]{2,1,0:T(8,128)}, u32[]{:S(2)}, u32[]{:S(2)}) async-start(f32[4,136,512]{2,1,0:T(8,128)} %shard_map.49), calls=%async_computation.2 | async-start | bytes 2228224 | tf_op jit(solution)/shard_map/all_to_all | solution.py:251
  100.4 30.1 %all-to-all-start.1 = ((f32[4,136,512]{2,1,0:T(8,128)}), f32[4,136,512]{2,1,0:T(8,128)S(1)}, u32[]{:S(2)}, u32[]{:S(2)}) async-start(f32[4,136,512]{2,1,0:T(8,128)} %shard_map.47), calls=%async_computation.1 | async-start | bytes 2228224 | tf_op jit(solution)/shard_map/all_to_all | solution.py:251
  130.6 1.0 copy-start.3
Sparse Core Ops, SparseCore 0:
  9.4 29.4 all-gather.2

commit v19 on v18

--- a/solution.py
+++ b/solution.py
@@ -17,7 +17,11 @@
 STAT_ROWS = 8
 
 
-def relayout_kernel(x_ref, out_ref, *, wanted, chunks):
+def relayout_kernel(x_ref, q_ref, sel_ref, out_ref, q_out_ref, *, wanted, chunks, heads):
+    rows = QUERY_GROUP_ROWS
+    for h in range(heads):
+        q_out_ref[h * rows:(h + 1) * rows] = q_ref[:, h * HEAD_SIZE:(h + 1) * HEAD_SIZE]
+    q_out_ref[heads * rows:] = sel_ref[...]
     for t, kv_head in enumerate(wanted):
         for c in range(chunks):
             tokens = slice(c * HEAD_SIZE, (c + 1) * HEAD_SIZE)
@@ -171,19 +175,18 @@
 
     wanted = tuple((t * heads) // head_group for t in range(groups))
     chunks = piece // HEAD_SIZE
-    send = pl.pallas_call(
-        functools.partial(relayout_kernel, wanted=wanted, chunks=chunks),
-        in_specs=[pl.BlockSpec(memory_space=pltpu.VMEM)],
-        out_specs=pl.BlockSpec(memory_space=pltpu.VMEM),
-        out_shape=jax.ShapeDtypeStruct((groups, 2, chunks, HEAD_SIZE, HEAD_SIZE), jnp.bfloat16),
-    )(cached_key_value)
-    held = lax.all_to_all(send, "blk", 0, 0, tiled=True)
-
-    q = jnp.transpose(queries.reshape(rows, heads, HEAD_SIZE), (1, 0, 2)).reshape(heads * rows, HEAD_SIZE)
     sel_rows = selected.reshape(picks // HEAD_SIZE, HEAD_SIZE).astype(jnp.bfloat16)
     sel_pad = -(-(picks // HEAD_SIZE) // 16) * 16
     sel_rows = jnp.pad(sel_rows, ((0, sel_pad - picks // HEAD_SIZE), (0, 0)))
-    q = jnp.concatenate([q, sel_rows], axis=0)
+    send, q = pl.pallas_call(
+        functools.partial(relayout_kernel, wanted=wanted, chunks=chunks, heads=heads),
+        in_specs=[pl.BlockSpec(memory_space=pltpu.VMEM)] * 3,
+        out_specs=[pl.BlockSpec(memory_space=pltpu.VMEM)] * 2,
+        out_shape=[jax.ShapeDtypeStruct((groups, 2, chunks, HEAD_SIZE, HEAD_SIZE), jnp.bfloat16),
+                   jax.ShapeDtypeStruct((heads * rows + sel_pad, HEAD_SIZE), jnp.bfloat16)],
+    )(cached_key_value, queries, sel_rows)
+    held = lax.all_to_all(send, "blk", 0, 0, tiled=True)
+
     q_all = lax.all_gather(q[None], "help", axis=0, tiled=True)
     sel_all = q_all[:, heads * rows:heads * rows + picks // HEAD_SIZE].astype(jnp.int32).reshape(
         query_blocks, selected.shape[1], selected.shape[2])

time: 142 us -> 144 us (1.014); the launches traced: 141 us -> 141 us
  starting transfers between devices: 16 us -> 12.3 us
  Pallas kernels: 58.7 us -> 61.8 us
  waiting for transfers between devices: 46.1 us -> 47.6 us
    all_to_all x2, starting transfers between devices: 11.6 us -> 7.91 us  [local(): got = lax.all_to_all(partial, 'help', 0, 0, tiled=True)]
    all_gather x1, waiting for transfers between devices: 21.3 us -> 24.7 us  [local(): q_all = lax.all_gather(q[None], 'help', axis=0, tiled=True)]
    pallas_call x2, Pallas kernels: 47.2 us -> 50.2 us  [local(): pl.pallas_call(kernel, grid_spec=pltpu.PrefetchScalarGridSpec(num_scalar_...]
    all_to_all x1, waiting for transfers between devices: 1.72 us -> 0.01 us  [local(): held = lax.all_to_all(send, 'blk', 0, 0, tiled=True)]
    unnamed x13 -> x12, local copies, waits for them, and re-layouts: 3.35 us -> 2.37 us
  transfers between devices with their start and end apart: 4 -> 4, of which waited for: 4 -> 3; matrix products, arithmetic and copies ran while one was open for 1% -> 1% of each run, Pallas kernels for 23% -> 21%
where the time goes in v19:
time: 144 us; the launch traced here: 141 us
  Pallas kernels  61.8 us (43%)
  waiting for transfers between devices  47.6 us (33%)
  between operations  13.6 us (9%)
  starting transfers between devices  12.3 us (9%)
  local copies, waits for them, and re-layouts  3.63 us (3%)
  other arithmetic  2.1 us (1%)
    pallas_call x2, Pallas kernels, local(): pl.pallas_call(kernel, grid_spec=pltpu.PrefetchScalarGridSpec(num_scalar_...  50.2 us
    all_gather x1, waiting for transfers between devices, local(): q_all = lax.all_gather(q[None], 'help', axis=0, tiled=True)  24.7 us
    all_to_all x2, waiting for transfers between devices, local(): got = lax.all_to_all(partial, 'help', 0, 0, tiled=True)  22.9 us
    all_to_all x2, starting transfers between devices, local(): got = lax.all_to_all(partial, 'help', 0, 0, tiled=True)  7.91 us
    pallas_call x2, Pallas kernels, local(): pl.pallas_call(functools.partial(join_kernel, sources=helpers, heads=part...  5.67 us
    all_to_all x1, starting transfers between devices, local(): held = lax.all_to_all(send, 'blk', 0, 0, tiled=True)  4.4 us
    pallas_call x1, Pallas kernels, local(): pl.pallas_call(functools.partial(relayout_kernel, wanted=wanted, chunks=c...  3.56 us
  transfers between devices with their start and end apart: 4, of which 3 were waited for; matrix products, arithmetic and copies ran while one was open for 1% of the time, Pallas kernels for 21%

profile of v19, /device:TPU:2, one launch (start us, length us, event | category | flops | bytes accessed | tf_op | source)
XLA Modules:
  0.0 141.1 jit_solution(1879199090840221117)
XLA Ops:
  6.5 0.0 all-gather.3.cloned.1.call-start
  6.5 0.7 convert_element_type.16
  7.2 0.1 copy.12
  7.3 0.1 convert_element_type.17
  7.4 0.6 pad.4.sel_ref
  8.0 3.6 %shard_map.46 = (bf16[8,2,4,128,128]{4,3,2,1,0:T(8,128)(2,1)}, bf16[1040,128]{1,0:T(8,128)(2,1)}) custom-call(bf16[512,2048]{1,0:T(8,128)(2,1)} %x_ref.1, bf16[128,1024]{1,0:T(8,128)(2,1)} %q_ref.3, bf16[16,128]{1,0:T(8,128)(2,1)} %pad.4.sel_ref), custom_call_target="tpu_custom_call" | custom-call | tf_op jit(solution)/shard_map/pallas_call | solution.py:181
  11.6 0.0 all-gather.3.cloned.1.call-update
  11.6 0.0 copy-start.4
  11.6 4.4 %all-to-all-start = ((bf16[8,2,4,128,128]{4,3,2,1,0:T(8,128)(2,1)}), bf16[8,2,4,128,128]{4,3,2,1,0:T(8,128)(2,1)S(1)}, u32[]{:S(2)}, u32[]{:S(2)}) async-start(bf16[8,2,4,128,128]{4,3,2,1,0:T(8,128)(2,1)} %get-tuple-element.8), calls=%async_computation | async-start | bytes 4194304 | tf_op jit(solution)/shard_map/all_to_all | solution.py:188
  16.0 0.0 copy-done.4
  16.0 0.1 copy.16
  16.2 0.1 constant_dynamic-slice_fusion
  16.3 0.1 copy.14
  16.5 0.0 copy-start
  16.5 24.7 %all-gather.3.cloned.1.call-done = bf16[4160,128]{1,0:T(8,128)(2,1)} async-done(((bf16[1040,128]{1,0:T(8,128)(2,1)}), bf16[4160,128]{1,0:T(8,128)(2,1)}) %all-gather.3.cloned.1.call-update) | async-done | bytes 1064976 | tf_op jit(solution)/shard_map/all_gather | solution.py:190
  41.2 0.7 slice_convert_fusion
  41.9 0.1 reshape.29
  42.0 0.7 compare_reduce_fusion
  42.7 0.1 reshape.30.sel_ref
  42.8 0.0 all-to-all-done.kv_ref
  42.9 0.0 copy-start.1
  42.9 1.2 copy-done.1
  44.1 25.2 %shard_map.49 = f32[4,136,512]{2,1,0:T(8,128)} custom-call(s32[256]{0:T(256)S(1)} %reshape.30.sel_ref, s32[1]{0:T(128)} %bitcast.1.home_ref, bf16[4,1040,128]{2,1,0:T(8,128)(2,1)S(1)} %bitcast.17, bf16[8,2,4,128,128]{4,3,2,1,0:T(8,128)(2,1)S(1)} %all-to-all-done.kv_ref, bf16[2,128,128]{2,1,0:T(8,128)(2,1)S(1)} %pad_maximum_fusion.own_ref), custom_call_target="tpu_custom_call" | custom-call | flops 4294967296 | bytes 3145728 | tf_op jit(solution)/shard_map/pallas_call | solution.py:222
  69.3 0.0 copy-start.2
  69.3 4.4 %all-to-all-start.2 = ((f32[4,136,512]{2,1,0:T(8,128)}), f32[4,136,512]{2,1,0:T(8,128)}, u32[]{:S(2)}, u32[]{:S(2)}) async-start(f32[4,136,512]{2,1,0:T(8,128)} %shard_map.49), calls=%async_computation.2 | async-start | bytes 2228224 | tf_op jit(solution)/shard_map/all_to_all | solution.py:254
  73.7 0.0 copy-done
  73.7 0.0 copy-done.2
  73.7 25.0 %shard_map.47 = f32[4,136,512]{2,1,0:T(8,128)} custom-call(s32[256]{0:T(256)S(1)} %reshape.30.sel_ref, s32[1]{0:T(128)} %bitcast.1.home_ref, bf16[4,1040,128]{2,1,0:T(8,128)(2,1)S(1)} %bitcast.18, bf16[8,2,4,128,128]{4,3,2,1,0:T(8,128)(2,1)S(1)} %all-to-all-done.kv_ref, bf16[2,128,128]{2,1,0:T(8,128)(2,1)S(1)} %pad_maximum_fusion.own_ref), custom_call_target="tpu_custom_call" | custom-call | flops 4294967296 | bytes 3145728 | tf_op jit(solution)/shard_map/pallas_call | solution.py:222
  98.7 1.5 %all-to-all-done.2.got_ref = f32[4,136,512]{2,1,0:T(8,128)} async-done(((f32[4,136,512]{2,1,0:T(8,128)}), f32[4,136,512]{2,1,0:T(8,128)}, u32[]{:S(2)}, u32[]{:S(2)}) %all-to-all-start.2) | async-done | bytes 1114144 | tf_op jit(solution)/shard_map/all_to_all | solution.py:254
  100.2 3.5 %all-to-all-start.1 = ((f32[4,136,512]{2,1,0:T(8,128)}), f32[4,136,512]{2,1,0:T(8,128)S(1)}, u32[]{:S(2)}, u32[]{:S(2)}) async-start(f32[4,136,512]{2,1,0:T(8,128)} %shard_map.47), calls=%async_computation.1 | async-start | bytes 2228224 | tf_op jit(solution)/shard_map/all_to_all | solution.py:254
  103.8 2.4 %shard_map.48.own_ref = f32[2,136,512]{2,1,0:T(8,128)} custom-call(bf16[128,1024]{1,0:T(8,128)(2,1)} %q_ref.3, bf16[2,128,128]{2,1,0:T(8,128)(2,1)} %copy-done), custom_call_target="tpu_custom_call" | custom-call | tf_op jit(solution)/shard_map/pallas_call | solution.py:209
  106.2 2.8 %shard_map.50.refs_0_ = f32[128,1024]{1,0:T(8,128)} custom-call(f32[4,136,512]{2,1,0:T(8,128)} %all-to-all-done.2.got_ref, f32[2,136,512]{2,1,0:T(8,128)} %shard_map.48.own_ref), custom_call_target="tpu_custom_call" | custom-call | tf_op jit(solution)/shard_map/pallas_call | solution.py:256
  109.0 21.4 %all-to-all-done.1.got_ref = f32[4,136,512]{2,1,0:T(8,128)S(1)} async-done(((f32[4,136,512]{2,1,0:T(8,128)}), f32[4,136,512]{2,1,0:T(8,128)S(1)}, u32[]{:S(2)}, u32[]{:S(2)}) %all-to-all-start.1) | async-done | bytes 1114144 | tf_op jit(solution)/shard_map/all_to_all | solution.py:254
  130.4 0.0 copy-start.3
  130.4 1.0 copy-done.3
  131.4 2.8 %shard_map.51 = f32[128,1024]{1,0:T(8,128)} custom-call(f32[4,136,512]{2,1,0:T(8,128)} %copy-done.3, f32[2,136,512]{2,1,0:T(8,128)} %shard_map.48.own_ref, f32[128,1024]{1,0:T(8,128)} %shard_map.50.refs_0_), custom_call_target="tpu_custom_call", output_to_operand_aliasing={{}: (2, {})} | custom-call | tf_op jit(solution)/shard_map/pallas_call | solution.py:256
  (6 shorter events, 0.1 us)
Async XLA Ops:
  6.5 34.7 %all-gather.3.cloned.1.call-start = ((), (), s32[]{:S(2)}) async-start(), calls=%async_computation.3 | async-start | bytes 1331200 | tf_op jit(solution)/shard_map/all_gather | solution.py:190
  11.6 4.4 %copy-start.4 = (bf16[128,2048]{1,0:T(8,128)(2,1)S(1)}, bf16[128,2048]{1,0:T(8,128)(2,1)}, u32[]{:S(2)}) copy-start(bf16[128,2048]{1,0:T(8,128)(2,1)} %param.5) | copy-start | bytes 1572868
  11.6 31.2 %all-to-all-start = ((bf16[8,2,4,128,128]{4,3,2,1,0:T(8,128)(2,1)}), bf16[8,2,4,128,128]{4,3,2,1,0:T(8,128)(2,1)S(1)}, u32[]{:S(2)}, u32[]{:S(2)}) async-start(bf16[8,2,4,128,128]{4,3,2,1,0:T(8,128)(2,1)} %get-tuple-element.8), calls=%async_computation | async-start | bytes 4194304 | tf_op jit(solution)/shard_map/all_to_all | solution.py:188
  16.5 57.2 %copy-start = (bf16[2,128,128]{2,1,0:T(8,128)(2,1)}, bf16[2,128,128]{2,1,0:T(8,128)(2,1)S(1)}, u32[]{:S(2)}) copy-start(bf16[2,128,128]{2,1,0:T(8,128)(2,1)S(1)} %pad_maximum_fusion.own_ref) | copy-start | bytes 196612
  42.9 1.2 copy-start.1
  69.3 4.4 %copy-start.2 = (bf16[4160,128]{1,0:T(8,128)(2,1)S(1)}, bf16[4160,128]{1,0:T(8,128)(2,1)}, u32[]{:S(2)}) copy-start(bf16[4160,128]{1,0:T(8,128)(2,1)} %all-gather.3.cloned.1.call-done) | copy-start | bytes 3194884
  69.3 30.9 %all-to-all-start.2 = ((f32[4,136,512]{2,1,0:T(8,128)}), f32[4,136,512]{2,1,0:T(8,128)}, u32[]{:S(2)}, u32[]{:S(2)}) async-start(f32[4,136,512]{2,1,0:T(8,128)} %shard_map.49), calls=%async_computation.2 | async-start | bytes 2228224 | tf_op jit(solution)/shard_map/all_to_all | solution.py:254
  100.2 30.1 %all-to-all-start.1 = ((f32[4,136,512]{2,1,0:T(8,128)}), f32[4,136,512]{2,1,0:T(8,128)S(1)}, u32[]{:S(2)}, u32[]{:S(2)}) async-start(f32[4,136,512]{2,1,0:T(8,128)} %shard_map.47), calls=%async_computation.1 | async-start | bytes 2228224 | tf_op jit(solution)/shard_map/all_to_all | solution.py:254
  130.4 1.0 copy-start.3
Sparse Core Ops, SparseCore 0:
  11.7 29.4 all-gather.2
